TPU v7x, 32 devices: a whole 2x2x4 slice. The times are simulated.
32 devices in a mesh: gz: 8 (over y, x, core), sa: 4 (over z).
Axes of the slice: x: 2, y: 2, z: 4, core: 2. Of those that a mesh axis runs over, the one named last changes fastest.
Arguments:
- volume: bfloat16 [4, 4, 32, 16, 512], P('sa', None, 'gz'), may hold values from -6 to 6
- kernel_one: bfloat16 [32, 4, 3, 3, 3], replicated, may hold values from -0.625 to 0.625
- kernel_two: bfloat16 [64, 32, 3, 3, 3], replicated, may hold values from -0.21875 to 0.21875
- cotangent: bfloat16 [4, 64, 8, 4, 128], P('sa', None, 'gz'), may hold values from -6 to 6
Outputs:
- level_two: bfloat16 [4, 64, 8, 4, 128], P('sa', None, 'gz')
- grad_level_one: bfloat16 [4, 32, 16, 8, 256], P('sa', None, 'gz')
- grad_kernel_one: float32 [32, 4, 3, 3, 3], replicated
- grad_kernel_two: float32 [64, 32, 3, 3, 3], replicated
All inputs are finite; a program needn't handle non-finite values.
Results may differ from a plain program's by a relative error of at most 0.0057.
Values may be sent and summed in bfloat16 or wider, within the bound.
No kernel may reach another device: no remote copies, remote signals or barrier semaphores. Data moves between devices by JAX's collectives and lax.ppermute only.
A program may use at most 128 MiB of HBM per device.

v0:
```python
import math

import jax
import jax.numpy as jnp
from jax import lax
from jax.experimental import pallas as pl
from jax.experimental.pallas import tpu as pltpu
from jax.sharding import PartitionSpec as P

F32 = jnp.float32
BF16 = jnp.bfloat16


def shifted(block, axis, distance):
    devices = range(lax.axis_size(axis))
    route = [(i - distance, i) for i in devices if i - distance in devices]
    return lax.ppermute(block, axis, route)


def _sigmoid(v):
    return 1.0 / (1.0 + jnp.exp(-v))


def _shift_right(x):
    lane = lax.broadcasted_iota(jnp.int32, x.shape, x.ndim - 1)
    return jnp.where(lane == 0, 0.0, pltpu.roll(x, 1, x.ndim - 1))


def _shift_left(x):
    n = x.shape[-1]
    lane = lax.broadcasted_iota(jnp.int32, x.shape, x.ndim - 1)
    return jnp.where(lane == n - 1, 0.0, pltpu.roll(x, n - 1, x.ndim - 1))


def _nt(a, b):
    return lax.dot_general(a, b, (((1,), (1,)), ((), ())), preferred_element_type=F32)


def _kernel(vz_ref, k1_ref, k2_ref, k2t_ref, cot_ref,
            lvl_ref, g1_ref, s1_ref, s2_ref,
            tp, p1, t2, pre1, p2, bt, gs, gacc, b1, g1s):
    nzi, ny, rows0, lanes = vz_ref.shape
    n_act = p1.shape[0]
    ny1 = ny // 2
    ny2 = ny1 // 2
    c2 = t2.shape[2]
    c1 = c2 // 2

    tp[:, 0] = jnp.zeros((nzi, 2 * rows0, lanes), BF16)
    for zi in range(nzi):
        x = vz_ref[zi].astype(F32)
        tp[zi, 1:] = jnp.concatenate([x, _shift_right(x)], axis=1).astype(BF16)

    for a in range(n_act):
        for d in range(3):
            for y1 in range(ny1):
                p1[a, d * 3 * 2 * rows0:(d + 1) * 3 * 2 * rows0, y1 * lanes:(y1 + 1) * lanes] = (
                    tp[2 * a + d, 2 * y1:2 * y1 + 3].reshape(3 * 2 * rows0, lanes))

    k1 = k1_ref[...]
    t2[:, 0] = jnp.zeros((n_act, c2, lanes), BF16)
    for a in range(n_act):
        pre = jnp.dot(k1, p1[a], preferred_element_type=F32)
        if a in (1, 2):
            pre1[a - 1] = pre
        act = pre * _sigmoid(pre)
        for y1 in range(ny1):
            blk = act[:, y1 * lanes:(y1 + 1) * lanes]
            t2[a, y1 + 1] = jnp.concatenate([blk, _shift_right(blk)], axis=0).astype(BF16)

    for tt in range(2):
        for d in range(3):
            for y2 in range(ny2):
                p2[tt, d * 3 * c2:(d + 1) * 3 * c2, y2 * lanes:(y2 + 1) * lanes] = (
                    t2[2 * tt + d, 2 * y2:2 * y2 + 3].reshape(3 * c2, lanes))

    k2 = k2_ref[...]
    for tt in range(2):
        pre = jnp.dot(k2, p2[tt], preferred_element_type=F32)
        sig = _sigmoid(pre)
        if tt == 0:
            lvl_ref[...] = (pre * sig).astype(BF16)
        slope = sig * (1.0 + pre * (1.0 - sig))
        bt[tt] = (cot_ref[tt].astype(F32) * slope).astype(BF16)

    s2_ref[...] = _nt(bt[0], p2[0])

    gacc[...] = jnp.zeros(gacc.shape, F32)
    k2t = k2t_ref[...]
    for tt in range(2):
        if tt == 0:
            gs[...] = jnp.dot(k2t, bt[0], preferred_element_type=F32)
            taps_d = (1, 2)
        else:
            gs[0:3 * c2] = jnp.dot(k2t[0:3 * c2], bt[1], preferred_element_type=F32)
            taps_d = (0,)
        for d in taps_d:
            a = 2 * tt + d
            for h in range(3):
                for y2 in range(ny2):
                    y1 = 2 * y2 + h - 1
                    if y1 < 0:
                        continue
                    r0 = (d * 3 + h) * c2
                    blk = gs[r0:r0 + c2, y2 * lanes:(y2 + 1) * lanes]
                    gacc[a - 1, :, y1 * lanes:(y1 + 1) * lanes] += blk[:c1] + _shift_left(blk[c1:])

    half = c1 // 2
    for a_ in range(2):
        g = gacc[a_]
        pre = pre1[a_]
        sig = _sigmoid(pre)
        slope = sig * (1.0 + pre * (1.0 - sig))
        b1[a_] = (g * slope).astype(BF16)
        gb = g.astype(BF16)
        for y1 in range(ny1):
            blk = gb[:, y1 * lanes:(y1 + 1) * lanes]
            r0 = (a_ * ny1 + y1) * half
            g1s[r0:r0 + half] = jnp.concatenate([blk[:half], blk[half:]], axis=1)
    s1_ref[...] = _nt(b1[0], p1[1]) + _nt(b1[1], p1[2])

    n2 = 2 * lanes
    row = lax.broadcasted_iota(jnp.int32, (n2, n2), 0)
    col = lax.broadcasted_iota(jnp.int32, (n2, n2), 1)
    inter = jnp.where(col == 2 * (row % lanes) + row // lanes, 1.0, 0.0).astype(BF16)
    g1_ref[...] = jnp.dot(g1s[...], inter, preferred_element_type=F32).astype(BF16)


def _level_one_weights(k1):
    kt = jnp.transpose(k1, (0, 2, 3, 1, 4))
    w0, w1, w2 = kt[..., 0], kt[..., 1], kt[..., 2]
    z = jnp.zeros_like(w0)
    p0 = jnp.stack([jnp.stack([w1, w2, z, z], -1), jnp.stack([z, z, z, w0], -1)], 3)
    p1 = jnp.stack([jnp.stack([z, w0, w1, w2], -1), jnp.stack([z, z, z, z], -1)], 3)
    e = jnp.stack([p0, p1], 0)
    return e.reshape(2 * k1.shape[0], -1)


def _level_two_weights(k2):
    kt = jnp.transpose(k2, (0, 2, 3, 4, 1))
    w0, w1, w2 = kt[:, :, :, 0], kt[:, :, :, 1], kt[:, :, :, 2]
    z = jnp.zeros_like(w0)
    e = jnp.stack([jnp.stack([w1, w2], 3), jnp.stack([z, w0], 3)], 3)
    return e.reshape(k2.shape[0], -1)


def per_device(volume, kernel_one, kernel_two, cotangent):
    _, c0, nz, ny, nx = volume.shape
    c1 = kernel_one.shape[0]
    c2 = kernel_two.shape[0]
    assert nz == 4 and cotangent.shape[2] == 1
    q = nx // 4
    below = shifted(volume[:, :, 1:], "gz", 1)
    above = shifted(volume, "gz", -1)
    cot_above = shifted(cotangent, "gz", -1)
    ext = jnp.concatenate([below, volume, above], 2)[0]
    nzi = ext.shape[1]
    vz = ext.reshape(c0, nzi, ny, q, 4).transpose(1, 2, 0, 4, 3).reshape(nzi, ny, 4 * c0, q)
    n2 = cotangent.shape[3] * cotangent.shape[4]
    cots = jnp.concatenate([cotangent, cot_above], 2)[0].transpose(1, 0, 2, 3).reshape(2, c2, n2)

    k1m = _level_one_weights(kernel_one)
    k2m = _level_two_weights(kernel_two)
    k2t = k2m.T

    ny1, ny2 = ny // 2, ny // 4
    n_act = 5
    vm = pltpu.VMEM
    lvl, g1, s1, s2 = pl.pallas_call(
        _kernel,
        out_shape=(
            jax.ShapeDtypeStruct((c2, n2), BF16),
            jax.ShapeDtypeStruct((2 * ny1 * c1, 2 * q), BF16),
            jax.ShapeDtypeStruct(k1m.shape, F32),
            jax.ShapeDtypeStruct(k2m.shape, F32),
        ),
        scratch_shapes=[
            vm((nzi, ny + 1, 8 * c0, q), BF16),
            vm((n_act, k1m.shape[1], ny1 * q), BF16),
            vm((n_act, ny1 + 1, 4 * c1, q), BF16),
            vm((2, 2 * c1, ny1 * q), F32),
            vm((2, k2m.shape[1], n2), BF16),
            vm((2, c2, n2), BF16),
            vm((k2m.shape[1], n2), F32),
            vm((2, 2 * c1, ny1 * q), F32),
            vm((2, 2 * c1, ny1 * q), BF16),
            vm((2 * ny1 * c1, 2 * q), BF16),
        ],
        cost_estimate=pl.CostEstimate(flops=60_000_000, transcendentals=200_000, bytes_accessed=3_000_000),
    )(vz, k1m, k2m, k2t, cots)

    level_two = lvl.reshape(1, c2, 1, ny2, n2 // ny2)
    grad_one = g1.reshape(2, ny1, c1, 2 * q).transpose(2, 0, 1, 3)[None]

    s2r = s2.reshape(c2, 3, 3, 2, 2, c1)
    gk2 = jnp.stack([s2r[:, :, :, 1, 1], s2r[:, :, :, 0, 0], s2r[:, :, :, 0, 1]], -1)
    gk2 = gk2.transpose(0, 3, 1, 2, 4)
    s1r = s1.reshape(2, c1, 3, 3, 2, c0, 4)
    gk1 = jnp.stack([
        s1r[0, :, :, :, 1, :, 3] + s1r[1, :, :, :, 0, :, 1],
        s1r[0, :, :, :, 0, :, 0] + s1r[1, :, :, :, 0, :, 2],
        s1r[0, :, :, :, 0, :, 1] + s1r[1, :, :, :, 0, :, 3],
    ], -1).transpose(0, 3, 1, 2, 4)

    n1 = gk1.size
    total = lax.psum(jnp.concatenate([gk1.reshape(-1), gk2.reshape(-1)]), ("gz", "sa"))
    samples = volume.shape[0] * lax.axis_size("sa")
    cells_one = samples * (nz // 2) * lax.axis_size("gz") * ny1 * (nx // 2)
    cells_two = samples * cotangent.shape[2] * lax.axis_size("gz") * cotangent.shape[3] * cotangent.shape[4]
    grad_kernel_one = total[:n1].reshape(gk1.shape) / math.sqrt(float(cells_one))
    grad_kernel_two = total[n1:].reshape(gk2.shape) / math.sqrt(float(cells_two))
    return (level_two, grad_one, grad_kernel_one, grad_kernel_two)


def solution(mesh):
    placed = (P("sa", None, "gz", None, None), P(), P(), P("sa", None, "gz", None, None))
    return jax.shard_map(
        per_device,
        mesh=mesh,
        in_specs=placed,
        out_specs=(P("sa", None, "gz", None, None), P("sa", None, "gz", None, None), P(), P()),
        check_vma=False,
    )
```

profile of v0, /device:TPU:0, one launch (start us, length us, event | category | flops | bytes accessed | tf_op | source)
XLA Modules:
  0.0 227.2 jit_solution(5006716902975068902)
XLA Ops:
  7.2 0.0 all-reduce.6.cloned.1.call-start
  7.2 1.3 collective-permute-start.2
  8.5 1.3 collective-permute-start.1
  9.8 0.9 slice.67
  10.8 3.7 %collective-permute-start = (bf16[1,4,3,16,512]{4,3,2,1,0:T(8,128)(2,1)S(1)}, bf16[1,4,3,16,512]{4,3,2,1,0:T(8,128)(2,1)S(1)}, u32[]{:S(2)}, u32[]{:S(2)}) collective-permute-start(bf16[1,4,3,16,512]{4,3,2,1,0:T(8,128)(2,1)S(1)} %slice.67), channel_id=1, source_target_pairs={{0,4},{4,8},{8,12},{12,16},{16,20},{20,24},{24,28},{1,5},{5,9},{9,... | collective-permute-start | bytes 589832 | tf_op jit(solution)/shard_map/ppermute | solution.py:17
  14.4 0.7 slice.83
  15.2 0.7 slice.82
  15.9 0.8 pad_bitcast_fusion.2
  16.7 0.9 slice.84
  17.6 0.9 slice_bitcast_fusion.3
  18.5 0.1 pad_maximum_fusion.4
  18.6 0.1 maximum_bitcast_fusion.4
  18.7 0.1 maximum_bitcast_fusion.2
  18.8 0.1 pad_maximum_fusion.3
  18.9 0.1 copy.23
  19.0 0.1 reshape.115
  19.2 0.7 copy.26.k1_ref
  19.9 0.1 pad_maximum_fusion.1
  20.0 0.0 copy-start
  20.0 0.8 copy.27.k2_ref
  20.8 0.0 collective-permute-done.2
  20.8 0.9 maximum_bitcast_fusion.1
  21.8 0.1 reshape.124
  21.8 0.7 copy.41.cot_ref
  22.5 0.0 collective-permute-done
  22.5 0.0 collective-permute-done.1
  22.5 1.0 pad_maximum_fusion
  23.5 4.4 %copy.21 = bf16[1,4,11,16,512]{3,4,2,1,0:T(8,128)(2,1)} copy(bf16[1,4,11,16,512]{4,3,2,1,0:T(8,128)(2,1)S(1)} %pad_maximum_fusion) | data formatting | bytes 1441792 | tf_op jit(solution)/shard_map/concatenate | solution.py:156
  27.9 9.2 %copy.22 = bf16[11,16,4,4,128]{4,3,2,1,0:T(4,128)(2,1)} copy(bf16[11,16,4,4,128]{1,3,4,0,2:T(4,128)(2,1)} %bitcast.64) | data formatting | bytes 1441792 | tf_op jit(solution)/shard_map/transpose | solution.py:158
  37.1 0.0 copy-done
  37.1 5.1 %shard_map.75 = (bf16[64,512]{1,0:T(8,128)(2,1)}, bf16[512,256]{1,0:T(8,128)(2,1)}, f32[64,288]{1,0:T(8,128)}, f32[64,1152]{1,0:T(8,128)}) custom-call(bf16[11,16,16,128]{3,2,1,0:T(8,128)(2,1)} %bitcast.65, bf16[64,288]{1,0:T(8,128)(2,1)} %copy.26.k1_ref, bf16[64,1152]{1,0:T(8,128)(2,1)} %copy.27.k2_ref, bf16[1152,64]{1,0:T(8,128)(2,1)} %bitcast.67, ...), custom_call_target="tpu_custom_call" | custom-call | flops 60000000 | bytes 3000000 | tf_op jit(solution)/shard_map/pallas_call | solution.py:169
  42.2 1.0 copy.29
  43.2 0.2 reshape.120
  43.4 0.1 fusion
  43.5 1.2 copy.34
  44.8 0.5 copy.33
  45.3 0.4 reshape.121
  45.8 0.0 copy-start.2
  45.8 0.0 copy-start.1
  45.8 12.3 %copy.37 = f32[64,32,3,3,3]{4,3,2,1,0:T(4,128)} copy(f32[64,32,3,3,3]{0,1,3,2,4:T(8,128)S(1)} %maximum_bitcast_fusion) | data formatting | bytes 442368 | tf_op jit(solution)/shard_map/transpose | solution.py:197
  58.1 10.4 %reshape.123 = f32[55296]{0:T(1024)S(1)} reshape(f32[64,32,3,3,3]{4,3,2,1,0:T(4,128)} %copy.37) | data formatting | bytes 442368 | tf_op jit(solution)/shard_map/reshape | solution.py:206
  68.5 0.7 pad_maximum_fusion.2
  69.2 0.0 all-reduce.6.cloned.1.call-update
  69.2 0.0 copy-done.2
  69.2 0.6 reshape.118
  69.9 0.0 copy-done.1
  69.9 0.9 copy.47
  70.7 126.4 %all-reduce.6.cloned.1.call-done = f32[58752]{0:T(1024)} async-done(((f32[58752]{0:T(1024)}), f32[58752]{0:T(1024)}) %all-reduce.6.cloned.1.call-update) | async-done | bytes 235024 | tf_op jit(solution)/shard_map/psum | solution.py:206
  197.2 0.7 slice_multiply_fusion.1
  197.9 0.5 div.18
  198.4 1.0 copy.39
  199.5 1.0 slice_multiply_fusion
  200.4 8.3 %div.21 = f32[64,32,3,3,3]{4,3,2,1,0:T(4,128)} reshape(f32[55296]{0:T(1024)S(1)} %slice_multiply_fusion) | data formatting | bytes 442368 | tf_op jit(solution)/shard_map/div | solution.py:211
  208.7 11.7 %copy.40 = f32[64,32,3,3,3]{0,1,4,3,2:T(8,128)} copy(f32[64,32,3,3,3]{4,3,2,1,0:T(4,128)} %div.21) | data formatting | bytes 442368
  (7 shorter events, 0.1 us)
Async XLA Ops:
  7.2 190.0 %all-reduce.6.cloned.1.call-start = ((), (), s32[]{:S(2)}) async-start(), calls=%async_computation | async-start | bytes 475136 | tf_op jit(solution)/shard_map/psum | solution.py:206
  7.2 13.6 %collective-permute-start.2 = (bf16[1,64,1,4,128]{4,3,2,1,0:T(4,128)(2,1)}, bf16[1,64,1,4,128]{4,3,2,1,0:T(4,128)(2,1)S(1)}, u32[]{:S(2)}, u32[]{:S(2)}) collective-permute-start(bf16[1,64,1,4,128]{4,3,2,1,0:T(4,128)(2,1)} %param.7), channel_id=1, source_target_pairs={{4,0},{8,4},{12,8},{16,12},{20,16},{24,20},{28,24},{5,1},{9,5},{13... | collective-permute-start | bytes 196616 | tf_op jit(solution)/shard_map/ppermute | solution.py:17
  8.5 14.0 %collective-permute-start.1 = (bf16[1,4,4,16,512]{4,3,2,1,0:T(8,128)(2,1)}, bf16[1,4,4,16,512]{4,3,2,1,0:T(8,128)(2,1)S(1)}, u32[]{:S(2)}, u32[]{:S(2)}) collective-permute-start(bf16[1,4,4,16,512]{4,3,2,1,0:T(8,128)(2,1)} %param.4), channel_id=1, source_target_pairs={{4,0},{8,4},{12,8},{16,12},{20,16},{24,20},{28,24},{5,1},{9,5},{13... | collective-permute-start | bytes 786440 | tf_op jit(solution)/shard_map/ppermute | solution.py:17
  10.8 11.7 %collective-permute-start = (bf16[1,4,3,16,512]{4,3,2,1,0:T(8,128)(2,1)S(1)}, bf16[1,4,3,16,512]{4,3,2,1,0:T(8,128)(2,1)S(1)}, u32[]{:S(2)}, u32[]{:S(2)}) collective-permute-start(bf16[1,4,3,16,512]{4,3,2,1,0:T(8,128)(2,1)S(1)} %slice.67), channel_id=1, source_target_pairs={{0,4},{4,8},{8,12},{12,16},{16,20},{20,24},{24,28},{1,5},{5,9},{9,... | collective-permute-start | bytes 589832 | tf_op jit(solution)/shard_map/ppermute | solution.py:17
  20.0 17.1 %copy-start = (bf16[64,3,3,2,2,32]{0,5,4,3,2,1:T(8,128)(2,1)}, bf16[64,3,3,2,2,32]{0,5,4,3,2,1:T(8,128)(2,1)S(1)}, u32[]{:S(2)}) copy-start(bf16[64,3,3,2,2,32]{0,5,4,3,2,1:T(8,128)(2,1)S(1)} %copy.24) | copy-start | bytes 442372
  45.8 23.4 %copy-start.2 = (bf16[64,512]{1,0:T(8,128)(2,1)S(1)}, bf16[64,512]{1,0:T(8,128)(2,1)}, u32[]{:S(2)}) copy-start(bf16[64,512]{1,0:T(8,128)(2,1)} %get-tuple-element.8) | copy-start | bytes 196612
  45.8 24.1 %copy-start.1 = (bf16[512,256]{1,0:T(8,128)(2,1)S(1)}, bf16[512,256]{1,0:T(8,128)(2,1)}, u32[]{:S(2)}) copy-start(bf16[512,256]{1,0:T(8,128)(2,1)} %get-tuple-element.9) | copy-start | bytes 786436
Sparse Core Ops, SparseCore 0:
  69.3 127.7 all-reduce.5
where the time goes:
time: 228 us; the launch traced here: 227 us
  waiting for transfers between devices  126 us (55%)
  local copies, waits for them, and re-layouts  70.2 us (31%)
  between operations  14.3 us (6%)
  starting transfers between devices  6.3 us (3%)
  Pallas kernels  5.13 us (2%)
  other arithmetic  4.92 us (2%)
    psum x1, waiting for transfers between devices, per_device(): lax.psum(jnp.concatenate([gk1.reshape(-1), gk2.reshape(-1)]), ('gz', 'sa'))  126 us
    unnamed x8, local copies, waits for them, and re-layouts  12.7 us
    transpose x1, local copies, waits for them, and re-layouts, per_device(): gk2 = gk2.transpose(0, 3, 1, 2, 4)  12.3 us
    reshape x1, local copies, waits for them, and re-layouts, per_device(): gk2.reshape(-1)  10.4 us
    transpose x1, local copies, waits for them, and re-layouts, per_device(): ext.reshape(c0, nzi, ny, q, 4).transpose(1, 2, 0, 4, 3)  9.18 us
    div x1, local copies, waits for them, and re-layouts, per_device(): total[n1:].reshape(gk2.shape) / math.sqrt(float(cells_two))  8.31 us
    ppermute x3, starting transfers between devices, shifted(): return lax.ppermute(block, axis, route)  6.26 us
    pallas_call x1, Pallas kernels, per_device(): pl.pallas_call(_kernel, out_shape=(jax.ShapeDtypeStruct((c2, n2), BF16),...  5.13 us
  transfers between devices with their start and end apart: 4, of which 1 were waited for; matrix products, arithmetic and copies ran while one was open for 5% of the time, Pallas kernels for 0%

commit v1 on v0

--- a/solution.py
+++ b/solution.py
@@ -15,6 +15,17 @@
     devices = range(lax.axis_size(axis))
     route = [(i - distance, i) for i in devices if i - distance in devices]
     return lax.ppermute(block, axis, route)
+
+
+def _all_sum(x, axes):
+    for axis in axes:
+        n = lax.axis_size(axis)
+        assert n & (n - 1) == 0
+        k = 1
+        while k < n:
+            x = x + lax.ppermute(x, axis, [(i, i ^ k) for i in range(n)])
+            k *= 2
+    return x
 
 
 def _sigmoid(v):
@@ -83,7 +94,15 @@
         slope = sig * (1.0 + pre * (1.0 - sig))
         bt[tt] = (cot_ref[tt].astype(F32) * slope).astype(BF16)
 
-    s2_ref[...] = _nt(bt[0], p2[0])
+    dup = _nt(p2[0], jnp.concatenate([bt[0], bt[0]], axis=0))
+    c2n = dup.shape[1] // 2
+    qi = c1 // 4
+    lane2 = lax.broadcasted_iota(jnp.int32, (qi, 2 * c2n), 1)
+    for dh in range(9):
+        for w, off in enumerate((3 * c1 // 2, 0, c1 // 2)):
+            r0 = dh * c2 + off
+            s2_ref[(dh * 3 + w) * qi:(dh * 3 + w + 1) * qi] = jnp.where(
+                lane2 < c2n, dup[r0:r0 + qi], dup[r0 + qi:r0 + 2 * qi])
 
     gacc[...] = jnp.zeros(gacc.shape, F32)
     k2t = k2t_ref[...]
@@ -117,7 +136,7 @@
             blk = gb[:, y1 * lanes:(y1 + 1) * lanes]
             r0 = (a_ * ny1 + y1) * half
             g1s[r0:r0 + half] = jnp.concatenate([blk[:half], blk[half:]], axis=1)
-    s1_ref[...] = _nt(b1[0], p1[1]) + _nt(b1[1], p1[2])
+    s1_ref[...] = _nt(p1[1], b1[0]) + _nt(p1[2], b1[1])
 
     n2 = 2 * lanes
     row = lax.broadcasted_iota(jnp.int32, (n2, n2), 0)
@@ -171,8 +190,8 @@
         out_shape=(
             jax.ShapeDtypeStruct((c2, n2), BF16),
             jax.ShapeDtypeStruct((2 * ny1 * c1, 2 * q), BF16),
-            jax.ShapeDtypeStruct(k1m.shape, F32),
-            jax.ShapeDtypeStruct(k2m.shape, F32),
+            jax.ShapeDtypeStruct((k1m.shape[1], k1m.shape[0]), F32),
+            jax.ShapeDtypeStruct((27 * c1 // 2, 2 * c2), F32),
         ),
         scratch_shapes=[
             vm((nzi, ny + 1, 8 * c0, q), BF16),
@@ -192,23 +211,22 @@
     level_two = lvl.reshape(1, c2, 1, ny2, n2 // ny2)
     grad_one = g1.reshape(2, ny1, c1, 2 * q).transpose(2, 0, 1, 3)[None]
 
-    s2r = s2.reshape(c2, 3, 3, 2, 2, c1)
-    gk2 = jnp.stack([s2r[:, :, :, 1, 1], s2r[:, :, :, 0, 0], s2r[:, :, :, 0, 1]], -1)
-    gk2 = gk2.transpose(0, 3, 1, 2, 4)
-    s1r = s1.reshape(2, c1, 3, 3, 2, c0, 4)
+    s1r = s1.reshape(3, 3, 2, c0, 4, 2, c1)
     gk1 = jnp.stack([
-        s1r[0, :, :, :, 1, :, 3] + s1r[1, :, :, :, 0, :, 1],
-        s1r[0, :, :, :, 0, :, 0] + s1r[1, :, :, :, 0, :, 2],
-        s1r[0, :, :, :, 0, :, 1] + s1r[1, :, :, :, 0, :, 3],
-    ], -1).transpose(0, 3, 1, 2, 4)
-
-    n1 = gk1.size
-    total = lax.psum(jnp.concatenate([gk1.reshape(-1), gk2.reshape(-1)]), ("gz", "sa"))
+        s1r[:, :, 1, :, 3, 0] + s1r[:, :, 0, :, 1, 1],
+        s1r[:, :, 0, :, 0, 0] + s1r[:, :, 0, :, 2, 1],
+        s1r[:, :, 0, :, 1, 0] + s1r[:, :, 0, :, 3, 1],
+    ], 2)
+    rows1 = gk1.size // s2.shape[1]
+    total = _all_sum(jnp.concatenate([gk1.reshape(rows1, s2.shape[1]), s2], 0), ("gz", "sa"))
     samples = volume.shape[0] * lax.axis_size("sa")
     cells_one = samples * (nz // 2) * lax.axis_size("gz") * ny1 * (nx // 2)
     cells_two = samples * cotangent.shape[2] * lax.axis_size("gz") * cotangent.shape[3] * cotangent.shape[4]
-    grad_kernel_one = total[:n1].reshape(gk1.shape) / math.sqrt(float(cells_one))
-    grad_kernel_two = total[n1:].reshape(gk2.shape) / math.sqrt(float(cells_two))
+    t1 = total[:rows1] / math.sqrt(float(cells_one))
+    t2 = total[rows1:] / math.sqrt(float(cells_two))
+    grad_kernel_one = t1.reshape(3, 3, 3, c0, c1).transpose(4, 3, 0, 1, 2)
+    t2 = t2.reshape(27, c1 // 2, 2, c2).transpose(0, 2, 1, 3).reshape(3, 3, 3, c1, c2)
+    grad_kernel_two = t2.transpose(4, 3, 0, 1, 2)
     return (level_two, grad_one, grad_kernel_one, grad_kernel_two)
 
 

time: 228 us -> 80.8 us (0.35)
  waiting for transfers between devices: 126 us -> 23 us
  local copies, waits for them, and re-layouts: 70.2 us -> 27.4 us
  between operations: 14.3 us -> 0.84 us
  starting transfers between devices: 6.3 us -> 18.6 us
    psum x1 -> x0, waiting for transfers between devices: 126 us -> none  [per_device(): lax.psum(jnp.concatenate([gk1.reshape(-1), gk2.reshape(-1)]), ('gz', 'sa'))]
    ppermute x0 -> x5, waiting for transfers between devices: none -> 23 us  [_all_sum(): x = x + lax.ppermute(x, axis, [(i, i ^ k) for i in range(n)])]
    ppermute x0 -> x5, starting transfers between devices: none -> 13 us  [_all_sum(): x = x + lax.ppermute(x, axis, [(i, i ^ k) for i in range(n)])]
    unnamed x8 -> x2, local copies, waits for them, and re-layouts: 12.7 us -> 0.01 us
    transpose x2 -> x1, local copies, waits for them, and re-layouts: 12.8 us -> 0.79 us  [per_device(): t2.reshape(27, c1 // 2, 2, c2).transpose(0, 2, 1, 3)]
    div x2 -> x0, local copies, waits for them, and re-layouts: 8.82 us -> none  [the longest x1 8.31 us: per_device(): total[n1:].reshape(gk2.shape) / math.sqrt(float(cells_two))]
    reshape x3 -> x4, local copies, waits for them, and re-layouts: 11 us -> 2.18 us  [the longest x1 1.11 us: per_device(): s1r = s1.reshape(3, 3, 2, c0, 4, 2, c1)]
  transfers between devices with their start and end apart: 4 -> 8, of which waited for: 1 -> 5; matrix products, arithmetic and copies ran while one was open for 5% -> 15% of each run, Pallas kernels for 0% -> 0%
where the time goes in v1:
time: 80.8 us; the launch traced here: 80 us
  local copies, waits for them, and re-layouts  27.4 us (34%)
  waiting for transfers between devices  23 us (28%)
  starting transfers between devices  18.6 us (23%)
  Pallas kernels  5.5 us (7%)
  other arithmetic  4.59 us (6%)
  between operations  0.84 us (1%)
    ppermute x5, waiting for transfers between devices, _all_sum(): x = x + lax.ppermute(x, axis, [(i, i ^ k) for i in range(n)])  23 us
    ppermute x5, starting transfers between devices, _all_sum(): x = x + lax.ppermute(x, axis, [(i, i ^ k) for i in range(n)])  13 us
    transpose x1, local copies, waits for them, and re-layouts, per_device(): ext.reshape(c0, nzi, ny, q, 4).transpose(1, 2, 0, 4, 3)  9.19 us
    ppermute x3, starting transfers between devices, shifted(): return lax.ppermute(block, axis, route)  5.63 us
    pallas_call x1, Pallas kernels, per_device(): pl.pallas_call(_kernel, out_shape=(jax.ShapeDtypeStruct((c2, n2), BF16),...  5.5 us
    concatenate x1, local copies, waits for them, and re-layouts, per_device(): ext = jnp.concatenate([below, volume, above], 2)[0]  4.39 us
    reshape x1, local copies, waits for them, and re-layouts, per_device(): grad_one = g1.reshape(2, ny1, c1, 2 * q).transpose(2, 0, 1, 3)[None]  1.8 us
  transfers between devices with their start and end apart: 8, of which 5 were waited for; matrix products, arithmetic and copies ran while one was open for 15% of the time, Pallas kernels for 0%

profile of v1, /device:TPU:0, one launch (start us, length us, event | category | flops | bytes accessed | tf_op | source)
XLA Modules:
  0.0 80.0 jit_solution(10428846025228042111)
XLA Ops:
  0.6 1.3 %collective-permute-start.1 = (bf16[1,4,4,16,512]{4,3,2,1,0:T(8,128)(2,1)}, bf16[1,4,4,16,512]{4,3,2,1,0:T(8,128)(2,1)S(1)}, u32[]{:S(2)}, u32[]{:S(2)}) collective-permute-start(bf16[1,4,4,16,512]{4,3,2,1,0:T(8,128)(2,1)} %param.4), channel_id=1, source_target_pairs={{4,0},{8,4},{12,8},{16,12},{20,16},{24,20},{28,24},{5,1},{9,5},{13... | collective-permute-start | bytes 786440 | tf_op jit(solution)/shard_map/ppermute | solution.py:17
  1.9 0.9 %slice.42 = bf16[1,4,3,16,512]{4,3,2,1,0:T(8,128)(2,1)S(1)} slice(bf16[1,4,4,16,512]{4,3,2,1,0:T(8,128)(2,1)} %param.4), slice={[0:1], [0:4], [1:4], [0:16], [0:512]} | slice | bytes 393216 | tf_op jit(solution)/shard_map/slice | solution.py:172
  2.9 3.0 %collective-permute-start = (bf16[1,4,3,16,512]{4,3,2,1,0:T(8,128)(2,1)S(1)}, bf16[1,4,3,16,512]{4,3,2,1,0:T(8,128)(2,1)S(1)}, u32[]{:S(2)}, u32[]{:S(2)}) collective-permute-start(bf16[1,4,3,16,512]{4,3,2,1,0:T(8,128)(2,1)S(1)} %slice.42), channel_id=1, source_target_pairs={{0,4},{4,8},{8,12},{12,16},{16,20},{20,24},{24,28},{1,5},{5,9},{9,... | collective-permute-start | bytes 589832 | tf_op jit(solution)/shard_map/ppermute | solution.py:17
  5.9 1.3 %collective-permute-start.2 = (bf16[1,64,1,4,128]{4,3,2,1,0:T(4,128)(2,1)}, bf16[1,64,1,4,128]{4,3,2,1,0:T(4,128)(2,1)S(1)}, u32[]{:S(2)}, u32[]{:S(2)}) collective-permute-start(bf16[1,64,1,4,128]{4,3,2,1,0:T(4,128)(2,1)} %param.7), channel_id=1, source_target_pairs={{4,0},{8,4},{12,8},{16,12},{20,16},{24,20},{28,24},{5,1},{9,5},{13... | collective-permute-start | bytes 196616 | tf_op jit(solution)/shard_map/ppermute | solution.py:17
  7.2 0.8 pad_bitcast_fusion.2
  8.0 0.7 slice.55
  8.7 0.7 slice.54
  9.5 0.9 %slice.56 = bf16[64,3,3,1,32]{0,4,3,2,1:T(8,128)(2,1)S(1)} slice(bf16[64,3,3,3,32]{0,4,3,2,1:T(8,128)(2,1)} %bitcast.61), slice={[0:64], [0:3], [0:3], [0:1], [0:32]} | slice | bytes 73728 | tf_op jit(solution)/shard_map/slice | solution.py:160
  10.4 0.9 %slice_bitcast_fusion = (bf16[64,3,3,1,2,32]{0,5,4,2,1,3:T(8,128)(2,1)S(1)}, bf16[64,3,3,1,2,32]{0,5,4,2,1,3:T(8,128)(2,1)S(1)}) fusion(bf16[64,3,3,3,32]{0,4,3,2,1:T(8,128)(2,1)} %bitcast.62, bf16[64,3,3,1,32]{0,4,3,2,1:T(8,128)(2,1)S(1)} %slice.56), kind=kLoop, calls=%fused_computation.5 | loop fusion | bytes 258048 | tf_op jit(solution)/shard_map/stack | solution.py:162
  11.3 0.1 pad_maximum_fusion.5
  11.4 0.1 maximum_bitcast_fusion.2
  11.5 0.1 maximum_bitcast_fusion.1
  11.6 0.1 pad_maximum_fusion.3
  11.7 0.1 copy.24
  11.8 0.1 reshape.96
  12.0 0.7 copy.27.k1_ref
  12.7 0.1 pad_maximum_fusion.1
  12.8 0.0 copy-start
  12.8 0.8 %copy.28.k2_ref = bf16[64,1152]{1,0:T(8,128)(2,1)} copy(bf16[64,1152]{0,1:T(8,128)(2,1)S(1)} %bitcast.55) | data formatting | bytes 294912 | tf_op jit(solution)/shard_map/reshape | solution.py:163
  13.6 0.0 collective-permute-done.2
  13.6 0.9 %maximum_bitcast_fusion = bf16[2,64,4,128]{3,2,0,1:T(4,128)(2,1)S(1)} fusion(bf16[1,64,1,4,128]{4,3,2,1,0:T(4,128)(2,1)S(1)} %collective-permute-done.2, bf16[1,64,1,4,128]{4,3,2,1,0:T(4,128)(2,1)} %param.7), kind=kLoop, calls=%fused_computation.8 | loop fusion | flops 65536 | bytes 262144 | tf_op jit(solution)/shard_map/transpose | solution.py:179
  14.5 0.1 reshape.106
  14.6 0.7 copy.37.cot_ref
  15.3 0.0 collective-permute-done
  15.3 0.0 collective-permute-done.1
  15.3 1.0 %pad_maximum_fusion = bf16[1,4,11,16,512]{4,3,2,1,0:T(8,128)(2,1)S(1)} fusion(bf16[1,4,4,16,512]{4,3,2,1,0:T(8,128)(2,1)S(1)} %collective-permute-done.1, bf16[1,4,4,16,512]{4,3,2,1,0:T(8,128)(2,1)} %param.4, bf16[1,4,3,16,512]{4,3,2,1,0:T(8,128)(2,1)S(1)} %collective-permute-done), kind=kLoop, calls=%fused_computation | loop fusion | flops 720896 | bytes 1441792 | tf_op jit(solution)/shard_map/concatenate | solution.py:175
  16.3 4.4 %copy.22 = bf16[1,4,11,16,512]{3,4,2,1,0:T(8,128)(2,1)} copy(bf16[1,4,11,16,512]{4,3,2,1,0:T(8,128)(2,1)S(1)} %pad_maximum_fusion) | data formatting | bytes 1441792 | tf_op jit(solution)/shard_map/concatenate | solution.py:175
  20.7 9.2 %copy.23 = bf16[11,16,4,4,128]{4,3,2,1,0:T(4,128)(2,1)} copy(bf16[11,16,4,4,128]{1,3,4,0,2:T(4,128)(2,1)} %bitcast.53) | data formatting | bytes 1441792 | tf_op jit(solution)/shard_map/transpose | solution.py:177
  29.9 0.0 copy-done
  29.9 5.5 %shard_map.75 = (bf16[64,512]{1,0:T(8,128)(2,1)}, bf16[512,256]{1,0:T(8,128)(2,1)}, f32[288,64]{1,0:T(8,128)}, f32[432,128]{1,0:T(8,128)}) custom-call(bf16[11,16,16,128]{3,2,1,0:T(8,128)(2,1)} %bitcast.54, bf16[64,288]{1,0:T(8,128)(2,1)} %copy.27.k1_ref, bf16[64,1152]{1,0:T(8,128)(2,1)} %copy.28.k2_ref, bf16[1152,64]{1,0:T(8,128)(2,1)} %bitcast.56, ...), custom_call_target="tpu_custom_call" | custom-call | flops 60000000 | bytes 3000000 | tf_op jit(solution)/shard_map/pallas_call | solution.py:188
  35.4 1.1 %reshape.101 = f32[3,3,2,4,4,2,32]{6,5,4,3,2,1,0:T(2,128)S(1)} reshape(f32[288,64]{1,0:T(8,128)} %get-tuple-element.10) | data formatting | bytes 147456 | tf_op jit(solution)/shard_map/reshape | solution.py:214
  36.5 0.1 fusion.1
  36.7 0.1 reshape.102
  36.8 1.0 %pad_maximum_fusion.2 = f32[459,128]{1,0:T(8,128)S(1)} fusion(f32[432,128]{1,0:T(8,128)} %get-tuple-element.11, f32[27,128]{1,0:T(8,128)S(1)} %reshape.102), kind=kLoop, calls=%fused_computation.3 | loop fusion | flops 58752 | bytes 470016 | tf_op jit(solution)/shard_map/concatenate | solution.py:221
  37.7 3.3 %collective-permute-start.3 = (f32[459,128]{1,0:T(8,128)S(1)}, f32[459,128]{1,0:T(8,128)S(1)}, u32[]{:S(2)}, u32[]{:S(2)}) collective-permute-start(f32[459,128]{1,0:T(8,128)S(1)} %pad_maximum_fusion.2), channel_id=1, source_target_pairs={{0,4},{4,0},{8,12},{12,8},{16,20},{20,16},{24,28},{28,24},{1,5},{5... | collective-permute-start | bytes 705032 | tf_op jit(solution)/shard_map/ppermute | solution.py:26
  41.0 1.1 %collective-permute-done.3 = f32[459,128]{1,0:T(8,128)S(1)} collective-permute-done((f32[459,128]{1,0:T(8,128)S(1)}, f32[459,128]{1,0:T(8,128)S(1)}, u32[]{:S(2)}, u32[]{:S(2)}) %collective-permute-start.3) | collective-permute-done | bytes 235040 | tf_op jit(solution)/shard_map/ppermute | solution.py:26
  42.1 1.0 %fusion = f32[459,128]{1,0:T(8,128)S(1)} fusion(f32[459,128]{1,0:T(8,128)S(1)} %collective-permute-done.3, f32[432,128]{1,0:T(8,128)} %get-tuple-element.11, f32[27,128]{1,0:T(8,128)S(1)} %reshape.102), kind=kLoop, calls=%fused_computation.20 | loop fusion | flops 117504 | bytes 705024 | tf_op jit(solution)/shard_map/add | solution.py:26
  43.1 2.4 %collective-permute-start.4 = (f32[459,128]{1,0:T(8,128)S(1)}, f32[459,128]{1,0:T(8,128)S(1)}, u32[]{:S(2)}, u32[]{:S(2)}) collective-permute-start(f32[459,128]{1,0:T(8,128)S(1)} %fusion), channel_id=1, source_target_pairs={{0,8},{4,12},{8,0},{12,4},{16,24},{20,28},{24,16},{28,20},{1,9},{5... | collective-permute-start | bytes 705032 | tf_op jit(solution)/shard_map/ppermute | solution.py:26
  45.5 6.3 %collective-permute-done.4 = f32[459,128]{1,0:T(8,128)S(1)} collective-permute-done((f32[459,128]{1,0:T(8,128)S(1)}, f32[459,128]{1,0:T(8,128)S(1)}, u32[]{:S(2)}, u32[]{:S(2)}) %collective-permute-start.4) | collective-permute-done | bytes 235040 | tf_op jit(solution)/shard_map/ppermute | solution.py:26
  51.8 3.0 %collective-permute-start.5 = (f32[459,128]{1,0:T(8,128)S(1)}, f32[459,128]{1,0:T(8,128)S(1)}, u32[]{:S(2)}, u32[]{:S(2)}) collective-permute-start(f32[459,128]{1,0:T(8,128)S(1)} %add.69), channel_id=1, source_target_pairs={{0,16},{4,20},{8,24},{12,28},{16,0},{20,4},{24,8},{28,12},{1,17},{... | collective-permute-start | bytes 705032 | tf_op jit(solution)/shard_map/ppermute | solution.py:26
  54.8 5.3 %collective-permute-done.5 = f32[459,128]{1,0:T(8,128)S(1)} collective-permute-done((f32[459,128]{1,0:T(8,128)S(1)}, f32[459,128]{1,0:T(8,128)S(1)}, u32[]{:S(2)}, u32[]{:S(2)}) %collective-permute-start.5) | collective-permute-done | bytes 235040 | tf_op jit(solution)/shard_map/ppermute | solution.py:26
  60.1 1.6 %collective-permute-start.6 = (f32[459,128]{1,0:T(8,128)S(1)}, f32[459,128]{1,0:T(8,128)S(1)}, u32[]{:S(2)}, u32[]{:S(2)}) collective-permute-start(f32[459,128]{1,0:T(8,128)S(1)} %add.70), channel_id=1, source_target_pairs={{0,1},{1,0},{2,3},{3,2},{4,5},{5,4},{6,7},{7,6},{8,9},{9,8},{10,11... | collective-permute-start | bytes 705032 | tf_op jit(solution)/shard_map/ppermute | solution.py:26
  61.8 4.8 %collective-permute-done.6 = f32[459,128]{1,0:T(8,128)S(1)} collective-permute-done((f32[459,128]{1,0:T(8,128)S(1)}, f32[459,128]{1,0:T(8,128)S(1)}, u32[]{:S(2)}, u32[]{:S(2)}) %collective-permute-start.6) | collective-permute-done | bytes 235040 | tf_op jit(solution)/shard_map/ppermute | solution.py:26
  66.6 2.7 %collective-permute-start.7 = (f32[459,128]{1,0:T(8,128)S(1)}, f32[459,128]{1,0:T(8,128)S(1)}, u32[]{:S(2)}, u32[]{:S(2)}) collective-permute-start(f32[459,128]{1,0:T(8,128)S(1)} %add.71), channel_id=1, source_target_pairs={{0,2},{1,3},{2,0},{3,1},{4,6},{5,7},{6,4},{7,5},{8,10},{9,11},{10,... | collective-permute-start | bytes 705032 | tf_op jit(solution)/shard_map/ppermute | solution.py:26
  69.3 1.5 %reshape.99 = bf16[1,64,1,4,128]{4,3,1,2,0:T(4,128)(2,1)} reshape(bf16[64,512]{1,0:T(8,128)(2,1)} %get-tuple-element.8) | data formatting | bytes 131072 | tf_op jit(solution)/shard_map/reshape | solution.py:211
  70.7 1.8 %copy.43 = bf16[2,8,32,256]{3,1,0,2:T(8,128)(2,1)} copy(bf16[2,8,32,256]{3,2,1,0:T(8,128)(2,1)} %bitcast.59) | data formatting | bytes 524288 | tf_op jit(solution)/shard_map/reshape | solution.py:212
  72.5 5.6 %collective-permute-done.7 = f32[459,128]{1,0:T(8,128)S(1)} collective-permute-done((f32[459,128]{1,0:T(8,128)S(1)}, f32[459,128]{1,0:T(8,128)S(1)}, u32[]{:S(2)}, u32[]{:S(2)}) %collective-permute-start.7) | collective-permute-done | bytes 235040 | tf_op jit(solution)/shard_map/ppermute | solution.py:26
  78.2 0.7 reshape.103
  78.9 0.3 reshape.104
  79.2 0.8 copy.35
  (13 shorter events, 0.3 us)
Async XLA Ops:
  0.6 14.6 %collective-permute-start.1 = (bf16[1,4,4,16,512]{4,3,2,1,0:T(8,128)(2,1)}, bf16[1,4,4,16,512]{4,3,2,1,0:T(8,128)(2,1)S(1)}, u32[]{:S(2)}, u32[]{:S(2)}) collective-permute-start(bf16[1,4,4,16,512]{4,3,2,1,0:T(8,128)(2,1)} %param.4), channel_id=1, source_target_pairs={{4,0},{8,4},{12,8},{16,12},{20,16},{24,20},{28,24},{5,1},{9,5},{13... | collective-permute-start | bytes 786440 | tf_op jit(solution)/shard_map/ppermute | solution.py:17
  2.9 12.4 %collective-permute-start = (bf16[1,4,3,16,512]{4,3,2,1,0:T(8,128)(2,1)S(1)}, bf16[1,4,3,16,512]{4,3,2,1,0:T(8,128)(2,1)S(1)}, u32[]{:S(2)}, u32[]{:S(2)}) collective-permute-start(bf16[1,4,3,16,512]{4,3,2,1,0:T(8,128)(2,1)S(1)} %slice.42), channel_id=1, source_target_pairs={{0,4},{4,8},{8,12},{12,16},{16,20},{20,24},{24,28},{1,5},{5,9},{9,... | collective-permute-start | bytes 589832 | tf_op jit(solution)/shard_map/ppermute | solution.py:17
  5.9 7.7 %collective-permute-start.2 = (bf16[1,64,1,4,128]{4,3,2,1,0:T(4,128)(2,1)}, bf16[1,64,1,4,128]{4,3,2,1,0:T(4,128)(2,1)S(1)}, u32[]{:S(2)}, u32[]{:S(2)}) collective-permute-start(bf16[1,64,1,4,128]{4,3,2,1,0:T(4,128)(2,1)} %param.7), channel_id=1, source_target_pairs={{4,0},{8,4},{12,8},{16,12},{20,16},{24,20},{28,24},{5,1},{9,5},{13... | collective-permute-start | bytes 196616 | tf_op jit(solution)/shard_map/ppermute | solution.py:17
  12.8 17.1 %copy-start = (bf16[64,3,3,2,2,32]{0,5,4,3,2,1:T(8,128)(2,1)}, bf16[64,3,3,2,2,32]{0,5,4,3,2,1:T(8,128)(2,1)S(1)}, u32[]{:S(2)}) copy-start(bf16[64,3,3,2,2,32]{0,5,4,3,2,1:T(8,128)(2,1)S(1)} %copy.25) | copy-start | bytes 442372
  37.7 4.4 %collective-permute-start.3 = (f32[459,128]{1,0:T(8,128)S(1)}, f32[459,128]{1,0:T(8,128)S(1)}, u32[]{:S(2)}, u32[]{:S(2)}) collective-permute-start(f32[459,128]{1,0:T(8,128)S(1)} %pad_maximum_fusion.2), channel_id=1, source_target_pairs={{0,4},{4,0},{8,12},{12,8},{16,20},{20,16},{24,28},{28,24},{1,5},{5... | collective-permute-start | bytes 705032 | tf_op jit(solution)/shard_map/ppermute | solution.py:26
  43.1 8.7 %collective-permute-start.4 = (f32[459,128]{1,0:T(8,128)S(1)}, f32[459,128]{1,0:T(8,128)S(1)}, u32[]{:S(2)}, u32[]{:S(2)}) collective-permute-start(f32[459,128]{1,0:T(8,128)S(1)} %fusion), channel_id=1, source_target_pairs={{0,8},{4,12},{8,0},{12,4},{16,24},{20,28},{24,16},{28,20},{1,9},{5... | collective-permute-start | bytes 705032 | tf_op jit(solution)/shard_map/ppermute | solution.py:26
  51.8 8.2 %collective-permute-start.5 = (f32[459,128]{1,0:T(8,128)S(1)}, f32[459,128]{1,0:T(8,128)S(1)}, u32[]{:S(2)}, u32[]{:S(2)}) collective-permute-start(f32[459,128]{1,0:T(8,128)S(1)} %add.69), channel_id=1, source_target_pairs={{0,16},{4,20},{8,24},{12,28},{16,0},{20,4},{24,8},{28,12},{1,17},{... | collective-permute-start | bytes 705032 | tf_op jit(solution)/shard_map/ppermute | solution.py:26
  60.1 6.4 %collective-permute-start.6 = (f32[459,128]{1,0:T(8,128)S(1)}, f32[459,128]{1,0:T(8,128)S(1)}, u32[]{:S(2)}, u32[]{:S(2)}) collective-permute-start(f32[459,128]{1,0:T(8,128)S(1)} %add.70), channel_id=1, source_target_pairs={{0,1},{1,0},{2,3},{3,2},{4,5},{5,4},{6,7},{7,6},{8,9},{9,8},{10,11... | collective-permute-start | bytes 705032 | tf_op jit(solution)/shard_map/ppermute | solution.py:26
  66.6 11.5 %collective-permute-start.7 = (f32[459,128]{1,0:T(8,128)S(1)}, f32[459,128]{1,0:T(8,128)S(1)}, u32[]{:S(2)}, u32[]{:S(2)}) collective-permute-start(f32[459,128]{1,0:T(8,128)S(1)} %add.71), channel_id=1, source_target_pairs={{0,2},{1,3},{2,0},{3,1},{4,6},{5,7},{6,4},{7,5},{8,10},{9,11},{10,... | collective-permute-start | bytes 705032 | tf_op jit(solution)/shard_map/ppermute | solution.py:26

commit v2 on v1

--- a/solution.py
+++ b/solution.py
@@ -47,20 +47,39 @@
     return lax.dot_general(a, b, (((1,), (1,)), ((), ())), preferred_element_type=F32)
 
 
-def _kernel(vz_ref, k1_ref, k2_ref, k2t_ref, cot_ref,
+def _kernel(vb_ref, vo_ref, va_ref, k1_ref, k2_ref, k2t_ref, cot_ref,
             lvl_ref, g1_ref, s1_ref, s2_ref,
             tp, p1, t2, pre1, p2, bt, gs, gacc, b1, g1s):
-    nzi, ny, rows0, lanes = vz_ref.shape
+    c0, ny, nx = vo_ref.shape[1], vo_ref.shape[3], vo_ref.shape[4]
+    lanes = nx // 4
+    nzi = tp.shape[0]
     n_act = p1.shape[0]
     ny1 = ny // 2
     ny2 = ny1 // 2
     c2 = t2.shape[2]
     c1 = c2 // 2
+    rows0 = 4 * c0
+
+    xs = lax.broadcasted_iota(jnp.int32, (nx, nx), 0)
+    cs = lax.broadcasted_iota(jnp.int32, (nx, nx), 1)
+    sel_x = jnp.where(xs == 4 * (cs % lanes) + cs // lanes, 1.0, 0.0).astype(BF16)
+    nq = 2 * rows0 * ny
+    orow = lax.broadcasted_iota(jnp.int32, (nq, nq), 0)
+    icol = lax.broadcasted_iota(jnp.int32, (nq, nq), 1)
+    y_, s_ = orow // (2 * rows0), (orow // rows0) % 2
+    i_, r_ = (orow // 4) % c0, orow % 4
+    perm = jnp.where(icol == ((s_ * 4 + r_) * c0 + i_) * ny + y_, 1.0, 0.0).astype(BF16)
 
     tp[:, 0] = jnp.zeros((nzi, 2 * rows0, lanes), BF16)
-    for zi in range(nzi):
-        x = vz_ref[zi].astype(F32)
-        tp[zi, 1:] = jnp.concatenate([x, _shift_right(x)], axis=1).astype(BF16)
+    pieces = [(vb_ref, z) for z in range(vb_ref.shape[2])] + [(vo_ref, z) for z in range(vo_ref.shape[2])] + [
+        (va_ref, z) for z in range(va_ref.shape[2])]
+    for zi, (ref, z) in enumerate(pieces):
+        zmat = ref[0, :, z].reshape(c0 * ny, nx)
+        ymat = jnp.dot(zmat, sel_x, preferred_element_type=F32)
+        blocks = [ymat[:, r * lanes:(r + 1) * lanes] for r in range(4)]
+        q = jnp.concatenate(blocks + [_shift_right(b) for b in blocks], axis=0).astype(BF16)
+        t = jnp.dot(perm, q, preferred_element_type=F32).astype(BF16)
+        tp[zi, 1:] = t.reshape(ny, 2 * rows0, lanes)
 
     for a in range(n_act):
         for d in range(3):
@@ -172,9 +191,7 @@
     below = shifted(volume[:, :, 1:], "gz", 1)
     above = shifted(volume, "gz", -1)
     cot_above = shifted(cotangent, "gz", -1)
-    ext = jnp.concatenate([below, volume, above], 2)[0]
-    nzi = ext.shape[1]
-    vz = ext.reshape(c0, nzi, ny, q, 4).transpose(1, 2, 0, 4, 3).reshape(nzi, ny, 4 * c0, q)
+    nzi = below.shape[2] + nz + above.shape[2]
     n2 = cotangent.shape[3] * cotangent.shape[4]
     cots = jnp.concatenate([cotangent, cot_above], 2)[0].transpose(1, 0, 2, 3).reshape(2, c2, n2)
 
@@ -206,7 +223,7 @@
             vm((2 * ny1 * c1, 2 * q), BF16),
         ],
         cost_estimate=pl.CostEstimate(flops=60_000_000, transcendentals=200_000, bytes_accessed=3_000_000),
-    )(vz, k1m, k2m, k2t, cots)
+    )(below, volume, above, k1m, k2m, k2t, cots)
 
     level_two = lvl.reshape(1, c2, 1, ny2, n2 // ny2)
     grad_one = g1.reshape(2, ny1, c1, 2 * q).transpose(2, 0, 1, 3)[None]

time: 80.8 us -> 64.4 us (0.80)
  local copies, waits for them, and re-layouts: 27.4 us -> 9.69 us
  other arithmetic: 4.59 us -> 0.84 us
  Pallas kernels: 5.5 us -> 8.41 us
  waiting for transfers between devices: 23 us -> 24.8 us
    transpose x1 -> x0, local copies, waits for them, and re-layouts: 9.19 us -> none  [per_device(): ext.reshape(c0, nzi, ny, q, 4).transpose(1, 2, 0, 4, 3)]
    concatenate x1 -> x0, local copies, waits for them, and re-layouts: 4.39 us -> none  [per_device(): ext = jnp.concatenate([below, volume, above], 2)[0]]
    pallas_call x1, Pallas kernels: 5.5 us -> 8.41 us  [per_device(): pl.pallas_call(_kernel, out_shape=(jax.ShapeDtypeStruct((c2, n2), BF16),...]
    ppermute x5, waiting for transfers between devices: 23 us -> 24.8 us  [_all_sum(): x = x + lax.ppermute(x, axis, [(i, i ^ k) for i in range(n)])]
    unnamed x2 -> x18, local copies, waits for them, and re-layouts: 0.01 us -> 1.63 us
    slice x2, local copies, waits for them, and re-layouts: 1.44 us -> 0.02 us  [_level_one_weights(): w0, w1, w2 = (kt[..., 0], kt[..., 1], kt[..., 2])]
    concatenate x1 -> x0, other arithmetic: 1.03 us -> none  [per_device(): ext = jnp.concatenate([below, volume, above], 2)[0]]
    reshape x1, local copies, waits for them, and re-layouts: 1.8 us -> 0.85 us  [per_device(): grad_one = g1.reshape(2, ny1, c1, 2 * q).transpose(2, 0, 1, 3)[None]]
  transfers between devices with their start and end apart: 8 -> 8, of which waited for: 5 -> 5; matrix products, arithmetic and copies ran while one was open for 15% -> 9% of each run, Pallas kernels for 0% -> 0%
where the time goes in v2:
time: 64.4 us; the launch traced here: 64 us
  waiting for transfers between devices  24.8 us (39%)
  starting transfers between devices  19.3 us (30%)
  local copies, waits for them, and re-layouts  9.69 us (15%)
  Pallas kernels  8.41 us (13%)
  between operations  0.95 us (1%)
  other arithmetic  0.84 us (1%)
    ppermute x5, waiting for transfers between devices, _all_sum(): x = x + lax.ppermute(x, axis, [(i, i ^ k) for i in range(n)])  24.8 us
    ppermute x5, starting transfers between devices, _all_sum(): x = x + lax.ppermute(x, axis, [(i, i ^ k) for i in range(n)])  12.9 us
    pallas_call x1, Pallas kernels, per_device(): pl.pallas_call(_kernel, out_shape=(jax.ShapeDtypeStruct((c2, n2), BF16),...  8.41 us
    ppermute x3, starting transfers between devices, shifted(): return lax.ppermute(block, axis, route)  6.39 us
    unnamed x18, local copies, waits for them, and re-layouts  1.63 us
  transfers between devices with their start and end apart: 8, of which 5 were waited for; matrix products, arithmetic and copies ran while one was open for 9% of the time, Pallas kernels for 0%

profile of v2, /device:TPU:0, one launch (start us, length us, event | category | flops | bytes accessed | tf_op | source)
XLA Modules:
  0.0 64.0 jit_solution(16513810795295290860)
XLA Ops:
  0.6 0.0 copy-start.6
  0.6 0.0 copy-start.4
  0.7 1.4 %collective-permute-start.2 = (bf16[1,64,1,4,128]{4,3,2,1,0:T(4,128)(2,1)}, bf16[1,64,1,4,128]{4,3,2,1,0:T(4,128)(2,1)S(1)}, u32[]{:S(2)}, u32[]{:S(2)}) collective-permute-start(bf16[1,64,1,4,128]{4,3,2,1,0:T(4,128)(2,1)} %param.7), channel_id=1, source_target_pairs={{4,0},{8,4},{12,8},{16,12},{20,16},{24,20},{28,24},{5,1},{9,5},{13... | collective-permute-start | bytes 196616 | tf_op jit(solution)/shard_map/ppermute | solution.py:17
  2.1 1.3 %collective-permute-start.1 = (bf16[1,4,4,16,512]{4,3,2,1,0:T(8,128)(2,1)}, bf16[1,4,4,16,512]{4,3,2,1,0:T(8,128)(2,1)S(1)}, u32[]{:S(2)}, u32[]{:S(2)}) collective-permute-start(bf16[1,4,4,16,512]{4,3,2,1,0:T(8,128)(2,1)} %vo_ref.1), channel_id=1, source_target_pairs={{4,0},{8,4},{12,8},{16,12},{20,16},{24,20},{28,24},{5,1},{9,5},{13... | collective-permute-start | bytes 786440 | tf_op jit(solution)/shard_map/ppermute | solution.py:17
  3.4 0.9 %slice.42 = bf16[1,4,3,16,512]{4,3,2,1,0:T(8,128)(2,1)S(1)} slice(bf16[1,4,4,16,512]{4,3,2,1,0:T(8,128)(2,1)} %vo_ref.1), slice={[0:1], [0:4], [1:4], [0:16], [0:512]} | slice | bytes 393216 | tf_op jit(solution)/shard_map/slice | solution.py:191
  4.3 3.7 %collective-permute-start = (bf16[1,4,3,16,512]{4,3,2,1,0:T(8,128)(2,1)S(1)}, bf16[1,4,3,16,512]{4,3,2,1,0:T(8,128)(2,1)S(1)}, u32[]{:S(2)}, u32[]{:S(2)}) collective-permute-start(bf16[1,4,3,16,512]{4,3,2,1,0:T(8,128)(2,1)S(1)} %slice.42), channel_id=1, source_target_pairs={{0,4},{4,8},{8,12},{12,16},{16,20},{20,24},{24,28},{1,5},{5,9},{9,... | collective-permute-start | bytes 589832 | tf_op jit(solution)/shard_map/ppermute | solution.py:17
  8.0 0.0 copy-done.6
  8.1 0.0 copy-done.4
  8.2 0.1 pad_maximum_fusion.4
  8.3 0.1 maximum_bitcast_fusion.2
  8.4 0.1 maximum_bitcast_fusion.1
  8.4 0.1 pad_maximum_fusion.2
  8.6 0.1 copy.21
  8.7 0.1 reshape.92
  8.8 0.7 %copy.24.k1_ref = bf16[64,288]{1,0:T(8,128)(2,1)} copy(bf16[64,288]{0,1:T(8,128)(2,1)S(1)} %reshape.92) | data formatting | bytes 73728 | tf_op jit(solution)/shard_map/reshape | solution.py:174
  9.5 0.1 pad_maximum_fusion
  9.6 0.0 copy-start
  9.6 0.0 copy-start.8
  9.7 0.8 %copy.25.k2_ref = bf16[64,1152]{1,0:T(8,128)(2,1)} copy(bf16[64,1152]{0,1:T(8,128)(2,1)S(1)} %bitcast.49) | data formatting | bytes 294912 | tf_op jit(solution)/shard_map/reshape | solution.py:182
  10.5 0.0 collective-permute-done.2
  10.5 0.1 copy-done.8
  10.6 0.1 maximum_bitcast_fusion
  10.7 0.0 copy-done
  10.7 0.1 reshape.102
  10.7 0.7 %copy.34.cot_ref = bf16[2,64,512]{2,1,0:T(8,128)(2,1)} copy(bf16[2,64,512]{2,0,1:T(2,128)(2,1)S(1)} %reshape.102) | data formatting | bytes 262144 | tf_op jit(solution)/shard_map/reshape | solution.py:196
  11.4 0.0 collective-permute-done.vb_ref
  11.4 0.0 copy-start.5
  11.4 0.0 collective-permute-done.1.va_ref
  11.4 0.0 copy-start.3
  11.4 0.7 %copy-done.5 = bf16[1,4,3,16,512]{4,3,2,1,0:T(8,128)(2,1)} copy-done((bf16[1,4,3,16,512]{4,3,2,1,0:T(8,128)(2,1)}, bf16[1,4,3,16,512]{4,3,2,1,0:T(8,128)(2,1)S(1)}, u32[]{:S(2)}) %copy-start.5) | copy-done | bytes 196632
  12.1 0.1 copy-done.3
  12.2 8.4 %shard_map.75 = (bf16[64,512]{1,0:T(8,128)(2,1)}, bf16[512,256]{1,0:T(8,128)(2,1)}, f32[288,64]{1,0:T(8,128)}, f32[432,128]{1,0:T(8,128)}) custom-call(bf16[1,4,3,16,512]{4,3,2,1,0:T(8,128)(2,1)} %copy-done.5, bf16[1,4,4,16,512]{4,3,2,1,0:T(8,128)(2,1)} %vo_ref.1, bf16[1,4,4,16,512]{4,3,2,1,0:T(8,128)(2,1)} %copy-done.3, bf16[64,288]{1,0:T(8,128)(2,1)} %copy.24.k1_ref, ...), custom_call_target="tpu_custom_call" | custom-call | flops 60000000 | bytes 3000000 | tf_op jit(solution)/shard_map/pallas_call | solution.py:205
  20.6 1.1 %reshape.97 = f32[3,3,2,4,4,2,32]{6,5,4,3,2,1,0:T(2,128)S(1)} reshape(f32[288,64]{1,0:T(8,128)} %get-tuple-element.10) | data formatting | bytes 147456 | tf_op jit(solution)/shard_map/reshape | solution.py:231
  21.7 0.1 fusion.1
  21.8 0.0 copy-start.1
  21.9 0.1 reshape.98
  22.0 0.8 %copy-done.1 = f32[432,128]{1,0:T(8,128)S(1)} copy-done((f32[432,128]{1,0:T(8,128)S(1)}, f32[432,128]{1,0:T(8,128)}, u32[]{:S(2)}) %copy-start.1) | copy-done | bytes 221208
  22.8 2.6 %collective-permute-start.3 = (f32[459,128]{1,0:T(8,128)S(1)}, f32[459,128]{1,0:T(8,128)S(1)}, u32[]{:S(2)}, u32[]{:S(2)}) collective-permute-start(f32[459,128]{1,0:T(8,128)S(1)} %pad_maximum_fusion.1), channel_id=1, source_target_pairs={{0,4},{4,0},{8,12},{12,8},{16,20},{20,16},{24,28},{28,24},{1,5},{5... | collective-permute-start | bytes 705032 | tf_op jit(solution)/shard_map/ppermute | solution.py:26
  25.4 1.1 %collective-permute-done.3 = f32[459,128]{1,0:T(8,128)S(1)} collective-permute-done((f32[459,128]{1,0:T(8,128)S(1)}, f32[459,128]{1,0:T(8,128)S(1)}, u32[]{:S(2)}, u32[]{:S(2)}) %collective-permute-start.3) | collective-permute-done | bytes 235040 | tf_op jit(solution)/shard_map/ppermute | solution.py:26
  26.5 3.1 %collective-permute-start.4 = (f32[459,128]{1,0:T(8,128)S(1)}, f32[459,128]{1,0:T(8,128)S(1)}, u32[]{:S(2)}, u32[]{:S(2)}) collective-permute-start(f32[459,128]{1,0:T(8,128)S(1)} %fusion), channel_id=1, source_target_pairs={{0,8},{4,12},{8,0},{12,4},{16,24},{20,28},{24,16},{28,20},{1,9},{5... | collective-permute-start | bytes 705032 | tf_op jit(solution)/shard_map/ppermute | solution.py:26
  29.6 6.3 %collective-permute-done.4 = f32[459,128]{1,0:T(8,128)S(1)} collective-permute-done((f32[459,128]{1,0:T(8,128)S(1)}, f32[459,128]{1,0:T(8,128)S(1)}, u32[]{:S(2)}, u32[]{:S(2)}) %collective-permute-start.4) | collective-permute-done | bytes 235040 | tf_op jit(solution)/shard_map/ppermute | solution.py:26
  36.0 2.9 %collective-permute-start.5 = (f32[459,128]{1,0:T(8,128)S(1)}, f32[459,128]{1,0:T(8,128)S(1)}, u32[]{:S(2)}, u32[]{:S(2)}) collective-permute-start(f32[459,128]{1,0:T(8,128)S(1)} %add.69), channel_id=1, source_target_pairs={{0,16},{4,20},{8,24},{12,28},{16,0},{20,4},{24,8},{28,12},{1,17},{... | collective-permute-start | bytes 705032 | tf_op jit(solution)/shard_map/ppermute | solution.py:26
  38.9 5.3 %collective-permute-done.5 = f32[459,128]{1,0:T(8,128)S(1)} collective-permute-done((f32[459,128]{1,0:T(8,128)S(1)}, f32[459,128]{1,0:T(8,128)S(1)}, u32[]{:S(2)}, u32[]{:S(2)}) %collective-permute-start.5) | collective-permute-done | bytes 235040 | tf_op jit(solution)/shard_map/ppermute | solution.py:26
  44.2 0.0 copy-start.7
  44.2 0.0 copy-start.2
  44.2 1.6 %collective-permute-start.6 = (f32[459,128]{1,0:T(8,128)S(1)}, f32[459,128]{1,0:T(8,128)S(1)}, u32[]{:S(2)}, u32[]{:S(2)}) collective-permute-start(f32[459,128]{1,0:T(8,128)S(1)} %add.70), channel_id=1, source_target_pairs={{0,1},{1,0},{2,3},{3,2},{4,5},{5,4},{6,7},{7,6},{8,9},{9,8},{10,11... | collective-permute-start | bytes 705032 | tf_op jit(solution)/shard_map/ppermute | solution.py:26
  45.9 4.8 %collective-permute-done.6 = f32[459,128]{1,0:T(8,128)S(1)} collective-permute-done((f32[459,128]{1,0:T(8,128)S(1)}, f32[459,128]{1,0:T(8,128)S(1)}, u32[]{:S(2)}, u32[]{:S(2)}) %collective-permute-start.6) | collective-permute-done | bytes 235040 | tf_op jit(solution)/shard_map/ppermute | solution.py:26
  50.7 2.6 %collective-permute-start.7 = (f32[459,128]{1,0:T(8,128)S(1)}, f32[459,128]{1,0:T(8,128)S(1)}, u32[]{:S(2)}, u32[]{:S(2)}) collective-permute-start(f32[459,128]{1,0:T(8,128)S(1)} %add.71), channel_id=1, source_target_pairs={{0,2},{1,3},{2,0},{3,1},{4,6},{5,7},{6,4},{7,5},{8,10},{9,11},{10,... | collective-permute-start | bytes 705032 | tf_op jit(solution)/shard_map/ppermute | solution.py:26
  53.3 0.0 copy-done.7
  53.3 0.6 %reshape.95 = bf16[1,64,1,4,128]{4,3,1,2,0:T(4,128)(2,1)} reshape(bf16[64,512]{1,0:T(8,128)(2,1)S(1)} %copy-done.7) | data formatting | bytes 131072 | tf_op jit(solution)/shard_map/reshape | solution.py:228
  54.0 0.0 copy-done.2
  54.0 0.9 %copy.40 = bf16[2,8,32,256]{3,1,0,2:T(8,128)(2,1)} copy(bf16[2,8,32,256]{3,2,1,0:T(8,128)(2,1)S(1)} %bitcast.53) | data formatting | bytes 524288 | tf_op jit(solution)/shard_map/reshape | solution.py:229
  54.8 7.4 %collective-permute-done.7 = f32[459,128]{1,0:T(8,128)S(1)} collective-permute-done((f32[459,128]{1,0:T(8,128)S(1)}, f32[459,128]{1,0:T(8,128)S(1)}, u32[]{:S(2)}, u32[]{:S(2)}) %collective-permute-start.7) | collective-permute-done | bytes 235040 | tf_op jit(solution)/shard_map/ppermute | solution.py:26
  62.3 0.7 %reshape.99 = f32[3,3,3,4,32]{4,3,2,1,0:T(4,128)} reshape(f32[27,128]{1,0:T(8,128)S(1)} %slice_multiply_fusion.1) | data formatting | bytes 27648 | tf_op jit(solution)/shard_map/reshape | solution.py:244
  63.0 0.3 reshape.100
  63.3 0.8 %copy.32 = f32[27,2,16,64]{3,2,1,0:T(8,128)} copy(f32[27,2,16,64]{3,1,2,0:T(2,128)S(1)} %bitcast.51) | data formatting | bytes 442368 | tf_op jit(solution)/shard_map/transpose | solution.py:245
  (20 shorter events, 0.4 us)
Async XLA Ops:
  0.6 7.4 %copy-start.6 = (bf16[32,4,3,3,3]{0,1,4,3,2:T(4,128)(2,1)S(1)}, bf16[32,4,3,3,3]{0,1,4,3,2:T(4,128)(2,1)}, u32[]{:S(2)}) copy-start(bf16[32,4,3,3,3]{0,1,4,3,2:T(4,128)(2,1)} %param.5) | copy-start | bytes 20740
  0.6 7.5 %copy-start.4 = (bf16[64,32,3,3,3]{0,1,4,3,2:T(8,128)(2,1)S(1)}, bf16[64,32,3,3,3]{0,1,4,3,2:T(8,128)(2,1)}, u32[]{:S(2)}) copy-start(bf16[64,32,3,3,3]{0,1,4,3,2:T(8,128)(2,1)} %param.6) | copy-start | bytes 331780
  0.7 9.8 %collective-permute-start.2 = (bf16[1,64,1,4,128]{4,3,2,1,0:T(4,128)(2,1)}, bf16[1,64,1,4,128]{4,3,2,1,0:T(4,128)(2,1)S(1)}, u32[]{:S(2)}, u32[]{:S(2)}) collective-permute-start(bf16[1,64,1,4,128]{4,3,2,1,0:T(4,128)(2,1)} %param.7), channel_id=1, source_target_pairs={{4,0},{8,4},{12,8},{16,12},{20,16},{24,20},{28,24},{5,1},{9,5},{13... | collective-permute-start | bytes 196616 | tf_op jit(solution)/shard_map/ppermute | solution.py:17
  2.1 9.3 %collective-permute-start.1 = (bf16[1,4,4,16,512]{4,3,2,1,0:T(8,128)(2,1)}, bf16[1,4,4,16,512]{4,3,2,1,0:T(8,128)(2,1)S(1)}, u32[]{:S(2)}, u32[]{:S(2)}) collective-permute-start(bf16[1,4,4,16,512]{4,3,2,1,0:T(8,128)(2,1)} %vo_ref.1), channel_id=1, source_target_pairs={{4,0},{8,4},{12,8},{16,12},{20,16},{24,20},{28,24},{5,1},{9,5},{13... | collective-permute-start | bytes 786440 | tf_op jit(solution)/shard_map/ppermute | solution.py:17
  4.3 7.1 %collective-permute-start = (bf16[1,4,3,16,512]{4,3,2,1,0:T(8,128)(2,1)S(1)}, bf16[1,4,3,16,512]{4,3,2,1,0:T(8,128)(2,1)S(1)}, u32[]{:S(2)}, u32[]{:S(2)}) collective-permute-start(bf16[1,4,3,16,512]{4,3,2,1,0:T(8,128)(2,1)S(1)} %slice.42), channel_id=1, source_target_pairs={{0,4},{4,8},{8,12},{12,16},{16,20},{20,24},{24,28},{1,5},{5,9},{9,... | collective-permute-start | bytes 589832 | tf_op jit(solution)/shard_map/ppermute | solution.py:17
  9.6 1.0 %copy-start = (bf16[64,3,3,2,2,32]{0,5,4,3,2,1:T(8,128)(2,1)}, bf16[64,3,3,2,2,32]{0,5,4,3,2,1:T(8,128)(2,1)S(1)}, u32[]{:S(2)}) copy-start(bf16[64,3,3,2,2,32]{0,5,4,3,2,1:T(8,128)(2,1)S(1)} %copy.22) | copy-start | bytes 442372
  9.6 0.9 %copy-start.8 = (bf16[1,64,1,4,128]{4,3,2,1,0:T(4,128)(2,1)S(1)}, bf16[1,64,1,4,128]{4,3,2,1,0:T(4,128)(2,1)}, u32[]{:S(2)}) copy-start(bf16[1,64,1,4,128]{4,3,2,1,0:T(4,128)(2,1)} %param.7) | copy-start | bytes 196612
  11.4 0.7 %copy-start.5 = (bf16[1,4,3,16,512]{4,3,2,1,0:T(8,128)(2,1)}, bf16[1,4,3,16,512]{4,3,2,1,0:T(8,128)(2,1)S(1)}, u32[]{:S(2)}) copy-start(bf16[1,4,3,16,512]{4,3,2,1,0:T(8,128)(2,1)S(1)} %collective-permute-done.vb_ref) | copy-start | bytes 589828
  11.4 0.8 %copy-start.3 = (bf16[1,4,4,16,512]{4,3,2,1,0:T(8,128)(2,1)}, bf16[1,4,4,16,512]{4,3,2,1,0:T(8,128)(2,1)S(1)}, u32[]{:S(2)}) copy-start(bf16[1,4,4,16,512]{4,3,2,1,0:T(8,128)(2,1)S(1)} %collective-permute-done.1.va_ref) | copy-start | bytes 786436
  21.8 0.9 %copy-start.1 = (f32[432,128]{1,0:T(8,128)S(1)}, f32[432,128]{1,0:T(8,128)}, u32[]{:S(2)}) copy-start(f32[432,128]{1,0:T(8,128)} %get-tuple-element.11) | copy-start | bytes 663556
  22.8 3.7 %collective-permute-start.3 = (f32[459,128]{1,0:T(8,128)S(1)}, f32[459,128]{1,0:T(8,128)S(1)}, u32[]{:S(2)}, u32[]{:S(2)}) collective-permute-start(f32[459,128]{1,0:T(8,128)S(1)} %pad_maximum_fusion.1), channel_id=1, source_target_pairs={{0,4},{4,0},{8,12},{12,8},{16,20},{20,16},{24,28},{28,24},{1,5},{5... | collective-permute-start | bytes 705032 | tf_op jit(solution)/shard_map/ppermute | solution.py:26
  26.5 9.4 %collective-permute-start.4 = (f32[459,128]{1,0:T(8,128)S(1)}, f32[459,128]{1,0:T(8,128)S(1)}, u32[]{:S(2)}, u32[]{:S(2)}) collective-permute-start(f32[459,128]{1,0:T(8,128)S(1)} %fusion), channel_id=1, source_target_pairs={{0,8},{4,12},{8,0},{12,4},{16,24},{20,28},{24,16},{28,20},{1,9},{5... | collective-permute-start | bytes 705032 | tf_op jit(solution)/shard_map/ppermute | solution.py:26
  36.0 8.2 %collective-permute-start.5 = (f32[459,128]{1,0:T(8,128)S(1)}, f32[459,128]{1,0:T(8,128)S(1)}, u32[]{:S(2)}, u32[]{:S(2)}) collective-permute-start(f32[459,128]{1,0:T(8,128)S(1)} %add.69), channel_id=1, source_target_pairs={{0,16},{4,20},{8,24},{12,28},{16,0},{20,4},{24,8},{28,12},{1,17},{... | collective-permute-start | bytes 705032 | tf_op jit(solution)/shard_map/ppermute | solution.py:26
  44.2 9.1 %copy-start.7 = (bf16[64,512]{1,0:T(8,128)(2,1)S(1)}, bf16[64,512]{1,0:T(8,128)(2,1)}, u32[]{:S(2)}) copy-start(bf16[64,512]{1,0:T(8,128)(2,1)} %get-tuple-element.8) | copy-start | bytes 196612
  44.2 9.8 %copy-start.2 = (bf16[512,256]{1,0:T(8,128)(2,1)S(1)}, bf16[512,256]{1,0:T(8,128)(2,1)}, u32[]{:S(2)}) copy-start(bf16[512,256]{1,0:T(8,128)(2,1)} %get-tuple-element.9) | copy-start | bytes 786436
  44.2 6.4 %collective-permute-start.6 = (f32[459,128]{1,0:T(8,128)S(1)}, f32[459,128]{1,0:T(8,128)S(1)}, u32[]{:S(2)}, u32[]{:S(2)}) collective-permute-start(f32[459,128]{1,0:T(8,128)S(1)} %add.70), channel_id=1, source_target_pairs={{0,1},{1,0},{2,3},{3,2},{4,5},{5,4},{6,7},{7,6},{8,9},{9,8},{10,11... | collective-permute-start | bytes 705032 | tf_op jit(solution)/shard_map/ppermute | solution.py:26
  50.7 11.5 %collective-permute-start.7 = (f32[459,128]{1,0:T(8,128)S(1)}, f32[459,128]{1,0:T(8,128)S(1)}, u32[]{:S(2)}, u32[]{:S(2)}) collective-permute-start(f32[459,128]{1,0:T(8,128)S(1)} %add.71), channel_id=1, source_target_pairs={{0,2},{1,3},{2,0},{3,1},{4,6},{5,7},{6,4},{7,5},{8,10},{9,11},{10,... | collective-permute-start | bytes 705032 | tf_op jit(solution)/shard_map/ppermute | solution.py:26

commit v3 on v2

--- a/solution.py
+++ b/solution.py
@@ -18,14 +18,22 @@
 
 
 def _all_sum(x, axes):
+    steps = []
     for axis in axes:
         n = lax.axis_size(axis)
         assert n & (n - 1) == 0
         k = 1
         while k < n:
-            x = x + lax.ppermute(x, axis, [(i, i ^ k) for i in range(n)])
+            steps.append((axis, n, k))
             k *= 2
-    return x
+    m = len(steps)
+    size = -(-x.shape[0] // (8 * m)) * 8
+    chunks = [x[c * size:(c + 1) * size] for c in range(m) if c * size < x.shape[0]]
+    for j in range(m):
+        for c in range(len(chunks)):
+            axis, n, k = steps[(c + j) % m]
+            chunks[c] = chunks[c] + lax.ppermute(chunks[c], axis, [(i, i ^ k) for i in range(n)])
+    return jnp.concatenate(chunks, 0)
 
 
 def _sigmoid(v):

time: 64.4 us -> 65.3 us (1.014)
  starting transfers between devices: 19.3 us -> 33.3 us
  waiting for transfers between devices: 24.8 us -> 12.4 us
  local copies, waits for them, and re-layouts: 9.69 us -> 8.94 us
    ppermute x5 -> x25, starting transfers between devices: 12.9 us -> 26.9 us  [_all_sum(): lax.ppermute(chunks[c], axis, [(i, i ^ k) for i in range(n)])]
    ppermute x5 -> x25, waiting for transfers between devices: 24.8 us -> 12.4 us  [_all_sum(): lax.ppermute(chunks[c], axis, [(i, i ^ k) for i in range(n)])]
    slice x0 -> x2, local copies, waits for them, and re-layouts: none -> 0.92 us  [_all_sum(): x[c * size:(c + 1) * size]]
    reshape x1, local copies, waits for them, and re-layouts: 1.11 us -> 0.2 us  [per_device(): s1r = s1.reshape(3, 3, 2, c0, 4, 2, c1)]
    unnamed x18 -> x20, local copies, waits for them, and re-layouts: 1.63 us -> 0.86 us
  transfers between devices with their start and end apart: 8 -> 28, of which waited for: 5 -> 7; matrix products, arithmetic and copies ran while one was open for 9% -> 10% of each run, Pallas kernels for 0% -> 0%
where the time goes in v3:
time: 65.3 us; the launch traced here: 65 us
  starting transfers between devices  33.3 us (51%)
  waiting for transfers between devices  12.4 us (19%)
  local copies, waits for them, and re-layouts  8.94 us (14%)
  Pallas kernels  8.38 us (13%)
  between operations  1.14 us (2%)
  other arithmetic  0.87 us (1%)
    ppermute x25, starting transfers between devices, _all_sum(): lax.ppermute(chunks[c], axis, [(i, i ^ k) for i in range(n)])  26.9 us
    ppermute x25, waiting for transfers between devices, _all_sum(): lax.ppermute(chunks[c], axis, [(i, i ^ k) for i in range(n)])  12.4 us
    pallas_call x1, Pallas kernels, per_device(): pl.pallas_call(_kernel, out_shape=(jax.ShapeDtypeStruct((c2, n2), BF16),...  8.38 us
    ppermute x3, starting transfers between devices, shifted(): return lax.ppermute(block, axis, route)  6.39 us
  transfers between devices with their start and end apart: 28, of which 7 were waited for; matrix products, arithmetic and copies ran while one was open for 10% of the time, Pallas kernels for 0%

profile of v3, /device:TPU:0, one launch (start us, length us, event | category | flops | bytes accessed | tf_op | source)
XLA Modules:
  0.0 65.0 jit_solution(14010336786121511782)
XLA Ops:
  0.7 1.4 %collective-permute-start.2 = (bf16[1,64,1,4,128]{4,3,2,1,0:T(4,128)(2,1)}, bf16[1,64,1,4,128]{4,3,2,1,0:T(4,128)(2,1)S(1)}, u32[]{:S(2)}, u32[]{:S(2)}) collective-permute-start(bf16[1,64,1,4,128]{4,3,2,1,0:T(4,128)(2,1)} %param.7), channel_id=1, source_target_pairs={{4,0},{8,4},{12,8},{16,12},{20,16},{24,20},{28,24},{5,1},{9,5},{13... | collective-permute-start | bytes 196616 | tf_op jit(solution)/shard_map/ppermute | solution.py:17
  2.1 1.3 %collective-permute-start.1 = (bf16[1,4,4,16,512]{4,3,2,1,0:T(8,128)(2,1)}, bf16[1,4,4,16,512]{4,3,2,1,0:T(8,128)(2,1)S(1)}, u32[]{:S(2)}, u32[]{:S(2)}) collective-permute-start(bf16[1,4,4,16,512]{4,3,2,1,0:T(8,128)(2,1)} %vo_ref.1), channel_id=1, source_target_pairs={{4,0},{8,4},{12,8},{16,12},{20,16},{24,20},{28,24},{5,1},{9,5},{13... | collective-permute-start | bytes 786440 | tf_op jit(solution)/shard_map/ppermute | solution.py:17
  3.4 0.9 %slice.57 = bf16[1,4,3,16,512]{4,3,2,1,0:T(8,128)(2,1)S(1)} slice(bf16[1,4,4,16,512]{4,3,2,1,0:T(8,128)(2,1)} %vo_ref.1), slice={[0:1], [0:4], [1:4], [0:16], [0:512]} | slice | bytes 393216 | tf_op jit(solution)/shard_map/slice | solution.py:199
  4.3 3.7 %collective-permute-start = (bf16[1,4,3,16,512]{4,3,2,1,0:T(8,128)(2,1)S(1)}, bf16[1,4,3,16,512]{4,3,2,1,0:T(8,128)(2,1)S(1)}, u32[]{:S(2)}, u32[]{:S(2)}) collective-permute-start(bf16[1,4,3,16,512]{4,3,2,1,0:T(8,128)(2,1)S(1)} %slice.57), channel_id=1, source_target_pairs={{0,4},{4,8},{8,12},{12,16},{16,20},{20,24},{24,28},{1,5},{5,9},{9,... | collective-permute-start | bytes 589832 | tf_op jit(solution)/shard_map/ppermute | solution.py:17
  8.2 0.1 pad_maximum_fusion.4
  8.3 0.1 maximum_bitcast_fusion.2
  8.4 0.1 maximum_bitcast_fusion.1
  8.4 0.1 pad_maximum_fusion.1
  8.6 0.1 copy.21
  8.7 0.1 reshape.92
  8.8 0.7 %copy.24.k1_ref = bf16[64,288]{1,0:T(8,128)(2,1)} copy(bf16[64,288]{0,1:T(8,128)(2,1)S(1)} %reshape.92) | data formatting | bytes 73728 | tf_op jit(solution)/shard_map/reshape | solution.py:182
  9.5 0.1 pad_maximum_fusion
  9.6 0.0 copy-start
  9.6 0.0 copy-start.9
  9.7 0.8 %copy.25.k2_ref = bf16[64,1152]{1,0:T(8,128)(2,1)} copy(bf16[64,1152]{0,1:T(8,128)(2,1)S(1)} %bitcast.49) | data formatting | bytes 294912 | tf_op jit(solution)/shard_map/reshape | solution.py:190
  10.5 0.1 copy-done.9
  10.6 0.1 maximum_bitcast_fusion
  10.7 0.1 reshape.102
  10.7 0.7 %copy.34.cot_ref = bf16[2,64,512]{2,1,0:T(8,128)(2,1)} copy(bf16[2,64,512]{2,0,1:T(2,128)(2,1)S(1)} %reshape.102) | data formatting | bytes 262144 | tf_op jit(solution)/shard_map/reshape | solution.py:204
  11.4 0.0 copy-start.3
  11.4 0.7 %copy-done.5 = bf16[1,4,3,16,512]{4,3,2,1,0:T(8,128)(2,1)} copy-done((bf16[1,4,3,16,512]{4,3,2,1,0:T(8,128)(2,1)}, bf16[1,4,3,16,512]{4,3,2,1,0:T(8,128)(2,1)S(1)}, u32[]{:S(2)}) %copy-start.5) | copy-done | bytes 196632
  12.1 0.1 copy-done.3
  12.2 8.4 %shard_map.75 = (bf16[64,512]{1,0:T(8,128)(2,1)}, bf16[512,256]{1,0:T(8,128)(2,1)}, f32[288,64]{1,0:T(8,128)}, f32[432,128]{1,0:T(8,128)}) custom-call(bf16[1,4,3,16,512]{4,3,2,1,0:T(8,128)(2,1)} %copy-done.5, bf16[1,4,4,16,512]{4,3,2,1,0:T(8,128)(2,1)} %vo_ref.1, bf16[1,4,4,16,512]{4,3,2,1,0:T(8,128)(2,1)} %copy-done.3, bf16[64,288]{1,0:T(8,128)(2,1)} %copy.24.k1_ref, ...), custom_call_target="tpu_custom_call" | custom-call | flops 60000000 | bytes 3000000 | tf_op jit(solution)/shard_map/pallas_call | solution.py:213
  20.6 0.9 %fusion.1 = (f32[96,128]{1,0:T(8,128)S(1)}, f32[96,128]{1,0:T(8,128)S(1)}, f32[96,128]{1,0:T(8,128)S(1)}) fusion(f32[432,128]{1,0:T(8,128)} %get-tuple-element.11), kind=kLoop, calls=%fused_computation.29 | loop fusion | bytes 294912 | tf_op jit(solution)/shard_map/slice | solution.py:31
  21.5 3.1 %collective-permute-start.18 = (f32[96,128]{1,0:T(8,128)S(1)}, f32[96,128]{1,0:T(8,128)S(1)}, u32[]{:S(2)}, u32[]{:S(2)}) collective-permute-start(f32[96,128]{1,0:T(8,128)S(1)} %get-tuple-element.31), channel_id=1, source_target_pairs={{0,1},{1,0},{2,3},{3,2},{4,5},{5,4},{6,7},{7,6},{8,9},{9,8},{10,11... | collective-permute-start | bytes 147464 | tf_op jit(solution)/shard_map/ppermute | solution.py:35
  24.6 5.1 %collective-permute-start.13 = (f32[96,128]{1,0:T(8,128)S(1)}, f32[96,128]{1,0:T(8,128)S(1)}, u32[]{:S(2)}, u32[]{:S(2)}) collective-permute-start(f32[96,128]{1,0:T(8,128)S(1)} %get-tuple-element.32), channel_id=1, source_target_pairs={{0,16},{4,20},{8,24},{12,28},{16,0},{20,4},{24,8},{28,12},{1,17},{... | collective-permute-start | bytes 147464 | tf_op jit(solution)/shard_map/ppermute | solution.py:35
  29.7 0.2 reshape.97
  29.9 0.1 fusion
  30.1 0.1 reshape.98
  30.2 1.6 %collective-permute-done.13 = f32[96,128]{1,0:T(8,128)S(1)} collective-permute-done((f32[96,128]{1,0:T(8,128)S(1)}, f32[96,128]{1,0:T(8,128)S(1)}, u32[]{:S(2)}, u32[]{:S(2)}) %collective-permute-start.13) | collective-permute-done | bytes 49184 | tf_op jit(solution)/shard_map/ppermute | solution.py:35
  31.8 2.0 %collective-permute-done.8 = f32[96,128]{1,0:T(8,128)S(1)} collective-permute-done((f32[96,128]{1,0:T(8,128)S(1)}, f32[96,128]{1,0:T(8,128)S(1)}, u32[]{:S(2)}, u32[]{:S(2)}) %collective-permute-start.8) | collective-permute-done | bytes 49184 | tf_op jit(solution)/shard_map/ppermute | solution.py:35
  33.8 0.1 collective-permute-start.3
  33.9 1.2 %collective-permute-done.3 = f32[96,128]{1,0:T(8,128)S(1)} collective-permute-done((f32[96,128]{1,0:T(8,128)S(1)}, f32[96,128]{1,0:T(8,128)S(1)}, u32[]{:S(2)}, u32[]{:S(2)}) %collective-permute-start.3) | collective-permute-done | bytes 49184 | tf_op jit(solution)/shard_map/ppermute | solution.py:35
  35.1 0.1 collective-permute-start.4
  35.2 2.6 %collective-permute-start.23 = (f32[75,128]{1,0:T(8,128)S(1)}, f32[75,128]{1,0:T(8,128)S(1)}, u32[]{:S(2)}, u32[]{:S(2)}) collective-permute-start(f32[75,128]{1,0:T(8,128)S(1)} %slice.72), channel_id=1, source_target_pairs={{0,2},{1,3},{2,0},{3,1},{4,6},{5,7},{6,4},{7,5},{8,10},{9,11},{10,... | collective-permute-start | bytes 115208 | tf_op jit(solution)/shard_map/ppermute | solution.py:35
  37.8 0.3 collective-permute-start.19
  38.2 0.1 collective-permute-start.9
  38.3 0.3 collective-permute-start.14
  38.6 0.6 collective-permute-done.4
  39.3 1.5 %collective-permute-start.5 = (f32[96,128]{1,0:T(8,128)S(1)}, f32[96,128]{1,0:T(8,128)S(1)}, u32[]{:S(2)}, u32[]{:S(2)}) collective-permute-start(f32[96,128]{1,0:T(8,128)S(1)} %add.129), channel_id=1, source_target_pairs={{0,16},{4,20},{8,24},{12,28},{16,0},{20,4},{24,8},{28,12},{1,17},{... | collective-permute-start | bytes 147464 | tf_op jit(solution)/shard_map/ppermute | solution.py:35
  40.8 0.1 collective-permute-start.24
  40.8 2.4 %collective-permute-done.19 = f32[96,128]{1,0:T(8,128)S(1)} collective-permute-done((f32[96,128]{1,0:T(8,128)S(1)}, f32[96,128]{1,0:T(8,128)S(1)}, u32[]{:S(2)}, u32[]{:S(2)}) %collective-permute-start.19) | collective-permute-done | bytes 49184 | tf_op jit(solution)/shard_map/ppermute | solution.py:35
  43.3 0.1 collective-permute-start.20
  43.4 0.5 collective-permute-start.10
  43.8 2.3 %collective-permute-start.15 = (f32[96,128]{1,0:T(8,128)S(1)}, f32[96,128]{1,0:T(8,128)S(1)}, u32[]{:S(2)}, u32[]{:S(2)}) collective-permute-start(f32[96,128]{1,0:T(8,128)S(1)} %add.139), channel_id=1, source_target_pairs={{0,2},{1,3},{2,0},{3,1},{4,6},{5,7},{6,4},{7,5},{8,10},{9,11},{10,... | collective-permute-start | bytes 147464 | tf_op jit(solution)/shard_map/ppermute | solution.py:35
  46.1 1.0 %collective-permute-start.6 = (f32[96,128]{1,0:T(8,128)S(1)}, f32[96,128]{1,0:T(8,128)S(1)}, u32[]{:S(2)}, u32[]{:S(2)}) collective-permute-start(f32[96,128]{1,0:T(8,128)S(1)} %add.130), channel_id=1, source_target_pairs={{0,1},{1,0},{2,3},{3,2},{4,5},{5,4},{6,7},{7,6},{8,9},{9,8},{10,11... | collective-permute-start | bytes 147464 | tf_op jit(solution)/shard_map/ppermute | solution.py:35
  47.1 2.0 %collective-permute-start.25 = (f32[75,128]{1,0:T(8,128)S(1)}, f32[75,128]{1,0:T(8,128)S(1)}, u32[]{:S(2)}, u32[]{:S(2)}) collective-permute-start(f32[75,128]{1,0:T(8,128)S(1)} %add.149), channel_id=1, source_target_pairs={{0,8},{4,12},{8,0},{12,4},{16,24},{20,28},{24,16},{28,20},{1,9},{5... | collective-permute-start | bytes 115208 | tf_op jit(solution)/shard_map/ppermute | solution.py:35
  49.1 0.2 collective-permute-start.21
  49.3 1.5 %collective-permute-start.11 = (f32[96,128]{1,0:T(8,128)S(1)}, f32[96,128]{1,0:T(8,128)S(1)}, u32[]{:S(2)}, u32[]{:S(2)}) collective-permute-start(f32[96,128]{1,0:T(8,128)S(1)} %add.135), channel_id=1, source_target_pairs={{0,2},{1,3},{2,0},{3,1},{4,6},{5,7},{6,4},{7,5},{8,10},{9,11},{10,... | collective-permute-start | bytes 147464 | tf_op jit(solution)/shard_map/ppermute | solution.py:35
  50.8 0.1 collective-permute-start.16
  50.9 0.0 copy-start.8
  50.9 1.6 %collective-permute-start.7 = (f32[96,128]{1,0:T(8,128)S(1)}, f32[96,128]{1,0:T(8,128)S(1)}, u32[]{:S(2)}, u32[]{:S(2)}) collective-permute-start(f32[96,128]{1,0:T(8,128)S(1)} %add.131), channel_id=1, source_target_pairs={{0,2},{1,3},{2,0},{3,1},{4,6},{5,7},{6,4},{7,5},{8,10},{9,11},{10,... | collective-permute-start | bytes 147464 | tf_op jit(solution)/shard_map/ppermute | solution.py:35
  52.5 0.4 collective-permute-start.26
  53.0 0.6 reshape.95
  53.6 0.9 %copy.40 = bf16[2,8,32,256]{3,1,0,2:T(8,128)(2,1)} copy(bf16[2,8,32,256]{3,2,1,0:T(8,128)(2,1)S(1)} %bitcast.53) | data formatting | bytes 524288 | tf_op jit(solution)/shard_map/reshape | solution.py:237
  54.5 2.1 %collective-permute-done.26 = f32[75,128]{1,0:T(8,128)S(1)} collective-permute-done((f32[75,128]{1,0:T(8,128)S(1)}, f32[75,128]{1,0:T(8,128)S(1)}, u32[]{:S(2)}, u32[]{:S(2)}) %collective-permute-start.26) | collective-permute-done | bytes 38432 | tf_op jit(solution)/shard_map/ppermute | solution.py:35
  56.6 1.1 %collective-permute-start.27 = (f32[75,128]{1,0:T(8,128)S(1)}, f32[75,128]{1,0:T(8,128)S(1)}, u32[]{:S(2)}, u32[]{:S(2)}) collective-permute-start(f32[75,128]{1,0:T(8,128)S(1)} %add.151), channel_id=1, source_target_pairs={{0,1},{1,0},{2,3},{3,2},{4,5},{5,4},{6,7},{7,6},{8,9},{9,8},{10,11... | collective-permute-start | bytes 115208 | tf_op jit(solution)/shard_map/ppermute | solution.py:35
  57.7 0.9 %collective-permute-start.22 = (f32[96,128]{1,0:T(8,128)S(1)}, f32[96,128]{1,0:T(8,128)S(1)}, u32[]{:S(2)}, u32[]{:S(2)}) collective-permute-start(f32[96,128]{1,0:T(8,128)S(1)} %add.146), channel_id=1, source_target_pairs={{0,16},{4,20},{8,24},{12,28},{16,0},{20,4},{24,8},{28,12},{1,17},{... | collective-permute-start | bytes 147464 | tf_op jit(solution)/shard_map/ppermute | solution.py:35
  58.6 0.1 collective-permute-start.12
  58.7 2.0 %collective-permute-start.17 = (f32[96,128]{1,0:T(8,128)S(1)}, f32[96,128]{1,0:T(8,128)S(1)}, u32[]{:S(2)}, u32[]{:S(2)}) collective-permute-start(f32[96,128]{1,0:T(8,128)S(1)} %add.141), channel_id=1, source_target_pairs={{0,8},{4,12},{8,0},{12,4},{16,24},{20,28},{24,16},{28,20},{1,9},{5... | collective-permute-start | bytes 147464 | tf_op jit(solution)/shard_map/ppermute | solution.py:35
  60.8 2.3 %collective-permute-done.17 = f32[96,128]{1,0:T(8,128)S(1)} collective-permute-done((f32[96,128]{1,0:T(8,128)S(1)}, f32[96,128]{1,0:T(8,128)S(1)}, u32[]{:S(2)}, u32[]{:S(2)}) %collective-permute-start.17) | collective-permute-done | bytes 49184 | tf_op jit(solution)/shard_map/ppermute | solution.py:35
  63.2 0.7 %reshape.99 = f32[3,3,3,4,32]{4,3,2,1,0:T(4,128)} reshape(f32[27,128]{1,0:T(8,128)S(1)} %slice_multiply_fusion.1) | data formatting | bytes 27648 | tf_op jit(solution)/shard_map/reshape | solution.py:252
  64.0 0.3 reshape.100
  64.2 0.8 %copy.32 = f32[27,2,16,64]{3,2,1,0:T(8,128)} copy(f32[27,2,16,64]{3,1,2,0:T(2,128)S(1)} %bitcast.51) | data formatting | bytes 442368 | tf_op jit(solution)/shard_map/transpose | solution.py:253
  (73 shorter events, 0.5 us)
Async XLA Ops:
  0.6 7.4 %copy-start.7 = (bf16[32,4,3,3,3]{0,1,4,3,2:T(4,128)(2,1)S(1)}, bf16[32,4,3,3,3]{0,1,4,3,2:T(4,128)(2,1)}, u32[]{:S(2)}) copy-start(bf16[32,4,3,3,3]{0,1,4,3,2:T(4,128)(2,1)} %param.5) | copy-start | bytes 20740
  0.6 7.5 %copy-start.4 = (bf16[64,32,3,3,3]{0,1,4,3,2:T(8,128)(2,1)S(1)}, bf16[64,32,3,3,3]{0,1,4,3,2:T(8,128)(2,1)}, u32[]{:S(2)}) copy-start(bf16[64,32,3,3,3]{0,1,4,3,2:T(8,128)(2,1)} %param.6) | copy-start | bytes 331780
  0.7 9.8 %collective-permute-start.2 = (bf16[1,64,1,4,128]{4,3,2,1,0:T(4,128)(2,1)}, bf16[1,64,1,4,128]{4,3,2,1,0:T(4,128)(2,1)S(1)}, u32[]{:S(2)}, u32[]{:S(2)}) collective-permute-start(bf16[1,64,1,4,128]{4,3,2,1,0:T(4,128)(2,1)} %param.7), channel_id=1, source_target_pairs={{4,0},{8,4},{12,8},{16,12},{20,16},{24,20},{28,24},{5,1},{9,5},{13... | collective-permute-start | bytes 196616 | tf_op jit(solution)/shard_map/ppermute | solution.py:17
  2.1 9.3 %collective-permute-start.1 = (bf16[1,4,4,16,512]{4,3,2,1,0:T(8,128)(2,1)}, bf16[1,4,4,16,512]{4,3,2,1,0:T(8,128)(2,1)S(1)}, u32[]{:S(2)}, u32[]{:S(2)}) collective-permute-start(bf16[1,4,4,16,512]{4,3,2,1,0:T(8,128)(2,1)} %vo_ref.1), channel_id=1, source_target_pairs={{4,0},{8,4},{12,8},{16,12},{20,16},{24,20},{28,24},{5,1},{9,5},{13... | collective-permute-start | bytes 786440 | tf_op jit(solution)/shard_map/ppermute | solution.py:17
  4.3 7.1 %collective-permute-start = (bf16[1,4,3,16,512]{4,3,2,1,0:T(8,128)(2,1)S(1)}, bf16[1,4,3,16,512]{4,3,2,1,0:T(8,128)(2,1)S(1)}, u32[]{:S(2)}, u32[]{:S(2)}) collective-permute-start(bf16[1,4,3,16,512]{4,3,2,1,0:T(8,128)(2,1)S(1)} %slice.57), channel_id=1, source_target_pairs={{0,4},{4,8},{8,12},{12,16},{16,20},{20,24},{24,28},{1,5},{5,9},{9,... | collective-permute-start | bytes 589832 | tf_op jit(solution)/shard_map/ppermute | solution.py:17
  9.6 1.0 %copy-start = (bf16[64,3,3,2,2,32]{0,5,4,3,2,1:T(8,128)(2,1)}, bf16[64,3,3,2,2,32]{0,5,4,3,2,1:T(8,128)(2,1)S(1)}, u32[]{:S(2)}) copy-start(bf16[64,3,3,2,2,32]{0,5,4,3,2,1:T(8,128)(2,1)S(1)} %copy.22) | copy-start | bytes 442372
  9.6 0.9 %copy-start.9 = (bf16[1,64,1,4,128]{4,3,2,1,0:T(4,128)(2,1)S(1)}, bf16[1,64,1,4,128]{4,3,2,1,0:T(4,128)(2,1)}, u32[]{:S(2)}) copy-start(bf16[1,64,1,4,128]{4,3,2,1,0:T(4,128)(2,1)} %param.7) | copy-start | bytes 196612
  11.4 0.7 %copy-start.5 = (bf16[1,4,3,16,512]{4,3,2,1,0:T(8,128)(2,1)}, bf16[1,4,3,16,512]{4,3,2,1,0:T(8,128)(2,1)S(1)}, u32[]{:S(2)}) copy-start(bf16[1,4,3,16,512]{4,3,2,1,0:T(8,128)(2,1)S(1)} %collective-permute-done.vb_ref) | copy-start | bytes 589828
  11.4 0.8 %copy-start.3 = (bf16[1,4,4,16,512]{4,3,2,1,0:T(8,128)(2,1)}, bf16[1,4,4,16,512]{4,3,2,1,0:T(8,128)(2,1)S(1)}, u32[]{:S(2)}) copy-start(bf16[1,4,4,16,512]{4,3,2,1,0:T(8,128)(2,1)S(1)} %collective-permute-done.1.va_ref) | copy-start | bytes 786436
  20.6 9.1 %copy-start.6 = (f32[288,64]{1,0:T(8,128)S(1)}, f32[288,64]{1,0:T(8,128)}, u32[]{:S(2)}) copy-start(f32[288,64]{1,0:T(8,128)} %get-tuple-element.10) | copy-start | bytes 221188
  21.5 8.7 %collective-permute-start.18 = (f32[96,128]{1,0:T(8,128)S(1)}, f32[96,128]{1,0:T(8,128)S(1)}, u32[]{:S(2)}, u32[]{:S(2)}) collective-permute-start(f32[96,128]{1,0:T(8,128)S(1)} %get-tuple-element.31), channel_id=1, source_target_pairs={{0,1},{1,0},{2,3},{3,2},{4,5},{5,4},{6,7},{7,6},{8,9},{9,8},{10,11... | collective-permute-start | bytes 147464 | tf_op jit(solution)/shard_map/ppermute | solution.py:35
  24.6 7.2 %collective-permute-start.13 = (f32[96,128]{1,0:T(8,128)S(1)}, f32[96,128]{1,0:T(8,128)S(1)}, u32[]{:S(2)}, u32[]{:S(2)}) collective-permute-start(f32[96,128]{1,0:T(8,128)S(1)} %get-tuple-element.32), channel_id=1, source_target_pairs={{0,16},{4,20},{8,24},{12,28},{16,0},{20,4},{24,8},{28,12},{1,17},{... | collective-permute-start | bytes 147464 | tf_op jit(solution)/shard_map/ppermute | solution.py:35
  29.7 4.1 %collective-permute-start.8 = (f32[96,128]{1,0:T(8,128)S(1)}, f32[96,128]{1,0:T(8,128)S(1)}, u32[]{:S(2)}, u32[]{:S(2)}) collective-permute-start(f32[96,128]{1,0:T(8,128)S(1)} %get-tuple-element.33), channel_id=1, source_target_pairs={{0,8},{4,12},{8,0},{12,4},{16,24},{20,28},{24,16},{28,20},{1,9},{5... | collective-permute-start | bytes 147464 | tf_op jit(solution)/shard_map/ppermute | solution.py:35
  30.0 3.8 %copy-start.1 = (f32[432,128]{1,0:T(8,128)S(1)}, f32[432,128]{1,0:T(8,128)}, u32[]{:S(2)}) copy-start(f32[432,128]{1,0:T(8,128)} %get-tuple-element.11) | copy-start | bytes 663556
  33.8 1.3 %collective-permute-start.3 = (f32[96,128]{1,0:T(8,128)S(1)}, f32[96,128]{1,0:T(8,128)S(1)}, u32[]{:S(2)}, u32[]{:S(2)}) collective-permute-start(f32[96,128]{1,0:T(8,128)S(1)} %get-tuple-element.30), channel_id=1, source_target_pairs={{0,4},{4,0},{8,12},{12,8},{16,20},{20,16},{24,28},{28,24},{1,5},{5... | collective-permute-start | bytes 147464 | tf_op jit(solution)/shard_map/ppermute | solution.py:35
  35.1 4.2 %collective-permute-start.4 = (f32[96,128]{1,0:T(8,128)S(1)}, f32[96,128]{1,0:T(8,128)S(1)}, u32[]{:S(2)}, u32[]{:S(2)}) collective-permute-start(f32[96,128]{1,0:T(8,128)S(1)} %add.128), channel_id=1, source_target_pairs={{0,8},{4,12},{8,0},{12,4},{16,24},{20,28},{24,16},{28,20},{1,9},{5... | collective-permute-start | bytes 147464 | tf_op jit(solution)/shard_map/ppermute | solution.py:35
  35.2 5.5 %collective-permute-start.23 = (f32[75,128]{1,0:T(8,128)S(1)}, f32[75,128]{1,0:T(8,128)S(1)}, u32[]{:S(2)}, u32[]{:S(2)}) collective-permute-start(f32[75,128]{1,0:T(8,128)S(1)} %slice.72), channel_id=1, source_target_pairs={{0,2},{1,3},{2,0},{3,1},{4,6},{5,7},{6,4},{7,5},{8,10},{9,11},{10,... | collective-permute-start | bytes 115208 | tf_op jit(solution)/shard_map/ppermute | solution.py:35
  37.8 5.4 %collective-permute-start.19 = (f32[96,128]{1,0:T(8,128)S(1)}, f32[96,128]{1,0:T(8,128)S(1)}, u32[]{:S(2)}, u32[]{:S(2)}) collective-permute-start(f32[96,128]{1,0:T(8,128)S(1)} %get-tuple-element.27), channel_id=1, source_target_pairs={{0,2},{1,3},{2,0},{3,1},{4,6},{5,7},{6,4},{7,5},{8,10},{9,11},{10,... | collective-permute-start | bytes 147464 | tf_op jit(solution)/shard_map/ppermute | solution.py:35
  38.2 5.1 %collective-permute-start.9 = (f32[96,128]{1,0:T(8,128)S(1)}, f32[96,128]{1,0:T(8,128)S(1)}, u32[]{:S(2)}, u32[]{:S(2)}) collective-permute-start(f32[96,128]{1,0:T(8,128)S(1)} %get-tuple-element.28), channel_id=1, source_target_pairs={{0,16},{4,20},{8,24},{12,28},{16,0},{20,4},{24,8},{28,12},{1,17},{... | collective-permute-start | bytes 147464 | tf_op jit(solution)/shard_map/ppermute | solution.py:35
  38.3 5.5 %collective-permute-start.14 = (f32[96,128]{1,0:T(8,128)S(1)}, f32[96,128]{1,0:T(8,128)S(1)}, u32[]{:S(2)}, u32[]{:S(2)}) collective-permute-start(f32[96,128]{1,0:T(8,128)S(1)} %get-tuple-element.29), channel_id=1, source_target_pairs={{0,1},{1,0},{2,3},{3,2},{4,5},{5,4},{6,7},{7,6},{8,9},{9,8},{10,11... | collective-permute-start | bytes 147464 | tf_op jit(solution)/shard_map/ppermute | solution.py:35
  39.3 6.8 %collective-permute-start.5 = (f32[96,128]{1,0:T(8,128)S(1)}, f32[96,128]{1,0:T(8,128)S(1)}, u32[]{:S(2)}, u32[]{:S(2)}) collective-permute-start(f32[96,128]{1,0:T(8,128)S(1)} %add.129), channel_id=1, source_target_pairs={{0,16},{4,20},{8,24},{12,28},{16,0},{20,4},{24,8},{28,12},{1,17},{... | collective-permute-start | bytes 147464 | tf_op jit(solution)/shard_map/ppermute | solution.py:35
  40.8 6.4 %collective-permute-start.24 = (f32[75,128]{1,0:T(8,128)S(1)}, f32[75,128]{1,0:T(8,128)S(1)}, u32[]{:S(2)}, u32[]{:S(2)}) collective-permute-start(f32[75,128]{1,0:T(8,128)S(1)} %slice_add_fusion.1), channel_id=1, source_target_pairs={{0,4},{4,0},{8,12},{12,8},{16,20},{20,16},{24,28},{28,24},{1,5},{5... | collective-permute-start | bytes 115208 | tf_op jit(solution)/shard_map/ppermute | solution.py:35
  43.3 5.9 %collective-permute-start.20 = (f32[96,128]{1,0:T(8,128)S(1)}, f32[96,128]{1,0:T(8,128)S(1)}, u32[]{:S(2)}, u32[]{:S(2)}) collective-permute-start(f32[96,128]{1,0:T(8,128)S(1)} %add.144), channel_id=1, source_target_pairs={{0,4},{4,0},{8,12},{12,8},{16,20},{20,16},{24,28},{28,24},{1,5},{5... | collective-permute-start | bytes 147464 | tf_op jit(solution)/shard_map/ppermute | solution.py:35
  43.4 5.9 %collective-permute-start.10 = (f32[96,128]{1,0:T(8,128)S(1)}, f32[96,128]{1,0:T(8,128)S(1)}, u32[]{:S(2)}, u32[]{:S(2)}) collective-permute-start(f32[96,128]{1,0:T(8,128)S(1)} %add.134), channel_id=1, source_target_pairs={{0,1},{1,0},{2,3},{3,2},{4,5},{5,4},{6,7},{7,6},{8,9},{9,8},{10,11... | collective-permute-start | bytes 147464 | tf_op jit(solution)/shard_map/ppermute | solution.py:35
  43.8 7.0 %collective-permute-start.15 = (f32[96,128]{1,0:T(8,128)S(1)}, f32[96,128]{1,0:T(8,128)S(1)}, u32[]{:S(2)}, u32[]{:S(2)}) collective-permute-start(f32[96,128]{1,0:T(8,128)S(1)} %add.139), channel_id=1, source_target_pairs={{0,2},{1,3},{2,0},{3,1},{4,6},{5,7},{6,4},{7,5},{8,10},{9,11},{10,... | collective-permute-start | bytes 147464 | tf_op jit(solution)/shard_map/ppermute | solution.py:35
  46.1 4.8 %collective-permute-start.6 = (f32[96,128]{1,0:T(8,128)S(1)}, f32[96,128]{1,0:T(8,128)S(1)}, u32[]{:S(2)}, u32[]{:S(2)}) collective-permute-start(f32[96,128]{1,0:T(8,128)S(1)} %add.130), channel_id=1, source_target_pairs={{0,1},{1,0},{2,3},{3,2},{4,5},{5,4},{6,7},{7,6},{8,9},{9,8},{10,11... | collective-permute-start | bytes 147464 | tf_op jit(solution)/shard_map/ppermute | solution.py:35
  47.1 5.4 %collective-permute-start.25 = (f32[75,128]{1,0:T(8,128)S(1)}, f32[75,128]{1,0:T(8,128)S(1)}, u32[]{:S(2)}, u32[]{:S(2)}) collective-permute-start(f32[75,128]{1,0:T(8,128)S(1)} %add.149), channel_id=1, source_target_pairs={{0,8},{4,12},{8,0},{12,4},{16,24},{20,28},{24,16},{28,20},{1,9},{5... | collective-permute-start | bytes 115208 | tf_op jit(solution)/shard_map/ppermute | solution.py:35
  49.1 8.5 %collective-permute-start.21 = (f32[96,128]{1,0:T(8,128)S(1)}, f32[96,128]{1,0:T(8,128)S(1)}, u32[]{:S(2)}, u32[]{:S(2)}) collective-permute-start(f32[96,128]{1,0:T(8,128)S(1)} %add.145), channel_id=1, source_target_pairs={{0,8},{4,12},{8,0},{12,4},{16,24},{20,28},{24,16},{28,20},{1,9},{5... | collective-permute-start | bytes 147464 | tf_op jit(solution)/shard_map/ppermute | solution.py:35
  49.3 4.3 %copy-start.2 = (bf16[512,256]{1,0:T(8,128)(2,1)S(1)}, bf16[512,256]{1,0:T(8,128)(2,1)}, u32[]{:S(2)}) copy-start(bf16[512,256]{1,0:T(8,128)(2,1)} %get-tuple-element.9) | copy-start | bytes 786436
  49.3 9.3 %collective-permute-start.11 = (f32[96,128]{1,0:T(8,128)S(1)}, f32[96,128]{1,0:T(8,128)S(1)}, u32[]{:S(2)}, u32[]{:S(2)}) collective-permute-start(f32[96,128]{1,0:T(8,128)S(1)} %add.135), channel_id=1, source_target_pairs={{0,2},{1,3},{2,0},{3,1},{4,6},{5,7},{6,4},{7,5},{8,10},{9,11},{10,... | collective-permute-start | bytes 147464 | tf_op jit(solution)/shard_map/ppermute | solution.py:35
  50.8 7.9 %collective-permute-start.16 = (f32[96,128]{1,0:T(8,128)S(1)}, f32[96,128]{1,0:T(8,128)S(1)}, u32[]{:S(2)}, u32[]{:S(2)}) collective-permute-start(f32[96,128]{1,0:T(8,128)S(1)} %add.140), channel_id=1, source_target_pairs={{0,4},{4,0},{8,12},{12,8},{16,20},{20,16},{24,28},{28,24},{1,5},{5... | collective-permute-start | bytes 147464 | tf_op jit(solution)/shard_map/ppermute | solution.py:35
  50.9 2.0 %copy-start.8 = (bf16[64,512]{1,0:T(8,128)(2,1)S(1)}, bf16[64,512]{1,0:T(8,128)(2,1)}, u32[]{:S(2)}) copy-start(bf16[64,512]{1,0:T(8,128)(2,1)} %get-tuple-element.8) | copy-start | bytes 196612
  50.9 9.8 %collective-permute-start.7 = (f32[96,128]{1,0:T(8,128)S(1)}, f32[96,128]{1,0:T(8,128)S(1)}, u32[]{:S(2)}, u32[]{:S(2)}) collective-permute-start(f32[96,128]{1,0:T(8,128)S(1)} %add.131), channel_id=1, source_target_pairs={{0,2},{1,3},{2,0},{3,1},{4,6},{5,7},{6,4},{7,5},{8,10},{9,11},{10,... | collective-permute-start | bytes 147464 | tf_op jit(solution)/shard_map/ppermute | solution.py:35
  52.5 4.1 %collective-permute-start.26 = (f32[75,128]{1,0:T(8,128)S(1)}, f32[75,128]{1,0:T(8,128)S(1)}, u32[]{:S(2)}, u32[]{:S(2)}) collective-permute-start(f32[75,128]{1,0:T(8,128)S(1)} %add.150), channel_id=1, source_target_pairs={{0,16},{4,20},{8,24},{12,28},{16,0},{20,4},{24,8},{28,12},{1,17},{... | collective-permute-start | bytes 115208 | tf_op jit(solution)/shard_map/ppermute | solution.py:35
  56.6 6.6 %collective-permute-start.27 = (f32[75,128]{1,0:T(8,128)S(1)}, f32[75,128]{1,0:T(8,128)S(1)}, u32[]{:S(2)}, u32[]{:S(2)}) collective-permute-start(f32[75,128]{1,0:T(8,128)S(1)} %add.151), channel_id=1, source_target_pairs={{0,1},{1,0},{2,3},{3,2},{4,5},{5,4},{6,7},{7,6},{8,9},{9,8},{10,11... | collective-permute-start | bytes 115208 | tf_op jit(solution)/shard_map/ppermute | solution.py:35
  57.7 5.4 %collective-permute-start.22 = (f32[96,128]{1,0:T(8,128)S(1)}, f32[96,128]{1,0:T(8,128)S(1)}, u32[]{:S(2)}, u32[]{:S(2)}) collective-permute-start(f32[96,128]{1,0:T(8,128)S(1)} %add.146), channel_id=1, source_target_pairs={{0,16},{4,20},{8,24},{12,28},{16,0},{20,4},{24,8},{28,12},{1,17},{... | collective-permute-start | bytes 147464 | tf_op jit(solution)/shard_map/ppermute | solution.py:35
  58.6 2.1 %collective-permute-start.12 = (f32[96,128]{1,0:T(8,128)S(1)}, f32[96,128]{1,0:T(8,128)S(1)}, u32[]{:S(2)}, u32[]{:S(2)}) collective-permute-start(f32[96,128]{1,0:T(8,128)S(1)} %add.136), channel_id=1, source_target_pairs={{0,4},{4,0},{8,12},{12,8},{16,20},{20,16},{24,28},{28,24},{1,5},{5... | collective-permute-start | bytes 147464 | tf_op jit(solution)/shard_map/ppermute | solution.py:35
  58.7 4.4 %collective-permute-start.17 = (f32[96,128]{1,0:T(8,128)S(1)}, f32[96,128]{1,0:T(8,128)S(1)}, u32[]{:S(2)}, u32[]{:S(2)}) collective-permute-start(f32[96,128]{1,0:T(8,128)S(1)} %add.141), channel_id=1, source_target_pairs={{0,8},{4,12},{8,0},{12,4},{16,24},{20,28},{24,16},{28,20},{1,9},{5... | collective-permute-start | bytes 147464 | tf_op jit(solution)/shard_map/ppermute | solution.py:35

commit v4 on v2

--- a/solution.py
+++ b/solution.py
@@ -18,14 +18,26 @@
 
 
 def _all_sum(x, axes):
+    steps = []
     for axis in axes:
         n = lax.axis_size(axis)
         assert n & (n - 1) == 0
         k = 1
         while k < n:
-            x = x + lax.ppermute(x, axis, [(i, i ^ k) for i in range(n)])
+            steps.append((axis, n, k))
             k *= 2
-    return x
+    axis0, n0, k0 = steps[0]
+    rows = x.shape[0]
+    half = -(-rows // 16) * 8
+    x = jnp.pad(x, ((0, 2 * half - rows), (0, 0)))
+    low = (lax.axis_index(axis0) & k0) == 0
+    lo, hi = x[:half], x[half:]
+    pair = [(i, i ^ k0) for i in range(n0)]
+    part = jnp.where(low, lo, hi) + lax.ppermute(jnp.where(low, hi, lo), axis0, pair)
+    for axis, n, k in steps[1:]:
+        part = part + lax.ppermute(part, axis, [(i, i ^ k) for i in range(n)])
+    other = lax.ppermute(part, axis0, pair)
+    return jnp.where(low, jnp.concatenate([part, other], 0), jnp.concatenate([other, part], 0))[:rows]
 
 
 def _sigmoid(v):

time: 64.4 us -> 54.9 us (0.85)
  waiting for transfers between devices: 24.8 us -> 15.1 us
    ppermute x5 -> x6, waiting for transfers between devices: 24.8 us -> 15.1 us  [the longest x4 14.2 us: _all_sum(): part = part + lax.ppermute(part, axis, [(i, i ^ k) for i in range(n)])]
    ppermute x5 -> x6, starting transfers between devices: 12.9 us -> 13.1 us  [the longest x4 10.4 us: _all_sum(): part = part + lax.ppermute(part, axis, [(i, i ^ k) for i in range(n)])]
  transfers between devices with their start and end apart: 8 -> 9, of which waited for: 5 -> 5; matrix products, arithmetic and copies ran while one was open for 9% -> 10% of each run, Pallas kernels for 0% -> 0%
where the time goes in v4:
time: 54.9 us; the launch traced here: 54.5 us
  starting transfers between devices  19.5 us (36%)
  waiting for transfers between devices  15.1 us (28%)
  local copies, waits for them, and re-layouts  9.68 us (18%)
  Pallas kernels  8.39 us (15%)
  between operations  0.97 us (2%)
  other arithmetic  0.84 us (2%)
    ppermute x4, waiting for transfers between devices, _all_sum(): part = part + lax.ppermute(part, axis, [(i, i ^ k) for i in range(n)])  14.2 us
    ppermute x4, starting transfers between devices, _all_sum(): part = part + lax.ppermute(part, axis, [(i, i ^ k) for i in range(n)])  10.4 us
    pallas_call x1, Pallas kernels, per_device(): pl.pallas_call(_kernel, out_shape=(jax.ShapeDtypeStruct((c2, n2), BF16),...  8.39 us
    ppermute x3, starting transfers between devices, shifted(): return lax.ppermute(block, axis, route)  6.39 us
    ppermute x1, starting transfers between devices, _all_sum(): lax.ppermute(jnp.where(low, hi, lo), axis0, pair)  2.63 us
    unnamed x18, local copies, waits for them, and re-layouts  1.61 us
    reshape x1, local copies, waits for them, and re-layouts, per_device(): s1r = s1.reshape(3, 3, 2, c0, 4, 2, c1)  1.11 us
  transfers between devices with their start and end apart: 9, of which 5 were waited for; matrix products, arithmetic and copies ran while one was open for 10% of the time, Pallas kernels for 0%

profile of v4, /device:TPU:0, one launch (start us, length us, event | category | flops | bytes accessed | tf_op | source)
XLA Modules:
  0.0 54.5 jit_solution(18313457198232852031)
XLA Ops:
  0.6 0.0 copy-start.6
  0.6 0.0 copy-start.4
  0.7 1.4 %collective-permute-start.2 = (bf16[1,64,1,4,128]{4,3,2,1,0:T(4,128)(2,1)}, bf16[1,64,1,4,128]{4,3,2,1,0:T(4,128)(2,1)S(1)}, u32[]{:S(2)}, u32[]{:S(2)}) collective-permute-start(bf16[1,64,1,4,128]{4,3,2,1,0:T(4,128)(2,1)} %param.7), channel_id=1, source_target_pairs={{4,0},{8,4},{12,8},{16,12},{20,16},{24,20},{28,24},{5,1},{9,5},{13... | collective-permute-start | bytes 196616 | tf_op jit(solution)/shard_map/ppermute | solution.py:17
  2.1 1.3 %collective-permute-start.1 = (bf16[1,4,4,16,512]{4,3,2,1,0:T(8,128)(2,1)}, bf16[1,4,4,16,512]{4,3,2,1,0:T(8,128)(2,1)S(1)}, u32[]{:S(2)}, u32[]{:S(2)}) collective-permute-start(bf16[1,4,4,16,512]{4,3,2,1,0:T(8,128)(2,1)} %vo_ref.1), channel_id=1, source_target_pairs={{4,0},{8,4},{12,8},{16,12},{20,16},{24,20},{28,24},{5,1},{9,5},{13... | collective-permute-start | bytes 786440 | tf_op jit(solution)/shard_map/ppermute | solution.py:17
  3.4 0.9 %slice.52 = bf16[1,4,3,16,512]{4,3,2,1,0:T(8,128)(2,1)S(1)} slice(bf16[1,4,4,16,512]{4,3,2,1,0:T(8,128)(2,1)} %vo_ref.1), slice={[0:1], [0:4], [1:4], [0:16], [0:512]} | slice | bytes 393216 | tf_op jit(solution)/shard_map/slice | solution.py:203
  4.3 3.7 %collective-permute-start = (bf16[1,4,3,16,512]{4,3,2,1,0:T(8,128)(2,1)S(1)}, bf16[1,4,3,16,512]{4,3,2,1,0:T(8,128)(2,1)S(1)}, u32[]{:S(2)}, u32[]{:S(2)}) collective-permute-start(bf16[1,4,3,16,512]{4,3,2,1,0:T(8,128)(2,1)S(1)} %slice.52), channel_id=1, source_target_pairs={{0,4},{4,8},{8,12},{12,16},{16,20},{20,24},{24,28},{1,5},{5,9},{9,... | collective-permute-start | bytes 589832 | tf_op jit(solution)/shard_map/ppermute | solution.py:17
  8.0 0.0 copy-done.6
  8.1 0.0 copy-done.4
  8.2 0.1 pad_maximum_fusion.4
  8.3 0.1 maximum_bitcast_fusion.2
  8.4 0.1 maximum_bitcast_fusion.1
  8.4 0.1 pad_maximum_fusion.2
  8.6 0.1 copy.21
  8.7 0.1 reshape.92
  8.8 0.7 %copy.24.k1_ref = bf16[64,288]{1,0:T(8,128)(2,1)} copy(bf16[64,288]{0,1:T(8,128)(2,1)S(1)} %reshape.92) | data formatting | bytes 73728 | tf_op jit(solution)/shard_map/reshape | solution.py:186
  9.5 0.1 pad_maximum_fusion.1
  9.6 0.0 copy-start
  9.7 0.0 copy-start.8
  9.7 0.8 %copy.25.k2_ref = bf16[64,1152]{1,0:T(8,128)(2,1)} copy(bf16[64,1152]{0,1:T(8,128)(2,1)S(1)} %bitcast.49) | data formatting | bytes 294912 | tf_op jit(solution)/shard_map/reshape | solution.py:194
  10.5 0.0 collective-permute-done.2
  10.5 0.1 copy-done.8
  10.6 0.1 maximum_bitcast_fusion
  10.7 0.0 copy-done
  10.7 0.1 reshape.102
  10.7 0.7 %copy.34.cot_ref = bf16[2,64,512]{2,1,0:T(8,128)(2,1)} copy(bf16[2,64,512]{2,0,1:T(2,128)(2,1)S(1)} %reshape.102) | data formatting | bytes 262144 | tf_op jit(solution)/shard_map/reshape | solution.py:208
  11.4 0.0 collective-permute-done.vb_ref
  11.4 0.0 copy-start.5
  11.4 0.0 collective-permute-done.1.va_ref
  11.4 0.0 copy-start.3
  11.4 0.7 %copy-done.5 = bf16[1,4,3,16,512]{4,3,2,1,0:T(8,128)(2,1)} copy-done((bf16[1,4,3,16,512]{4,3,2,1,0:T(8,128)(2,1)}, bf16[1,4,3,16,512]{4,3,2,1,0:T(8,128)(2,1)S(1)}, u32[]{:S(2)}) %copy-start.5) | copy-done | bytes 196632
  12.1 0.1 copy-done.3
  12.2 8.4 %shard_map.75 = (bf16[64,512]{1,0:T(8,128)(2,1)}, bf16[512,256]{1,0:T(8,128)(2,1)}, f32[288,64]{1,0:T(8,128)}, f32[432,128]{1,0:T(8,128)}) custom-call(bf16[1,4,3,16,512]{4,3,2,1,0:T(8,128)(2,1)} %copy-done.5, bf16[1,4,4,16,512]{4,3,2,1,0:T(8,128)(2,1)} %vo_ref.1, bf16[1,4,4,16,512]{4,3,2,1,0:T(8,128)(2,1)} %copy-done.3, bf16[64,288]{1,0:T(8,128)(2,1)} %copy.24.k1_ref, ...), custom_call_target="tpu_custom_call" | custom-call | flops 60000000 | bytes 3000000 | tf_op jit(solution)/shard_map/pallas_call | solution.py:217
  20.6 1.1 %reshape.97 = f32[3,3,2,4,4,2,32]{6,5,4,3,2,1,0:T(2,128)S(1)} reshape(f32[288,64]{1,0:T(8,128)} %get-tuple-element.10) | data formatting | bytes 147456 | tf_op jit(solution)/shard_map/reshape | solution.py:243
  21.7 0.1 fusion.2
  21.8 0.0 copy-start.1
  21.9 0.1 reshape.98
  22.0 0.8 %copy-done.1 = f32[432,128]{1,0:T(8,128)S(1)} copy-done((f32[432,128]{1,0:T(8,128)S(1)}, f32[432,128]{1,0:T(8,128)}, u32[]{:S(2)}) %copy-start.1) | copy-done | bytes 221208
  22.8 2.6 %collective-permute-start.3 = (f32[232,128]{1,0:T(8,128)S(1)}, f32[232,128]{1,0:T(8,128)S(1)}, u32[]{:S(2)}, u32[]{:S(2)}) collective-permute-start(f32[232,128]{1,0:T(8,128)S(1)} %fusion.1), channel_id=1, source_target_pairs={{0,4},{4,0},{8,12},{12,8},{16,20},{20,16},{24,28},{28,24},{1,5},{5... | collective-permute-start | bytes 356360 | tf_op jit(solution)/shard_map/ppermute | solution.py:36
  25.4 1.0 %collective-permute-done.3 = f32[232,128]{1,0:T(8,128)S(1)} collective-permute-done((f32[232,128]{1,0:T(8,128)S(1)}, f32[232,128]{1,0:T(8,128)S(1)}, u32[]{:S(2)}, u32[]{:S(2)}) %collective-permute-start.3) | collective-permute-done | bytes 118816 | tf_op jit(solution)/shard_map/ppermute | solution.py:36
  26.4 3.1 %collective-permute-start.4 = (f32[232,128]{1,0:T(8,128)S(1)}, f32[232,128]{1,0:T(8,128)S(1)}, u32[]{:S(2)}, u32[]{:S(2)}) collective-permute-start(f32[232,128]{1,0:T(8,128)S(1)} %select_add_fusion), channel_id=1, source_target_pairs={{0,8},{4,12},{8,0},{12,4},{16,24},{20,28},{24,16},{28,20},{1,9},{5... | collective-permute-start | bytes 356360 | tf_op jit(solution)/shard_map/ppermute | solution.py:38
  29.5 3.7 %collective-permute-done.4 = f32[232,128]{1,0:T(8,128)S(1)} collective-permute-done((f32[232,128]{1,0:T(8,128)S(1)}, f32[232,128]{1,0:T(8,128)S(1)}, u32[]{:S(2)}, u32[]{:S(2)}) %collective-permute-start.4) | collective-permute-done | bytes 118816 | tf_op jit(solution)/shard_map/ppermute | solution.py:38
  33.3 3.0 %collective-permute-start.5 = (f32[232,128]{1,0:T(8,128)S(1)}, f32[232,128]{1,0:T(8,128)S(1)}, u32[]{:S(2)}, u32[]{:S(2)}) collective-permute-start(f32[232,128]{1,0:T(8,128)S(1)} %add.71), channel_id=1, source_target_pairs={{0,16},{4,20},{8,24},{12,28},{16,0},{20,4},{24,8},{28,12},{1,17},{... | collective-permute-start | bytes 356360 | tf_op jit(solution)/shard_map/ppermute | solution.py:38
  36.2 2.8 %collective-permute-done.5 = f32[232,128]{1,0:T(8,128)S(1)} collective-permute-done((f32[232,128]{1,0:T(8,128)S(1)}, f32[232,128]{1,0:T(8,128)S(1)}, u32[]{:S(2)}, u32[]{:S(2)}) %collective-permute-start.5) | collective-permute-done | bytes 118816 | tf_op jit(solution)/shard_map/ppermute | solution.py:38
  39.0 1.6 %collective-permute-start.6 = (f32[232,128]{1,0:T(8,128)S(1)}, f32[232,128]{1,0:T(8,128)S(1)}, u32[]{:S(2)}, u32[]{:S(2)}) collective-permute-start(f32[232,128]{1,0:T(8,128)S(1)} %add.72), channel_id=1, source_target_pairs={{0,1},{1,0},{2,3},{3,2},{4,5},{5,4},{6,7},{7,6},{8,9},{9,8},{10,11... | collective-permute-start | bytes 356360 | tf_op jit(solution)/shard_map/ppermute | solution.py:38
  40.7 3.3 %collective-permute-done.6 = f32[232,128]{1,0:T(8,128)S(1)} collective-permute-done((f32[232,128]{1,0:T(8,128)S(1)}, f32[232,128]{1,0:T(8,128)S(1)}, u32[]{:S(2)}, u32[]{:S(2)}) %collective-permute-start.6) | collective-permute-done | bytes 118816 | tf_op jit(solution)/shard_map/ppermute | solution.py:38
  44.0 0.0 copy-start.2
  44.0 2.7 %collective-permute-start.7 = (f32[232,128]{1,0:T(8,128)S(1)}, f32[232,128]{1,0:T(8,128)S(1)}, u32[]{:S(2)}, u32[]{:S(2)}) collective-permute-start(f32[232,128]{1,0:T(8,128)S(1)} %add.73), channel_id=1, source_target_pairs={{0,2},{1,3},{2,0},{3,1},{4,6},{5,7},{6,4},{7,5},{8,10},{9,11},{10,... | collective-permute-start | bytes 356360 | tf_op jit(solution)/shard_map/ppermute | solution.py:38
  46.7 4.3 %collective-permute-done.7 = f32[232,128]{1,0:T(8,128)S(1)} collective-permute-done((f32[232,128]{1,0:T(8,128)S(1)}, f32[232,128]{1,0:T(8,128)S(1)}, u32[]{:S(2)}, u32[]{:S(2)}) %collective-permute-start.7) | collective-permute-done | bytes 118816 | tf_op jit(solution)/shard_map/ppermute | solution.py:38
  51.1 0.1 collective-permute-start.8
  51.2 0.0 copy-done.2
  51.2 0.0 copy-start.7
  51.2 0.9 %copy.40 = bf16[2,8,32,256]{3,1,0,2:T(8,128)(2,1)} copy(bf16[2,8,32,256]{3,2,1,0:T(8,128)(2,1)S(1)} %bitcast.53) | data formatting | bytes 524288 | tf_op jit(solution)/shard_map/reshape | solution.py:241
  52.0 0.0 copy-done.7
  52.0 0.6 %reshape.95 = bf16[1,64,1,4,128]{4,3,1,2,0:T(4,128)(2,1)} reshape(bf16[64,512]{1,0:T(8,128)(2,1)S(1)} %copy-done.7) | data formatting | bytes 131072 | tf_op jit(solution)/shard_map/reshape | solution.py:240
  52.7 0.0 collective-permute-done.8
  52.8 0.3 reshape.100
  53.0 0.8 %copy.32 = f32[27,2,16,64]{3,2,1,0:T(8,128)} copy(f32[27,2,16,64]{3,1,2,0:T(2,128)S(1)} %bitcast.51) | data formatting | bytes 442368 | tf_op jit(solution)/shard_map/transpose | solution.py:257
  53.8 0.7 %reshape.99 = f32[3,3,3,4,32]{4,3,2,1,0:T(4,128)} reshape(f32[27,128]{1,0:T(8,128)S(1)} %slice_multiply_fusion.1) | data formatting | bytes 27648 | tf_op jit(solution)/shard_map/reshape | solution.py:256
  (22 shorter events, 0.4 us)
Async XLA Ops:
  0.6 7.4 %copy-start.6 = (bf16[32,4,3,3,3]{0,1,4,3,2:T(4,128)(2,1)S(1)}, bf16[32,4,3,3,3]{0,1,4,3,2:T(4,128)(2,1)}, u32[]{:S(2)}) copy-start(bf16[32,4,3,3,3]{0,1,4,3,2:T(4,128)(2,1)} %param.5) | copy-start | bytes 20740
  0.6 7.5 %copy-start.4 = (bf16[64,32,3,3,3]{0,1,4,3,2:T(8,128)(2,1)S(1)}, bf16[64,32,3,3,3]{0,1,4,3,2:T(8,128)(2,1)}, u32[]{:S(2)}) copy-start(bf16[64,32,3,3,3]{0,1,4,3,2:T(8,128)(2,1)} %param.6) | copy-start | bytes 331780
  0.7 9.8 %collective-permute-start.2 = (bf16[1,64,1,4,128]{4,3,2,1,0:T(4,128)(2,1)}, bf16[1,64,1,4,128]{4,3,2,1,0:T(4,128)(2,1)S(1)}, u32[]{:S(2)}, u32[]{:S(2)}) collective-permute-start(bf16[1,64,1,4,128]{4,3,2,1,0:T(4,128)(2,1)} %param.7), channel_id=1, source_target_pairs={{4,0},{8,4},{12,8},{16,12},{20,16},{24,20},{28,24},{5,1},{9,5},{13... | collective-permute-start | bytes 196616 | tf_op jit(solution)/shard_map/ppermute | solution.py:17
  2.1 9.3 %collective-permute-start.1 = (bf16[1,4,4,16,512]{4,3,2,1,0:T(8,128)(2,1)}, bf16[1,4,4,16,512]{4,3,2,1,0:T(8,128)(2,1)S(1)}, u32[]{:S(2)}, u32[]{:S(2)}) collective-permute-start(bf16[1,4,4,16,512]{4,3,2,1,0:T(8,128)(2,1)} %vo_ref.1), channel_id=1, source_target_pairs={{4,0},{8,4},{12,8},{16,12},{20,16},{24,20},{28,24},{5,1},{9,5},{13... | collective-permute-start | bytes 786440 | tf_op jit(solution)/shard_map/ppermute | solution.py:17
  4.3 7.1 %collective-permute-start = (bf16[1,4,3,16,512]{4,3,2,1,0:T(8,128)(2,1)S(1)}, bf16[1,4,3,16,512]{4,3,2,1,0:T(8,128)(2,1)S(1)}, u32[]{:S(2)}, u32[]{:S(2)}) collective-permute-start(bf16[1,4,3,16,512]{4,3,2,1,0:T(8,128)(2,1)S(1)} %slice.52), channel_id=1, source_target_pairs={{0,4},{4,8},{8,12},{12,16},{16,20},{20,24},{24,28},{1,5},{5,9},{9,... | collective-permute-start | bytes 589832 | tf_op jit(solution)/shard_map/ppermute | solution.py:17
  9.6 1.0 %copy-start = (bf16[64,3,3,2,2,32]{0,5,4,3,2,1:T(8,128)(2,1)}, bf16[64,3,3,2,2,32]{0,5,4,3,2,1:T(8,128)(2,1)S(1)}, u32[]{:S(2)}) copy-start(bf16[64,3,3,2,2,32]{0,5,4,3,2,1:T(8,128)(2,1)S(1)} %copy.22) | copy-start | bytes 442372
  9.7 0.9 %copy-start.8 = (bf16[1,64,1,4,128]{4,3,2,1,0:T(4,128)(2,1)S(1)}, bf16[1,64,1,4,128]{4,3,2,1,0:T(4,128)(2,1)}, u32[]{:S(2)}) copy-start(bf16[1,64,1,4,128]{4,3,2,1,0:T(4,128)(2,1)} %param.7) | copy-start | bytes 196612
  11.4 0.7 %copy-start.5 = (bf16[1,4,3,16,512]{4,3,2,1,0:T(8,128)(2,1)}, bf16[1,4,3,16,512]{4,3,2,1,0:T(8,128)(2,1)S(1)}, u32[]{:S(2)}) copy-start(bf16[1,4,3,16,512]{4,3,2,1,0:T(8,128)(2,1)S(1)} %collective-permute-done.vb_ref) | copy-start | bytes 589828
  11.4 0.8 %copy-start.3 = (bf16[1,4,4,16,512]{4,3,2,1,0:T(8,128)(2,1)}, bf16[1,4,4,16,512]{4,3,2,1,0:T(8,128)(2,1)S(1)}, u32[]{:S(2)}) copy-start(bf16[1,4,4,16,512]{4,3,2,1,0:T(8,128)(2,1)S(1)} %collective-permute-done.1.va_ref) | copy-start | bytes 786436
  21.8 0.9 %copy-start.1 = (f32[432,128]{1,0:T(8,128)S(1)}, f32[432,128]{1,0:T(8,128)}, u32[]{:S(2)}) copy-start(f32[432,128]{1,0:T(8,128)} %get-tuple-element.11) | copy-start | bytes 663556
  22.8 3.6 %collective-permute-start.3 = (f32[232,128]{1,0:T(8,128)S(1)}, f32[232,128]{1,0:T(8,128)S(1)}, u32[]{:S(2)}, u32[]{:S(2)}) collective-permute-start(f32[232,128]{1,0:T(8,128)S(1)} %fusion.1), channel_id=1, source_target_pairs={{0,4},{4,0},{8,12},{12,8},{16,20},{20,16},{24,28},{28,24},{1,5},{5... | collective-permute-start | bytes 356360 | tf_op jit(solution)/shard_map/ppermute | solution.py:36
  26.4 6.8 %collective-permute-start.4 = (f32[232,128]{1,0:T(8,128)S(1)}, f32[232,128]{1,0:T(8,128)S(1)}, u32[]{:S(2)}, u32[]{:S(2)}) collective-permute-start(f32[232,128]{1,0:T(8,128)S(1)} %select_add_fusion), channel_id=1, source_target_pairs={{0,8},{4,12},{8,0},{12,4},{16,24},{20,28},{24,16},{28,20},{1,9},{5... | collective-permute-start | bytes 356360 | tf_op jit(solution)/shard_map/ppermute | solution.py:38
  33.3 5.8 %collective-permute-start.5 = (f32[232,128]{1,0:T(8,128)S(1)}, f32[232,128]{1,0:T(8,128)S(1)}, u32[]{:S(2)}, u32[]{:S(2)}) collective-permute-start(f32[232,128]{1,0:T(8,128)S(1)} %add.71), channel_id=1, source_target_pairs={{0,16},{4,20},{8,24},{12,28},{16,0},{20,4},{24,8},{28,12},{1,17},{... | collective-permute-start | bytes 356360 | tf_op jit(solution)/shard_map/ppermute | solution.py:38
  39.0 4.9 %collective-permute-start.6 = (f32[232,128]{1,0:T(8,128)S(1)}, f32[232,128]{1,0:T(8,128)S(1)}, u32[]{:S(2)}, u32[]{:S(2)}) collective-permute-start(f32[232,128]{1,0:T(8,128)S(1)} %add.72), channel_id=1, source_target_pairs={{0,1},{1,0},{2,3},{3,2},{4,5},{5,4},{6,7},{7,6},{8,9},{9,8},{10,11... | collective-permute-start | bytes 356360 | tf_op jit(solution)/shard_map/ppermute | solution.py:38
  44.0 7.2 %copy-start.2 = (bf16[512,256]{1,0:T(8,128)(2,1)S(1)}, bf16[512,256]{1,0:T(8,128)(2,1)}, u32[]{:S(2)}) copy-start(bf16[512,256]{1,0:T(8,128)(2,1)} %get-tuple-element.9) | copy-start | bytes 786436
  44.0 7.1 %collective-permute-start.7 = (f32[232,128]{1,0:T(8,128)S(1)}, f32[232,128]{1,0:T(8,128)S(1)}, u32[]{:S(2)}, u32[]{:S(2)}) collective-permute-start(f32[232,128]{1,0:T(8,128)S(1)} %add.73), channel_id=1, source_target_pairs={{0,2},{1,3},{2,0},{3,1},{4,6},{5,7},{6,4},{7,5},{8,10},{9,11},{10,... | collective-permute-start | bytes 356360 | tf_op jit(solution)/shard_map/ppermute | solution.py:38
  51.1 1.6 %collective-permute-start.8 = (f32[232,128]{1,0:T(8,128)S(1)}, f32[232,128]{1,0:T(8,128)S(1)}, u32[]{:S(2)}, u32[]{:S(2)}) collective-permute-start(f32[232,128]{1,0:T(8,128)S(1)} %add.74), channel_id=1, source_target_pairs={{0,4},{4,0},{8,12},{12,8},{16,20},{20,16},{24,28},{28,24},{1,5},{5... | collective-permute-start | bytes 356360 | tf_op jit(solution)/shard_map/ppermute | solution.py:39
  51.2 0.9 %copy-start.7 = (bf16[64,512]{1,0:T(8,128)(2,1)S(1)}, bf16[64,512]{1,0:T(8,128)(2,1)}, u32[]{:S(2)}) copy-start(bf16[64,512]{1,0:T(8,128)(2,1)} %get-tuple-element.8) | copy-start | bytes 196612

commit v5 on v4

v5 whole, which is shorter than its diff:
```python
import math

import jax
import jax.numpy as jnp
from jax import lax
from jax.experimental import pallas as pl
from jax.experimental.pallas import tpu as pltpu
from jax.sharding import PartitionSpec as P

F32 = jnp.float32
BF16 = jnp.bfloat16


def shifted(block, axis, distance):
    devices = range(lax.axis_size(axis))
    route = [(i - distance, i) for i in devices if i - distance in devices]
    return lax.ppermute(block, axis, route)


def _all_sum(x, axes):
    steps = []
    for axis in axes:
        n = lax.axis_size(axis)
        assert n & (n - 1) == 0
        k = 1
        while k < n:
            steps.append((axis, n, k))
            k *= 2
    axis0, n0, k0 = steps[0]
    rows = x.shape[0]
    half = -(-rows // 16) * 8
    x = jnp.pad(x, ((0, 2 * half - rows), (0, 0)))
    low = (lax.axis_index(axis0) & k0) == 0
    lo, hi = x[:half], x[half:]
    pair = [(i, i ^ k0) for i in range(n0)]
    part = jnp.where(low, lo, hi) + lax.ppermute(jnp.where(low, hi, lo), axis0, pair)
    for axis, n, k in steps[1:]:
        part = part + lax.ppermute(part, axis, [(i, i ^ k) for i in range(n)])
    other = lax.ppermute(part, axis0, pair)
    return jnp.where(low, jnp.concatenate([part, other], 0), jnp.concatenate([other, part], 0))[:rows]


def _sigmoid(v):
    return 1.0 / (1.0 + jnp.exp(-v))


def _shift_right(x):
    lane = lax.broadcasted_iota(jnp.int32, x.shape, x.ndim - 1)
    return jnp.where(lane == 0, 0.0, pltpu.roll(x, 1, x.ndim - 1))


def _shift_left(x):
    n = x.shape[-1]
    lane = lax.broadcasted_iota(jnp.int32, x.shape, x.ndim - 1)
    return jnp.where(lane == n - 1, 0.0, pltpu.roll(x, n - 1, x.ndim - 1))


def _nt(a, b):
    return lax.dot_general(a, b, (((1,), (1,)), ((), ())), preferred_element_type=F32)


def _relayout_volume(pieces, tp, c0, ny, nx):
    lanes = nx // 4
    rows0 = 4 * c0
    xs = lax.broadcasted_iota(jnp.int32, (nx, nx), 0)
    cs = lax.broadcasted_iota(jnp.int32, (nx, nx), 1)
    sel_x = jnp.where(xs == 4 * (cs % lanes) + cs // lanes, 1.0, 0.0).astype(BF16)
    nq = 2 * rows0 * ny
    orow = lax.broadcasted_iota(jnp.int32, (nq, nq), 0)
    icol = lax.broadcasted_iota(jnp.int32, (nq, nq), 1)
    y_, s_ = orow // (2 * rows0), (orow // rows0) % 2
    i_, r_ = (orow // 4) % c0, orow % 4
    perm = jnp.where(icol == ((s_ * 4 + r_) * c0 + i_) * ny + y_, 1.0, 0.0).astype(BF16)
    tp[:, 0] = jnp.zeros((tp.shape[0], 2 * rows0, lanes), BF16)
    for zi, (ref, z) in enumerate(pieces):
        zmat = ref[0, :, z].reshape(c0 * ny, nx)
        ymat = jnp.dot(zmat, sel_x, preferred_element_type=F32)
        blocks = [ymat[:, r * lanes:(r + 1) * lanes] for r in range(4)]
        q = jnp.concatenate(blocks + [_shift_right(b) for b in blocks], axis=0).astype(BF16)
        t = jnp.dot(perm, q, preferred_element_type=F32).astype(BF16)
        tp[zi, 1:] = t.reshape(ny, 2 * rows0, lanes)


def _add_taps(gacc, slot, gs, row_base, ny2, lanes, c1):
    c2 = 2 * c1
    for h in range(3):
        for y2 in range(ny2):
            y1 = 2 * y2 + h - 1
            if y1 < 0:
                continue
            r0 = row_base + h * c2
            blk = gs[r0:r0 + c2, y2 * lanes:(y2 + 1) * lanes]
            gacc[slot, :, y1 * lanes:(y1 + 1) * lanes] += blk[:c1] + _shift_left(blk[c1:])


def _interleave(g, g1_ref, ny1, lanes):
    half = g.shape[0] // 2
    gb = g.astype(BF16)
    rows = [jnp.concatenate([gb[:half, y1 * lanes:(y1 + 1) * lanes], gb[half:, y1 * lanes:(y1 + 1) * lanes]], axis=1)
            for y1 in range(ny1)]
    n2 = 2 * lanes
    row = lax.broadcasted_iota(jnp.int32, (n2, n2), 0)
    col = lax.broadcasted_iota(jnp.int32, (n2, n2), 1)
    inter = jnp.where(col == 2 * (row % lanes) + row // lanes, 1.0, 0.0).astype(BF16)
    g1_ref[...] = jnp.dot(jnp.concatenate(rows, axis=0), inter, preferred_element_type=F32).astype(BF16)


def _slope(pre):
    sig = _sigmoid(pre)
    return sig * (1.0 + pre * (1.0 - sig))


def _kernel_a(vb_ref, vo_ref, k1_ref, k2_ref, k2t_ref, cot_ref,
              lvl_ref, bt_ref, s2_ref, s1_ref, g1_ref, gp_ref, sl_ref, p1o_ref,
              tp, p1, t2, p2, gs, gacc):
    c0, ny, nx = vo_ref.shape[1], vo_ref.shape[3], vo_ref.shape[4]
    lanes = nx // 4
    n_act = p1.shape[0]
    ny1 = ny // 2
    ny2 = ny1 // 2
    c2 = t2.shape[2]
    c1 = c2 // 2
    rows0 = 4 * c0

    pieces = [(vb_ref, z) for z in range(vb_ref.shape[2])] + [(vo_ref, z) for z in range(vo_ref.shape[2])]
    _relayout_volume(pieces, tp, c0, ny, nx)

    for a in range(n_act):
        for d in range(3):
            for y1 in range(ny1):
                p1[a, d * 3 * 2 * rows0:(d + 1) * 3 * 2 * rows0, y1 * lanes:(y1 + 1) * lanes] = (
                    tp[2 * a + d, 2 * y1:2 * y1 + 3].reshape(3 * 2 * rows0, lanes))

    k1 = k1_ref[...]
    t2[:, 0] = jnp.zeros((n_act, c2, lanes), BF16)
    slope1 = None
    for a in range(n_act):
        pre = jnp.dot(k1, p1[a], preferred_element_type=F32)
        if a == 1:
            slope1 = _slope(pre)
        if a == 2:
            sl_ref[...] = _slope(pre)
        act = pre * _sigmoid(pre)
        for y1 in range(ny1):
            blk = act[:, y1 * lanes:(y1 + 1) * lanes]
            t2[a, y1 + 1] = jnp.concatenate([blk, _shift_right(blk)], axis=0).astype(BF16)

    for d in range(3):
        for y2 in range(ny2):
            p2[d * 3 * c2:(d + 1) * 3 * c2, y2 * lanes:(y2 + 1) * lanes] = (
                t2[d, 2 * y2:2 * y2 + 3].reshape(3 * c2, lanes))

    pre = jnp.dot(k2_ref[...], p2[...], preferred_element_type=F32)
    sig = _sigmoid(pre)
    lvl_ref[...] = (pre * sig).astype(BF16)
    bt0 = (cot_ref[...].astype(F32) * (sig * (1.0 + pre * (1.0 - sig)))).astype(BF16)
    bt_ref[...] = bt0

    dup = _nt(p2[...], jnp.concatenate([bt0, bt0], axis=0))
    c2n = dup.shape[1] // 2
    qi = c1 // 4
    lane2 = lax.broadcasted_iota(jnp.int32, (qi, 2 * c2n), 1)
    for dh in range(9):
        for w, off in enumerate((3 * c1 // 2, 0, c1 // 2)):
            r0 = dh * c2 + off
            s2_ref[(dh * 3 + w) * qi:(dh * 3 + w + 1) * qi] = jnp.where(
                lane2 < c2n, dup[r0:r0 + qi], dup[r0 + qi:r0 + 2 * qi])

    gacc[...] = jnp.zeros(gacc.shape, F32)
    gs[...] = jnp.dot(k2t_ref[3 * c2:], bt0, preferred_element_type=F32)
    _add_taps(gacc, 0, gs, 0, ny2, lanes, c1)
    _add_taps(gacc, 1, gs, 3 * c2, ny2, lanes, c1)

    g = gacc[0]
    b1 = (g * slope1).astype(BF16)
    s1_ref[...] = _nt(p1[1], b1)
    _interleave(g, g1_ref, ny1, lanes)
    gp_ref[...] = gacc[1]
    p1o_ref[...] = p1[2]


def _kernel_b(bta_ref, k2t_ref, gp_ref, sl_ref, p1o_ref, s1_ref, g1_ref, gs, gacc):
    c1 = gp_ref.shape[0]
    lanes = bta_ref.shape[1] // 4
    ny2 = 4
    ny1 = gp_ref.shape[1] // lanes
    gacc[0] = gp_ref[...]
    gs[...] = jnp.dot(k2t_ref[:3 * 2 * c1], bta_ref[...], preferred_element_type=F32)
    _add_taps(gacc, 0, gs, 0, ny2, lanes, c1)
    g = gacc[0]
    b1 = (g * sl_ref[...]).astype(BF16)
    s1_ref[...] = _nt(p1o_ref[...], b1)
    _interleave(g, g1_ref, ny1, lanes)


def _level_one_weights(k1):
    kt = jnp.transpose(k1, (0, 2, 3, 1, 4))
    w0, w1, w2 = kt[..., 0], kt[..., 1], kt[..., 2]
    z = jnp.zeros_like(w0)
    p0 = jnp.stack([jnp.stack([w1, w2, z, z], -1), jnp.stack([z, z, z, w0], -1)], 3)
    p1 = jnp.stack([jnp.stack([z, w0, w1, w2], -1), jnp.stack([z, z, z, z], -1)], 3)
    e = jnp.stack([p0, p1], 0)
    return e.reshape(2 * k1.shape[0], -1)


def _level_two_weights(k2):
    kt = jnp.transpose(k2, (0, 2, 3, 4, 1))
    w0, w1, w2 = kt[:, :, :, 0], kt[:, :, :, 1], kt[:, :, :, 2]
    z = jnp.zeros_like(w0)
    e = jnp.stack([jnp.stack([w1, w2], 3), jnp.stack([z, w0], 3)], 3)
    return e.reshape(k2.shape[0], -1)


def per_device(volume, kernel_one, kernel_two, cotangent):
    _, c0, nz, ny, nx = volume.shape
    c1 = kernel_one.shape[0]
    c2 = kernel_two.shape[0]
    assert nz == 4 and cotangent.shape[2] == 1
    q = nx // 4
    below = shifted(volume[:, :, 1:], "gz", 1)
    n2 = cotangent.shape[3] * cotangent.shape[4]
    cot = cotangent[0, :, 0].reshape(c2, n2)

    k1m = _level_one_weights(kernel_one)
    k2m = _level_two_weights(kernel_two)
    k2t = k2m.T

    ny1, ny2 = ny // 2, ny // 4
    nzi = below.shape[2] + nz
    vm = pltpu.VMEM
    kk = k1m.shape[1]
    lvl, bt0, s2, s1a, g1a, gp, sl, p1o = pl.pallas_call(
        _kernel_a,
        out_shape=(
            jax.ShapeDtypeStruct((c2, n2), BF16),
            jax.ShapeDtypeStruct((c2, n2), BF16),
            jax.ShapeDtypeStruct((27 * c1 // 2, 2 * c2), F32),
            jax.ShapeDtypeStruct((kk, 2 * c1), F32),
            jax.ShapeDtypeStruct((ny1 * c1, 2 * q), BF16),
            jax.ShapeDtypeStruct((2 * c1, ny1 * q), F32),
            jax.ShapeDtypeStruct((2 * c1, ny1 * q), F32),
            jax.ShapeDtypeStruct((kk, ny1 * q), BF16),
        ),
        scratch_shapes=[
            vm((nzi, ny + 1, 8 * c0, q), BF16),
            vm((3, kk, ny1 * q), BF16),
            vm((3, ny1 + 1, 4 * c1, q), BF16),
            vm((k2m.shape[1], n2), BF16),
            vm((2 * 3 * 4 * c1, n2), F32),
            vm((2, 2 * c1, ny1 * q), F32),
        ],
        cost_estimate=pl.CostEstimate(flops=40_000_000, transcendentals=150_000, bytes_accessed=3_000_000),
    )(below, volume, k1m, k2m, k2t, cot)

    s1b, g1b = pl.pallas_call(
        _kernel_b,
        out_shape=(
            jax.ShapeDtypeStruct((kk, 2 * c1), F32),
            jax.ShapeDtypeStruct((ny1 * c1, 2 * q), BF16),
        ),
        scratch_shapes=[
            vm((3 * 4 * c1, n2), F32),
            vm((1, 2 * c1, ny1 * q), F32),
        ],
        cost_estimate=pl.CostEstimate(flops=15_000_000, transcendentals=0, bytes_accessed=2_500_000),
    )(shifted(bt0, "gz", -1), k2t, gp, sl, p1o)

    samples = volume.shape[0] * lax.axis_size("sa")
    cells_one = samples * (nz // 2) * lax.axis_size("gz") * ny1 * (nx // 2)
    cells_two = samples * cotangent.shape[2] * lax.axis_size("gz") * cotangent.shape[3] * cotangent.shape[4]

    t2 = _all_sum(s2, ("gz", "sa")) / math.sqrt(float(cells_two))
    t2 = t2.reshape(27, c1 // 2, 2, c2).transpose(0, 2, 1, 3).reshape(3, 3, 3, c1, c2)
    grad_kernel_two = t2.transpose(4, 3, 0, 1, 2)

    s1 = s1a + s1b
    s1r = s1.reshape(3, 3, 2, c0, 4, 2, c1)
    gk1 = jnp.stack([
        s1r[:, :, 1, :, 3, 0] + s1r[:, :, 0, :, 1, 1],
        s1r[:, :, 0, :, 0, 0] + s1r[:, :, 0, :, 2, 1],
        s1r[:, :, 0, :, 1, 0] + s1r[:, :, 0, :, 3, 1],
    ], 2)
    t1 = _all_sum(gk1.reshape(-1, 2 * c2), ("gz", "sa")) / math.sqrt(float(cells_one))
    grad_kernel_one = t1.reshape(3, 3, 3, c0, c1).transpose(4, 3, 0, 1, 2)

    level_two = lvl.reshape(1, c2, 1, ny2, n2 // ny2)
    g1 = jnp.concatenate([g1a, g1b], 0)
    grad_one = g1.reshape(2, ny1, c1, 2 * q).transpose(2, 0, 1, 3)[None]
    return (level_two, grad_one, grad_kernel_one, grad_kernel_two)


def solution(mesh):
    placed = (P("sa", None, "gz", None, None), P(), P(), P("sa", None, "gz", None, None))
    return jax.shard_map(
        per_device,
        mesh=mesh,
        in_specs=placed,
        out_specs=(P("sa", None, "gz", None, None), P("sa", None, "gz", None, None), P(), P()),
        check_vma=False,
    )
```

time: 54.9 us -> 66.5 us (1.21)
  waiting for transfers between devices: 15.1 us -> 20.4 us
  starting transfers between devices: 19.5 us -> 24.1 us
  other arithmetic: 0.84 us -> 2.58 us
    ppermute x4 -> x8, starting transfers between devices: 10.4 us -> 16.9 us  [_all_sum(): part = part + lax.ppermute(part, axis, [(i, i ^ k) for i in range(n)])]
    ppermute x4 -> x8, waiting for transfers between devices: 14.2 us -> 19.9 us  [_all_sum(): part = part + lax.ppermute(part, axis, [(i, i ^ k) for i in range(n)])]
    ppermute x3 -> x2, starting transfers between devices: 6.39 us -> 3.65 us  [shifted(): return lax.ppermute(block, axis, route)]
    unnamed x18 -> x23, local copies, waits for them, and re-layouts: 1.61 us -> 2.83 us
    reshape x4 -> x1, local copies, waits for them, and re-layouts: 1.08 us -> 0.09 us  [per_device(): gk1.reshape(-1, 2 * c2)]
    ppermute x1 -> x2, waiting for transfers between devices: 0.97 us -> 0.01 us  [_all_sum(): lax.ppermute(jnp.where(low, hi, lo), axis0, pair)]
    select_n x1 -> x2, other arithmetic: 0.02 us -> 0.97 us  [_all_sum(): jnp.where(low, hi, lo)]
    add x0 -> x1, other arithmetic: none -> 0.93 us  [per_device(): s1 = s1a + s1b]
  transfers between devices with their start and end apart: 9 -> 14, of which waited for: 5 -> 8; matrix products, arithmetic and copies ran while one was open for 10% -> 11% of each run, Pallas kernels for 0% -> 4%
where the time goes in v5:
time: 66.5 us; the launch traced here: 66.2 us
  starting transfers between devices  24.1 us (36%)
  waiting for transfers between devices  20.4 us (31%)
  local copies, waits for them, and re-layouts  9.31 us (14%)
  Pallas kernels  8.87 us (13%)
  other arithmetic  2.58 us (4%)
  between operations  0.96 us (1%)
    ppermute x8, waiting for transfers between devices, _all_sum(): part = part + lax.ppermute(part, axis, [(i, i ^ k) for i in range(n)])  19.9 us
    ppermute x8, starting transfers between devices, _all_sum(): part = part + lax.ppermute(part, axis, [(i, i ^ k) for i in range(n)])  16.9 us
    pallas_call x1, Pallas kernels, per_device(): pl.pallas_call(_kernel_a, out_shape=(jax.ShapeDtypeStruct((c2, n2), BF16)...  6.11 us
    ppermute x2, starting transfers between devices, shifted(): return lax.ppermute(block, axis, route)  3.65 us
    ppermute x2, starting transfers between devices, _all_sum(): lax.ppermute(jnp.where(low, hi, lo), axis0, pair)  3.29 us
    unnamed x23, local copies, waits for them, and re-layouts  2.83 us
    pallas_call x1, Pallas kernels, per_device(): pl.pallas_call(_kernel_b, out_shape=(jax.ShapeDtypeStruct((kk, 2 * c1), F...  2.76 us
  transfers between devices with their start and end apart: 14, of which 8 were waited for; matrix products, arithmetic and copies ran while one was open for 11% of the time, Pallas kernels for 4%

profile of v5, /device:TPU:0, one launch (start us, length us, event | category | flops | bytes accessed | tf_op | source)
XLA Modules:
  0.0 66.2 jit_solution(3357237419501141219)
XLA Ops:
  0.6 0.0 copy-start.7
  0.6 0.0 copy-start.2
  0.7 1.0 %slice.52 = bf16[1,4,3,16,512]{4,3,2,1,0:T(8,128)(2,1)S(1)} slice(bf16[1,4,4,16,512]{4,3,2,1,0:T(8,128)(2,1)} %vo_ref.1), slice={[0:1], [0:4], [1:4], [0:16], [0:512]} | slice | bytes 393216 | tf_op jit(solution)/shard_map/slice | solution.py:220
  1.6 2.4 %collective-permute-start = (bf16[1,4,3,16,512]{4,3,2,1,0:T(8,128)(2,1)S(1)}, bf16[1,4,3,16,512]{4,3,2,1,0:T(8,128)(2,1)S(1)}, u32[]{:S(2)}, u32[]{:S(2)}) collective-permute-start(bf16[1,4,3,16,512]{4,3,2,1,0:T(8,128)(2,1)S(1)} %slice.52), channel_id=1, source_target_pairs={{0,4},{4,8},{8,12},{12,16},{16,20},{20,24},{24,28},{1,5},{5,9},{9,... | collective-permute-start | bytes 589832 | tf_op jit(solution)/shard_map/ppermute | solution.py:17
  4.0 0.0 copy-done.7
  4.1 0.0 copy-done.2
  4.2 0.1 pad_maximum_fusion.6
  4.3 0.1 maximum_bitcast_fusion.1
  4.4 0.1 maximum_bitcast_fusion
  4.4 0.1 pad_maximum_fusion.2
  4.6 0.1 copy.18
  4.7 0.1 reshape.93
  4.8 0.7 %copy.20.k1_ref = bf16[64,288]{1,0:T(8,128)(2,1)} copy(bf16[64,288]{0,1:T(8,128)(2,1)S(1)} %reshape.93) | data formatting | bytes 73728 | tf_op jit(solution)/shard_map/reshape | solution.py:203
  5.5 0.1 pad_maximum_fusion
  5.6 0.0 copy-start
  5.7 0.0 copy-start.9
  5.7 0.8 %copy.21.k2_ref = bf16[64,1152]{1,0:T(8,128)(2,1)} copy(bf16[64,1152]{0,1:T(8,128)(2,1)S(1)} %bitcast.48) | data formatting | bytes 294912 | tf_op jit(solution)/shard_map/reshape | solution.py:211
  6.5 0.1 copy-done.9
  6.6 0.6 copy.38
  7.2 0.0 collective-permute-done.vb_ref
  7.2 0.0 copy-done
  7.2 0.7 %copy-done.3 = bf16[1,4,3,16,512]{4,3,2,1,0:T(8,128)(2,1)} copy-done((bf16[1,4,3,16,512]{4,3,2,1,0:T(8,128)(2,1)}, bf16[1,4,3,16,512]{4,3,2,1,0:T(8,128)(2,1)S(1)}, u32[]{:S(2)}) %copy-start.3) | copy-done | bytes 196632
  7.9 6.1 %shard_map.75 = (bf16[64,512]{1,0:T(8,128)(2,1)}, bf16[64,512]{1,0:T(8,128)(2,1)}, f32[432,128]{1,0:T(8,128)}, f32[288,64]{1,0:T(8,128)}, bf16[256,256]{1,0:T(8,...) custom-call(bf16[1,4,3,16,512]{4,3,2,1,0:T(8,128)(2,1)} %copy-done.3, ...), custom_call_target="tpu_custom_call" | custom-call | flops 40000000 | bytes 3000000 | tf_op jit(solution)/shard_map/pallas_call | solution.py:232
  14.0 1.3 %collective-permute-start.1 = (bf16[64,512]{1,0:T(8,128)(2,1)}, bf16[64,512]{1,0:T(8,128)(2,1)S(1)}, u32[]{:S(2)}, u32[]{:S(2)}) collective-permute-start(bf16[64,512]{1,0:T(8,128)(2,1)} %get-tuple-element.16), channel_id=1, source_target_pairs={{4,0},{8,4},{12,8},{16,12},{20,16},{24,20},{28,24},{5,1},{9,5},{13... | collective-permute-start | bytes 196616 | tf_op jit(solution)/shard_map/ppermute | solution.py:17
  15.3 1.0 %slice_select_fusion = f32[216,128]{1,0:T(8,128)S(1)} fusion(f32[432,128]{1,0:T(8,128)} %get-tuple-element.23, pred[]{:T(512)S(6)} %eq.4), kind=kLoop, calls=%fused_computation.9 | loop fusion | flops 27648 | bytes 331777 | tf_op jit(solution)/shard_map/jit(_where)/select_n | solution.py:36
  16.3 3.3 %collective-permute-start.8 = (f32[216,128]{1,0:T(8,128)S(1)}, f32[216,128]{1,0:T(8,128)S(1)}, u32[]{:S(2)}, u32[]{:S(2)}) collective-permute-start(f32[216,128]{1,0:T(8,128)S(1)} %slice_select_fusion), channel_id=1, source_target_pairs={{0,4},{4,0},{8,12},{12,8},{16,20},{20,16},{24,28},{28,24},{1,5},{5... | collective-permute-start | bytes 331784 | tf_op jit(solution)/shard_map/ppermute | solution.py:36
  19.5 0.0 collective-permute-done.1.bta_ref
  19.5 0.6 copy-done.8
  20.2 2.8 %shard_map.76 = (f32[288,64]{1,0:T(8,128)}, bf16[256,256]{1,0:T(8,128)(2,1)}) custom-call(bf16[64,512]{1,0:T(8,128)(2,1)} %copy-done.8, bf16[1152,64]{1,0:T(8,128)(2,1)} %bitcast.50, f32[64,1024]{1,0:T(8,128)} %get-tuple-element.17.gp_ref, f32[64,1024]{1,0:T(8,128)} %get-tuple-element.18.sl_ref, bf16[288,1024]{1,0:T(8,128)(2,1)} %get-tuple-element.19.p1o_ref), custom_call_target="tpu_custom_call" | custom-call | flops 15000000 | bytes 2500000 | tf_op jit(solution)/shard_map/pallas_call | solution.py:255
  22.9 0.0 copy-done.4
  22.9 0.9 %add.82 = f32[288,64]{1,0:T(8,128)S(1)} add(f32[288,64]{1,0:T(8,128)S(1)} %copy-done.4, f32[288,64]{1,0:T(8,128)} %get-tuple-element.22) | non-fusion elementwise | flops 18432 | bytes 221184 | tf_op jit(solution)/shard_map/add | solution.py:276
  23.9 0.2 reshape.97
  24.1 0.1 fusion.3
  24.2 0.0 collective-permute-done.8
  24.2 0.8 %copy-done.1 = f32[432,128]{1,0:T(8,128)S(1)} copy-done((f32[432,128]{1,0:T(8,128)S(1)}, f32[432,128]{1,0:T(8,128)}, u32[]{:S(2)}) %copy-start.1) | copy-done | bytes 221208
  25.0 3.0 %collective-permute-start.9 = (f32[216,128]{1,0:T(8,128)S(1)}, f32[216,128]{1,0:T(8,128)S(1)}, u32[]{:S(2)}, u32[]{:S(2)}) collective-permute-start(f32[216,128]{1,0:T(8,128)S(1)} %select_add_fusion), channel_id=1, source_target_pairs={{0,8},{4,12},{8,0},{12,4},{16,24},{20,28},{24,16},{28,20},{1,9},{5... | collective-permute-start | bytes 331784 | tf_op jit(solution)/shard_map/ppermute | solution.py:38
  28.1 0.1 reshape.98
  28.2 2.6 %collective-permute-done.9 = f32[216,128]{1,0:T(8,128)S(1)} collective-permute-done((f32[216,128]{1,0:T(8,128)S(1)}, f32[216,128]{1,0:T(8,128)S(1)}, u32[]{:S(2)}, u32[]{:S(2)}) %collective-permute-start.9) | collective-permute-done | bytes 110624 | tf_op jit(solution)/shard_map/ppermute | solution.py:38
  30.8 3.9 %collective-permute-start.10 = (f32[216,128]{1,0:T(8,128)S(1)}, f32[216,128]{1,0:T(8,128)S(1)}, u32[]{:S(2)}, u32[]{:S(2)}) collective-permute-start(f32[216,128]{1,0:T(8,128)S(1)} %add.95), channel_id=1, source_target_pairs={{0,16},{4,20},{8,24},{12,28},{16,0},{20,4},{24,8},{28,12},{1,17},{... | collective-permute-start | bytes 331784 | tf_op jit(solution)/shard_map/ppermute | solution.py:38
  34.6 0.0 collective-permute-start.2
  34.7 3.0 %collective-permute-done.10 = f32[216,128]{1,0:T(8,128)S(1)} collective-permute-done((f32[216,128]{1,0:T(8,128)S(1)}, f32[216,128]{1,0:T(8,128)S(1)}, u32[]{:S(2)}, u32[]{:S(2)}) %collective-permute-start.10) | collective-permute-done | bytes 110624 | tf_op jit(solution)/shard_map/ppermute | solution.py:38
  37.7 1.6 %collective-permute-start.11 = (f32[216,128]{1,0:T(8,128)S(1)}, f32[216,128]{1,0:T(8,128)S(1)}, u32[]{:S(2)}, u32[]{:S(2)}) collective-permute-start(f32[216,128]{1,0:T(8,128)S(1)} %add.96), channel_id=1, source_target_pairs={{0,1},{1,0},{2,3},{3,2},{4,5},{5,4},{6,7},{7,6},{8,9},{9,8},{10,11... | collective-permute-start | bytes 331784 | tf_op jit(solution)/shard_map/ppermute | solution.py:38
  39.3 0.0 collective-permute-done.2
  39.3 1.0 %collective-permute-start.3 = (f32[16,128]{1,0:T(8,128)S(1)}, f32[16,128]{1,0:T(8,128)S(1)}, u32[]{:S(2)}, u32[]{:S(2)}) collective-permute-start(f32[16,128]{1,0:T(8,128)S(1)} %select_add_fusion.1), channel_id=1, source_target_pairs={{0,8},{4,12},{8,0},{12,4},{16,24},{20,28},{24,16},{28,20},{1,9},{5... | collective-permute-start | bytes 24584 | tf_op jit(solution)/shard_map/ppermute | solution.py:38
  40.3 2.7 %collective-permute-done.3 = f32[16,128]{1,0:T(8,128)S(1)} collective-permute-done((f32[16,128]{1,0:T(8,128)S(1)}, f32[16,128]{1,0:T(8,128)S(1)}, u32[]{:S(2)}, u32[]{:S(2)}) %collective-permute-start.3) | collective-permute-done | bytes 8224 | tf_op jit(solution)/shard_map/ppermute | solution.py:38
  43.0 1.7 %collective-permute-start.4 = (f32[16,128]{1,0:T(8,128)S(1)}, f32[16,128]{1,0:T(8,128)S(1)}, u32[]{:S(2)}, u32[]{:S(2)}) collective-permute-start(f32[16,128]{1,0:T(8,128)S(1)} %add.90), channel_id=1, source_target_pairs={{0,16},{4,20},{8,24},{12,28},{16,0},{20,4},{24,8},{28,12},{1,17},{... | collective-permute-start | bytes 24584 | tf_op jit(solution)/shard_map/ppermute | solution.py:38
  44.8 1.9 %collective-permute-done.4 = f32[16,128]{1,0:T(8,128)S(1)} collective-permute-done((f32[16,128]{1,0:T(8,128)S(1)}, f32[16,128]{1,0:T(8,128)S(1)}, u32[]{:S(2)}, u32[]{:S(2)}) %collective-permute-start.4) | collective-permute-done | bytes 8224 | tf_op jit(solution)/shard_map/ppermute | solution.py:38
  46.7 0.5 collective-permute-start.5
  47.2 3.2 %collective-permute-done.5 = f32[16,128]{1,0:T(8,128)S(1)} collective-permute-done((f32[16,128]{1,0:T(8,128)S(1)}, f32[16,128]{1,0:T(8,128)S(1)}, u32[]{:S(2)}, u32[]{:S(2)}) %collective-permute-start.5) | collective-permute-done | bytes 8224 | tf_op jit(solution)/shard_map/ppermute | solution.py:38
  50.4 2.6 %collective-permute-start.6 = (f32[16,128]{1,0:T(8,128)S(1)}, f32[16,128]{1,0:T(8,128)S(1)}, u32[]{:S(2)}, u32[]{:S(2)}) collective-permute-start(f32[16,128]{1,0:T(8,128)S(1)} %add.92), channel_id=1, source_target_pairs={{0,2},{1,3},{2,0},{3,1},{4,6},{5,7},{6,4},{7,5},{8,10},{9,11},{10,... | collective-permute-start | bytes 24584 | tf_op jit(solution)/shard_map/ppermute | solution.py:38
  52.9 0.6 reshape.95
  53.6 1.3 %collective-permute-done.6 = f32[16,128]{1,0:T(8,128)S(1)} collective-permute-done((f32[16,128]{1,0:T(8,128)S(1)}, f32[16,128]{1,0:T(8,128)S(1)}, u32[]{:S(2)}, u32[]{:S(2)}) %collective-permute-start.6) | collective-permute-done | bytes 8224 | tf_op jit(solution)/shard_map/ppermute | solution.py:38
  54.9 0.1 collective-permute-start.7
  55.0 0.0 collective-permute-done.11
  55.0 2.7 %collective-permute-start.12 = (f32[216,128]{1,0:T(8,128)S(1)}, f32[216,128]{1,0:T(8,128)S(1)}, u32[]{:S(2)}, u32[]{:S(2)}) collective-permute-start(f32[216,128]{1,0:T(8,128)S(1)} %add.97), channel_id=1, source_target_pairs={{0,2},{1,3},{2,0},{3,1},{4,6},{5,7},{6,4},{7,5},{8,10},{9,11},{10,... | collective-permute-start | bytes 331784 | tf_op jit(solution)/shard_map/ppermute | solution.py:38
  57.7 0.0 copy-done.5
  57.7 0.9 %copy.37 = bf16[2,8,32,256]{3,1,0,2:T(8,128)(2,1)} copy(bf16[2,8,32,256]{3,2,1,0:T(8,128)(2,1)S(1)} %bitcast.52) | data formatting | bytes 524288 | tf_op jit(solution)/shard_map/reshape | solution.py:288
  58.6 5.1 %collective-permute-done.12 = f32[216,128]{1,0:T(8,128)S(1)} collective-permute-done((f32[216,128]{1,0:T(8,128)S(1)}, f32[216,128]{1,0:T(8,128)S(1)}, u32[]{:S(2)}, u32[]{:S(2)}) %collective-permute-start.12) | collective-permute-done | bytes 110624 | tf_op jit(solution)/shard_map/ppermute | solution.py:38
  63.7 0.1 collective-permute-start.13
  63.8 0.0 collective-permute-done.7
  63.9 0.7 %reshape.99 = f32[3,3,3,4,32]{4,3,2,1,0:T(4,128)} reshape(f32[27,128]{1,0:T(8,128)S(1)} %fusion.2) | data formatting | bytes 27648 | tf_op jit(solution)/shard_map/reshape | solution.py:284
  64.6 0.5 collective-permute-done.13
  65.1 0.3 div.18
  65.4 0.8 %copy.28 = f32[27,2,16,64]{3,2,1,0:T(8,128)} copy(f32[27,2,16,64]{3,1,2,0:T(2,128)S(1)} %bitcast.51) | data formatting | bytes 442368 | tf_op jit(solution)/shard_map/transpose | solution.py:273
  (35 shorter events, 0.3 us)
Async XLA Ops:
  0.6 3.4 %copy-start.7 = (bf16[32,4,3,3,3]{0,1,4,3,2:T(4,128)(2,1)S(1)}, bf16[32,4,3,3,3]{0,1,4,3,2:T(4,128)(2,1)}, u32[]{:S(2)}) copy-start(bf16[32,4,3,3,3]{0,1,4,3,2:T(4,128)(2,1)} %param.5) | copy-start | bytes 20740
  0.6 3.5 %copy-start.2 = (bf16[64,32,3,3,3]{0,1,4,3,2:T(8,128)(2,1)S(1)}, bf16[64,32,3,3,3]{0,1,4,3,2:T(8,128)(2,1)}, u32[]{:S(2)}) copy-start(bf16[64,32,3,3,3]{0,1,4,3,2:T(8,128)(2,1)} %param.6) | copy-start | bytes 331780
  1.6 5.6 %collective-permute-start = (bf16[1,4,3,16,512]{4,3,2,1,0:T(8,128)(2,1)S(1)}, bf16[1,4,3,16,512]{4,3,2,1,0:T(8,128)(2,1)S(1)}, u32[]{:S(2)}, u32[]{:S(2)}) collective-permute-start(bf16[1,4,3,16,512]{4,3,2,1,0:T(8,128)(2,1)S(1)} %slice.52), channel_id=1, source_target_pairs={{0,4},{4,8},{8,12},{12,16},{16,20},{20,24},{24,28},{1,5},{5,9},{9,... | collective-permute-start | bytes 589832 | tf_op jit(solution)/shard_map/ppermute | solution.py:17
  5.6 1.6 %copy-start = (bf16[64,3,3,2,2,32]{0,5,4,3,2,1:T(8,128)(2,1)}, bf16[64,3,3,2,2,32]{0,5,4,3,2,1:T(8,128)(2,1)S(1)}, u32[]{:S(2)}) copy-start(bf16[64,3,3,2,2,32]{0,5,4,3,2,1:T(8,128)(2,1)S(1)} %copy.19) | copy-start | bytes 442372
  5.7 0.9 %copy-start.9 = (bf16[1,64,1,4,128]{4,3,2,1,0:T(4,128)(2,1)S(1)}, bf16[1,64,1,4,128]{4,3,2,1,0:T(4,128)(2,1)}, u32[]{:S(2)}) copy-start(bf16[1,64,1,4,128]{4,3,2,1,0:T(4,128)(2,1)} %param.7) | copy-start | bytes 196612
  7.2 0.7 %copy-start.3 = (bf16[1,4,3,16,512]{4,3,2,1,0:T(8,128)(2,1)}, bf16[1,4,3,16,512]{4,3,2,1,0:T(8,128)(2,1)S(1)}, u32[]{:S(2)}) copy-start(bf16[1,4,3,16,512]{4,3,2,1,0:T(8,128)(2,1)S(1)} %collective-permute-done.vb_ref) | copy-start | bytes 589828
  14.0 5.5 %collective-permute-start.1 = (bf16[64,512]{1,0:T(8,128)(2,1)}, bf16[64,512]{1,0:T(8,128)(2,1)S(1)}, u32[]{:S(2)}, u32[]{:S(2)}) collective-permute-start(bf16[64,512]{1,0:T(8,128)(2,1)} %get-tuple-element.16), channel_id=1, source_target_pairs={{4,0},{8,4},{12,8},{16,12},{20,16},{24,20},{28,24},{5,1},{9,5},{13... | collective-permute-start | bytes 196616 | tf_op jit(solution)/shard_map/ppermute | solution.py:17
  16.3 8.0 %collective-permute-start.8 = (f32[216,128]{1,0:T(8,128)S(1)}, f32[216,128]{1,0:T(8,128)S(1)}, u32[]{:S(2)}, u32[]{:S(2)}) collective-permute-start(f32[216,128]{1,0:T(8,128)S(1)} %slice_select_fusion), channel_id=1, source_target_pairs={{0,4},{4,0},{8,12},{12,8},{16,20},{20,16},{24,28},{28,24},{1,5},{5... | collective-permute-start | bytes 331784 | tf_op jit(solution)/shard_map/ppermute | solution.py:36
  19.5 0.6 copy-start.8
  20.2 2.8 %copy-start.4 = (f32[288,64]{1,0:T(8,128)S(1)}, f32[288,64]{1,0:T(8,128)}, u32[]{:S(2)}) copy-start(f32[288,64]{1,0:T(8,128)} %get-tuple-element.21) | copy-start | bytes 221188
  24.1 0.9 %copy-start.1 = (f32[432,128]{1,0:T(8,128)S(1)}, f32[432,128]{1,0:T(8,128)}, u32[]{:S(2)}) copy-start(f32[432,128]{1,0:T(8,128)} %get-tuple-element.23) | copy-start | bytes 663556
  25.0 5.7 %collective-permute-start.9 = (f32[216,128]{1,0:T(8,128)S(1)}, f32[216,128]{1,0:T(8,128)S(1)}, u32[]{:S(2)}, u32[]{:S(2)}) collective-permute-start(f32[216,128]{1,0:T(8,128)S(1)} %select_add_fusion), channel_id=1, source_target_pairs={{0,8},{4,12},{8,0},{12,4},{16,24},{20,28},{24,16},{28,20},{1,9},{5... | collective-permute-start | bytes 331784 | tf_op jit(solution)/shard_map/ppermute | solution.py:38
  30.8 6.9 %collective-permute-start.10 = (f32[216,128]{1,0:T(8,128)S(1)}, f32[216,128]{1,0:T(8,128)S(1)}, u32[]{:S(2)}, u32[]{:S(2)}) collective-permute-start(f32[216,128]{1,0:T(8,128)S(1)} %add.95), channel_id=1, source_target_pairs={{0,16},{4,20},{8,24},{12,28},{16,0},{20,4},{24,8},{28,12},{1,17},{... | collective-permute-start | bytes 331784 | tf_op jit(solution)/shard_map/ppermute | solution.py:38
  34.6 4.7 %collective-permute-start.2 = (f32[16,128]{1,0:T(8,128)S(1)}, f32[16,128]{1,0:T(8,128)S(1)}, u32[]{:S(2)}, u32[]{:S(2)}) collective-permute-start(f32[16,128]{1,0:T(8,128)S(1)} %slice_select_fusion.1), channel_id=1, source_target_pairs={{0,4},{4,0},{8,12},{12,8},{16,20},{20,16},{24,28},{28,24},{1,5},{5... | collective-permute-start | bytes 24584 | tf_op jit(solution)/shard_map/ppermute | solution.py:36
  37.7 15.3 %copy-start.10 = (bf16[64,512]{1,0:T(8,128)(2,1)S(1)}, bf16[64,512]{1,0:T(8,128)(2,1)}, u32[]{:S(2)}) copy-start(bf16[64,512]{1,0:T(8,128)(2,1)} %get-tuple-element.14) | copy-start | bytes 196612
  37.7 17.3 %collective-permute-start.11 = (f32[216,128]{1,0:T(8,128)S(1)}, f32[216,128]{1,0:T(8,128)S(1)}, u32[]{:S(2)}, u32[]{:S(2)}) collective-permute-start(f32[216,128]{1,0:T(8,128)S(1)} %add.96), channel_id=1, source_target_pairs={{0,1},{1,0},{2,3},{3,2},{4,5},{5,4},{6,7},{7,6},{8,9},{9,8},{10,11... | collective-permute-start | bytes 331784 | tf_op jit(solution)/shard_map/ppermute | solution.py:38
  39.3 3.7 %collective-permute-start.3 = (f32[16,128]{1,0:T(8,128)S(1)}, f32[16,128]{1,0:T(8,128)S(1)}, u32[]{:S(2)}, u32[]{:S(2)}) collective-permute-start(f32[16,128]{1,0:T(8,128)S(1)} %select_add_fusion.1), channel_id=1, source_target_pairs={{0,8},{4,12},{8,0},{12,4},{16,24},{20,28},{24,16},{28,20},{1,9},{5... | collective-permute-start | bytes 24584 | tf_op jit(solution)/shard_map/ppermute | solution.py:38
  43.0 3.7 %collective-permute-start.4 = (f32[16,128]{1,0:T(8,128)S(1)}, f32[16,128]{1,0:T(8,128)S(1)}, u32[]{:S(2)}, u32[]{:S(2)}) collective-permute-start(f32[16,128]{1,0:T(8,128)S(1)} %add.90), channel_id=1, source_target_pairs={{0,16},{4,20},{8,24},{12,28},{16,0},{20,4},{24,8},{28,12},{1,17},{... | collective-permute-start | bytes 24584 | tf_op jit(solution)/shard_map/ppermute | solution.py:38
  46.7 3.7 %collective-permute-start.5 = (f32[16,128]{1,0:T(8,128)S(1)}, f32[16,128]{1,0:T(8,128)S(1)}, u32[]{:S(2)}, u32[]{:S(2)}) collective-permute-start(f32[16,128]{1,0:T(8,128)S(1)} %add.91), channel_id=1, source_target_pairs={{0,1},{1,0},{2,3},{3,2},{4,5},{5,4},{6,7},{7,6},{8,9},{9,8},{10,11... | collective-permute-start | bytes 24584 | tf_op jit(solution)/shard_map/ppermute | solution.py:38
  50.4 4.5 %collective-permute-start.6 = (f32[16,128]{1,0:T(8,128)S(1)}, f32[16,128]{1,0:T(8,128)S(1)}, u32[]{:S(2)}, u32[]{:S(2)}) collective-permute-start(f32[16,128]{1,0:T(8,128)S(1)} %add.92), channel_id=1, source_target_pairs={{0,2},{1,3},{2,0},{3,1},{4,6},{5,7},{6,4},{7,5},{8,10},{9,11},{10,... | collective-permute-start | bytes 24584 | tf_op jit(solution)/shard_map/ppermute | solution.py:38
  54.9 2.8 %copy-start.5 = (bf16[256,256]{1,0:T(8,128)(2,1)S(1)}, bf16[256,256]{1,0:T(8,128)(2,1)}, u32[]{:S(2)}) copy-start(bf16[256,256]{1,0:T(8,128)(2,1)} %get-tuple-element.15) | copy-start | bytes 393220
  54.9 2.8 %copy-start.6 = (bf16[256,256]{1,0:T(8,128)(2,1)S(1)}, bf16[256,256]{1,0:T(8,128)(2,1)}, u32[]{:S(2)}) copy-start(bf16[256,256]{1,0:T(8,128)(2,1)} %get-tuple-element.20) | copy-start | bytes 393220
  54.9 8.9 %collective-permute-start.7 = (f32[16,128]{1,0:T(8,128)S(1)}, f32[16,128]{1,0:T(8,128)S(1)}, u32[]{:S(2)}, u32[]{:S(2)}) collective-permute-start(f32[16,128]{1,0:T(8,128)S(1)} %add.93), channel_id=1, source_target_pairs={{0,4},{4,0},{8,12},{12,8},{16,20},{20,16},{24,28},{28,24},{1,5},{5... | collective-permute-start | bytes 24584 | tf_op jit(solution)/shard_map/ppermute | solution.py:39
  55.0 8.7 %collective-permute-start.12 = (f32[216,128]{1,0:T(8,128)S(1)}, f32[216,128]{1,0:T(8,128)S(1)}, u32[]{:S(2)}, u32[]{:S(2)}) collective-permute-start(f32[216,128]{1,0:T(8,128)S(1)} %add.97), channel_id=1, source_target_pairs={{0,2},{1,3},{2,0},{3,1},{4,6},{5,7},{6,4},{7,5},{8,10},{9,11},{10,... | collective-permute-start | bytes 331784 | tf_op jit(solution)/shard_map/ppermute | solution.py:38
  63.7 1.4 %collective-permute-start.13 = (f32[216,128]{1,0:T(8,128)S(1)}, f32[216,128]{1,0:T(8,128)S(1)}, u32[]{:S(2)}, u32[]{:S(2)}) collective-permute-start(f32[216,128]{1,0:T(8,128)S(1)} %add.98), channel_id=1, source_target_pairs={{0,4},{4,0},{8,12},{12,8},{16,20},{20,16},{24,28},{28,24},{1,5},{5... | collective-permute-start | bytes 331784 | tf_op jit(solution)/shard_map/ppermute | solution.py:39

commit v6 on v5

--- a/solution.py
+++ b/solution.py
@@ -179,7 +179,7 @@
     p1o_ref[...] = p1[2]
 
 
-def _kernel_b(bta_ref, k2t_ref, gp_ref, sl_ref, p1o_ref, s1_ref, g1_ref, gs, gacc):
+def _kernel_b(bta_ref, k2t_ref, gp_ref, sl_ref, p1o_ref, s1a_ref, s1_ref, g1_ref, gs, gacc):
     c1 = gp_ref.shape[0]
     lanes = bta_ref.shape[1] // 4
     ny2 = 4
@@ -189,7 +189,7 @@
     _add_taps(gacc, 0, gs, 0, ny2, lanes, c1)
     g = gacc[0]
     b1 = (g * sl_ref[...]).astype(BF16)
-    s1_ref[...] = _nt(p1o_ref[...], b1)
+    s1_ref[...] = s1a_ref[...] + _nt(p1o_ref[...], b1)
     _interleave(g, g1_ref, ny1, lanes)
 
 
@@ -252,7 +252,7 @@
         cost_estimate=pl.CostEstimate(flops=40_000_000, transcendentals=150_000, bytes_accessed=3_000_000),
     )(below, volume, k1m, k2m, k2t, cot)
 
-    s1b, g1b = pl.pallas_call(
+    s1, g1b = pl.pallas_call(
         _kernel_b,
         out_shape=(
             jax.ShapeDtypeStruct((kk, 2 * c1), F32),
@@ -263,25 +263,25 @@
             vm((1, 2 * c1, ny1 * q), F32),
         ],
         cost_estimate=pl.CostEstimate(flops=15_000_000, transcendentals=0, bytes_accessed=2_500_000),
-    )(shifted(bt0, "gz", -1), k2t, gp, sl, p1o)
+    )(shifted(bt0, "gz", -1), k2t, gp, sl, p1o, s1a)
 
     samples = volume.shape[0] * lax.axis_size("sa")
     cells_one = samples * (nz // 2) * lax.axis_size("gz") * ny1 * (nx // 2)
     cells_two = samples * cotangent.shape[2] * lax.axis_size("gz") * cotangent.shape[3] * cotangent.shape[4]
 
-    t2 = _all_sum(s2, ("gz", "sa")) / math.sqrt(float(cells_two))
-    t2 = t2.reshape(27, c1 // 2, 2, c2).transpose(0, 2, 1, 3).reshape(3, 3, 3, c1, c2)
-    grad_kernel_two = t2.transpose(4, 3, 0, 1, 2)
-
-    s1 = s1a + s1b
     s1r = s1.reshape(3, 3, 2, c0, 4, 2, c1)
     gk1 = jnp.stack([
         s1r[:, :, 1, :, 3, 0] + s1r[:, :, 0, :, 1, 1],
         s1r[:, :, 0, :, 0, 0] + s1r[:, :, 0, :, 2, 1],
         s1r[:, :, 0, :, 1, 0] + s1r[:, :, 0, :, 3, 1],
     ], 2)
-    t1 = _all_sum(gk1.reshape(-1, 2 * c2), ("gz", "sa")) / math.sqrt(float(cells_one))
+    rows1 = gk1.size // s2.shape[1]
+    total = _all_sum(jnp.concatenate([gk1.reshape(rows1, s2.shape[1]), s2], 0), ("gz", "sa"))
+    t1 = total[:rows1] / math.sqrt(float(cells_one))
+    t2 = total[rows1:] / math.sqrt(float(cells_two))
     grad_kernel_one = t1.reshape(3, 3, 3, c0, c1).transpose(4, 3, 0, 1, 2)
+    t2 = t2.reshape(27, c1 // 2, 2, c2).transpose(0, 2, 1, 3).reshape(3, 3, 3, c1, c2)
+    grad_kernel_two = t2.transpose(4, 3, 0, 1, 2)
 
     level_two = lvl.reshape(1, c2, 1, ny2, n2 // ny2)
     g1 = jnp.concatenate([g1a, g1b], 0)

time: 66.5 us -> 56 us (0.84)
  starting transfers between devices: 24.1 us -> 14.6 us
  other arithmetic: 2.58 us -> 0.76 us
  local copies, waits for them, and re-layouts: 9.31 us -> 10.2 us
    ppermute x8 -> x4, starting transfers between devices: 16.9 us -> 7.7 us  [_all_sum(): part = part + lax.ppermute(part, axis, [(i, i ^ k) for i in range(n)])]
    ppermute x8 -> x4, waiting for transfers between devices: 19.9 us -> 14.8 us  [_all_sum(): part = part + lax.ppermute(part, axis, [(i, i ^ k) for i in range(n)])]
    ppermute x2, waiting for transfers between devices: 0.01 us -> 4.15 us  [shifted(): return lax.ppermute(block, axis, route)]
    ppermute x2 -> x1, waiting for transfers between devices: 0.01 us -> 0.97 us  [_all_sum(): lax.ppermute(jnp.where(low, hi, lo), axis0, pair)]
    select_n x2 -> x1, other arithmetic: 0.97 us -> 0.02 us  [_all_sum(): jnp.where(low, hi, lo)]
    add x1 -> x0, other arithmetic: 0.93 us -> none  [per_device(): s1 = s1a + s1b]
    reshape x1, local copies, waits for them, and re-layouts: 0.2 us -> 1.11 us  [per_device(): s1r = s1.reshape(3, 3, 2, c0, 4, 2, c1)]
    ppermute x2 -> x1, starting transfers between devices: 3.29 us -> 3.14 us  [_all_sum(): lax.ppermute(jnp.where(low, hi, lo), axis0, pair)]
  transfers between devices with their start and end apart: 14 -> 8, of which waited for: 8 -> 7; matrix products, arithmetic and copies ran while one was open for 11% -> 8% of each run, Pallas kernels for 4% -> 0%
where the time goes in v6:
time: 56 us; the launch traced here: 55.6 us
  waiting for transfers between devices  20.3 us (36%)
  starting transfers between devices  14.6 us (26%)
  local copies, waits for them, and re-layouts  10.2 us (18%)
  Pallas kernels  8.8 us (16%)
  between operations  0.96 us (2%)
  other arithmetic  0.76 us (1%)
    ppermute x4, waiting for transfers between devices, _all_sum(): part = part + lax.ppermute(part, axis, [(i, i ^ k) for i in range(n)])  14.8 us
    ppermute x4, starting transfers between devices, _all_sum(): part = part + lax.ppermute(part, axis, [(i, i ^ k) for i in range(n)])  7.7 us
    pallas_call x1, Pallas kernels, per_device(): pl.pallas_call(_kernel_a, out_shape=(jax.ShapeDtypeStruct((c2, n2), BF16)...  6.13 us
    ppermute x2, waiting for transfers between devices, shifted(): return lax.ppermute(block, axis, route)  4.15 us
    ppermute x2, starting transfers between devices, shifted(): return lax.ppermute(block, axis, route)  3.65 us
    ppermute x1, starting transfers between devices, _all_sum(): lax.ppermute(jnp.where(low, hi, lo), axis0, pair)  3.14 us
    unnamed x21, local copies, waits for them, and re-layouts  2.83 us
    pallas_call x1, Pallas kernels, per_device(): pl.pallas_call(_kernel_b, out_shape=(jax.ShapeDtypeStruct((kk, 2 * c1), F...  2.68 us
  transfers between devices with their start and end apart: 8, of which 7 were waited for; matrix products, arithmetic and copies ran while one was open for 8% of the time, Pallas kernels for 0%

profile of v6, /device:TPU:0, one launch (start us, length us, event | category | flops | bytes accessed | tf_op | source)
XLA Modules:
  0.0 55.6 jit_solution(11340679854909092222)
XLA Ops:
  0.6 0.0 copy-start.6
  0.6 0.0 copy-start.2
  0.7 1.0 %slice.52 = bf16[1,4,3,16,512]{4,3,2,1,0:T(8,128)(2,1)S(1)} slice(bf16[1,4,4,16,512]{4,3,2,1,0:T(8,128)(2,1)} %vo_ref.1), slice={[0:1], [0:4], [1:4], [0:16], [0:512]} | slice | bytes 393216 | tf_op jit(solution)/shard_map/slice | solution.py:220
  1.6 2.4 %collective-permute-start = (bf16[1,4,3,16,512]{4,3,2,1,0:T(8,128)(2,1)S(1)}, bf16[1,4,3,16,512]{4,3,2,1,0:T(8,128)(2,1)S(1)}, u32[]{:S(2)}, u32[]{:S(2)}) collective-permute-start(bf16[1,4,3,16,512]{4,3,2,1,0:T(8,128)(2,1)S(1)} %slice.52), channel_id=1, source_target_pairs={{0,4},{4,8},{8,12},{12,16},{16,20},{20,24},{24,28},{1,5},{5,9},{9,... | collective-permute-start | bytes 589832 | tf_op jit(solution)/shard_map/ppermute | solution.py:17
  4.0 0.0 copy-done.6
  4.1 0.0 copy-done.2
  4.2 0.1 pad_maximum_fusion.5
  4.3 0.1 maximum_bitcast_fusion.1
  4.4 0.1 maximum_bitcast_fusion
  4.4 0.1 pad_maximum_fusion.3
  4.6 0.1 copy.19
  4.7 0.1 reshape.89
  4.8 0.7 %copy.21.k1_ref = bf16[64,288]{1,0:T(8,128)(2,1)} copy(bf16[64,288]{0,1:T(8,128)(2,1)S(1)} %reshape.89) | data formatting | bytes 73728 | tf_op jit(solution)/shard_map/reshape | solution.py:203
  5.5 0.1 pad_maximum_fusion.1
  5.6 0.0 copy-start
  5.7 0.0 copy-start.8
  5.7 0.8 %copy.22.k2_ref = bf16[64,1152]{1,0:T(8,128)(2,1)} copy(bf16[64,1152]{0,1:T(8,128)(2,1)S(1)} %bitcast.48) | data formatting | bytes 294912 | tf_op jit(solution)/shard_map/reshape | solution.py:211
  6.5 0.1 copy-done.8
  6.6 0.6 %copy.39 = bf16[8,8,4,128]{3,1,2,0:T(8,128)(2,1)} copy(bf16[8,8,4,128]{3,2,1,0:T(4,128)(2,1)S(1)} %bitcast.66) | data formatting | bytes 131072
  7.2 0.0 collective-permute-done.vb_ref
  7.2 0.0 copy-start.3
  7.2 0.0 copy-done
  7.2 0.7 %copy-done.3 = bf16[1,4,3,16,512]{4,3,2,1,0:T(8,128)(2,1)} copy-done((bf16[1,4,3,16,512]{4,3,2,1,0:T(8,128)(2,1)}, bf16[1,4,3,16,512]{4,3,2,1,0:T(8,128)(2,1)S(1)}, u32[]{:S(2)}) %copy-start.3) | copy-done | bytes 196632
  7.9 6.1 %shard_map.75 = (bf16[64,512]{1,0:T(8,128)(2,1)}, bf16[64,512]{1,0:T(8,128)(2,1)}, f32[432,128]{1,0:T(8,128)}, f32[288,64]{1,0:T(8,128)}, bf16[256,256]{1,0:T(8,...) custom-call(bf16[1,4,3,16,512]{4,3,2,1,0:T(8,128)(2,1)} %copy-done.3, ...), custom_call_target="tpu_custom_call" | custom-call | flops 40000000 | bytes 3000000 | tf_op jit(solution)/shard_map/pallas_call | solution.py:232
  14.0 1.3 %collective-permute-start.1 = (bf16[64,512]{1,0:T(8,128)(2,1)}, bf16[64,512]{1,0:T(8,128)(2,1)S(1)}, u32[]{:S(2)}, u32[]{:S(2)}) collective-permute-start(bf16[64,512]{1,0:T(8,128)(2,1)} %get-tuple-element.16), channel_id=1, source_target_pairs={{4,0},{8,4},{12,8},{16,12},{20,16},{24,20},{28,24},{5,1},{9,5},{13... | collective-permute-start | bytes 196616 | tf_op jit(solution)/shard_map/ppermute | solution.py:17
  15.3 4.2 %collective-permute-done.1.bta_ref = bf16[64,512]{1,0:T(8,128)(2,1)S(1)} collective-permute-done((bf16[64,512]{1,0:T(8,128)(2,1)}, bf16[64,512]{1,0:T(8,128)(2,1)S(1)}, u32[]{:S(2)}, u32[]{:S(2)}) %collective-permute-start.1) | collective-permute-done | bytes 65568 | tf_op jit(solution)/shard_map/ppermute | solution.py:17
  19.5 0.0 copy-start.7
  19.5 0.6 %copy-done.7 = bf16[64,512]{1,0:T(8,128)(2,1)} copy-done((bf16[64,512]{1,0:T(8,128)(2,1)}, bf16[64,512]{1,0:T(8,128)(2,1)S(1)}, u32[]{:S(2)}) %copy-start.7) | copy-done | bytes 65560
  20.1 2.7 %shard_map.76 = (f32[288,64]{1,0:T(8,128)}, bf16[256,256]{1,0:T(8,128)(2,1)}) custom-call(bf16[64,512]{1,0:T(8,128)(2,1)} %copy-done.7, bf16[1152,64]{1,0:T(8,128)(2,1)} %bitcast.50, f32[64,1024]{1,0:T(8,128)} %get-tuple-element.17.gp_ref, f32[64,1024]{1,0:T(8,128)} %get-tuple-element.18.sl_ref, bf16[288,1024]{1,0:T(8,128)(2,1)} %get-tuple-element.19.p1o_ref, ...), custom_call_target="tpu_custom_call" | custom-call | flops 15000000 | bytes 2500000 | tf_op jit(solution)/shard_map/pallas_call | solution.py:255
  22.8 1.1 %reshape.93 = f32[3,3,2,4,4,2,32]{6,5,4,3,2,1,0:T(2,128)S(1)} reshape(f32[288,64]{1,0:T(8,128)} %get-tuple-element.22) | data formatting | bytes 147456 | tf_op jit(solution)/shard_map/reshape | solution.py:272
  23.9 0.1 fusion.2
  24.0 0.0 copy-start.1
  24.1 0.1 reshape.94
  24.2 0.8 %copy-done.1 = f32[432,128]{1,0:T(8,128)S(1)} copy-done((f32[432,128]{1,0:T(8,128)S(1)}, f32[432,128]{1,0:T(8,128)}, u32[]{:S(2)}) %copy-start.1) | copy-done | bytes 221208
  25.0 3.1 %collective-permute-start.2 = (f32[232,128]{1,0:T(8,128)S(1)}, f32[232,128]{1,0:T(8,128)S(1)}, u32[]{:S(2)}, u32[]{:S(2)}) collective-permute-start(f32[232,128]{1,0:T(8,128)S(1)} %fusion.1), channel_id=1, source_target_pairs={{0,4},{4,0},{8,12},{12,8},{16,20},{20,16},{24,28},{28,24},{1,5},{5... | collective-permute-start | bytes 356360 | tf_op jit(solution)/shard_map/ppermute | solution.py:36
  28.1 1.0 %collective-permute-done.2 = f32[232,128]{1,0:T(8,128)S(1)} collective-permute-done((f32[232,128]{1,0:T(8,128)S(1)}, f32[232,128]{1,0:T(8,128)S(1)}, u32[]{:S(2)}, u32[]{:S(2)}) %collective-permute-start.2) | collective-permute-done | bytes 118816 | tf_op jit(solution)/shard_map/ppermute | solution.py:36
  29.1 2.5 %collective-permute-start.3 = (f32[232,128]{1,0:T(8,128)S(1)}, f32[232,128]{1,0:T(8,128)S(1)}, u32[]{:S(2)}, u32[]{:S(2)}) collective-permute-start(f32[232,128]{1,0:T(8,128)S(1)} %select_add_fusion), channel_id=1, source_target_pairs={{0,8},{4,12},{8,0},{12,4},{16,24},{20,28},{24,16},{28,20},{1,9},{5... | collective-permute-start | bytes 356360 | tf_op jit(solution)/shard_map/ppermute | solution.py:38
  31.6 3.7 %collective-permute-done.3 = f32[232,128]{1,0:T(8,128)S(1)} collective-permute-done((f32[232,128]{1,0:T(8,128)S(1)}, f32[232,128]{1,0:T(8,128)S(1)}, u32[]{:S(2)}, u32[]{:S(2)}) %collective-permute-start.3) | collective-permute-done | bytes 118816 | tf_op jit(solution)/shard_map/ppermute | solution.py:38
  35.3 0.9 %collective-permute-start.4 = (f32[232,128]{1,0:T(8,128)S(1)}, f32[232,128]{1,0:T(8,128)S(1)}, u32[]{:S(2)}, u32[]{:S(2)}) collective-permute-start(f32[232,128]{1,0:T(8,128)S(1)} %add.71), channel_id=1, source_target_pairs={{0,16},{4,20},{8,24},{12,28},{16,0},{20,4},{24,8},{28,12},{1,17},{... | collective-permute-start | bytes 356360 | tf_op jit(solution)/shard_map/ppermute | solution.py:38
  36.3 4.0 %collective-permute-done.4 = f32[232,128]{1,0:T(8,128)S(1)} collective-permute-done((f32[232,128]{1,0:T(8,128)S(1)}, f32[232,128]{1,0:T(8,128)S(1)}, u32[]{:S(2)}, u32[]{:S(2)}) %collective-permute-start.4) | collective-permute-done | bytes 118816 | tf_op jit(solution)/shard_map/ppermute | solution.py:38
  40.4 0.0 copy-start.9
  40.4 1.6 %collective-permute-start.5 = (f32[232,128]{1,0:T(8,128)S(1)}, f32[232,128]{1,0:T(8,128)S(1)}, u32[]{:S(2)}, u32[]{:S(2)}) collective-permute-start(f32[232,128]{1,0:T(8,128)S(1)} %add.72), channel_id=1, source_target_pairs={{0,1},{1,0},{2,3},{3,2},{4,5},{5,4},{6,7},{7,6},{8,9},{9,8},{10,11... | collective-permute-start | bytes 356360 | tf_op jit(solution)/shard_map/ppermute | solution.py:38
  42.0 3.3 %collective-permute-done.5 = f32[232,128]{1,0:T(8,128)S(1)} collective-permute-done((f32[232,128]{1,0:T(8,128)S(1)}, f32[232,128]{1,0:T(8,128)S(1)}, u32[]{:S(2)}, u32[]{:S(2)}) %collective-permute-start.5) | collective-permute-done | bytes 118816 | tf_op jit(solution)/shard_map/ppermute | solution.py:38
  45.3 2.7 %collective-permute-start.6 = (f32[232,128]{1,0:T(8,128)S(1)}, f32[232,128]{1,0:T(8,128)S(1)}, u32[]{:S(2)}, u32[]{:S(2)}) collective-permute-start(f32[232,128]{1,0:T(8,128)S(1)} %add.73), channel_id=1, source_target_pairs={{0,2},{1,3},{2,0},{3,1},{4,6},{5,7},{6,4},{7,5},{8,10},{9,11},{10,... | collective-permute-start | bytes 356360 | tf_op jit(solution)/shard_map/ppermute | solution.py:38
  47.9 0.0 copy-done.9
  47.9 0.6 %reshape.91 = bf16[1,64,1,4,128]{4,3,1,2,0:T(4,128)(2,1)} reshape(bf16[64,512]{1,0:T(8,128)(2,1)S(1)} %copy-done.9) | data formatting | bytes 131072 | tf_op jit(solution)/shard_map/reshape | solution.py:286
  48.6 0.0 copy-start.4
  48.6 0.0 copy-start.5
  48.6 3.8 %collective-permute-done.6 = f32[232,128]{1,0:T(8,128)S(1)} collective-permute-done((f32[232,128]{1,0:T(8,128)S(1)}, f32[232,128]{1,0:T(8,128)S(1)}, u32[]{:S(2)}, u32[]{:S(2)}) %collective-permute-start.6) | collective-permute-done | bytes 118816 | tf_op jit(solution)/shard_map/ppermute | solution.py:38
  52.4 0.1 collective-permute-start.7
  52.5 0.0 copy-done.4
  52.5 0.0 copy-done.5
  52.5 0.9 %copy.38 = bf16[2,8,32,256]{3,1,0,2:T(8,128)(2,1)} copy(bf16[2,8,32,256]{3,2,1,0:T(8,128)(2,1)S(1)} %bitcast.52) | data formatting | bytes 524288 | tf_op jit(solution)/shard_map/reshape | solution.py:288
  53.4 0.4 collective-permute-done.7
  53.8 0.3 reshape.96
  54.1 0.8 %copy.29 = f32[27,2,16,64]{3,2,1,0:T(8,128)} copy(f32[27,2,16,64]{3,1,2,0:T(2,128)S(1)} %bitcast.51) | data formatting | bytes 442368 | tf_op jit(solution)/shard_map/transpose | solution.py:283
  54.9 0.7 %reshape.95 = f32[3,3,3,4,32]{4,3,2,1,0:T(4,128)} reshape(f32[27,128]{1,0:T(8,128)S(1)} %slice_multiply_fusion.1) | data formatting | bytes 27648 | tf_op jit(solution)/shard_map/reshape | solution.py:282
  (23 shorter events, 0.4 us)
Async XLA Ops:
  0.6 3.4 %copy-start.6 = (bf16[32,4,3,3,3]{0,1,4,3,2:T(4,128)(2,1)S(1)}, bf16[32,4,3,3,3]{0,1,4,3,2:T(4,128)(2,1)}, u32[]{:S(2)}) copy-start(bf16[32,4,3,3,3]{0,1,4,3,2:T(4,128)(2,1)} %param.5) | copy-start | bytes 20740
  0.6 3.5 %copy-start.2 = (bf16[64,32,3,3,3]{0,1,4,3,2:T(8,128)(2,1)S(1)}, bf16[64,32,3,3,3]{0,1,4,3,2:T(8,128)(2,1)}, u32[]{:S(2)}) copy-start(bf16[64,32,3,3,3]{0,1,4,3,2:T(8,128)(2,1)} %param.6) | copy-start | bytes 331780
  1.6 5.6 %collective-permute-start = (bf16[1,4,3,16,512]{4,3,2,1,0:T(8,128)(2,1)S(1)}, bf16[1,4,3,16,512]{4,3,2,1,0:T(8,128)(2,1)S(1)}, u32[]{:S(2)}, u32[]{:S(2)}) collective-permute-start(bf16[1,4,3,16,512]{4,3,2,1,0:T(8,128)(2,1)S(1)} %slice.52), channel_id=1, source_target_pairs={{0,4},{4,8},{8,12},{12,16},{16,20},{20,24},{24,28},{1,5},{5,9},{9,... | collective-permute-start | bytes 589832 | tf_op jit(solution)/shard_map/ppermute | solution.py:17
  5.6 1.6 %copy-start = (bf16[64,3,3,2,2,32]{0,5,4,3,2,1:T(8,128)(2,1)}, bf16[64,3,3,2,2,32]{0,5,4,3,2,1:T(8,128)(2,1)S(1)}, u32[]{:S(2)}) copy-start(bf16[64,3,3,2,2,32]{0,5,4,3,2,1:T(8,128)(2,1)S(1)} %copy.20) | copy-start | bytes 442372
  5.7 0.9 %copy-start.8 = (bf16[1,64,1,4,128]{4,3,2,1,0:T(4,128)(2,1)S(1)}, bf16[1,64,1,4,128]{4,3,2,1,0:T(4,128)(2,1)}, u32[]{:S(2)}) copy-start(bf16[1,64,1,4,128]{4,3,2,1,0:T(4,128)(2,1)} %param.7) | copy-start | bytes 196612
  7.2 0.7 %copy-start.3 = (bf16[1,4,3,16,512]{4,3,2,1,0:T(8,128)(2,1)}, bf16[1,4,3,16,512]{4,3,2,1,0:T(8,128)(2,1)S(1)}, u32[]{:S(2)}) copy-start(bf16[1,4,3,16,512]{4,3,2,1,0:T(8,128)(2,1)S(1)} %collective-permute-done.vb_ref) | copy-start | bytes 589828
  14.0 5.4 %collective-permute-start.1 = (bf16[64,512]{1,0:T(8,128)(2,1)}, bf16[64,512]{1,0:T(8,128)(2,1)S(1)}, u32[]{:S(2)}, u32[]{:S(2)}) collective-permute-start(bf16[64,512]{1,0:T(8,128)(2,1)} %get-tuple-element.16), channel_id=1, source_target_pairs={{4,0},{8,4},{12,8},{16,12},{20,16},{24,20},{28,24},{5,1},{9,5},{13... | collective-permute-start | bytes 196616 | tf_op jit(solution)/shard_map/ppermute | solution.py:17
  19.5 0.6 %copy-start.7 = (bf16[64,512]{1,0:T(8,128)(2,1)}, bf16[64,512]{1,0:T(8,128)(2,1)S(1)}, u32[]{:S(2)}) copy-start(bf16[64,512]{1,0:T(8,128)(2,1)S(1)} %collective-permute-done.1.bta_ref) | copy-start | bytes 196612
  24.0 0.9 %copy-start.1 = (f32[432,128]{1,0:T(8,128)S(1)}, f32[432,128]{1,0:T(8,128)}, u32[]{:S(2)}) copy-start(f32[432,128]{1,0:T(8,128)} %get-tuple-element.23) | copy-start | bytes 663556
  25.0 4.1 %collective-permute-start.2 = (f32[232,128]{1,0:T(8,128)S(1)}, f32[232,128]{1,0:T(8,128)S(1)}, u32[]{:S(2)}, u32[]{:S(2)}) collective-permute-start(f32[232,128]{1,0:T(8,128)S(1)} %fusion.1), channel_id=1, source_target_pairs={{0,4},{4,0},{8,12},{12,8},{16,20},{20,16},{24,28},{28,24},{1,5},{5... | collective-permute-start | bytes 356360 | tf_op jit(solution)/shard_map/ppermute | solution.py:36
  29.1 6.2 %collective-permute-start.3 = (f32[232,128]{1,0:T(8,128)S(1)}, f32[232,128]{1,0:T(8,128)S(1)}, u32[]{:S(2)}, u32[]{:S(2)}) collective-permute-start(f32[232,128]{1,0:T(8,128)S(1)} %select_add_fusion), channel_id=1, source_target_pairs={{0,8},{4,12},{8,0},{12,4},{16,24},{20,28},{24,16},{28,20},{1,9},{5... | collective-permute-start | bytes 356360 | tf_op jit(solution)/shard_map/ppermute | solution.py:38
  35.3 5.0 %collective-permute-start.4 = (f32[232,128]{1,0:T(8,128)S(1)}, f32[232,128]{1,0:T(8,128)S(1)}, u32[]{:S(2)}, u32[]{:S(2)}) collective-permute-start(f32[232,128]{1,0:T(8,128)S(1)} %add.71), channel_id=1, source_target_pairs={{0,16},{4,20},{8,24},{12,28},{16,0},{20,4},{24,8},{28,12},{1,17},{... | collective-permute-start | bytes 356360 | tf_op jit(solution)/shard_map/ppermute | solution.py:38
  40.4 7.6 %copy-start.9 = (bf16[64,512]{1,0:T(8,128)(2,1)S(1)}, bf16[64,512]{1,0:T(8,128)(2,1)}, u32[]{:S(2)}) copy-start(bf16[64,512]{1,0:T(8,128)(2,1)} %get-tuple-element.14) | copy-start | bytes 196612
  40.4 4.9 %collective-permute-start.5 = (f32[232,128]{1,0:T(8,128)S(1)}, f32[232,128]{1,0:T(8,128)S(1)}, u32[]{:S(2)}, u32[]{:S(2)}) collective-permute-start(f32[232,128]{1,0:T(8,128)S(1)} %add.72), channel_id=1, source_target_pairs={{0,1},{1,0},{2,3},{3,2},{4,5},{5,4},{6,7},{7,6},{8,9},{9,8},{10,11... | collective-permute-start | bytes 356360 | tf_op jit(solution)/shard_map/ppermute | solution.py:38
  45.3 7.1 %collective-permute-start.6 = (f32[232,128]{1,0:T(8,128)S(1)}, f32[232,128]{1,0:T(8,128)S(1)}, u32[]{:S(2)}, u32[]{:S(2)}) collective-permute-start(f32[232,128]{1,0:T(8,128)S(1)} %add.73), channel_id=1, source_target_pairs={{0,2},{1,3},{2,0},{3,1},{4,6},{5,7},{6,4},{7,5},{8,10},{9,11},{10,... | collective-permute-start | bytes 356360 | tf_op jit(solution)/shard_map/ppermute | solution.py:38
  48.6 3.9 %copy-start.4 = (bf16[256,256]{1,0:T(8,128)(2,1)S(1)}, bf16[256,256]{1,0:T(8,128)(2,1)}, u32[]{:S(2)}) copy-start(bf16[256,256]{1,0:T(8,128)(2,1)} %get-tuple-element.15) | copy-start | bytes 393220
  48.6 3.9 %copy-start.5 = (bf16[256,256]{1,0:T(8,128)(2,1)S(1)}, bf16[256,256]{1,0:T(8,128)(2,1)}, u32[]{:S(2)}) copy-start(bf16[256,256]{1,0:T(8,128)(2,1)} %get-tuple-element.21) | copy-start | bytes 393220
  52.4 1.4 %collective-permute-start.7 = (f32[232,128]{1,0:T(8,128)S(1)}, f32[232,128]{1,0:T(8,128)S(1)}, u32[]{:S(2)}, u32[]{:S(2)}) collective-permute-start(f32[232,128]{1,0:T(8,128)S(1)} %add.74), channel_id=1, source_target_pairs={{0,4},{4,0},{8,12},{12,8},{16,20},{20,16},{24,28},{28,24},{1,5},{5... | collective-permute-start | bytes 356360 | tf_op jit(solution)/shard_map/ppermute | solution.py:39

commit v7 on v6

--- a/solution.py
+++ b/solution.py
@@ -17,7 +17,7 @@
     return lax.ppermute(block, axis, route)
 
 
-def _all_sum(x, axes):
+def _all_sum(x, y, axes):
     steps = []
     for axis in axes:
         n = lax.axis_size(axis)
@@ -34,10 +34,14 @@
     lo, hi = x[:half], x[half:]
     pair = [(i, i ^ k0) for i in range(n0)]
     part = jnp.where(low, lo, hi) + lax.ppermute(jnp.where(low, hi, lo), axis0, pair)
+    ry = y.shape[0]
+    cur = jnp.concatenate([part, jnp.pad(y, ((0, -ry % 8), (0, 0)))], 0)
     for axis, n, k in steps[1:]:
-        part = part + lax.ppermute(part, axis, [(i, i ^ k) for i in range(n)])
-    other = lax.ppermute(part, axis0, pair)
-    return jnp.where(low, jnp.concatenate([part, other], 0), jnp.concatenate([other, part], 0))[:rows]
+        cur = cur + lax.ppermute(cur, axis, [(i, i ^ k) for i in range(n)])
+    recv = lax.ppermute(cur, axis0, pair)
+    part, other = cur[:half], recv[:half]
+    xs = jnp.where(low, jnp.concatenate([part, other], 0), jnp.concatenate([other, part], 0))[:rows]
+    return xs, cur[half:half + ry] + recv[half:half + ry]
 
 
 def _sigmoid(v):
@@ -111,7 +115,7 @@
 
 
 def _kernel_a(vb_ref, vo_ref, k1_ref, k2_ref, k2t_ref, cot_ref,
-              lvl_ref, bt_ref, s2_ref, s1_ref, g1_ref, gp_ref, sl_ref, p1o_ref,
+              lvl_ref, s2_ref, s1_ref, g1_ref, gp_ref, sl_ref, p1o_ref, t2o_ref,
               tp, p1, t2, p2, gs, gacc):
     c0, ny, nx = vo_ref.shape[1], vo_ref.shape[3], vo_ref.shape[4]
     lanes = nx // 4
@@ -154,7 +158,7 @@
     sig = _sigmoid(pre)
     lvl_ref[...] = (pre * sig).astype(BF16)
     bt0 = (cot_ref[...].astype(F32) * (sig * (1.0 + pre * (1.0 - sig)))).astype(BF16)
-    bt_ref[...] = bt0
+    t2o_ref[...] = t2[2]
 
     dup = _nt(p2[...], jnp.concatenate([bt0, bt0], axis=0))
     c2n = dup.shape[1] // 2
@@ -179,13 +183,41 @@
     p1o_ref[...] = p1[2]
 
 
-def _kernel_b(bta_ref, k2t_ref, gp_ref, sl_ref, p1o_ref, s1a_ref, s1_ref, g1_ref, gs, gacc):
-    c1 = gp_ref.shape[0]
-    lanes = bta_ref.shape[1] // 4
-    ny2 = 4
-    ny1 = gp_ref.shape[1] // lanes
+def _kernel_b(vo_ref, va_ref, t2i_ref, k1_ref, k2_ref, k2t_ref, cota_ref, gp_ref, sl_ref, p1o_ref, s1a_ref,
+              s1_ref, g1_ref, tp, p1, t2, p2, gs, gacc):
+    c0, ny, nx = vo_ref.shape[1], vo_ref.shape[3], vo_ref.shape[4]
+    lanes = nx // 4
+    ny1 = ny // 2
+    ny2 = ny1 // 2
+    c2 = t2.shape[2]
+    c1 = c2 // 2
+    rows0 = 4 * c0
+    nz = vo_ref.shape[2]
+    pieces = [(vo_ref, nz - 1)] + [(va_ref, z) for z in range(va_ref.shape[2])]
+    _relayout_volume(pieces, tp, c0, ny, nx)
+    for a in range(2):
+        for d in range(3):
+            for y1 in range(ny1):
+                p1[a, d * 3 * 2 * rows0:(d + 1) * 3 * 2 * rows0, y1 * lanes:(y1 + 1) * lanes] = (
+                    tp[2 * a + d, 2 * y1:2 * y1 + 3].reshape(3 * 2 * rows0, lanes))
+    k1 = k1_ref[...]
+    t2[0] = t2i_ref[...]
+    t2[1:, 0] = jnp.zeros((2, c2, lanes), BF16)
+    for a in range(2):
+        pre = jnp.dot(k1, p1[a], preferred_element_type=F32)
+        act = pre * _sigmoid(pre)
+        for y1 in range(ny1):
+            blk = act[:, y1 * lanes:(y1 + 1) * lanes]
+            t2[a + 1, y1 + 1] = jnp.concatenate([blk, _shift_right(blk)], axis=0).astype(BF16)
+    for d in range(3):
+        for y2 in range(ny2):
+            p2[d * 3 * c2:(d + 1) * 3 * c2, y2 * lanes:(y2 + 1) * lanes] = (
+                t2[d, 2 * y2:2 * y2 + 3].reshape(3 * c2, lanes))
+    pre = jnp.dot(k2_ref[...], p2[...], preferred_element_type=F32)
+    bt1 = (cota_ref[...].astype(F32) * _slope(pre)).astype(BF16)
+
     gacc[0] = gp_ref[...]
-    gs[...] = jnp.dot(k2t_ref[:3 * 2 * c1], bta_ref[...], preferred_element_type=F32)
+    gs[...] = jnp.dot(k2t_ref[:3 * c2], bt1, preferred_element_type=F32)
     _add_taps(gacc, 0, gs, 0, ny2, lanes, c1)
     g = gacc[0]
     b1 = (g * sl_ref[...]).astype(BF16)
@@ -218,8 +250,10 @@
     assert nz == 4 and cotangent.shape[2] == 1
     q = nx // 4
     below = shifted(volume[:, :, 1:], "gz", 1)
+    above = shifted(volume, "gz", -1)
     n2 = cotangent.shape[3] * cotangent.shape[4]
     cot = cotangent[0, :, 0].reshape(c2, n2)
+    cot_above = shifted(cot, "gz", -1)
 
     k1m = _level_one_weights(kernel_one)
     k2m = _level_two_weights(kernel_two)
@@ -229,10 +263,9 @@
     nzi = below.shape[2] + nz
     vm = pltpu.VMEM
     kk = k1m.shape[1]
-    lvl, bt0, s2, s1a, g1a, gp, sl, p1o = pl.pallas_call(
+    lvl, s2, s1a, g1a, gp, sl, p1o, t2o = pl.pallas_call(
         _kernel_a,
         out_shape=(
-            jax.ShapeDtypeStruct((c2, n2), BF16),
             jax.ShapeDtypeStruct((c2, n2), BF16),
             jax.ShapeDtypeStruct((27 * c1 // 2, 2 * c2), F32),
             jax.ShapeDtypeStruct((kk, 2 * c1), F32),
@@ -240,6 +273,7 @@
             jax.ShapeDtypeStruct((2 * c1, ny1 * q), F32),
             jax.ShapeDtypeStruct((2 * c1, ny1 * q), F32),
             jax.ShapeDtypeStruct((kk, ny1 * q), BF16),
+            jax.ShapeDtypeStruct((ny1 + 1, 4 * c1, q), BF16),
         ),
         scratch_shapes=[
             vm((nzi, ny + 1, 8 * c0, q), BF16),
@@ -259,11 +293,15 @@
             jax.ShapeDtypeStruct((ny1 * c1, 2 * q), BF16),
         ),
         scratch_shapes=[
+            vm((1 + above.shape[2], ny + 1, 8 * c0, q), BF16),
+            vm((2, kk, ny1 * q), BF16),
+            vm((3, ny1 + 1, 4 * c1, q), BF16),
+            vm((k2m.shape[1], n2), BF16),
             vm((3 * 4 * c1, n2), F32),
             vm((1, 2 * c1, ny1 * q), F32),
         ],
-        cost_estimate=pl.CostEstimate(flops=15_000_000, transcendentals=0, bytes_accessed=2_500_000),
-    )(shifted(bt0, "gz", -1), k2t, gp, sl, p1o, s1a)
+        cost_estimate=pl.CostEstimate(flops=25_000_000, transcendentals=70_000, bytes_accessed=3_000_000),
+    )(volume, above, t2o, k1m, k2m, k2t, cot_above, gp, sl, p1o, s1a)
 
     samples = volume.shape[0] * lax.axis_size("sa")
     cells_one = samples * (nz // 2) * lax.axis_size("gz") * ny1 * (nx // 2)
@@ -276,9 +314,9 @@
         s1r[:, :, 0, :, 1, 0] + s1r[:, :, 0, :, 3, 1],
     ], 2)
     rows1 = gk1.size // s2.shape[1]
-    total = _all_sum(jnp.concatenate([gk1.reshape(rows1, s2.shape[1]), s2], 0), ("gz", "sa"))
-    t1 = total[:rows1] / math.sqrt(float(cells_one))
-    t2 = total[rows1:] / math.sqrt(float(cells_two))
+    t2, t1 = _all_sum(s2, gk1.reshape(rows1, s2.shape[1]), ("gz", "sa"))
+    t1 = t1 / math.sqrt(float(cells_one))
+    t2 = t2 / math.sqrt(float(cells_two))
     grad_kernel_one = t1.reshape(3, 3, 3, c0, c1).transpose(4, 3, 0, 1, 2)
     t2 = t2.reshape(27, c1 // 2, 2, c2).transpose(0, 2, 1, 3).reshape(3, 3, 3, c1, c2)
     grad_kernel_two = t2.transpose(4, 3, 0, 1, 2)

time: 56 us -> 58.4 us (1.043)
  waiting for transfers between devices: 20.3 us -> 14.8 us
  starting transfers between devices: 14.6 us -> 19.3 us
  Pallas kernels: 8.8 us -> 11.5 us
  other arithmetic: 0.76 us -> 1.64 us
    ppermute x2 -> x3, waiting for transfers between devices: 4.15 us -> 0.01 us  [shifted(): return lax.ppermute(block, axis, route)]
    pallas_call x1, Pallas kernels: 2.68 us -> 5.45 us  [per_device(): pl.pallas_call(_kernel_b, out_shape=(jax.ShapeDtypeStruct((kk, 2 * c1), F...]
    ppermute x5, starting transfers between devices: 7.77 us -> 10.1 us  [the longest x4 10.1 us: _all_sum(): cur = cur + lax.ppermute(cur, axis, [(i, i ^ k) for i in range(n)])]
    ppermute x2 -> x3, starting transfers between devices: 3.65 us -> 5.89 us  [shifted(): return lax.ppermute(block, axis, route)]
    ppermute x1, waiting for transfers between devices: 0.97 us -> 0.01 us  [_all_sum(): lax.ppermute(jnp.where(low, hi, lo), axis0, pair)]
    select_n x1, other arithmetic: 0.02 us -> 0.96 us  [_all_sum(): jnp.where(low, hi, lo)]
    unnamed x21 -> x25, local copies, waits for them, and re-layouts: 2.83 us -> 2.38 us
  transfers between devices with their start and end apart: 8 -> 9, of which waited for: 7 -> 4; matrix products, arithmetic and copies ran while one was open for 8% -> 12% of each run, Pallas kernels for 0% -> 20%
where the time goes in v7:
time: 58.4 us; the launch traced here: 58 us
  starting transfers between devices  19.3 us (33%)
  waiting for transfers between devices  14.8 us (25%)
  Pallas kernels  11.5 us (20%)
  local copies, waits for them, and re-layouts  9.75 us (17%)
  other arithmetic  1.64 us (3%)
  between operations  1.02 us (2%)
    ppermute x4, waiting for transfers between devices, _all_sum(): cur = cur + lax.ppermute(cur, axis, [(i, i ^ k) for i in range(n)])  14.8 us
    ppermute x4, starting transfers between devices, _all_sum(): cur = cur + lax.ppermute(cur, axis, [(i, i ^ k) for i in range(n)])  10.1 us
    pallas_call x1, Pallas kernels, per_device(): pl.pallas_call(_kernel_a, out_shape=(jax.ShapeDtypeStruct((c2, n2), BF16)...  6 us
    ppermute x3, starting transfers between devices, shifted(): return lax.ppermute(block, axis, route)  5.89 us
    pallas_call x1, Pallas kernels, per_device(): pl.pallas_call(_kernel_b, out_shape=(jax.ShapeDtypeStruct((kk, 2 * c1), F...  5.45 us
    ppermute x1, starting transfers between devices, _all_sum(): lax.ppermute(jnp.where(low, hi, lo), axis0, pair)  3.28 us
    unnamed x25, local copies, waits for them, and re-layouts  2.38 us
  transfers between devices with their start and end apart: 9, of which 4 were waited for; matrix products, arithmetic and copies ran while one was open for 12% of the time, Pallas kernels for 20%

profile of v7, /device:TPU:0, one launch (start us, length us, event | category | flops | bytes accessed | tf_op | source)
XLA Modules:
  0.0 58.0 jit_solution(1575435850972406872)
XLA Ops:
  0.6 0.0 copy-start.10
  0.6 1.4 %collective-permute-start.1 = (bf16[1,4,4,16,512]{4,3,2,1,0:T(8,128)(2,1)}, bf16[1,4,4,16,512]{4,3,2,1,0:T(8,128)(2,1)S(1)}, u32[]{:S(2)}, u32[]{:S(2)}) collective-permute-start(bf16[1,4,4,16,512]{4,3,2,1,0:T(8,128)(2,1)} %vo_ref.3), channel_id=1, source_target_pairs={{4,0},{8,4},{12,8},{16,12},{20,16},{24,20},{28,24},{5,1},{9,5},{13... | collective-permute-start | bytes 786440 | tf_op jit(solution)/shard_map/ppermute | solution.py:17
  2.1 0.0 copy-start.8
  2.1 0.9 %slice.54 = bf16[1,4,3,16,512]{4,3,2,1,0:T(8,128)(2,1)S(1)} slice(bf16[1,4,4,16,512]{4,3,2,1,0:T(8,128)(2,1)} %vo_ref.3), slice={[0:1], [0:4], [1:4], [0:16], [0:512]} | slice | bytes 393216 | tf_op jit(solution)/shard_map/slice | solution.py:252
  3.0 0.0 copy-start.4
  3.0 3.2 %collective-permute-start = (bf16[1,4,3,16,512]{4,3,2,1,0:T(8,128)(2,1)S(1)}, bf16[1,4,3,16,512]{4,3,2,1,0:T(8,128)(2,1)S(1)}, u32[]{:S(2)}, u32[]{:S(2)}) collective-permute-start(bf16[1,4,3,16,512]{4,3,2,1,0:T(8,128)(2,1)S(1)} %slice.54), channel_id=1, source_target_pairs={{0,4},{4,8},{8,12},{12,16},{16,20},{20,24},{24,28},{1,5},{5,9},{9,... | collective-permute-start | bytes 589832 | tf_op jit(solution)/shard_map/ppermute | solution.py:17
  6.2 0.0 copy-done.10
  6.3 0.0 copy-start.3
  6.3 1.3 %collective-permute-start.2 = (bf16[64,512]{1,0:T(8,128)(2,1)S(1)}, bf16[64,512]{1,0:T(8,128)(2,1)S(1)}, u32[]{:S(2)}, u32[]{:S(2)}) collective-permute-start(bf16[64,512]{1,0:T(8,128)(2,1)S(1)} %bitcast.54), channel_id=1, source_target_pairs={{4,0},{8,4},{12,8},{16,12},{20,16},{24,20},{28,24},{5,1},{9,5},{13... | collective-permute-start | bytes 196616 | tf_op jit(solution)/shard_map/ppermute | solution.py:17
  7.6 0.0 copy-done.8
  7.7 0.0 copy-done.3
  7.7 0.0 copy-done.4
  7.8 0.1 pad_maximum_fusion.4
  7.8 0.1 pad_maximum_fusion
  7.9 0.1 maximum_bitcast_fusion.1
  8.0 0.1 maximum_bitcast_fusion
  8.1 0.1 pad_maximum_fusion.2
  8.2 0.1 copy.20
  8.3 0.1 reshape.93
  8.5 0.7 %copy.22.k1_ref = bf16[64,288]{1,0:T(8,128)(2,1)} copy(bf16[64,288]{0,1:T(8,128)(2,1)S(1)} %reshape.93) | data formatting | bytes 73728 | tf_op jit(solution)/shard_map/reshape | solution.py:235
  9.2 0.0 copy-start
  9.2 0.8 %copy.23.k2_ref = bf16[64,1152]{1,0:T(8,128)(2,1)} copy(bf16[64,1152]{0,1:T(8,128)(2,1)S(1)} %bitcast.48) | data formatting | bytes 294912 | tf_op jit(solution)/shard_map/reshape | solution.py:243
  10.0 0.0 collective-permute-done.vb_ref
  10.0 0.0 copy-start.5
  10.1 0.0 copy-done
  10.1 0.7 %copy-done.5 = bf16[1,4,3,16,512]{4,3,2,1,0:T(8,128)(2,1)} copy-done((bf16[1,4,3,16,512]{4,3,2,1,0:T(8,128)(2,1)}, bf16[1,4,3,16,512]{4,3,2,1,0:T(8,128)(2,1)S(1)}, u32[]{:S(2)}) %copy-start.5) | copy-done | bytes 196632
  10.7 6.0 %shard_map.75 = (bf16[64,512]{1,0:T(8,128)(2,1)}, f32[432,128]{1,0:T(8,128)}, f32[288,64]{1,0:T(8,128)}, bf16[256,256]{1,0:T(8,128)(2,1)}, f32[64,1024]{1,0:T(8,...) custom-call(bf16[1,4,3,16,512]{4,3,2,1,0:T(8,128)(2,1)} %copy-done.5, ...), custom_call_target="tpu_custom_call" | custom-call | flops 40000000 | bytes 3000000 | tf_op jit(solution)/shard_map/pallas_call | solution.py:266
  16.7 1.0 %slice_select_fusion = f32[216,128]{1,0:T(8,128)S(1)} fusion(f32[432,128]{1,0:T(8,128)} %get-tuple-element.22, pred[]{:T(512)S(6)} %eq.3), kind=kLoop, calls=%fused_computation.11 | loop fusion | flops 27648 | bytes 331777 | tf_op jit(solution)/shard_map/jit(_where)/select_n | solution.py:36
  17.7 3.3 %collective-permute-start.3 = (f32[216,128]{1,0:T(8,128)S(1)}, f32[216,128]{1,0:T(8,128)S(1)}, u32[]{:S(2)}, u32[]{:S(2)}) collective-permute-start(f32[216,128]{1,0:T(8,128)S(1)} %slice_select_fusion), channel_id=1, source_target_pairs={{0,4},{4,0},{8,12},{12,8},{16,20},{20,16},{24,28},{28,24},{1,5},{5... | collective-permute-start | bytes 331784 | tf_op jit(solution)/shard_map/ppermute | solution.py:36
  21.0 0.0 collective-permute-done.2.cota_ref
  21.0 0.0 copy-start.9
  21.0 0.0 collective-permute-done.1.va_ref
  21.0 0.0 copy-start.2
  21.0 0.6 %copy-done.9 = bf16[64,512]{1,0:T(8,128)(2,1)} copy-done((bf16[64,512]{1,0:T(8,128)(2,1)}, bf16[64,512]{1,0:T(8,128)(2,1)S(1)}, u32[]{:S(2)}) %copy-start.9) | copy-done | bytes 65560
  21.6 0.1 copy-done.2
  21.7 5.4 %shard_map.76 = (f32[288,64]{1,0:T(8,128)}, bf16[256,256]{1,0:T(8,128)(2,1)}) custom-call(bf16[1,4,4,16,512]{4,3,2,1,0:T(8,128)(2,1)} %vo_ref.3, bf16[1,4,4,16,512]{4,3,2,1,0:T(8,128)(2,1)} %copy-done.2, bf16[9,128,128]{2,1,0:T(8,128)(2,1)} %get-tuple-element.16.t2i_ref, bf16[64,288]{1,0:T(8,128)(2,1)} %copy.22.k1_ref, bf16[64,1152]{1,0:T(8,128)(2,1)} %copy.23.k2_ref, ...), custom_call_target="tpu_custom_call" | custom-call | flops 25000000 | bytes 3000000 | tf_op jit(solution)/shard_map/pallas_call | solution.py:289
  27.1 1.1 %reshape.97 = f32[3,3,2,4,4,2,32]{6,5,4,3,2,1,0:T(2,128)S(1)} reshape(f32[288,64]{1,0:T(8,128)} %get-tuple-element.23) | data formatting | bytes 147456 | tf_op jit(solution)/shard_map/reshape | solution.py:310
  28.3 0.1 fusion.3
  28.4 0.0 copy-start.1
  28.4 0.1 reshape.98
  28.5 0.0 collective-permute-done.3
  28.5 0.8 %copy-done.1 = f32[432,128]{1,0:T(8,128)S(1)} copy-done((f32[432,128]{1,0:T(8,128)S(1)}, f32[432,128]{1,0:T(8,128)}, u32[]{:S(2)}) %copy-start.1) | copy-done | bytes 221208
  29.3 2.4 %collective-permute-start.4 = (f32[248,128]{1,0:T(8,128)S(1)}, f32[248,128]{1,0:T(8,128)S(1)}, u32[]{:S(2)}, u32[]{:S(2)}) collective-permute-start(f32[248,128]{1,0:T(8,128)S(1)} %select_maximum_fusion), channel_id=1, source_target_pairs={{0,8},{4,12},{8,0},{12,4},{16,24},{20,28},{24,16},{28,20},{1,9},{5... | collective-permute-start | bytes 380936 | tf_op jit(solution)/shard_map/ppermute | solution.py:40
  31.7 3.6 %collective-permute-done.4 = f32[248,128]{1,0:T(8,128)S(1)} collective-permute-done((f32[248,128]{1,0:T(8,128)S(1)}, f32[248,128]{1,0:T(8,128)S(1)}, u32[]{:S(2)}, u32[]{:S(2)}) %collective-permute-start.4) | collective-permute-done | bytes 127008 | tf_op jit(solution)/shard_map/ppermute | solution.py:40
  35.4 3.4 %collective-permute-start.5 = (f32[248,128]{1,0:T(8,128)S(1)}, f32[248,128]{1,0:T(8,128)S(1)}, u32[]{:S(2)}, u32[]{:S(2)}) collective-permute-start(f32[248,128]{1,0:T(8,128)S(1)} %fusion.2), channel_id=1, source_target_pairs={{0,16},{4,20},{8,24},{12,28},{16,0},{20,4},{24,8},{28,12},{1,17},{... | collective-permute-start | bytes 380936 | tf_op jit(solution)/shard_map/ppermute | solution.py:40
  38.7 3.3 %collective-permute-done.5 = f32[248,128]{1,0:T(8,128)S(1)} collective-permute-done((f32[248,128]{1,0:T(8,128)S(1)}, f32[248,128]{1,0:T(8,128)S(1)}, u32[]{:S(2)}, u32[]{:S(2)}) %collective-permute-start.5) | collective-permute-done | bytes 127008 | tf_op jit(solution)/shard_map/ppermute | solution.py:40
  42.0 1.6 %collective-permute-start.6 = (f32[248,128]{1,0:T(8,128)S(1)}, f32[248,128]{1,0:T(8,128)S(1)}, u32[]{:S(2)}, u32[]{:S(2)}) collective-permute-start(f32[248,128]{1,0:T(8,128)S(1)} %add.75), channel_id=1, source_target_pairs={{0,1},{1,0},{2,3},{3,2},{4,5},{5,4},{6,7},{7,6},{8,9},{9,8},{10,11... | collective-permute-start | bytes 380936 | tf_op jit(solution)/shard_map/ppermute | solution.py:40
  43.6 3.4 %collective-permute-done.6 = f32[248,128]{1,0:T(8,128)S(1)} collective-permute-done((f32[248,128]{1,0:T(8,128)S(1)}, f32[248,128]{1,0:T(8,128)S(1)}, u32[]{:S(2)}, u32[]{:S(2)}) %collective-permute-start.6) | collective-permute-done | bytes 127008 | tf_op jit(solution)/shard_map/ppermute | solution.py:40
  47.0 0.0 copy-start.11
  47.0 2.7 %collective-permute-start.7 = (f32[248,128]{1,0:T(8,128)S(1)}, f32[248,128]{1,0:T(8,128)S(1)}, u32[]{:S(2)}, u32[]{:S(2)}) collective-permute-start(f32[248,128]{1,0:T(8,128)S(1)} %add.76), channel_id=1, source_target_pairs={{0,2},{1,3},{2,0},{3,1},{4,6},{5,7},{6,4},{7,5},{8,10},{9,11},{10,... | collective-permute-start | bytes 380936 | tf_op jit(solution)/shard_map/ppermute | solution.py:40
  49.7 4.6 %collective-permute-done.7 = f32[248,128]{1,0:T(8,128)S(1)} collective-permute-done((f32[248,128]{1,0:T(8,128)S(1)}, f32[248,128]{1,0:T(8,128)S(1)}, u32[]{:S(2)}, u32[]{:S(2)}) %collective-permute-start.7) | collective-permute-done | bytes 127008 | tf_op jit(solution)/shard_map/ppermute | solution.py:40
  54.3 0.0 copy-start.7
  54.3 0.0 copy-start.6
  54.3 0.1 collective-permute-start.8
  54.4 0.0 copy-done.11
  54.4 0.6 %reshape.95 = bf16[1,64,1,4,128]{4,3,1,2,0:T(4,128)(2,1)} reshape(bf16[64,512]{1,0:T(8,128)(2,1)S(1)} %copy-done.11) | data formatting | bytes 131072 | tf_op jit(solution)/shard_map/reshape | solution.py:324
  55.0 0.1 copy-done.7
  55.2 0.1 copy-done.6
  55.3 0.9 %copy.41 = bf16[2,8,32,256]{3,1,0,2:T(8,128)(2,1)} copy(bf16[2,8,32,256]{3,2,1,0:T(8,128)(2,1)S(1)} %bitcast.52) | data formatting | bytes 524288 | tf_op jit(solution)/shard_map/reshape | solution.py:326
  56.1 0.0 collective-permute-done.8
  56.2 0.3 div.18
  56.5 0.8 %copy.32 = f32[27,2,16,64]{3,2,1,0:T(8,128)} copy(f32[27,2,16,64]{3,1,2,0:T(2,128)S(1)} %bitcast.51) | data formatting | bytes 442368 | tf_op jit(solution)/shard_map/transpose | solution.py:321
  57.3 0.7 %reshape.99 = f32[3,3,3,4,32]{4,3,2,1,0:T(4,128)} reshape(f32[27,128]{1,0:T(8,128)S(1)} %fusion.1) | data formatting | bytes 27648 | tf_op jit(solution)/shard_map/reshape | solution.py:320
  (24 shorter events, 0.3 us)
Async XLA Ops:
  0.6 5.6 %copy-start.10 = (bf16[1,64,1,4,128]{4,3,2,1,0:T(4,128)(2,1)S(1)}, bf16[1,64,1,4,128]{4,3,2,1,0:T(4,128)(2,1)}, u32[]{:S(2)}) copy-start(bf16[1,64,1,4,128]{4,3,2,1,0:T(4,128)(2,1)} %param.7) | copy-start | bytes 196612
  0.6 20.3 %collective-permute-start.1 = (bf16[1,4,4,16,512]{4,3,2,1,0:T(8,128)(2,1)}, bf16[1,4,4,16,512]{4,3,2,1,0:T(8,128)(2,1)S(1)}, u32[]{:S(2)}, u32[]{:S(2)}) collective-permute-start(bf16[1,4,4,16,512]{4,3,2,1,0:T(8,128)(2,1)} %vo_ref.3), channel_id=1, source_target_pairs={{4,0},{8,4},{12,8},{16,12},{20,16},{24,20},{28,24},{5,1},{9,5},{13... | collective-permute-start | bytes 786440 | tf_op jit(solution)/shard_map/ppermute | solution.py:17
  2.1 5.5 %copy-start.8 = (bf16[32,4,3,3,3]{0,1,4,3,2:T(4,128)(2,1)S(1)}, bf16[32,4,3,3,3]{0,1,4,3,2:T(4,128)(2,1)}, u32[]{:S(2)}) copy-start(bf16[32,4,3,3,3]{0,1,4,3,2:T(4,128)(2,1)} %param.5) | copy-start | bytes 20740
  3.0 4.7 %copy-start.4 = (bf16[64,32,3,3,3]{0,1,4,3,2:T(8,128)(2,1)S(1)}, bf16[64,32,3,3,3]{0,1,4,3,2:T(8,128)(2,1)}, u32[]{:S(2)}) copy-start(bf16[64,32,3,3,3]{0,1,4,3,2:T(8,128)(2,1)} %param.6) | copy-start | bytes 331780
  3.0 7.0 %collective-permute-start = (bf16[1,4,3,16,512]{4,3,2,1,0:T(8,128)(2,1)S(1)}, bf16[1,4,3,16,512]{4,3,2,1,0:T(8,128)(2,1)S(1)}, u32[]{:S(2)}, u32[]{:S(2)}) collective-permute-start(bf16[1,4,3,16,512]{4,3,2,1,0:T(8,128)(2,1)S(1)} %slice.54), channel_id=1, source_target_pairs={{0,4},{4,8},{8,12},{12,16},{16,20},{20,24},{24,28},{1,5},{5,9},{9,... | collective-permute-start | bytes 589832 | tf_op jit(solution)/shard_map/ppermute | solution.py:17
  6.3 1.4 %copy-start.3 = (bf16[8,8,4,128]{3,1,2,0:T(8,128)(2,1)}, bf16[8,8,4,128]{3,1,2,0:T(8,128)(2,1)S(1)}, u32[]{:S(2)}) copy-start(bf16[8,8,4,128]{3,1,2,0:T(8,128)(2,1)S(1)} %copy.42) | copy-start | bytes 196612
  6.3 14.7 %collective-permute-start.2 = (bf16[64,512]{1,0:T(8,128)(2,1)S(1)}, bf16[64,512]{1,0:T(8,128)(2,1)S(1)}, u32[]{:S(2)}, u32[]{:S(2)}) collective-permute-start(bf16[64,512]{1,0:T(8,128)(2,1)S(1)} %bitcast.54), channel_id=1, source_target_pairs={{4,0},{8,4},{12,8},{16,12},{20,16},{24,20},{28,24},{5,1},{9,5},{13... | collective-permute-start | bytes 196616 | tf_op jit(solution)/shard_map/ppermute | solution.py:17
  9.2 0.9 %copy-start = (bf16[64,3,3,2,2,32]{0,5,4,3,2,1:T(8,128)(2,1)}, bf16[64,3,3,2,2,32]{0,5,4,3,2,1:T(8,128)(2,1)S(1)}, u32[]{:S(2)}) copy-start(bf16[64,3,3,2,2,32]{0,5,4,3,2,1:T(8,128)(2,1)S(1)} %copy.21) | copy-start | bytes 442372
  10.0 0.7 %copy-start.5 = (bf16[1,4,3,16,512]{4,3,2,1,0:T(8,128)(2,1)}, bf16[1,4,3,16,512]{4,3,2,1,0:T(8,128)(2,1)S(1)}, u32[]{:S(2)}) copy-start(bf16[1,4,3,16,512]{4,3,2,1,0:T(8,128)(2,1)S(1)} %collective-permute-done.vb_ref) | copy-start | bytes 589828
  17.7 10.8 %collective-permute-start.3 = (f32[216,128]{1,0:T(8,128)S(1)}, f32[216,128]{1,0:T(8,128)S(1)}, u32[]{:S(2)}, u32[]{:S(2)}) collective-permute-start(f32[216,128]{1,0:T(8,128)S(1)} %slice_select_fusion), channel_id=1, source_target_pairs={{0,4},{4,0},{8,12},{12,8},{16,20},{20,16},{24,28},{28,24},{1,5},{5... | collective-permute-start | bytes 331784 | tf_op jit(solution)/shard_map/ppermute | solution.py:36
  21.0 0.6 %copy-start.9 = (bf16[64,512]{1,0:T(8,128)(2,1)}, bf16[64,512]{1,0:T(8,128)(2,1)S(1)}, u32[]{:S(2)}) copy-start(bf16[64,512]{1,0:T(8,128)(2,1)S(1)} %collective-permute-done.2.cota_ref) | copy-start | bytes 196612
  21.0 0.7 %copy-start.2 = (bf16[1,4,4,16,512]{4,3,2,1,0:T(8,128)(2,1)}, bf16[1,4,4,16,512]{4,3,2,1,0:T(8,128)(2,1)S(1)}, u32[]{:S(2)}) copy-start(bf16[1,4,4,16,512]{4,3,2,1,0:T(8,128)(2,1)S(1)} %collective-permute-done.1.va_ref) | copy-start | bytes 786436
  28.4 0.9 %copy-start.1 = (f32[432,128]{1,0:T(8,128)S(1)}, f32[432,128]{1,0:T(8,128)}, u32[]{:S(2)}) copy-start(f32[432,128]{1,0:T(8,128)} %get-tuple-element.22) | copy-start | bytes 663556
  29.3 6.0 %collective-permute-start.4 = (f32[248,128]{1,0:T(8,128)S(1)}, f32[248,128]{1,0:T(8,128)S(1)}, u32[]{:S(2)}, u32[]{:S(2)}) collective-permute-start(f32[248,128]{1,0:T(8,128)S(1)} %select_maximum_fusion), channel_id=1, source_target_pairs={{0,8},{4,12},{8,0},{12,4},{16,24},{20,28},{24,16},{28,20},{1,9},{5... | collective-permute-start | bytes 380936 | tf_op jit(solution)/shard_map/ppermute | solution.py:40
  35.4 6.6 %collective-permute-start.5 = (f32[248,128]{1,0:T(8,128)S(1)}, f32[248,128]{1,0:T(8,128)S(1)}, u32[]{:S(2)}, u32[]{:S(2)}) collective-permute-start(f32[248,128]{1,0:T(8,128)S(1)} %fusion.2), channel_id=1, source_target_pairs={{0,16},{4,20},{8,24},{12,28},{16,0},{20,4},{24,8},{28,12},{1,17},{... | collective-permute-start | bytes 380936 | tf_op jit(solution)/shard_map/ppermute | solution.py:40
  42.0 5.0 %collective-permute-start.6 = (f32[248,128]{1,0:T(8,128)S(1)}, f32[248,128]{1,0:T(8,128)S(1)}, u32[]{:S(2)}, u32[]{:S(2)}) collective-permute-start(f32[248,128]{1,0:T(8,128)S(1)} %add.75), channel_id=1, source_target_pairs={{0,1},{1,0},{2,3},{3,2},{4,5},{5,4},{6,7},{7,6},{8,9},{9,8},{10,11... | collective-permute-start | bytes 380936 | tf_op jit(solution)/shard_map/ppermute | solution.py:40
  47.0 7.4 %copy-start.11 = (bf16[64,512]{1,0:T(8,128)(2,1)S(1)}, bf16[64,512]{1,0:T(8,128)(2,1)}, u32[]{:S(2)}) copy-start(bf16[64,512]{1,0:T(8,128)(2,1)} %get-tuple-element.14) | copy-start | bytes 196612
  47.0 7.2 %collective-permute-start.7 = (f32[248,128]{1,0:T(8,128)S(1)}, f32[248,128]{1,0:T(8,128)S(1)}, u32[]{:S(2)}, u32[]{:S(2)}) collective-permute-start(f32[248,128]{1,0:T(8,128)S(1)} %add.76), channel_id=1, source_target_pairs={{0,2},{1,3},{2,0},{3,1},{4,6},{5,7},{6,4},{7,5},{8,10},{9,11},{10,... | collective-permute-start | bytes 380936 | tf_op jit(solution)/shard_map/ppermute | solution.py:40
  54.3 0.9 %copy-start.7 = (bf16[256,256]{1,0:T(8,128)(2,1)S(1)}, bf16[256,256]{1,0:T(8,128)(2,1)}, u32[]{:S(2)}) copy-start(bf16[256,256]{1,0:T(8,128)(2,1)} %get-tuple-element.21) | copy-start | bytes 393220
  54.3 1.0 %copy-start.6 = (bf16[256,256]{1,0:T(8,128)(2,1)S(1)}, bf16[256,256]{1,0:T(8,128)(2,1)}, u32[]{:S(2)}) copy-start(bf16[256,256]{1,0:T(8,128)(2,1)} %get-tuple-element.15) | copy-start | bytes 393220
  54.3 1.8 %collective-permute-start.8 = (f32[248,128]{1,0:T(8,128)S(1)}, f32[248,128]{1,0:T(8,128)S(1)}, u32[]{:S(2)}, u32[]{:S(2)}) collective-permute-start(f32[248,128]{1,0:T(8,128)S(1)} %add.77), channel_id=1, source_target_pairs={{0,4},{4,0},{8,12},{12,8},{16,20},{20,16},{24,28},{28,24},{1,5},{5... | collective-permute-start | bytes 380936 | tf_op jit(solution)/shard_map/ppermute | solution.py:41

commit v8 on v4

--- a/solution.py
+++ b/solution.py
@@ -83,15 +83,17 @@
     perm = jnp.where(icol == ((s_ * 4 + r_) * c0 + i_) * ny + y_, 1.0, 0.0).astype(BF16)
 
     tp[:, 0] = jnp.zeros((nzi, 2 * rows0, lanes), BF16)
-    pieces = [(vb_ref, z) for z in range(vb_ref.shape[2])] + [(vo_ref, z) for z in range(vo_ref.shape[2])] + [
-        (va_ref, z) for z in range(va_ref.shape[2])]
-    for zi, (ref, z) in enumerate(pieces):
-        zmat = ref[0, :, z].reshape(c0 * ny, nx)
-        ymat = jnp.dot(zmat, sel_x, preferred_element_type=F32)
-        blocks = [ymat[:, r * lanes:(r + 1) * lanes] for r in range(4)]
-        q = jnp.concatenate(blocks + [_shift_right(b) for b in blocks], axis=0).astype(BF16)
-        t = jnp.dot(perm, q, preferred_element_type=F32).astype(BF16)
-        tp[zi, 1:] = t.reshape(ny, 2 * rows0, lanes)
+    zi = 0
+    for ref in (vb_ref, vo_ref, va_ref):
+        nzp = ref.shape[2]
+        whole = jnp.dot(ref[0].reshape(c0 * nzp * ny, nx), sel_x, preferred_element_type=F32)
+        for z in range(nzp):
+            ymat = jnp.concatenate([whole[(i * nzp + z) * ny:(i * nzp + z + 1) * ny] for i in range(c0)], axis=0)
+            blocks = [ymat[:, r * lanes:(r + 1) * lanes] for r in range(4)]
+            q = jnp.concatenate(blocks + [_shift_right(b) for b in blocks], axis=0).astype(BF16)
+            t = jnp.dot(perm, q, preferred_element_type=F32).astype(BF16)
+            tp[zi, 1:] = t.reshape(ny, 2 * rows0, lanes)
+            zi += 1
 
     for a in range(n_act):
         for d in range(3):

time: 54.9 us -> 54.3 us (0.989)
  Pallas kernels: 8.39 us -> 7.73 us
    pallas_call x1, Pallas kernels: 8.39 us -> 7.73 us  [per_device(): pl.pallas_call(_kernel, out_shape=(jax.ShapeDtypeStruct((c2, n2), BF16),...]
where the time goes in v8:
time: 54.3 us; the launch traced here: 53.9 us
  starting transfers between devices  19.5 us (36%)
  waiting for transfers between devices  15.2 us (28%)
  local copies, waits for them, and re-layouts  9.68 us (18%)
  Pallas kernels  7.73 us (14%)
  between operations  0.97 us (2%)
  other arithmetic  0.84 us (2%)
    ppermute x4, waiting for transfers between devices, _all_sum(): part = part + lax.ppermute(part, axis, [(i, i ^ k) for i in range(n)])  14.2 us
    ppermute x4, starting transfers between devices, _all_sum(): part = part + lax.ppermute(part, axis, [(i, i ^ k) for i in range(n)])  10.4 us
    pallas_call x1, Pallas kernels, per_device(): pl.pallas_call(_kernel, out_shape=(jax.ShapeDtypeStruct((c2, n2), BF16),...  7.73 us
    ppermute x3, starting transfers between devices, shifted(): return lax.ppermute(block, axis, route)  6.39 us
    ppermute x1, starting transfers between devices, _all_sum(): lax.ppermute(jnp.where(low, hi, lo), axis0, pair)  2.63 us
    unnamed x18, local copies, waits for them, and re-layouts  1.61 us
    reshape x1, local copies, waits for them, and re-layouts, per_device(): s1r = s1.reshape(3, 3, 2, c0, 4, 2, c1)  1.11 us
  transfers between devices with their start and end apart: 9, of which 5 were waited for; matrix products, arithmetic and copies ran while one was open for 10% of the time, Pallas kernels for 0%

profile of v8, /device:TPU:0, one launch (start us, length us, event | category | flops | bytes accessed | tf_op | source)
XLA Modules:
  0.0 53.9 jit_solution(10413877373931051430)
XLA Ops:
  0.6 0.0 copy-start.6
  0.6 0.0 copy-start.4
  0.7 1.4 %collective-permute-start.2 = (bf16[1,64,1,4,128]{4,3,2,1,0:T(4,128)(2,1)}, bf16[1,64,1,4,128]{4,3,2,1,0:T(4,128)(2,1)S(1)}, u32[]{:S(2)}, u32[]{:S(2)}) collective-permute-start(bf16[1,64,1,4,128]{4,3,2,1,0:T(4,128)(2,1)} %param.7), channel_id=1, source_target_pairs={{4,0},{8,4},{12,8},{16,12},{20,16},{24,20},{28,24},{5,1},{9,5},{13... | collective-permute-start | bytes 196616 | tf_op jit(solution)/shard_map/ppermute | solution.py:17
  2.1 1.3 %collective-permute-start.1 = (bf16[1,4,4,16,512]{4,3,2,1,0:T(8,128)(2,1)}, bf16[1,4,4,16,512]{4,3,2,1,0:T(8,128)(2,1)S(1)}, u32[]{:S(2)}, u32[]{:S(2)}) collective-permute-start(bf16[1,4,4,16,512]{4,3,2,1,0:T(8,128)(2,1)} %vo_ref.1), channel_id=1, source_target_pairs={{4,0},{8,4},{12,8},{16,12},{20,16},{24,20},{28,24},{5,1},{9,5},{13... | collective-permute-start | bytes 786440 | tf_op jit(solution)/shard_map/ppermute | solution.py:17
  3.4 0.9 %slice.52 = bf16[1,4,3,16,512]{4,3,2,1,0:T(8,128)(2,1)S(1)} slice(bf16[1,4,4,16,512]{4,3,2,1,0:T(8,128)(2,1)} %vo_ref.1), slice={[0:1], [0:4], [1:4], [0:16], [0:512]} | slice | bytes 393216 | tf_op jit(solution)/shard_map/slice | solution.py:205
  4.3 3.7 %collective-permute-start = (bf16[1,4,3,16,512]{4,3,2,1,0:T(8,128)(2,1)S(1)}, bf16[1,4,3,16,512]{4,3,2,1,0:T(8,128)(2,1)S(1)}, u32[]{:S(2)}, u32[]{:S(2)}) collective-permute-start(bf16[1,4,3,16,512]{4,3,2,1,0:T(8,128)(2,1)S(1)} %slice.52), channel_id=1, source_target_pairs={{0,4},{4,8},{8,12},{12,16},{16,20},{20,24},{24,28},{1,5},{5,9},{9,... | collective-permute-start | bytes 589832 | tf_op jit(solution)/shard_map/ppermute | solution.py:17
  8.0 0.0 copy-done.6
  8.1 0.0 copy-done.4
  8.2 0.1 pad_maximum_fusion.4
  8.3 0.1 maximum_bitcast_fusion.2
  8.4 0.1 maximum_bitcast_fusion.1
  8.4 0.1 pad_maximum_fusion.2
  8.6 0.1 copy.21
  8.7 0.1 reshape.92
  8.8 0.7 %copy.24.k1_ref = bf16[64,288]{1,0:T(8,128)(2,1)} copy(bf16[64,288]{0,1:T(8,128)(2,1)S(1)} %reshape.92) | data formatting | bytes 73728 | tf_op jit(solution)/shard_map/reshape | solution.py:188
  9.5 0.1 pad_maximum_fusion.1
  9.6 0.0 copy-start
  9.7 0.0 copy-start.8
  9.7 0.8 %copy.25.k2_ref = bf16[64,1152]{1,0:T(8,128)(2,1)} copy(bf16[64,1152]{0,1:T(8,128)(2,1)S(1)} %bitcast.49) | data formatting | bytes 294912 | tf_op jit(solution)/shard_map/reshape | solution.py:196
  10.5 0.0 collective-permute-done.2
  10.5 0.1 copy-done.8
  10.6 0.1 maximum_bitcast_fusion
  10.7 0.0 copy-done
  10.7 0.1 reshape.102
  10.7 0.7 %copy.34.cot_ref = bf16[2,64,512]{2,1,0:T(8,128)(2,1)} copy(bf16[2,64,512]{2,0,1:T(2,128)(2,1)S(1)} %reshape.102) | data formatting | bytes 262144 | tf_op jit(solution)/shard_map/reshape | solution.py:210
  11.4 0.0 collective-permute-done.vb_ref
  11.4 0.0 copy-start.5
  11.4 0.0 collective-permute-done.1.va_ref
  11.4 0.0 copy-start.3
  11.4 0.7 %copy-done.5 = bf16[1,4,3,16,512]{4,3,2,1,0:T(8,128)(2,1)} copy-done((bf16[1,4,3,16,512]{4,3,2,1,0:T(8,128)(2,1)}, bf16[1,4,3,16,512]{4,3,2,1,0:T(8,128)(2,1)S(1)}, u32[]{:S(2)}) %copy-start.5) | copy-done | bytes 196632
  12.1 0.1 copy-done.3
  12.2 7.7 %shard_map.75 = (bf16[64,512]{1,0:T(8,128)(2,1)}, bf16[512,256]{1,0:T(8,128)(2,1)}, f32[288,64]{1,0:T(8,128)}, f32[432,128]{1,0:T(8,128)}) custom-call(bf16[1,4,3,16,512]{4,3,2,1,0:T(8,128)(2,1)} %copy-done.5, bf16[1,4,4,16,512]{4,3,2,1,0:T(8,128)(2,1)} %vo_ref.1, bf16[1,4,4,16,512]{4,3,2,1,0:T(8,128)(2,1)} %copy-done.3, bf16[64,288]{1,0:T(8,128)(2,1)} %copy.24.k1_ref, ...), custom_call_target="tpu_custom_call" | custom-call | flops 60000000 | bytes 3000000 | tf_op jit(solution)/shard_map/pallas_call | solution.py:219
  19.9 1.1 %reshape.97 = f32[3,3,2,4,4,2,32]{6,5,4,3,2,1,0:T(2,128)S(1)} reshape(f32[288,64]{1,0:T(8,128)} %get-tuple-element.10) | data formatting | bytes 147456 | tf_op jit(solution)/shard_map/reshape | solution.py:245
  21.0 0.1 fusion.2
  21.1 0.0 copy-start.1
  21.2 0.1 reshape.98
  21.3 0.8 %copy-done.1 = f32[432,128]{1,0:T(8,128)S(1)} copy-done((f32[432,128]{1,0:T(8,128)S(1)}, f32[432,128]{1,0:T(8,128)}, u32[]{:S(2)}) %copy-start.1) | copy-done | bytes 221208
  22.1 2.6 %collective-permute-start.3 = (f32[232,128]{1,0:T(8,128)S(1)}, f32[232,128]{1,0:T(8,128)S(1)}, u32[]{:S(2)}, u32[]{:S(2)}) collective-permute-start(f32[232,128]{1,0:T(8,128)S(1)} %fusion.1), channel_id=1, source_target_pairs={{0,4},{4,0},{8,12},{12,8},{16,20},{20,16},{24,28},{28,24},{1,5},{5... | collective-permute-start | bytes 356360 | tf_op jit(solution)/shard_map/ppermute | solution.py:36
  24.7 1.0 %collective-permute-done.3 = f32[232,128]{1,0:T(8,128)S(1)} collective-permute-done((f32[232,128]{1,0:T(8,128)S(1)}, f32[232,128]{1,0:T(8,128)S(1)}, u32[]{:S(2)}, u32[]{:S(2)}) %collective-permute-start.3) | collective-permute-done | bytes 118816 | tf_op jit(solution)/shard_map/ppermute | solution.py:36
  25.7 3.1 %collective-permute-start.4 = (f32[232,128]{1,0:T(8,128)S(1)}, f32[232,128]{1,0:T(8,128)S(1)}, u32[]{:S(2)}, u32[]{:S(2)}) collective-permute-start(f32[232,128]{1,0:T(8,128)S(1)} %select_add_fusion), channel_id=1, source_target_pairs={{0,8},{4,12},{8,0},{12,4},{16,24},{20,28},{24,16},{28,20},{1,9},{5... | collective-permute-start | bytes 356360 | tf_op jit(solution)/shard_map/ppermute | solution.py:38
  28.8 3.7 %collective-permute-done.4 = f32[232,128]{1,0:T(8,128)S(1)} collective-permute-done((f32[232,128]{1,0:T(8,128)S(1)}, f32[232,128]{1,0:T(8,128)S(1)}, u32[]{:S(2)}, u32[]{:S(2)}) %collective-permute-start.4) | collective-permute-done | bytes 118816 | tf_op jit(solution)/shard_map/ppermute | solution.py:38
  32.6 3.0 %collective-permute-start.5 = (f32[232,128]{1,0:T(8,128)S(1)}, f32[232,128]{1,0:T(8,128)S(1)}, u32[]{:S(2)}, u32[]{:S(2)}) collective-permute-start(f32[232,128]{1,0:T(8,128)S(1)} %add.71), channel_id=1, source_target_pairs={{0,16},{4,20},{8,24},{12,28},{16,0},{20,4},{24,8},{28,12},{1,17},{... | collective-permute-start | bytes 356360 | tf_op jit(solution)/shard_map/ppermute | solution.py:38
  35.5 2.8 %collective-permute-done.5 = f32[232,128]{1,0:T(8,128)S(1)} collective-permute-done((f32[232,128]{1,0:T(8,128)S(1)}, f32[232,128]{1,0:T(8,128)S(1)}, u32[]{:S(2)}, u32[]{:S(2)}) %collective-permute-start.5) | collective-permute-done | bytes 118816 | tf_op jit(solution)/shard_map/ppermute | solution.py:38
  38.4 1.6 %collective-permute-start.6 = (f32[232,128]{1,0:T(8,128)S(1)}, f32[232,128]{1,0:T(8,128)S(1)}, u32[]{:S(2)}, u32[]{:S(2)}) collective-permute-start(f32[232,128]{1,0:T(8,128)S(1)} %add.72), channel_id=1, source_target_pairs={{0,1},{1,0},{2,3},{3,2},{4,5},{5,4},{6,7},{7,6},{8,9},{9,8},{10,11... | collective-permute-start | bytes 356360 | tf_op jit(solution)/shard_map/ppermute | solution.py:38
  40.0 3.3 %collective-permute-done.6 = f32[232,128]{1,0:T(8,128)S(1)} collective-permute-done((f32[232,128]{1,0:T(8,128)S(1)}, f32[232,128]{1,0:T(8,128)S(1)}, u32[]{:S(2)}, u32[]{:S(2)}) %collective-permute-start.6) | collective-permute-done | bytes 118816 | tf_op jit(solution)/shard_map/ppermute | solution.py:38
  43.3 0.0 copy-start.2
  43.3 2.7 %collective-permute-start.7 = (f32[232,128]{1,0:T(8,128)S(1)}, f32[232,128]{1,0:T(8,128)S(1)}, u32[]{:S(2)}, u32[]{:S(2)}) collective-permute-start(f32[232,128]{1,0:T(8,128)S(1)} %add.73), channel_id=1, source_target_pairs={{0,2},{1,3},{2,0},{3,1},{4,6},{5,7},{6,4},{7,5},{8,10},{9,11},{10,... | collective-permute-start | bytes 356360 | tf_op jit(solution)/shard_map/ppermute | solution.py:38
  46.0 4.4 %collective-permute-done.7 = f32[232,128]{1,0:T(8,128)S(1)} collective-permute-done((f32[232,128]{1,0:T(8,128)S(1)}, f32[232,128]{1,0:T(8,128)S(1)}, u32[]{:S(2)}, u32[]{:S(2)}) %collective-permute-start.7) | collective-permute-done | bytes 118816 | tf_op jit(solution)/shard_map/ppermute | solution.py:38
  50.4 0.1 collective-permute-start.8
  50.5 0.0 copy-done.2
  50.5 0.0 copy-start.7
  50.5 0.9 %copy.40 = bf16[2,8,32,256]{3,1,0,2:T(8,128)(2,1)} copy(bf16[2,8,32,256]{3,2,1,0:T(8,128)(2,1)S(1)} %bitcast.53) | data formatting | bytes 524288 | tf_op jit(solution)/shard_map/reshape | solution.py:243
  51.4 0.0 copy-done.7
  51.4 0.6 %reshape.95 = bf16[1,64,1,4,128]{4,3,1,2,0:T(4,128)(2,1)} reshape(bf16[64,512]{1,0:T(8,128)(2,1)S(1)} %copy-done.7) | data formatting | bytes 131072 | tf_op jit(solution)/shard_map/reshape | solution.py:242
  52.0 0.0 collective-permute-done.8
  52.1 0.3 reshape.100
  52.4 0.8 %copy.32 = f32[27,2,16,64]{3,2,1,0:T(8,128)} copy(f32[27,2,16,64]{3,1,2,0:T(2,128)S(1)} %bitcast.51) | data formatting | bytes 442368 | tf_op jit(solution)/shard_map/transpose | solution.py:259
  53.2 0.7 %reshape.99 = f32[3,3,3,4,32]{4,3,2,1,0:T(4,128)} reshape(f32[27,128]{1,0:T(8,128)S(1)} %slice_multiply_fusion.1) | data formatting | bytes 27648 | tf_op jit(solution)/shard_map/reshape | solution.py:258
  (22 shorter events, 0.4 us)
Async XLA Ops:
  0.6 7.4 %copy-start.6 = (bf16[32,4,3,3,3]{0,1,4,3,2:T(4,128)(2,1)S(1)}, bf16[32,4,3,3,3]{0,1,4,3,2:T(4,128)(2,1)}, u32[]{:S(2)}) copy-start(bf16[32,4,3,3,3]{0,1,4,3,2:T(4,128)(2,1)} %param.5) | copy-start | bytes 20740
  0.6 7.5 %copy-start.4 = (bf16[64,32,3,3,3]{0,1,4,3,2:T(8,128)(2,1)S(1)}, bf16[64,32,3,3,3]{0,1,4,3,2:T(8,128)(2,1)}, u32[]{:S(2)}) copy-start(bf16[64,32,3,3,3]{0,1,4,3,2:T(8,128)(2,1)} %param.6) | copy-start | bytes 331780
  0.7 9.8 %collective-permute-start.2 = (bf16[1,64,1,4,128]{4,3,2,1,0:T(4,128)(2,1)}, bf16[1,64,1,4,128]{4,3,2,1,0:T(4,128)(2,1)S(1)}, u32[]{:S(2)}, u32[]{:S(2)}) collective-permute-start(bf16[1,64,1,4,128]{4,3,2,1,0:T(4,128)(2,1)} %param.7), channel_id=1, source_target_pairs={{4,0},{8,4},{12,8},{16,12},{20,16},{24,20},{28,24},{5,1},{9,5},{13... | collective-permute-start | bytes 196616 | tf_op jit(solution)/shard_map/ppermute | solution.py:17
  2.1 9.3 %collective-permute-start.1 = (bf16[1,4,4,16,512]{4,3,2,1,0:T(8,128)(2,1)}, bf16[1,4,4,16,512]{4,3,2,1,0:T(8,128)(2,1)S(1)}, u32[]{:S(2)}, u32[]{:S(2)}) collective-permute-start(bf16[1,4,4,16,512]{4,3,2,1,0:T(8,128)(2,1)} %vo_ref.1), channel_id=1, source_target_pairs={{4,0},{8,4},{12,8},{16,12},{20,16},{24,20},{28,24},{5,1},{9,5},{13... | collective-permute-start | bytes 786440 | tf_op jit(solution)/shard_map/ppermute | solution.py:17
  4.3 7.1 %collective-permute-start = (bf16[1,4,3,16,512]{4,3,2,1,0:T(8,128)(2,1)S(1)}, bf16[1,4,3,16,512]{4,3,2,1,0:T(8,128)(2,1)S(1)}, u32[]{:S(2)}, u32[]{:S(2)}) collective-permute-start(bf16[1,4,3,16,512]{4,3,2,1,0:T(8,128)(2,1)S(1)} %slice.52), channel_id=1, source_target_pairs={{0,4},{4,8},{8,12},{12,16},{16,20},{20,24},{24,28},{1,5},{5,9},{9,... | collective-permute-start | bytes 589832 | tf_op jit(solution)/shard_map/ppermute | solution.py:17
  9.6 1.0 %copy-start = (bf16[64,3,3,2,2,32]{0,5,4,3,2,1:T(8,128)(2,1)}, bf16[64,3,3,2,2,32]{0,5,4,3,2,1:T(8,128)(2,1)S(1)}, u32[]{:S(2)}) copy-start(bf16[64,3,3,2,2,32]{0,5,4,3,2,1:T(8,128)(2,1)S(1)} %copy.22) | copy-start | bytes 442372
  9.7 0.9 %copy-start.8 = (bf16[1,64,1,4,128]{4,3,2,1,0:T(4,128)(2,1)S(1)}, bf16[1,64,1,4,128]{4,3,2,1,0:T(4,128)(2,1)}, u32[]{:S(2)}) copy-start(bf16[1,64,1,4,128]{4,3,2,1,0:T(4,128)(2,1)} %param.7) | copy-start | bytes 196612
  11.4 0.7 %copy-start.5 = (bf16[1,4,3,16,512]{4,3,2,1,0:T(8,128)(2,1)}, bf16[1,4,3,16,512]{4,3,2,1,0:T(8,128)(2,1)S(1)}, u32[]{:S(2)}) copy-start(bf16[1,4,3,16,512]{4,3,2,1,0:T(8,128)(2,1)S(1)} %collective-permute-done.vb_ref) | copy-start | bytes 589828
  11.4 0.8 %copy-start.3 = (bf16[1,4,4,16,512]{4,3,2,1,0:T(8,128)(2,1)}, bf16[1,4,4,16,512]{4,3,2,1,0:T(8,128)(2,1)S(1)}, u32[]{:S(2)}) copy-start(bf16[1,4,4,16,512]{4,3,2,1,0:T(8,128)(2,1)S(1)} %collective-permute-done.1.va_ref) | copy-start | bytes 786436
  21.1 0.9 %copy-start.1 = (f32[432,128]{1,0:T(8,128)S(1)}, f32[432,128]{1,0:T(8,128)}, u32[]{:S(2)}) copy-start(f32[432,128]{1,0:T(8,128)} %get-tuple-element.11) | copy-start | bytes 663556
  22.1 3.6 %collective-permute-start.3 = (f32[232,128]{1,0:T(8,128)S(1)}, f32[232,128]{1,0:T(8,128)S(1)}, u32[]{:S(2)}, u32[]{:S(2)}) collective-permute-start(f32[232,128]{1,0:T(8,128)S(1)} %fusion.1), channel_id=1, source_target_pairs={{0,4},{4,0},{8,12},{12,8},{16,20},{20,16},{24,28},{28,24},{1,5},{5... | collective-permute-start | bytes 356360 | tf_op jit(solution)/shard_map/ppermute | solution.py:36
  25.7 6.8 %collective-permute-start.4 = (f32[232,128]{1,0:T(8,128)S(1)}, f32[232,128]{1,0:T(8,128)S(1)}, u32[]{:S(2)}, u32[]{:S(2)}) collective-permute-start(f32[232,128]{1,0:T(8,128)S(1)} %select_add_fusion), channel_id=1, source_target_pairs={{0,8},{4,12},{8,0},{12,4},{16,24},{20,28},{24,16},{28,20},{1,9},{5... | collective-permute-start | bytes 356360 | tf_op jit(solution)/shard_map/ppermute | solution.py:38
  32.6 5.8 %collective-permute-start.5 = (f32[232,128]{1,0:T(8,128)S(1)}, f32[232,128]{1,0:T(8,128)S(1)}, u32[]{:S(2)}, u32[]{:S(2)}) collective-permute-start(f32[232,128]{1,0:T(8,128)S(1)} %add.71), channel_id=1, source_target_pairs={{0,16},{4,20},{8,24},{12,28},{16,0},{20,4},{24,8},{28,12},{1,17},{... | collective-permute-start | bytes 356360 | tf_op jit(solution)/shard_map/ppermute | solution.py:38
  38.4 4.9 %collective-permute-start.6 = (f32[232,128]{1,0:T(8,128)S(1)}, f32[232,128]{1,0:T(8,128)S(1)}, u32[]{:S(2)}, u32[]{:S(2)}) collective-permute-start(f32[232,128]{1,0:T(8,128)S(1)} %add.72), channel_id=1, source_target_pairs={{0,1},{1,0},{2,3},{3,2},{4,5},{5,4},{6,7},{7,6},{8,9},{9,8},{10,11... | collective-permute-start | bytes 356360 | tf_op jit(solution)/shard_map/ppermute | solution.py:38
  43.3 7.2 %copy-start.2 = (bf16[512,256]{1,0:T(8,128)(2,1)S(1)}, bf16[512,256]{1,0:T(8,128)(2,1)}, u32[]{:S(2)}) copy-start(bf16[512,256]{1,0:T(8,128)(2,1)} %get-tuple-element.9) | copy-start | bytes 786436
  43.3 7.1 %collective-permute-start.7 = (f32[232,128]{1,0:T(8,128)S(1)}, f32[232,128]{1,0:T(8,128)S(1)}, u32[]{:S(2)}, u32[]{:S(2)}) collective-permute-start(f32[232,128]{1,0:T(8,128)S(1)} %add.73), channel_id=1, source_target_pairs={{0,2},{1,3},{2,0},{3,1},{4,6},{5,7},{6,4},{7,5},{8,10},{9,11},{10,... | collective-permute-start | bytes 356360 | tf_op jit(solution)/shard_map/ppermute | solution.py:38
  50.4 1.6 %collective-permute-start.8 = (f32[232,128]{1,0:T(8,128)S(1)}, f32[232,128]{1,0:T(8,128)S(1)}, u32[]{:S(2)}, u32[]{:S(2)}) collective-permute-start(f32[232,128]{1,0:T(8,128)S(1)} %add.74), channel_id=1, source_target_pairs={{0,4},{4,0},{8,12},{12,8},{16,20},{20,16},{24,28},{28,24},{1,5},{5... | collective-permute-start | bytes 356360 | tf_op jit(solution)/shard_map/ppermute | solution.py:39
  50.5 0.9 %copy-start.7 = (bf16[64,512]{1,0:T(8,128)(2,1)S(1)}, bf16[64,512]{1,0:T(8,128)(2,1)}, u32[]{:S(2)}) copy-start(bf16[64,512]{1,0:T(8,128)(2,1)} %get-tuple-element.8) | copy-start | bytes 196612

commit v9 on v8

--- a/solution.py
+++ b/solution.py
@@ -84,9 +84,13 @@
 
     tp[:, 0] = jnp.zeros((nzi, 2 * rows0, lanes), BF16)
     zi = 0
-    for ref in (vb_ref, vo_ref, va_ref):
-        nzp = ref.shape[2]
-        whole = jnp.dot(ref[0].reshape(c0 * nzp * ny, nx), sel_x, preferred_element_type=F32)
+    nz_own = vo_ref.shape[2]
+    for ref, nzp in ((vb_ref, vb_ref.shape[2]), (vo_ref, nz_own), (va_ref, nz_own)):
+        if ref is va_ref:
+            zmat = ref[0:c0 * nzp * ny]
+        else:
+            zmat = ref[0].reshape(c0 * nzp * ny, nx)
+        whole = jnp.dot(zmat, sel_x, preferred_element_type=F32)
         for z in range(nzp):
             ymat = jnp.concatenate([whole[(i * nzp + z) * ny:(i * nzp + z + 1) * ny] for i in range(c0)], axis=0)
             blocks = [ymat[:, r * lanes:(r + 1) * lanes] for r in range(4)]
@@ -125,7 +129,8 @@
         if tt == 0:
             lvl_ref[...] = (pre * sig).astype(BF16)
         slope = sig * (1.0 + pre * (1.0 - sig))
-        bt[tt] = (cot_ref[tt].astype(F32) * slope).astype(BF16)
+        cot_t = cot_ref[...] if tt == 0 else va_ref[va_ref.shape[0] - c1:]
+        bt[tt] = (cot_t.astype(F32) * slope).astype(BF16)
 
     dup = _nt(p2[0], jnp.concatenate([bt[0], bt[0]], axis=0))
     c2n = dup.shape[1] // 2
@@ -203,11 +208,10 @@
     assert nz == 4 and cotangent.shape[2] == 1
     q = nx // 4
     below = shifted(volume[:, :, 1:], "gz", 1)
-    above = shifted(volume, "gz", -1)
-    cot_above = shifted(cotangent, "gz", -1)
-    nzi = below.shape[2] + nz + above.shape[2]
+    cot = cotangent[0, :, 0].reshape(cotangent.shape[1], -1)
+    above = shifted(jnp.concatenate([volume[0].reshape(-1, nx), cot], 0), "gz", -1)
+    nzi = below.shape[2] + 2 * nz
     n2 = cotangent.shape[3] * cotangent.shape[4]
-    cots = jnp.concatenate([cotangent, cot_above], 2)[0].transpose(1, 0, 2, 3).reshape(2, c2, n2)
 
     k1m = _level_one_weights(kernel_one)
     k2m = _level_two_weights(kernel_two)
@@ -237,7 +241,7 @@
             vm((2 * ny1 * c1, 2 * q), BF16),
         ],
         cost_estimate=pl.CostEstimate(flops=60_000_000, transcendentals=200_000, bytes_accessed=3_000_000),
-    )(below, volume, above, k1m, k2m, k2t, cots)
+    )(below, volume, above, k1m, k2m, k2t, cot)
 
     level_two = lvl.reshape(1, c2, 1, ny2, n2 // ny2)
     grad_one = g1.reshape(2, ny1, c1, 2 * q).transpose(2, 0, 1, 3)[None]

time: 54.3 us -> 52.6 us (0.969)
  starting transfers between devices: 19.5 us -> 17.8 us
  other arithmetic: 0.84 us -> 1.78 us
  local copies, waits for them, and re-layouts: 9.68 us -> 8.81 us
    ppermute x3 -> x2, starting transfers between devices: 6.39 us -> 4.47 us  [shifted(): return lax.ppermute(block, axis, route)]
    concatenate x0 -> x1, other arithmetic: none -> 1.04 us  [per_device(): jnp.concatenate([volume[0].reshape(-1, nx), cot], 0)]
    slice x1, local copies, waits for them, and re-layouts: 0.95 us -> 0.01 us  [per_device(): below = shifted(volume[:, :, 1:], 'gz', 1)]
    unnamed x18 -> x21, local copies, waits for them, and re-layouts: 1.61 us -> 2.42 us
    reshape x2 -> x0, local copies, waits for them, and re-layouts: 0.73 us -> none  [per_device(): jnp.concatenate([cotangent, cot_above], 2)[0].transpose(1, 0, 2, 3)]
  transfers between devices with their start and end apart: 9 -> 8, of which waited for: 5 -> 5; matrix products, arithmetic and copies ran while one was open for 10% -> 7% of each run, Pallas kernels for 0% -> 0%
where the time goes in v9:
time: 52.6 us; the launch traced here: 52.3 us
  starting transfers between devices  17.8 us (34%)
  waiting for transfers between devices  15.2 us (29%)
  local copies, waits for them, and re-layouts  8.81 us (17%)
  Pallas kernels  7.71 us (15%)
  other arithmetic  1.78 us (3%)
  between operations  0.99 us (2%)
    ppermute x4, waiting for transfers between devices, _all_sum(): part = part + lax.ppermute(part, axis, [(i, i ^ k) for i in range(n)])  14.2 us
    ppermute x4, starting transfers between devices, _all_sum(): part = part + lax.ppermute(part, axis, [(i, i ^ k) for i in range(n)])  10.4 us
    pallas_call x1, Pallas kernels, per_device(): pl.pallas_call(_kernel, out_shape=(jax.ShapeDtypeStruct((c2, n2), BF16),...  7.71 us
    ppermute x2, starting transfers between devices, shifted(): return lax.ppermute(block, axis, route)  4.47 us
    ppermute x1, starting transfers between devices, _all_sum(): lax.ppermute(jnp.where(low, hi, lo), axis0, pair)  2.87 us
    unnamed x21, local copies, waits for them, and re-layouts  2.42 us
    reshape x1, local copies, waits for them, and re-layouts, per_device(): s1r = s1.reshape(3, 3, 2, c0, 4, 2, c1)  1.11 us
  transfers between devices with their start and end apart: 8, of which 5 were waited for; matrix products, arithmetic and copies ran while one was open for 7% of the time, Pallas kernels for 0%

profile of v9, /device:TPU:0, one launch (start us, length us, event | category | flops | bytes accessed | tf_op | source)
XLA Modules:
  0.0 52.3 jit_solution(11134904600334410173)
XLA Ops:
  0.6 0.9 %copy.40 = bf16[8,8,4,128]{3,1,2,0:T(8,128)(2,1)S(1)} copy(bf16[8,8,4,128]{3,2,1,0:T(4,128)(2,1)} %bitcast.68) | data formatting | bytes 131072
  1.5 0.0 copy-start.3
  1.5 0.0 copy-start.2
  1.5 1.0 %pad_maximum_fusion.1 = bf16[320,512]{1,0:T(8,128)(2,1)S(1)} fusion(bf16[64,512]{1,0:T(8,128)(2,1)S(1)} %bitcast.53, bf16[256,512]{1,0:T(8,128)(2,1)} %bitcast.51), kind=kLoop, calls=%fused_computation.2 | loop fusion | flops 655360 | bytes 655360 | tf_op jit(solution)/shard_map/concatenate | solution.py:212
  2.5 0.0 copy-done.3
  2.6 0.0 copy-start.8
  2.6 0.0 copy-start.6
  2.6 1.4 %collective-permute-start.1 = (bf16[320,512]{1,0:T(8,128)(2,1)S(1)}, bf16[320,512]{1,0:T(8,128)(2,1)S(1)}, u32[]{:S(2)}, u32[]{:S(2)}) collective-permute-start(bf16[320,512]{1,0:T(8,128)(2,1)S(1)} %pad_maximum_fusion.1), channel_id=1, source_target_pairs={{4,0},{8,4},{12,8},{16,12},{20,16},{24,20},{28,24},{5,1},{9,5},{13... | collective-permute-start | bytes 983048 | tf_op jit(solution)/shard_map/ppermute | solution.py:17
  4.0 0.0 copy-done.2
  4.0 3.0 %collective-permute-start = (bf16[1,4,3,16,512]{4,3,2,1,0:T(8,128)(2,1)S(1)}, bf16[1,4,3,16,512]{4,3,2,1,0:T(8,128)(2,1)S(1)}, u32[]{:S(2)}, u32[]{:S(2)}) collective-permute-start(bf16[1,4,3,16,512]{4,3,2,1,0:T(8,128)(2,1)S(1)} %slice.52), channel_id=1, source_target_pairs={{0,4},{4,8},{8,12},{12,16},{16,20},{20,24},{24,28},{1,5},{5,9},{9,... | collective-permute-start | bytes 589832 | tf_op jit(solution)/shard_map/ppermute | solution.py:17
  7.1 0.0 copy-done.8
  7.2 0.0 copy-done.6
  7.3 0.1 pad_maximum_fusion.5
  7.4 0.1 maximum_bitcast_fusion.1
  7.5 0.1 maximum_bitcast_fusion
  7.5 0.1 pad_maximum_fusion.3
  7.7 0.1 copy.20
  7.8 0.1 reshape.89
  7.9 0.7 %copy.22.k1_ref = bf16[64,288]{1,0:T(8,128)(2,1)} copy(bf16[64,288]{0,1:T(8,128)(2,1)S(1)} %reshape.89) | data formatting | bytes 73728 | tf_op jit(solution)/shard_map/reshape | solution.py:193
  8.6 0.1 pad_maximum_fusion.2
  8.7 0.0 copy-start
  8.7 0.8 %copy.23.k2_ref = bf16[64,1152]{1,0:T(8,128)(2,1)} copy(bf16[64,1152]{0,1:T(8,128)(2,1)S(1)} %bitcast.49) | data formatting | bytes 294912 | tf_op jit(solution)/shard_map/reshape | solution.py:201
  9.5 0.0 collective-permute-done.vb_ref
  9.5 0.0 copy-start.7
  9.5 0.0 collective-permute-done.1.va_ref
  9.6 0.0 copy-start.4
  9.6 0.0 copy-done
  9.6 0.6 %copy-done.7 = bf16[1,4,3,16,512]{4,3,2,1,0:T(8,128)(2,1)} copy-done((bf16[1,4,3,16,512]{4,3,2,1,0:T(8,128)(2,1)}, bf16[1,4,3,16,512]{4,3,2,1,0:T(8,128)(2,1)S(1)}, u32[]{:S(2)}) %copy-start.7) | copy-done | bytes 196632
  10.2 0.1 copy-done.4
  10.3 7.7 %shard_map.75 = (bf16[64,512]{1,0:T(8,128)(2,1)}, bf16[512,256]{1,0:T(8,128)(2,1)}, f32[288,64]{1,0:T(8,128)}, f32[432,128]{1,0:T(8,128)}) custom-call(bf16[1,4,3,16,512]{4,3,2,1,0:T(8,128)(2,1)} %copy-done.7, bf16[1,4,4,16,512]{4,3,2,1,0:T(8,128)(2,1)} %vo_ref.1, bf16[320,512]{1,0:T(8,128)(2,1)} %copy-done.4, bf16[64,288]{1,0:T(8,128)(2,1)} %copy.22.k1_ref, ...), custom_call_target="tpu_custom_call" | custom-call | flops 60000000 | bytes 3000000 | tf_op jit(solution)/shard_map/pallas_call | solution.py:223
  18.0 1.1 %reshape.93 = f32[3,3,2,4,4,2,32]{6,5,4,3,2,1,0:T(2,128)S(1)} reshape(f32[288,64]{1,0:T(8,128)} %get-tuple-element.10) | data formatting | bytes 147456 | tf_op jit(solution)/shard_map/reshape | solution.py:249
  19.2 0.1 fusion.2
  19.3 0.0 copy-start.1
  19.3 0.1 reshape.94
  19.4 0.8 %copy-done.1 = f32[432,128]{1,0:T(8,128)S(1)} copy-done((f32[432,128]{1,0:T(8,128)S(1)}, f32[432,128]{1,0:T(8,128)}, u32[]{:S(2)}) %copy-start.1) | copy-done | bytes 221208
  20.2 2.9 %collective-permute-start.2 = (f32[232,128]{1,0:T(8,128)S(1)}, f32[232,128]{1,0:T(8,128)S(1)}, u32[]{:S(2)}, u32[]{:S(2)}) collective-permute-start(f32[232,128]{1,0:T(8,128)S(1)} %fusion.1), channel_id=1, source_target_pairs={{0,4},{4,0},{8,12},{12,8},{16,20},{20,16},{24,28},{28,24},{1,5},{5... | collective-permute-start | bytes 356360 | tf_op jit(solution)/shard_map/ppermute | solution.py:36
  23.1 1.0 %collective-permute-done.2 = f32[232,128]{1,0:T(8,128)S(1)} collective-permute-done((f32[232,128]{1,0:T(8,128)S(1)}, f32[232,128]{1,0:T(8,128)S(1)}, u32[]{:S(2)}, u32[]{:S(2)}) %collective-permute-start.2) | collective-permute-done | bytes 118816 | tf_op jit(solution)/shard_map/ppermute | solution.py:36
  24.1 3.9 %collective-permute-start.3 = (f32[232,128]{1,0:T(8,128)S(1)}, f32[232,128]{1,0:T(8,128)S(1)}, u32[]{:S(2)}, u32[]{:S(2)}) collective-permute-start(f32[232,128]{1,0:T(8,128)S(1)} %select_add_fusion), channel_id=1, source_target_pairs={{0,8},{4,12},{8,0},{12,4},{16,24},{20,28},{24,16},{28,20},{1,9},{5... | collective-permute-start | bytes 356360 | tf_op jit(solution)/shard_map/ppermute | solution.py:38
  28.0 3.7 %collective-permute-done.3 = f32[232,128]{1,0:T(8,128)S(1)} collective-permute-done((f32[232,128]{1,0:T(8,128)S(1)}, f32[232,128]{1,0:T(8,128)S(1)}, u32[]{:S(2)}, u32[]{:S(2)}) %collective-permute-start.3) | collective-permute-done | bytes 118816 | tf_op jit(solution)/shard_map/ppermute | solution.py:38
  31.8 2.2 %collective-permute-start.4 = (f32[232,128]{1,0:T(8,128)S(1)}, f32[232,128]{1,0:T(8,128)S(1)}, u32[]{:S(2)}, u32[]{:S(2)}) collective-permute-start(f32[232,128]{1,0:T(8,128)S(1)} %add.71), channel_id=1, source_target_pairs={{0,16},{4,20},{8,24},{12,28},{16,0},{20,4},{24,8},{28,12},{1,17},{... | collective-permute-start | bytes 356360 | tf_op jit(solution)/shard_map/ppermute | solution.py:38
  34.0 2.8 %collective-permute-done.4 = f32[232,128]{1,0:T(8,128)S(1)} collective-permute-done((f32[232,128]{1,0:T(8,128)S(1)}, f32[232,128]{1,0:T(8,128)S(1)}, u32[]{:S(2)}, u32[]{:S(2)}) %collective-permute-start.4) | collective-permute-done | bytes 118816 | tf_op jit(solution)/shard_map/ppermute | solution.py:38
  36.8 1.6 %collective-permute-start.5 = (f32[232,128]{1,0:T(8,128)S(1)}, f32[232,128]{1,0:T(8,128)S(1)}, u32[]{:S(2)}, u32[]{:S(2)}) collective-permute-start(f32[232,128]{1,0:T(8,128)S(1)} %add.72), channel_id=1, source_target_pairs={{0,1},{1,0},{2,3},{3,2},{4,5},{5,4},{6,7},{7,6},{8,9},{9,8},{10,11... | collective-permute-start | bytes 356360 | tf_op jit(solution)/shard_map/ppermute | solution.py:38
  38.4 3.3 %collective-permute-done.5 = f32[232,128]{1,0:T(8,128)S(1)} collective-permute-done((f32[232,128]{1,0:T(8,128)S(1)}, f32[232,128]{1,0:T(8,128)S(1)}, u32[]{:S(2)}, u32[]{:S(2)}) %collective-permute-start.5) | collective-permute-done | bytes 118816 | tf_op jit(solution)/shard_map/ppermute | solution.py:38
  41.7 0.0 copy-start.5
  41.7 2.7 %collective-permute-start.6 = (f32[232,128]{1,0:T(8,128)S(1)}, f32[232,128]{1,0:T(8,128)S(1)}, u32[]{:S(2)}, u32[]{:S(2)}) collective-permute-start(f32[232,128]{1,0:T(8,128)S(1)} %add.73), channel_id=1, source_target_pairs={{0,2},{1,3},{2,0},{3,1},{4,6},{5,7},{6,4},{7,5},{8,10},{9,11},{10,... | collective-permute-start | bytes 356360 | tf_op jit(solution)/shard_map/ppermute | solution.py:38
  44.4 4.4 %collective-permute-done.6 = f32[232,128]{1,0:T(8,128)S(1)} collective-permute-done((f32[232,128]{1,0:T(8,128)S(1)}, f32[232,128]{1,0:T(8,128)S(1)}, u32[]{:S(2)}, u32[]{:S(2)}) %collective-permute-start.6) | collective-permute-done | bytes 118816 | tf_op jit(solution)/shard_map/ppermute | solution.py:38
  48.8 0.1 collective-permute-start.7
  48.9 0.0 copy-done.5
  48.9 0.0 copy-start.9
  48.9 0.9 %copy.39 = bf16[2,8,32,256]{3,1,0,2:T(8,128)(2,1)} copy(bf16[2,8,32,256]{3,2,1,0:T(8,128)(2,1)S(1)} %bitcast.56) | data formatting | bytes 524288 | tf_op jit(solution)/shard_map/reshape | solution.py:247
  49.8 0.0 copy-done.9
  49.8 0.6 %reshape.91 = bf16[1,64,1,4,128]{4,3,1,2,0:T(4,128)(2,1)} reshape(bf16[64,512]{1,0:T(8,128)(2,1)S(1)} %copy-done.9) | data formatting | bytes 131072 | tf_op jit(solution)/shard_map/reshape | solution.py:246
  50.4 0.0 collective-permute-done.7
  50.5 0.3 reshape.96
  50.8 0.8 %copy.30 = f32[27,2,16,64]{3,2,1,0:T(8,128)} copy(f32[27,2,16,64]{3,1,2,0:T(2,128)S(1)} %bitcast.52) | data formatting | bytes 442368 | tf_op jit(solution)/shard_map/transpose | solution.py:263
  51.6 0.7 %reshape.95 = f32[3,3,3,4,32]{4,3,2,1,0:T(4,128)} reshape(f32[27,128]{1,0:T(8,128)S(1)} %slice_multiply_fusion.1) | data formatting | bytes 27648 | tf_op jit(solution)/shard_map/reshape | solution.py:262
  (23 shorter events, 0.4 us)
Async XLA Ops:
  1.5 1.1 %copy-start.3 = (bf16[8,8,4,128]{3,1,2,0:T(8,128)(2,1)}, bf16[8,8,4,128]{3,1,2,0:T(8,128)(2,1)S(1)}, u32[]{:S(2)}) copy-start(bf16[8,8,4,128]{3,1,2,0:T(8,128)(2,1)S(1)} %copy.40) | copy-start | bytes 196612
  1.5 2.5 %copy-start.2 = (bf16[1,4,4,16,512]{4,3,2,1,0:T(8,128)(2,1)S(1)}, bf16[1,4,4,16,512]{4,3,2,1,0:T(8,128)(2,1)}, u32[]{:S(2)}) copy-start(bf16[1,4,4,16,512]{4,3,2,1,0:T(8,128)(2,1)} %vo_ref.1) | copy-start | bytes 786436
  2.6 4.5 %copy-start.8 = (bf16[32,4,3,3,3]{0,1,4,3,2:T(4,128)(2,1)S(1)}, bf16[32,4,3,3,3]{0,1,4,3,2:T(4,128)(2,1)}, u32[]{:S(2)}) copy-start(bf16[32,4,3,3,3]{0,1,4,3,2:T(4,128)(2,1)} %param.5) | copy-start | bytes 20740
  2.6 4.6 %copy-start.6 = (bf16[64,32,3,3,3]{0,1,4,3,2:T(8,128)(2,1)S(1)}, bf16[64,32,3,3,3]{0,1,4,3,2:T(8,128)(2,1)}, u32[]{:S(2)}) copy-start(bf16[64,32,3,3,3]{0,1,4,3,2:T(8,128)(2,1)} %param.6) | copy-start | bytes 331780
  2.6 7.0 %collective-permute-start.1 = (bf16[320,512]{1,0:T(8,128)(2,1)S(1)}, bf16[320,512]{1,0:T(8,128)(2,1)S(1)}, u32[]{:S(2)}, u32[]{:S(2)}) collective-permute-start(bf16[320,512]{1,0:T(8,128)(2,1)S(1)} %pad_maximum_fusion.1), channel_id=1, source_target_pairs={{4,0},{8,4},{12,8},{16,12},{20,16},{24,20},{28,24},{5,1},{9,5},{13... | collective-permute-start | bytes 983048 | tf_op jit(solution)/shard_map/ppermute | solution.py:17
  4.0 5.5 %collective-permute-start = (bf16[1,4,3,16,512]{4,3,2,1,0:T(8,128)(2,1)S(1)}, bf16[1,4,3,16,512]{4,3,2,1,0:T(8,128)(2,1)S(1)}, u32[]{:S(2)}, u32[]{:S(2)}) collective-permute-start(bf16[1,4,3,16,512]{4,3,2,1,0:T(8,128)(2,1)S(1)} %slice.52), channel_id=1, source_target_pairs={{0,4},{4,8},{8,12},{12,16},{16,20},{20,24},{24,28},{1,5},{5,9},{9,... | collective-permute-start | bytes 589832 | tf_op jit(solution)/shard_map/ppermute | solution.py:17
  8.7 0.9 %copy-start = (bf16[64,3,3,2,2,32]{0,5,4,3,2,1:T(8,128)(2,1)}, bf16[64,3,3,2,2,32]{0,5,4,3,2,1:T(8,128)(2,1)S(1)}, u32[]{:S(2)}) copy-start(bf16[64,3,3,2,2,32]{0,5,4,3,2,1:T(8,128)(2,1)S(1)} %copy.21) | copy-start | bytes 442372
  9.5 0.7 %copy-start.7 = (bf16[1,4,3,16,512]{4,3,2,1,0:T(8,128)(2,1)}, bf16[1,4,3,16,512]{4,3,2,1,0:T(8,128)(2,1)S(1)}, u32[]{:S(2)}) copy-start(bf16[1,4,3,16,512]{4,3,2,1,0:T(8,128)(2,1)S(1)} %collective-permute-done.vb_ref) | copy-start | bytes 589828
  9.6 0.8 %copy-start.4 = (bf16[320,512]{1,0:T(8,128)(2,1)}, bf16[320,512]{1,0:T(8,128)(2,1)S(1)}, u32[]{:S(2)}) copy-start(bf16[320,512]{1,0:T(8,128)(2,1)S(1)} %collective-permute-done.1.va_ref) | copy-start | bytes 983044
  19.3 0.9 %copy-start.1 = (f32[432,128]{1,0:T(8,128)S(1)}, f32[432,128]{1,0:T(8,128)}, u32[]{:S(2)}) copy-start(f32[432,128]{1,0:T(8,128)} %get-tuple-element.11) | copy-start | bytes 663556
  20.2 3.8 %collective-permute-start.2 = (f32[232,128]{1,0:T(8,128)S(1)}, f32[232,128]{1,0:T(8,128)S(1)}, u32[]{:S(2)}, u32[]{:S(2)}) collective-permute-start(f32[232,128]{1,0:T(8,128)S(1)} %fusion.1), channel_id=1, source_target_pairs={{0,4},{4,0},{8,12},{12,8},{16,20},{20,16},{24,28},{28,24},{1,5},{5... | collective-permute-start | bytes 356360 | tf_op jit(solution)/shard_map/ppermute | solution.py:36
  24.1 7.6 %collective-permute-start.3 = (f32[232,128]{1,0:T(8,128)S(1)}, f32[232,128]{1,0:T(8,128)S(1)}, u32[]{:S(2)}, u32[]{:S(2)}) collective-permute-start(f32[232,128]{1,0:T(8,128)S(1)} %select_add_fusion), channel_id=1, source_target_pairs={{0,8},{4,12},{8,0},{12,4},{16,24},{20,28},{24,16},{28,20},{1,9},{5... | collective-permute-start | bytes 356360 | tf_op jit(solution)/shard_map/ppermute | solution.py:38
  31.8 5.0 %collective-permute-start.4 = (f32[232,128]{1,0:T(8,128)S(1)}, f32[232,128]{1,0:T(8,128)S(1)}, u32[]{:S(2)}, u32[]{:S(2)}) collective-permute-start(f32[232,128]{1,0:T(8,128)S(1)} %add.71), channel_id=1, source_target_pairs={{0,16},{4,20},{8,24},{12,28},{16,0},{20,4},{24,8},{28,12},{1,17},{... | collective-permute-start | bytes 356360 | tf_op jit(solution)/shard_map/ppermute | solution.py:38
  36.8 4.9 %collective-permute-start.5 = (f32[232,128]{1,0:T(8,128)S(1)}, f32[232,128]{1,0:T(8,128)S(1)}, u32[]{:S(2)}, u32[]{:S(2)}) collective-permute-start(f32[232,128]{1,0:T(8,128)S(1)} %add.72), channel_id=1, source_target_pairs={{0,1},{1,0},{2,3},{3,2},{4,5},{5,4},{6,7},{7,6},{8,9},{9,8},{10,11... | collective-permute-start | bytes 356360 | tf_op jit(solution)/shard_map/ppermute | solution.py:38
  41.7 7.2 %copy-start.5 = (bf16[512,256]{1,0:T(8,128)(2,1)S(1)}, bf16[512,256]{1,0:T(8,128)(2,1)}, u32[]{:S(2)}) copy-start(bf16[512,256]{1,0:T(8,128)(2,1)} %get-tuple-element.9) | copy-start | bytes 786436
  41.7 7.1 %collective-permute-start.6 = (f32[232,128]{1,0:T(8,128)S(1)}, f32[232,128]{1,0:T(8,128)S(1)}, u32[]{:S(2)}, u32[]{:S(2)}) collective-permute-start(f32[232,128]{1,0:T(8,128)S(1)} %add.73), channel_id=1, source_target_pairs={{0,2},{1,3},{2,0},{3,1},{4,6},{5,7},{6,4},{7,5},{8,10},{9,11},{10,... | collective-permute-start | bytes 356360 | tf_op jit(solution)/shard_map/ppermute | solution.py:38
  48.8 1.6 %collective-permute-start.7 = (f32[232,128]{1,0:T(8,128)S(1)}, f32[232,128]{1,0:T(8,128)S(1)}, u32[]{:S(2)}, u32[]{:S(2)}) collective-permute-start(f32[232,128]{1,0:T(8,128)S(1)} %add.74), channel_id=1, source_target_pairs={{0,4},{4,0},{8,12},{12,8},{16,20},{20,16},{24,28},{28,24},{1,5},{5... | collective-permute-start | bytes 356360 | tf_op jit(solution)/shard_map/ppermute | solution.py:39
  48.9 0.9 %copy-start.9 = (bf16[64,512]{1,0:T(8,128)(2,1)S(1)}, bf16[64,512]{1,0:T(8,128)(2,1)}, u32[]{:S(2)}) copy-start(bf16[64,512]{1,0:T(8,128)(2,1)} %get-tuple-element.8) | copy-start | bytes 196612

commit v10 on v9

--- a/solution.py
+++ b/solution.py
@@ -136,6 +136,8 @@
     c2n = dup.shape[1] // 2
     qi = c1 // 4
     lane2 = lax.broadcasted_iota(jnp.int32, (qi, 2 * c2n), 1)
+    n_s2 = 27 * qi
+    s2_ref[n_s2:] = jnp.zeros((s2_ref.shape[0] - n_s2, s2_ref.shape[1]), F32)
     for dh in range(9):
         for w, off in enumerate((3 * c1 // 2, 0, c1 // 2)):
             r0 = dh * c2 + off
@@ -174,7 +176,9 @@
             blk = gb[:, y1 * lanes:(y1 + 1) * lanes]
             r0 = (a_ * ny1 + y1) * half
             g1s[r0:r0 + half] = jnp.concatenate([blk[:half], blk[half:]], axis=1)
-    s1_ref[...] = _nt(p1[1], b1[0]) + _nt(p1[2], b1[1])
+    zb = jnp.zeros(b1.shape[1:], BF16)
+    s1_ref[...] = (_nt(p1[1], jnp.concatenate([b1[0], zb], axis=0))
+                   + _nt(p1[2], jnp.concatenate([b1[1], zb], axis=0)))
 
     n2 = 2 * lanes
     row = lax.broadcasted_iota(jnp.int32, (n2, n2), 0)
@@ -219,14 +223,17 @@
 
     ny1, ny2 = ny // 2, ny // 4
     n_act = 5
+    n_s2 = 27 * c1 // 2
+    n_g1 = 27 * c0 * c1 // (2 * c2)
+    n_pay = -(-(n_s2 + n_g1) // 16) * 16
     vm = pltpu.VMEM
-    lvl, g1, s1, s2 = pl.pallas_call(
+    lvl, g1, s1, pay = pl.pallas_call(
         _kernel,
         out_shape=(
             jax.ShapeDtypeStruct((c2, n2), BF16),
             jax.ShapeDtypeStruct((2 * ny1 * c1, 2 * q), BF16),
-            jax.ShapeDtypeStruct((k1m.shape[1], k1m.shape[0]), F32),
-            jax.ShapeDtypeStruct((27 * c1 // 2, 2 * c2), F32),
+            jax.ShapeDtypeStruct((k1m.shape[1], 2 * k1m.shape[0]), F32),
+            jax.ShapeDtypeStruct((n_pay, 2 * c2), F32),
         ),
         scratch_shapes=[
             vm((nzi, ny + 1, 8 * c0, q), BF16),
@@ -246,19 +253,19 @@
     level_two = lvl.reshape(1, c2, 1, ny2, n2 // ny2)
     grad_one = g1.reshape(2, ny1, c1, 2 * q).transpose(2, 0, 1, 3)[None]
 
-    s1r = s1.reshape(3, 3, 2, c0, 4, 2, c1)
+    s1r = s1.reshape(3, 3, 2, c0, 4, 2 * 2 * c1)[..., :2 * c1].reshape(3, 3, 2, c0, 4, 2, c1)
     gk1 = jnp.stack([
         s1r[:, :, 1, :, 3, 0] + s1r[:, :, 0, :, 1, 1],
         s1r[:, :, 0, :, 0, 0] + s1r[:, :, 0, :, 2, 1],
         s1r[:, :, 0, :, 1, 0] + s1r[:, :, 0, :, 3, 1],
     ], 2)
-    rows1 = gk1.size // s2.shape[1]
-    total = _all_sum(jnp.concatenate([gk1.reshape(rows1, s2.shape[1]), s2], 0), ("gz", "sa"))
+    pay = lax.dynamic_update_slice(pay, gk1.reshape(n_g1, 2 * c2), (n_s2, 0))
+    total = _all_sum(pay, ("gz", "sa"))
     samples = volume.shape[0] * lax.axis_size("sa")
     cells_one = samples * (nz // 2) * lax.axis_size("gz") * ny1 * (nx // 2)
     cells_two = samples * cotangent.shape[2] * lax.axis_size("gz") * cotangent.shape[3] * cotangent.shape[4]
-    t1 = total[:rows1] / math.sqrt(float(cells_one))
-    t2 = total[rows1:] / math.sqrt(float(cells_two))
+    t1 = total[n_s2:n_s2 + n_g1] / math.sqrt(float(cells_one))
+    t2 = total[:n_s2] / math.sqrt(float(cells_two))
     grad_kernel_one = t1.reshape(3, 3, 3, c0, c1).transpose(4, 3, 0, 1, 2)
     t2 = t2.reshape(27, c1 // 2, 2, c2).transpose(0, 2, 1, 3).reshape(3, 3, 3, c1, c2)
     grad_kernel_two = t2.transpose(4, 3, 0, 1, 2)

time: 52.6 us -> 52.7 us (level)
  no operation moved by 1% of the time
where the time goes in v10:
time: 52.7 us; the launch traced here: 52.3 us
  starting transfers between devices  17.8 us (34%)
  waiting for transfers between devices  15.2 us (29%)
  local copies, waits for them, and re-layouts  8.91 us (17%)
  Pallas kernels  7.7 us (15%)
  other arithmetic  1.73 us (3%)
  between operations  1 us (2%)
    ppermute x4, waiting for transfers between devices, _all_sum(): part = part + lax.ppermute(part, axis, [(i, i ^ k) for i in range(n)])  14.2 us
    ppermute x4, starting transfers between devices, _all_sum(): part = part + lax.ppermute(part, axis, [(i, i ^ k) for i in range(n)])  10.4 us
    pallas_call x1, Pallas kernels, per_device(): pl.pallas_call(_kernel, out_shape=(jax.ShapeDtypeStruct((c2, n2), BF16),...  7.7 us
    ppermute x2, starting transfers between devices, shifted(): return lax.ppermute(block, axis, route)  4.47 us
    ppermute x1, starting transfers between devices, _all_sum(): lax.ppermute(jnp.where(low, hi, lo), axis0, pair)  2.87 us
    unnamed x21, local copies, waits for them, and re-layouts  2.42 us
    reshape x1, local copies, waits for them, and re-layouts, per_device(): s1.reshape(3, 3, 2, c0, 4, 2 * 2 * c1)[..., :2 * c1]  1.11 us
  transfers between devices with their start and end apart: 8, of which 5 were waited for; matrix products, arithmetic and copies ran while one was open for 7% of the time, Pallas kernels for 0%

profile of v10, /device:TPU:0, one launch (start us, length us, event | category | flops | bytes accessed | tf_op | source)
XLA Modules:
  0.0 52.3 jit_solution(12689543332923180938)
XLA Ops:
  0.6 0.9 %copy.36 = bf16[8,8,4,128]{3,1,2,0:T(8,128)(2,1)S(1)} copy(bf16[8,8,4,128]{3,2,1,0:T(4,128)(2,1)} %bitcast.71) | data formatting | bytes 131072
  1.5 0.0 copy-start.3
  1.5 0.0 copy-start.1
  1.5 1.0 %pad_maximum_fusion = bf16[320,512]{1,0:T(8,128)(2,1)S(1)} fusion(bf16[64,512]{1,0:T(8,128)(2,1)S(1)} %bitcast.55, bf16[256,512]{1,0:T(8,128)(2,1)} %bitcast.53), kind=kLoop, calls=%fused_computation | loop fusion | flops 655360 | bytes 655360 | tf_op jit(solution)/shard_map/concatenate | solution.py:216
  2.5 0.0 copy-done.3
  2.6 0.0 copy-start.8
  2.6 0.0 copy-start.6
  2.6 1.4 %collective-permute-start.1 = (bf16[320,512]{1,0:T(8,128)(2,1)S(1)}, bf16[320,512]{1,0:T(8,128)(2,1)S(1)}, u32[]{:S(2)}, u32[]{:S(2)}) collective-permute-start(bf16[320,512]{1,0:T(8,128)(2,1)S(1)} %pad_maximum_fusion), channel_id=1, source_target_pairs={{4,0},{8,4},{12,8},{16,12},{20,16},{24,20},{28,24},{5,1},{9,5},{13... | collective-permute-start | bytes 983048 | tf_op jit(solution)/shard_map/ppermute | solution.py:17
  4.0 0.0 copy-done.1
  4.0 3.0 %collective-permute-start = (bf16[1,4,3,16,512]{4,3,2,1,0:T(8,128)(2,1)S(1)}, bf16[1,4,3,16,512]{4,3,2,1,0:T(8,128)(2,1)S(1)}, u32[]{:S(2)}, u32[]{:S(2)}) collective-permute-start(bf16[1,4,3,16,512]{4,3,2,1,0:T(8,128)(2,1)S(1)} %slice.51), channel_id=1, source_target_pairs={{0,4},{4,8},{8,12},{12,16},{16,20},{20,24},{24,28},{1,5},{5,9},{9,... | collective-permute-start | bytes 589832 | tf_op jit(solution)/shard_map/ppermute | solution.py:17
  7.1 0.0 copy-done.8
  7.2 0.0 copy-done.6
  7.3 0.1 pad_maximum_fusion.4
  7.4 0.1 maximum_bitcast_fusion.1
  7.5 0.1 maximum_bitcast_fusion
  7.5 0.1 pad_maximum_fusion.2
  7.7 0.1 copy.16
  7.8 0.1 reshape.92
  7.9 0.7 %copy.18.k1_ref = bf16[64,288]{1,0:T(8,128)(2,1)} copy(bf16[64,288]{0,1:T(8,128)(2,1)S(1)} %reshape.92) | data formatting | bytes 73728 | tf_op jit(solution)/shard_map/reshape | solution.py:197
  8.6 0.1 pad_maximum_fusion.1
  8.7 0.0 copy-start
  8.7 0.8 %copy.19.k2_ref = bf16[64,1152]{1,0:T(8,128)(2,1)} copy(bf16[64,1152]{0,1:T(8,128)(2,1)S(1)} %bitcast.51) | data formatting | bytes 294912 | tf_op jit(solution)/shard_map/reshape | solution.py:205
  9.5 0.0 collective-permute-done.vb_ref
  9.5 0.0 copy-start.7
  9.5 0.0 collective-permute-done.1.va_ref
  9.6 0.0 copy-start.4
  9.6 0.0 copy-done
  9.6 0.7 %copy-done.7 = bf16[1,4,3,16,512]{4,3,2,1,0:T(8,128)(2,1)} copy-done((bf16[1,4,3,16,512]{4,3,2,1,0:T(8,128)(2,1)}, bf16[1,4,3,16,512]{4,3,2,1,0:T(8,128)(2,1)S(1)}, u32[]{:S(2)}) %copy-start.7) | copy-done | bytes 196632
  10.2 0.1 copy-done.4
  10.3 7.7 %shard_map.75 = (bf16[64,512]{1,0:T(8,128)(2,1)}, bf16[512,256]{1,0:T(8,128)(2,1)}, f32[288,128]{1,0:T(8,128)}, f32[464,128]{1,0:T(8,128)}) custom-call(bf16[1,4,3,16,512]{4,3,2,1,0:T(8,128)(2,1)} %copy-done.7, bf16[1,4,4,16,512]{4,3,2,1,0:T(8,128)(2,1)} %vo_ref.1, bf16[320,512]{1,0:T(8,128)(2,1)} %copy-done.4, bf16[64,288]{1,0:T(8,128)(2,1)} %copy.18.k1_ref, ...), custom_call_target="tpu_custom_call" | custom-call | flops 60000000 | bytes 3000000 | tf_op jit(solution)/shard_map/pallas_call | solution.py:230
  18.0 1.1 %reshape.97 = f32[3,3,2,4,4,2,32]{6,5,4,3,2,1,0:T(2,128)S(1)} reshape(f32[3,3,2,4,4,64]{5,4,3,2,1,0:T(4,128)} %bitcast.62) | data formatting | bytes 147456 | tf_op jit(solution)/shard_map/reshape | solution.py:256
  19.2 0.1 fusion
  19.3 0.0 copy-start.2
  19.3 0.1 reshape.98
  19.4 0.8 %copy-done.2 = f32[464,128]{1,0:T(8,128)S(1)} copy-done((f32[464,128]{1,0:T(8,128)S(1)}, f32[464,128]{1,0:T(8,128)}, u32[]{:S(2)}) %copy-start.2) | copy-done | bytes 237592
  20.2 0.1 dynamic_update_slice.3
  20.3 2.9 %collective-permute-start.2 = (f32[232,128]{1,0:T(8,128)S(1)}, f32[232,128]{1,0:T(8,128)S(1)}, u32[]{:S(2)}, u32[]{:S(2)}) collective-permute-start(f32[232,128]{1,0:T(8,128)S(1)} %slice_select_fusion), channel_id=1, source_target_pairs={{0,4},{4,0},{8,12},{12,8},{16,20},{20,16},{24,28},{28,24},{1,5},{5... | collective-permute-start | bytes 356360 | tf_op jit(solution)/shard_map/ppermute | solution.py:36
  23.2 1.0 %collective-permute-done.2 = f32[232,128]{1,0:T(8,128)S(1)} collective-permute-done((f32[232,128]{1,0:T(8,128)S(1)}, f32[232,128]{1,0:T(8,128)S(1)}, u32[]{:S(2)}, u32[]{:S(2)}) %collective-permute-start.2) | collective-permute-done | bytes 118816 | tf_op jit(solution)/shard_map/ppermute | solution.py:36
  24.2 3.9 %collective-permute-start.3 = (f32[232,128]{1,0:T(8,128)S(1)}, f32[232,128]{1,0:T(8,128)S(1)}, u32[]{:S(2)}, u32[]{:S(2)}) collective-permute-start(f32[232,128]{1,0:T(8,128)S(1)} %select_add_fusion), channel_id=1, source_target_pairs={{0,8},{4,12},{8,0},{12,4},{16,24},{20,28},{24,16},{28,20},{1,9},{5... | collective-permute-start | bytes 356360 | tf_op jit(solution)/shard_map/ppermute | solution.py:38
  28.1 3.7 %collective-permute-done.3 = f32[232,128]{1,0:T(8,128)S(1)} collective-permute-done((f32[232,128]{1,0:T(8,128)S(1)}, f32[232,128]{1,0:T(8,128)S(1)}, u32[]{:S(2)}, u32[]{:S(2)}) %collective-permute-start.3) | collective-permute-done | bytes 118816 | tf_op jit(solution)/shard_map/ppermute | solution.py:38
  31.8 2.2 %collective-permute-start.4 = (f32[232,128]{1,0:T(8,128)S(1)}, f32[232,128]{1,0:T(8,128)S(1)}, u32[]{:S(2)}, u32[]{:S(2)}) collective-permute-start(f32[232,128]{1,0:T(8,128)S(1)} %add.69), channel_id=1, source_target_pairs={{0,16},{4,20},{8,24},{12,28},{16,0},{20,4},{24,8},{28,12},{1,17},{... | collective-permute-start | bytes 356360 | tf_op jit(solution)/shard_map/ppermute | solution.py:38
  34.0 2.8 %collective-permute-done.4 = f32[232,128]{1,0:T(8,128)S(1)} collective-permute-done((f32[232,128]{1,0:T(8,128)S(1)}, f32[232,128]{1,0:T(8,128)S(1)}, u32[]{:S(2)}, u32[]{:S(2)}) %collective-permute-start.4) | collective-permute-done | bytes 118816 | tf_op jit(solution)/shard_map/ppermute | solution.py:38
  36.9 1.6 %collective-permute-start.5 = (f32[232,128]{1,0:T(8,128)S(1)}, f32[232,128]{1,0:T(8,128)S(1)}, u32[]{:S(2)}, u32[]{:S(2)}) collective-permute-start(f32[232,128]{1,0:T(8,128)S(1)} %add.70), channel_id=1, source_target_pairs={{0,1},{1,0},{2,3},{3,2},{4,5},{5,4},{6,7},{7,6},{8,9},{9,8},{10,11... | collective-permute-start | bytes 356360 | tf_op jit(solution)/shard_map/ppermute | solution.py:38
  38.5 3.3 %collective-permute-done.5 = f32[232,128]{1,0:T(8,128)S(1)} collective-permute-done((f32[232,128]{1,0:T(8,128)S(1)}, f32[232,128]{1,0:T(8,128)S(1)}, u32[]{:S(2)}, u32[]{:S(2)}) %collective-permute-start.5) | collective-permute-done | bytes 118816 | tf_op jit(solution)/shard_map/ppermute | solution.py:38
  41.8 0.0 copy-start.5
  41.8 2.7 %collective-permute-start.6 = (f32[232,128]{1,0:T(8,128)S(1)}, f32[232,128]{1,0:T(8,128)S(1)}, u32[]{:S(2)}, u32[]{:S(2)}) collective-permute-start(f32[232,128]{1,0:T(8,128)S(1)} %add.71), channel_id=1, source_target_pairs={{0,2},{1,3},{2,0},{3,1},{4,6},{5,7},{6,4},{7,5},{8,10},{9,11},{10,... | collective-permute-start | bytes 356360 | tf_op jit(solution)/shard_map/ppermute | solution.py:38
  44.5 4.4 %collective-permute-done.6 = f32[232,128]{1,0:T(8,128)S(1)} collective-permute-done((f32[232,128]{1,0:T(8,128)S(1)}, f32[232,128]{1,0:T(8,128)S(1)}, u32[]{:S(2)}, u32[]{:S(2)}) %collective-permute-start.6) | collective-permute-done | bytes 118816 | tf_op jit(solution)/shard_map/ppermute | solution.py:38
  48.9 0.1 collective-permute-start.7
  49.0 0.0 copy-done.5
  49.0 0.0 copy-start.9
  49.0 0.9 %copy.35 = bf16[2,8,32,256]{3,1,0,2:T(8,128)(2,1)} copy(bf16[2,8,32,256]{3,2,1,0:T(8,128)(2,1)S(1)} %bitcast.58) | data formatting | bytes 524288 | tf_op jit(solution)/shard_map/reshape | solution.py:254
  49.8 0.0 copy-done.9
  49.8 0.6 %reshape.94 = bf16[1,64,1,4,128]{4,3,1,2,0:T(4,128)(2,1)} reshape(bf16[64,512]{1,0:T(8,128)(2,1)S(1)} %copy-done.9) | data formatting | bytes 131072 | tf_op jit(solution)/shard_map/reshape | solution.py:253
  50.5 0.0 collective-permute-done.7
  50.6 0.3 reshape.100
  50.8 0.8 %copy.26 = f32[27,2,16,64]{3,2,1,0:T(8,128)} copy(f32[27,2,16,64]{3,1,2,0:T(2,128)S(1)} %bitcast.54) | data formatting | bytes 442368 | tf_op jit(solution)/shard_map/transpose | solution.py:270
  51.6 0.7 %reshape.99 = f32[3,3,3,4,32]{4,3,2,1,0:T(4,128)} reshape(f32[27,128]{1,0:T(8,128)S(1)} %slice_multiply_fusion.1) | data formatting | bytes 27648 | tf_op jit(solution)/shard_map/reshape | solution.py:269
  (22 shorter events, 0.3 us)
Async XLA Ops:
  1.5 1.1 %copy-start.3 = (bf16[8,8,4,128]{3,1,2,0:T(8,128)(2,1)}, bf16[8,8,4,128]{3,1,2,0:T(8,128)(2,1)S(1)}, u32[]{:S(2)}) copy-start(bf16[8,8,4,128]{3,1,2,0:T(8,128)(2,1)S(1)} %copy.36) | copy-start | bytes 196612
  1.5 2.5 %copy-start.1 = (bf16[1,4,4,16,512]{4,3,2,1,0:T(8,128)(2,1)S(1)}, bf16[1,4,4,16,512]{4,3,2,1,0:T(8,128)(2,1)}, u32[]{:S(2)}) copy-start(bf16[1,4,4,16,512]{4,3,2,1,0:T(8,128)(2,1)} %vo_ref.1) | copy-start | bytes 786436
  2.6 4.5 %copy-start.8 = (bf16[32,4,3,3,3]{0,1,4,3,2:T(4,128)(2,1)S(1)}, bf16[32,4,3,3,3]{0,1,4,3,2:T(4,128)(2,1)}, u32[]{:S(2)}) copy-start(bf16[32,4,3,3,3]{0,1,4,3,2:T(4,128)(2,1)} %param.5) | copy-start | bytes 20740
  2.6 4.6 %copy-start.6 = (bf16[64,32,3,3,3]{0,1,4,3,2:T(8,128)(2,1)S(1)}, bf16[64,32,3,3,3]{0,1,4,3,2:T(8,128)(2,1)}, u32[]{:S(2)}) copy-start(bf16[64,32,3,3,3]{0,1,4,3,2:T(8,128)(2,1)} %param.6) | copy-start | bytes 331780
  2.6 7.0 %collective-permute-start.1 = (bf16[320,512]{1,0:T(8,128)(2,1)S(1)}, bf16[320,512]{1,0:T(8,128)(2,1)S(1)}, u32[]{:S(2)}, u32[]{:S(2)}) collective-permute-start(bf16[320,512]{1,0:T(8,128)(2,1)S(1)} %pad_maximum_fusion), channel_id=1, source_target_pairs={{4,0},{8,4},{12,8},{16,12},{20,16},{24,20},{28,24},{5,1},{9,5},{13... | collective-permute-start | bytes 983048 | tf_op jit(solution)/shard_map/ppermute | solution.py:17
  4.0 5.5 %collective-permute-start = (bf16[1,4,3,16,512]{4,3,2,1,0:T(8,128)(2,1)S(1)}, bf16[1,4,3,16,512]{4,3,2,1,0:T(8,128)(2,1)S(1)}, u32[]{:S(2)}, u32[]{:S(2)}) collective-permute-start(bf16[1,4,3,16,512]{4,3,2,1,0:T(8,128)(2,1)S(1)} %slice.51), channel_id=1, source_target_pairs={{0,4},{4,8},{8,12},{12,16},{16,20},{20,24},{24,28},{1,5},{5,9},{9,... | collective-permute-start | bytes 589832 | tf_op jit(solution)/shard_map/ppermute | solution.py:17
  8.7 0.9 %copy-start = (bf16[64,3,3,2,2,32]{0,5,4,3,2,1:T(8,128)(2,1)}, bf16[64,3,3,2,2,32]{0,5,4,3,2,1:T(8,128)(2,1)S(1)}, u32[]{:S(2)}) copy-start(bf16[64,3,3,2,2,32]{0,5,4,3,2,1:T(8,128)(2,1)S(1)} %copy.17) | copy-start | bytes 442372
  9.5 0.7 %copy-start.7 = (bf16[1,4,3,16,512]{4,3,2,1,0:T(8,128)(2,1)}, bf16[1,4,3,16,512]{4,3,2,1,0:T(8,128)(2,1)S(1)}, u32[]{:S(2)}) copy-start(bf16[1,4,3,16,512]{4,3,2,1,0:T(8,128)(2,1)S(1)} %collective-permute-done.vb_ref) | copy-start | bytes 589828
  9.6 0.8 %copy-start.4 = (bf16[320,512]{1,0:T(8,128)(2,1)}, bf16[320,512]{1,0:T(8,128)(2,1)S(1)}, u32[]{:S(2)}) copy-start(bf16[320,512]{1,0:T(8,128)(2,1)S(1)} %collective-permute-done.1.va_ref) | copy-start | bytes 983044
  19.3 0.9 %copy-start.2 = (f32[464,128]{1,0:T(8,128)S(1)}, f32[464,128]{1,0:T(8,128)}, u32[]{:S(2)}) copy-start(f32[464,128]{1,0:T(8,128)} %get-tuple-element.10) | copy-start | bytes 712708
  20.3 3.8 %collective-permute-start.2 = (f32[232,128]{1,0:T(8,128)S(1)}, f32[232,128]{1,0:T(8,128)S(1)}, u32[]{:S(2)}, u32[]{:S(2)}) collective-permute-start(f32[232,128]{1,0:T(8,128)S(1)} %slice_select_fusion), channel_id=1, source_target_pairs={{0,4},{4,0},{8,12},{12,8},{16,20},{20,16},{24,28},{28,24},{1,5},{5... | collective-permute-start | bytes 356360 | tf_op jit(solution)/shard_map/ppermute | solution.py:36
  24.2 7.6 %collective-permute-start.3 = (f32[232,128]{1,0:T(8,128)S(1)}, f32[232,128]{1,0:T(8,128)S(1)}, u32[]{:S(2)}, u32[]{:S(2)}) collective-permute-start(f32[232,128]{1,0:T(8,128)S(1)} %select_add_fusion), channel_id=1, source_target_pairs={{0,8},{4,12},{8,0},{12,4},{16,24},{20,28},{24,16},{28,20},{1,9},{5... | collective-permute-start | bytes 356360 | tf_op jit(solution)/shard_map/ppermute | solution.py:38
  31.8 5.0 %collective-permute-start.4 = (f32[232,128]{1,0:T(8,128)S(1)}, f32[232,128]{1,0:T(8,128)S(1)}, u32[]{:S(2)}, u32[]{:S(2)}) collective-permute-start(f32[232,128]{1,0:T(8,128)S(1)} %add.69), channel_id=1, source_target_pairs={{0,16},{4,20},{8,24},{12,28},{16,0},{20,4},{24,8},{28,12},{1,17},{... | collective-permute-start | bytes 356360 | tf_op jit(solution)/shard_map/ppermute | solution.py:38
  36.9 4.9 %collective-permute-start.5 = (f32[232,128]{1,0:T(8,128)S(1)}, f32[232,128]{1,0:T(8,128)S(1)}, u32[]{:S(2)}, u32[]{:S(2)}) collective-permute-start(f32[232,128]{1,0:T(8,128)S(1)} %add.70), channel_id=1, source_target_pairs={{0,1},{1,0},{2,3},{3,2},{4,5},{5,4},{6,7},{7,6},{8,9},{9,8},{10,11... | collective-permute-start | bytes 356360 | tf_op jit(solution)/shard_map/ppermute | solution.py:38
  41.8 7.2 %copy-start.5 = (bf16[512,256]{1,0:T(8,128)(2,1)S(1)}, bf16[512,256]{1,0:T(8,128)(2,1)}, u32[]{:S(2)}) copy-start(bf16[512,256]{1,0:T(8,128)(2,1)} %get-tuple-element.9) | copy-start | bytes 786436
  41.8 7.1 %collective-permute-start.6 = (f32[232,128]{1,0:T(8,128)S(1)}, f32[232,128]{1,0:T(8,128)S(1)}, u32[]{:S(2)}, u32[]{:S(2)}) collective-permute-start(f32[232,128]{1,0:T(8,128)S(1)} %add.71), channel_id=1, source_target_pairs={{0,2},{1,3},{2,0},{3,1},{4,6},{5,7},{6,4},{7,5},{8,10},{9,11},{10,... | collective-permute-start | bytes 356360 | tf_op jit(solution)/shard_map/ppermute | solution.py:38
  48.9 1.6 %collective-permute-start.7 = (f32[232,128]{1,0:T(8,128)S(1)}, f32[232,128]{1,0:T(8,128)S(1)}, u32[]{:S(2)}, u32[]{:S(2)}) collective-permute-start(f32[232,128]{1,0:T(8,128)S(1)} %add.72), channel_id=1, source_target_pairs={{0,4},{4,0},{8,12},{12,8},{16,20},{20,16},{24,28},{28,24},{1,5},{5... | collective-permute-start | bytes 356360 | tf_op jit(solution)/shard_map/ppermute | solution.py:39
  49.0 0.9 %copy-start.9 = (bf16[64,512]{1,0:T(8,128)(2,1)S(1)}, bf16[64,512]{1,0:T(8,128)(2,1)}, u32[]{:S(2)}) copy-start(bf16[64,512]{1,0:T(8,128)(2,1)} %get-tuple-element.8) | copy-start | bytes 196612

commit v11 on v9

--- a/solution.py
+++ b/solution.py
@@ -91,7 +91,7 @@
         else:
             zmat = ref[0].reshape(c0 * nzp * ny, nx)
         whole = jnp.dot(zmat, sel_x, preferred_element_type=F32)
-        for z in range(nzp):
+        for z in range(1 if ref is vb_ref else 0, nzp):
             ymat = jnp.concatenate([whole[(i * nzp + z) * ny:(i * nzp + z + 1) * ny] for i in range(c0)], axis=0)
             blocks = [ymat[:, r * lanes:(r + 1) * lanes] for r in range(4)]
             q = jnp.concatenate(blocks + [_shift_right(b) for b in blocks], axis=0).astype(BF16)
@@ -207,10 +207,10 @@
     c2 = kernel_two.shape[0]
     assert nz == 4 and cotangent.shape[2] == 1
     q = nx // 4
-    below = shifted(volume[:, :, 1:], "gz", 1)
+    below = shifted(volume, "gz", 1)
     cot = cotangent[0, :, 0].reshape(cotangent.shape[1], -1)
     above = shifted(jnp.concatenate([volume[0].reshape(-1, nx), cot], 0), "gz", -1)
-    nzi = below.shape[2] + 2 * nz
+    nzi = below.shape[2] - 1 + 2 * nz
     n2 = cotangent.shape[3] * cotangent.shape[4]
 
     k1m = _level_one_weights(kernel_one)

time: 52.6 us -> 54.7 us (1.040)
  waiting for transfers between devices: 15.2 us -> 18.3 us
  starting transfers between devices: 17.8 us -> 16.8 us
    ppermute x4, starting transfers between devices: 10.4 us -> 7.67 us  [_all_sum(): part = part + lax.ppermute(part, axis, [(i, i ^ k) for i in range(n)])]
    ppermute x1, starting transfers between devices: 2.87 us -> 5.44 us  [_all_sum(): lax.ppermute(jnp.where(low, hi, lo), axis0, pair)]
    ppermute x2, waiting for transfers between devices: 0.01 us -> 1.78 us  [shifted(): return lax.ppermute(block, axis, route)]
    ppermute x4, waiting for transfers between devices: 14.2 us -> 15.5 us  [_all_sum(): part = part + lax.ppermute(part, axis, [(i, i ^ k) for i in range(n)])]
    ppermute x2, starting transfers between devices: 4.47 us -> 3.67 us  [shifted(): return lax.ppermute(block, axis, route)]
    unnamed x21 -> x19, local copies, waits for them, and re-layouts: 2.42 us -> 2.45 us
  transfers between devices with their start and end apart: 8 -> 8, of which waited for: 5 -> 6; matrix products, arithmetic and copies ran while one was open for 7% -> 10% of each run, Pallas kernels for 0% -> 0%
where the time goes in v11:
time: 54.7 us; the launch traced here: 54.4 us
  waiting for transfers between devices  18.3 us (33%)
  starting transfers between devices  16.8 us (31%)
  local copies, waits for them, and re-layouts  8.82 us (16%)
  Pallas kernels  7.76 us (14%)
  other arithmetic  1.74 us (3%)
  between operations  0.94 us (2%)
    ppermute x4, waiting for transfers between devices, _all_sum(): part = part + lax.ppermute(part, axis, [(i, i ^ k) for i in range(n)])  15.5 us
    pallas_call x1, Pallas kernels, per_device(): pl.pallas_call(_kernel, out_shape=(jax.ShapeDtypeStruct((c2, n2), BF16),...  7.76 us
    ppermute x4, starting transfers between devices, _all_sum(): part = part + lax.ppermute(part, axis, [(i, i ^ k) for i in range(n)])  7.67 us
    ppermute x1, starting transfers between devices, _all_sum(): lax.ppermute(jnp.where(low, hi, lo), axis0, pair)  5.44 us
    ppermute x2, starting transfers between devices, shifted(): return lax.ppermute(block, axis, route)  3.67 us
    unnamed x19, local copies, waits for them, and re-layouts  2.45 us
    ppermute x2, waiting for transfers between devices, shifted(): return lax.ppermute(block, axis, route)  1.78 us
    reshape x1, local copies, waits for them, and re-layouts, per_device(): s1r = s1.reshape(3, 3, 2, c0, 4, 2, c1)  1.11 us
  transfers between devices with their start and end apart: 8, of which 6 were waited for; matrix products, arithmetic and copies ran while one was open for 10% of the time, Pallas kernels for 0%

profile of v11, /device:TPU:0, one launch (start us, length us, event | category | flops | bytes accessed | tf_op | source)
XLA Modules:
  0.0 54.4 jit_solution(17181200049620160251)
XLA Ops:
  0.6 2.4 %collective-permute-start = (bf16[1,4,4,16,512]{4,3,2,1,0:T(8,128)(2,1)}, bf16[1,4,4,16,512]{4,3,2,1,0:T(8,128)(2,1)S(1)}, u32[]{:S(2)}, u32[]{:S(2)}) collective-permute-start(bf16[1,4,4,16,512]{4,3,2,1,0:T(8,128)(2,1)} %vo_ref.1), channel_id=1, source_target_pairs={{0,4},{4,8},{8,12},{12,16},{16,20},{20,24},{24,28},{1,5},{5,9},{9,... | collective-permute-start | bytes 786440 | tf_op jit(solution)/shard_map/ppermute | solution.py:17
  3.0 0.9 %copy.40 = bf16[8,8,4,128]{3,1,2,0:T(8,128)(2,1)S(1)} copy(bf16[8,8,4,128]{3,2,1,0:T(4,128)(2,1)} %bitcast.68) | data formatting | bytes 131072
  3.9 0.0 copy-start.2
  3.9 0.0 copy-start.7
  3.9 1.0 %pad_maximum_fusion.1 = bf16[320,512]{1,0:T(8,128)(2,1)S(1)} fusion(bf16[64,512]{1,0:T(8,128)(2,1)S(1)} %bitcast.53, bf16[256,512]{1,0:T(8,128)(2,1)} %bitcast.52), kind=kLoop, calls=%fused_computation.2 | loop fusion | flops 655360 | bytes 655360 | tf_op jit(solution)/shard_map/concatenate | solution.py:212
  4.9 0.0 copy-done.2
  4.9 1.3 %collective-permute-start.1 = (bf16[320,512]{1,0:T(8,128)(2,1)S(1)}, bf16[320,512]{1,0:T(8,128)(2,1)S(1)}, u32[]{:S(2)}, u32[]{:S(2)}) collective-permute-start(bf16[320,512]{1,0:T(8,128)(2,1)S(1)} %pad_maximum_fusion.1), channel_id=1, source_target_pairs={{4,0},{8,4},{12,8},{16,12},{20,16},{24,20},{28,24},{5,1},{9,5},{13... | collective-permute-start | bytes 983048 | tf_op jit(solution)/shard_map/ppermute | solution.py:17
  6.2 0.0 copy-done.7
  6.3 0.1 pad_maximum_fusion.5
  6.4 0.1 maximum_bitcast_fusion.1
  6.5 0.1 maximum_bitcast_fusion
  6.6 0.1 pad_maximum_fusion.3
  6.7 0.1 copy.20
  6.8 0.0 copy-start.6
  6.8 0.1 reshape.89
  7.0 0.7 %copy.22.k1_ref = bf16[64,288]{1,0:T(8,128)(2,1)} copy(bf16[64,288]{0,1:T(8,128)(2,1)S(1)} %reshape.89) | data formatting | bytes 73728 | tf_op jit(solution)/shard_map/reshape | solution.py:193
  7.7 0.1 copy-done.6
  7.8 0.1 pad_maximum_fusion.2
  7.9 0.0 copy-start
  7.9 0.8 %copy.23.k2_ref = bf16[64,1152]{1,0:T(8,128)(2,1)} copy(bf16[64,1152]{0,1:T(8,128)(2,1)S(1)} %bitcast.49) | data formatting | bytes 294912 | tf_op jit(solution)/shard_map/reshape | solution.py:201
  8.7 0.0 collective-permute-done.vb_ref
  8.7 0.0 copy-start.5
  8.7 1.8 %collective-permute-done.1.va_ref = bf16[320,512]{1,0:T(8,128)(2,1)S(1)} collective-permute-done((bf16[320,512]{1,0:T(8,128)(2,1)S(1)}, bf16[320,512]{1,0:T(8,128)(2,1)S(1)}, u32[]{:S(2)}, u32[]{:S(2)}) %collective-permute-start.1) | collective-permute-done | bytes 327712 | tf_op jit(solution)/shard_map/ppermute | solution.py:17
  10.5 0.0 copy-start.3
  10.5 0.0 copy-done
  10.5 0.0 copy-done.5
  10.5 0.7 %copy-done.3 = bf16[320,512]{1,0:T(8,128)(2,1)} copy-done((bf16[320,512]{1,0:T(8,128)(2,1)}, bf16[320,512]{1,0:T(8,128)(2,1)S(1)}, u32[]{:S(2)}) %copy-start.3) | copy-done | bytes 327704
  11.2 7.8 %shard_map.75 = (bf16[64,512]{1,0:T(8,128)(2,1)}, bf16[512,256]{1,0:T(8,128)(2,1)}, f32[288,64]{1,0:T(8,128)}, f32[432,128]{1,0:T(8,128)}) custom-call(bf16[1,4,4,16,512]{4,3,2,1,0:T(8,128)(2,1)} %copy-done.5, bf16[1,4,4,16,512]{4,3,2,1,0:T(8,128)(2,1)} %vo_ref.1, bf16[320,512]{1,0:T(8,128)(2,1)} %copy-done.3, bf16[64,288]{1,0:T(8,128)(2,1)} %copy.22.k1_ref, ...), custom_call_target="tpu_custom_call" | custom-call | flops 60000000 | bytes 3000000 | tf_op jit(solution)/shard_map/pallas_call | solution.py:223
  19.0 1.1 %reshape.93 = f32[3,3,2,4,4,2,32]{6,5,4,3,2,1,0:T(2,128)S(1)} reshape(f32[288,64]{1,0:T(8,128)} %get-tuple-element.10) | data formatting | bytes 147456 | tf_op jit(solution)/shard_map/reshape | solution.py:249
  20.1 0.1 fusion.2
  20.2 0.0 copy-start.1
  20.3 0.1 reshape.94
  20.4 0.8 %copy-done.1 = f32[432,128]{1,0:T(8,128)S(1)} copy-done((f32[432,128]{1,0:T(8,128)S(1)}, f32[432,128]{1,0:T(8,128)}, u32[]{:S(2)}) %copy-start.1) | copy-done | bytes 221208
  21.2 5.4 %collective-permute-start.2 = (f32[232,128]{1,0:T(8,128)S(1)}, f32[232,128]{1,0:T(8,128)S(1)}, u32[]{:S(2)}, u32[]{:S(2)}) collective-permute-start(f32[232,128]{1,0:T(8,128)S(1)} %fusion.1), channel_id=1, source_target_pairs={{0,4},{4,0},{8,12},{12,8},{16,20},{20,16},{24,28},{28,24},{1,5},{5... | collective-permute-start | bytes 356360 | tf_op jit(solution)/shard_map/ppermute | solution.py:36
  26.6 1.0 %collective-permute-done.2 = f32[232,128]{1,0:T(8,128)S(1)} collective-permute-done((f32[232,128]{1,0:T(8,128)S(1)}, f32[232,128]{1,0:T(8,128)S(1)}, u32[]{:S(2)}, u32[]{:S(2)}) %collective-permute-start.2) | collective-permute-done | bytes 118816 | tf_op jit(solution)/shard_map/ppermute | solution.py:36
  27.6 2.5 %collective-permute-start.3 = (f32[232,128]{1,0:T(8,128)S(1)}, f32[232,128]{1,0:T(8,128)S(1)}, u32[]{:S(2)}, u32[]{:S(2)}) collective-permute-start(f32[232,128]{1,0:T(8,128)S(1)} %select_add_fusion), channel_id=1, source_target_pairs={{0,8},{4,12},{8,0},{12,4},{16,24},{20,28},{24,16},{28,20},{1,9},{5... | collective-permute-start | bytes 356360 | tf_op jit(solution)/shard_map/ppermute | solution.py:38
  30.1 3.7 %collective-permute-done.3 = f32[232,128]{1,0:T(8,128)S(1)} collective-permute-done((f32[232,128]{1,0:T(8,128)S(1)}, f32[232,128]{1,0:T(8,128)S(1)}, u32[]{:S(2)}, u32[]{:S(2)}) %collective-permute-start.3) | collective-permute-done | bytes 118816 | tf_op jit(solution)/shard_map/ppermute | solution.py:38
  33.9 0.9 %collective-permute-start.4 = (f32[232,128]{1,0:T(8,128)S(1)}, f32[232,128]{1,0:T(8,128)S(1)}, u32[]{:S(2)}, u32[]{:S(2)}) collective-permute-start(f32[232,128]{1,0:T(8,128)S(1)} %add.71), channel_id=1, source_target_pairs={{0,16},{4,20},{8,24},{12,28},{16,0},{20,4},{24,8},{28,12},{1,17},{... | collective-permute-start | bytes 356360 | tf_op jit(solution)/shard_map/ppermute | solution.py:38
  34.8 4.1 %collective-permute-done.4 = f32[232,128]{1,0:T(8,128)S(1)} collective-permute-done((f32[232,128]{1,0:T(8,128)S(1)}, f32[232,128]{1,0:T(8,128)S(1)}, u32[]{:S(2)}, u32[]{:S(2)}) %collective-permute-start.4) | collective-permute-done | bytes 118816 | tf_op jit(solution)/shard_map/ppermute | solution.py:38
  38.9 1.6 %collective-permute-start.5 = (f32[232,128]{1,0:T(8,128)S(1)}, f32[232,128]{1,0:T(8,128)S(1)}, u32[]{:S(2)}, u32[]{:S(2)}) collective-permute-start(f32[232,128]{1,0:T(8,128)S(1)} %add.72), channel_id=1, source_target_pairs={{0,1},{1,0},{2,3},{3,2},{4,5},{5,4},{6,7},{7,6},{8,9},{9,8},{10,11... | collective-permute-start | bytes 356360 | tf_op jit(solution)/shard_map/ppermute | solution.py:38
  40.5 3.3 %collective-permute-done.5 = f32[232,128]{1,0:T(8,128)S(1)} collective-permute-done((f32[232,128]{1,0:T(8,128)S(1)}, f32[232,128]{1,0:T(8,128)S(1)}, u32[]{:S(2)}, u32[]{:S(2)}) %collective-permute-start.5) | collective-permute-done | bytes 118816 | tf_op jit(solution)/shard_map/ppermute | solution.py:38
  43.8 0.0 copy-start.4
  43.8 2.6 %collective-permute-start.6 = (f32[232,128]{1,0:T(8,128)S(1)}, f32[232,128]{1,0:T(8,128)S(1)}, u32[]{:S(2)}, u32[]{:S(2)}) collective-permute-start(f32[232,128]{1,0:T(8,128)S(1)} %add.73), channel_id=1, source_target_pairs={{0,2},{1,3},{2,0},{3,1},{4,6},{5,7},{6,4},{7,5},{8,10},{9,11},{10,... | collective-permute-start | bytes 356360 | tf_op jit(solution)/shard_map/ppermute | solution.py:38
  46.5 4.4 %collective-permute-done.6 = f32[232,128]{1,0:T(8,128)S(1)} collective-permute-done((f32[232,128]{1,0:T(8,128)S(1)}, f32[232,128]{1,0:T(8,128)S(1)}, u32[]{:S(2)}, u32[]{:S(2)}) %collective-permute-start.6) | collective-permute-done | bytes 118816 | tf_op jit(solution)/shard_map/ppermute | solution.py:38
  50.9 0.1 collective-permute-start.7
  51.0 0.0 copy-done.4
  51.0 0.0 copy-start.8
  51.0 0.9 %copy.39 = bf16[2,8,32,256]{3,1,0,2:T(8,128)(2,1)} copy(bf16[2,8,32,256]{3,2,1,0:T(8,128)(2,1)S(1)} %bitcast.56) | data formatting | bytes 524288 | tf_op jit(solution)/shard_map/reshape | solution.py:247
  51.9 0.0 copy-done.8
  51.9 0.6 %reshape.91 = bf16[1,64,1,4,128]{4,3,1,2,0:T(4,128)(2,1)} reshape(bf16[64,512]{1,0:T(8,128)(2,1)S(1)} %copy-done.8) | data formatting | bytes 131072 | tf_op jit(solution)/shard_map/reshape | solution.py:246
  52.5 0.0 collective-permute-done.7
  52.6 0.3 reshape.96
  52.9 0.8 %copy.30 = f32[27,2,16,64]{3,2,1,0:T(8,128)} copy(f32[27,2,16,64]{3,1,2,0:T(2,128)S(1)} %bitcast.51) | data formatting | bytes 442368 | tf_op jit(solution)/shard_map/transpose | solution.py:263
  53.7 0.7 %reshape.95 = f32[3,3,3,4,32]{4,3,2,1,0:T(4,128)} reshape(f32[27,128]{1,0:T(8,128)S(1)} %slice_multiply_fusion.1) | data formatting | bytes 27648 | tf_op jit(solution)/shard_map/reshape | solution.py:262
  (22 shorter events, 0.4 us)
Async XLA Ops:
  0.6 8.1 %collective-permute-start = (bf16[1,4,4,16,512]{4,3,2,1,0:T(8,128)(2,1)}, bf16[1,4,4,16,512]{4,3,2,1,0:T(8,128)(2,1)S(1)}, u32[]{:S(2)}, u32[]{:S(2)}) collective-permute-start(bf16[1,4,4,16,512]{4,3,2,1,0:T(8,128)(2,1)} %vo_ref.1), channel_id=1, source_target_pairs={{0,4},{4,8},{8,12},{12,16},{16,20},{20,24},{24,28},{1,5},{5,9},{9,... | collective-permute-start | bytes 786440 | tf_op jit(solution)/shard_map/ppermute | solution.py:17
  3.9 1.0 %copy-start.2 = (bf16[8,8,4,128]{3,1,2,0:T(8,128)(2,1)}, bf16[8,8,4,128]{3,1,2,0:T(8,128)(2,1)S(1)}, u32[]{:S(2)}) copy-start(bf16[8,8,4,128]{3,1,2,0:T(8,128)(2,1)S(1)} %copy.40) | copy-start | bytes 196612
  3.9 2.3 %copy-start.7 = (bf16[32,4,3,3,3]{0,1,4,3,2:T(4,128)(2,1)S(1)}, bf16[32,4,3,3,3]{0,1,4,3,2:T(4,128)(2,1)}, u32[]{:S(2)}) copy-start(bf16[32,4,3,3,3]{0,1,4,3,2:T(4,128)(2,1)} %param.5) | copy-start | bytes 20740
  4.9 5.6 %collective-permute-start.1 = (bf16[320,512]{1,0:T(8,128)(2,1)S(1)}, bf16[320,512]{1,0:T(8,128)(2,1)S(1)}, u32[]{:S(2)}, u32[]{:S(2)}) collective-permute-start(bf16[320,512]{1,0:T(8,128)(2,1)S(1)} %pad_maximum_fusion.1), channel_id=1, source_target_pairs={{4,0},{8,4},{12,8},{16,12},{20,16},{24,20},{28,24},{5,1},{9,5},{13... | collective-permute-start | bytes 983048 | tf_op jit(solution)/shard_map/ppermute | solution.py:17
  6.8 0.9 %copy-start.6 = (bf16[64,32,3,3,3]{0,1,4,3,2:T(8,128)(2,1)S(1)}, bf16[64,32,3,3,3]{0,1,4,3,2:T(8,128)(2,1)}, u32[]{:S(2)}) copy-start(bf16[64,32,3,3,3]{0,1,4,3,2:T(8,128)(2,1)} %param.6) | copy-start | bytes 331780
  7.9 2.6 %copy-start = (bf16[64,3,3,2,2,32]{0,5,4,3,2,1:T(8,128)(2,1)}, bf16[64,3,3,2,2,32]{0,5,4,3,2,1:T(8,128)(2,1)S(1)}, u32[]{:S(2)}) copy-start(bf16[64,3,3,2,2,32]{0,5,4,3,2,1:T(8,128)(2,1)S(1)} %copy.21) | copy-start | bytes 442372
  8.7 1.8 %copy-start.5 = (bf16[1,4,4,16,512]{4,3,2,1,0:T(8,128)(2,1)}, bf16[1,4,4,16,512]{4,3,2,1,0:T(8,128)(2,1)S(1)}, u32[]{:S(2)}) copy-start(bf16[1,4,4,16,512]{4,3,2,1,0:T(8,128)(2,1)S(1)} %collective-permute-done.vb_ref) | copy-start | bytes 786436
  10.5 0.7 %copy-start.3 = (bf16[320,512]{1,0:T(8,128)(2,1)}, bf16[320,512]{1,0:T(8,128)(2,1)S(1)}, u32[]{:S(2)}) copy-start(bf16[320,512]{1,0:T(8,128)(2,1)S(1)} %collective-permute-done.1.va_ref) | copy-start | bytes 983044
  20.2 0.9 %copy-start.1 = (f32[432,128]{1,0:T(8,128)S(1)}, f32[432,128]{1,0:T(8,128)}, u32[]{:S(2)}) copy-start(f32[432,128]{1,0:T(8,128)} %get-tuple-element.11) | copy-start | bytes 663556
  21.2 6.4 %collective-permute-start.2 = (f32[232,128]{1,0:T(8,128)S(1)}, f32[232,128]{1,0:T(8,128)S(1)}, u32[]{:S(2)}, u32[]{:S(2)}) collective-permute-start(f32[232,128]{1,0:T(8,128)S(1)} %fusion.1), channel_id=1, source_target_pairs={{0,4},{4,0},{8,12},{12,8},{16,20},{20,16},{24,28},{28,24},{1,5},{5... | collective-permute-start | bytes 356360 | tf_op jit(solution)/shard_map/ppermute | solution.py:36
  27.6 6.2 %collective-permute-start.3 = (f32[232,128]{1,0:T(8,128)S(1)}, f32[232,128]{1,0:T(8,128)S(1)}, u32[]{:S(2)}, u32[]{:S(2)}) collective-permute-start(f32[232,128]{1,0:T(8,128)S(1)} %select_add_fusion), channel_id=1, source_target_pairs={{0,8},{4,12},{8,0},{12,4},{16,24},{20,28},{24,16},{28,20},{1,9},{5... | collective-permute-start | bytes 356360 | tf_op jit(solution)/shard_map/ppermute | solution.py:38
  33.9 5.0 %collective-permute-start.4 = (f32[232,128]{1,0:T(8,128)S(1)}, f32[232,128]{1,0:T(8,128)S(1)}, u32[]{:S(2)}, u32[]{:S(2)}) collective-permute-start(f32[232,128]{1,0:T(8,128)S(1)} %add.71), channel_id=1, source_target_pairs={{0,16},{4,20},{8,24},{12,28},{16,0},{20,4},{24,8},{28,12},{1,17},{... | collective-permute-start | bytes 356360 | tf_op jit(solution)/shard_map/ppermute | solution.py:38
  38.9 4.9 %collective-permute-start.5 = (f32[232,128]{1,0:T(8,128)S(1)}, f32[232,128]{1,0:T(8,128)S(1)}, u32[]{:S(2)}, u32[]{:S(2)}) collective-permute-start(f32[232,128]{1,0:T(8,128)S(1)} %add.72), channel_id=1, source_target_pairs={{0,1},{1,0},{2,3},{3,2},{4,5},{5,4},{6,7},{7,6},{8,9},{9,8},{10,11... | collective-permute-start | bytes 356360 | tf_op jit(solution)/shard_map/ppermute | solution.py:38
  43.8 7.2 %copy-start.4 = (bf16[512,256]{1,0:T(8,128)(2,1)S(1)}, bf16[512,256]{1,0:T(8,128)(2,1)}, u32[]{:S(2)}) copy-start(bf16[512,256]{1,0:T(8,128)(2,1)} %get-tuple-element.9) | copy-start | bytes 786436
  43.8 7.1 %collective-permute-start.6 = (f32[232,128]{1,0:T(8,128)S(1)}, f32[232,128]{1,0:T(8,128)S(1)}, u32[]{:S(2)}, u32[]{:S(2)}) collective-permute-start(f32[232,128]{1,0:T(8,128)S(1)} %add.73), channel_id=1, source_target_pairs={{0,2},{1,3},{2,0},{3,1},{4,6},{5,7},{6,4},{7,5},{8,10},{9,11},{10,... | collective-permute-start | bytes 356360 | tf_op jit(solution)/shard_map/ppermute | solution.py:38
  50.9 1.6 %collective-permute-start.7 = (f32[232,128]{1,0:T(8,128)S(1)}, f32[232,128]{1,0:T(8,128)S(1)}, u32[]{:S(2)}, u32[]{:S(2)}) collective-permute-start(f32[232,128]{1,0:T(8,128)S(1)} %add.74), channel_id=1, source_target_pairs={{0,4},{4,0},{8,12},{12,8},{16,20},{20,16},{24,28},{28,24},{1,5},{5... | collective-permute-start | bytes 356360 | tf_op jit(solution)/shard_map/ppermute | solution.py:39
  51.0 0.9 %copy-start.8 = (bf16[64,512]{1,0:T(8,128)(2,1)S(1)}, bf16[64,512]{1,0:T(8,128)(2,1)}, u32[]{:S(2)}) copy-start(bf16[64,512]{1,0:T(8,128)(2,1)} %get-tuple-element.8) | copy-start | bytes 196612

commit v12 on v9

--- a/solution.py
+++ b/solution.py
@@ -61,7 +61,7 @@
 
 def _kernel(vb_ref, vo_ref, va_ref, k1_ref, k2_ref, k2t_ref, cot_ref,
             lvl_ref, g1_ref, s1_ref, s2_ref,
-            tp, p1, t2, pre1, p2, bt, gs, gacc, b1, g1s):
+            tp, p1, t2, pre1, p2, bt, gs, gacc, b1, g1s, qs):
     c0, ny, nx = vo_ref.shape[1], vo_ref.shape[3], vo_ref.shape[4]
     lanes = nx // 4
     nzi = tp.shape[0]
@@ -94,10 +94,12 @@
         for z in range(nzp):
             ymat = jnp.concatenate([whole[(i * nzp + z) * ny:(i * nzp + z + 1) * ny] for i in range(c0)], axis=0)
             blocks = [ymat[:, r * lanes:(r + 1) * lanes] for r in range(4)]
-            q = jnp.concatenate(blocks + [_shift_right(b) for b in blocks], axis=0).astype(BF16)
-            t = jnp.dot(perm, q, preferred_element_type=F32).astype(BF16)
-            tp[zi, 1:] = t.reshape(ny, 2 * rows0, lanes)
+            qs[:, zi * lanes:(zi + 1) * lanes] = jnp.concatenate(
+                blocks + [_shift_right(b) for b in blocks], axis=0).astype(BF16)
             zi += 1
+    tall = jnp.dot(perm, qs[...], preferred_element_type=F32).astype(BF16)
+    for zi in range(nzi):
+        tp[zi, 1:] = tall[:, zi * lanes:(zi + 1) * lanes].reshape(ny, 2 * rows0, lanes)
 
     for a in range(n_act):
         for d in range(3):
@@ -239,6 +241,7 @@
             vm((2, 2 * c1, ny1 * q), F32),
             vm((2, 2 * c1, ny1 * q), BF16),
             vm((2 * ny1 * c1, 2 * q), BF16),
+            vm((8 * c0 * ny, nzi * q), BF16),
         ],
         cost_estimate=pl.CostEstimate(flops=60_000_000, transcendentals=200_000, bytes_accessed=3_000_000),
     )(below, volume, above, k1m, k2m, k2t, cot)

time: 52.6 us -> 51.3 us (0.975)
  Pallas kernels: 7.71 us -> 6.35 us
    pallas_call x1, Pallas kernels: 7.71 us -> 6.35 us  [per_device(): pl.pallas_call(_kernel, out_shape=(jax.ShapeDtypeStruct((c2, n2), BF16),...]
  transfers between devices with their start and end apart: 8 -> 8, of which waited for: 5 -> 5; matrix products, arithmetic and copies ran while one was open for 7% -> 8% of each run, Pallas kernels for 0% -> 0%
where the time goes in v12:
time: 51.3 us; the launch traced here: 50.9 us
  starting transfers between devices  17.8 us (35%)
  waiting for transfers between devices  15.2 us (30%)
  local copies, waits for them, and re-layouts  8.81 us (17%)
  Pallas kernels  6.35 us (12%)
  other arithmetic  1.78 us (3%)
  between operations  0.99 us (2%)
    ppermute x4, waiting for transfers between devices, _all_sum(): part = part + lax.ppermute(part, axis, [(i, i ^ k) for i in range(n)])  14.2 us
    ppermute x4, starting transfers between devices, _all_sum(): part = part + lax.ppermute(part, axis, [(i, i ^ k) for i in range(n)])  10.4 us
    pallas_call x1, Pallas kernels, per_device(): pl.pallas_call(_kernel, out_shape=(jax.ShapeDtypeStruct((c2, n2), BF16),...  6.35 us
    ppermute x2, starting transfers between devices, shifted(): return lax.ppermute(block, axis, route)  4.47 us
    ppermute x1, starting transfers between devices, _all_sum(): lax.ppermute(jnp.where(low, hi, lo), axis0, pair)  2.88 us
    unnamed x21, local copies, waits for them, and re-layouts  2.42 us
    reshape x1, local copies, waits for them, and re-layouts, per_device(): s1r = s1.reshape(3, 3, 2, c0, 4, 2, c1)  1.11 us
    concatenate x1, other arithmetic, per_device(): jnp.concatenate([volume[0].reshape(-1, nx), cot], 0)  1.04 us
  transfers between devices with their start and end apart: 8, of which 5 were waited for; matrix products, arithmetic and copies ran while one was open for 8% of the time, Pallas kernels for 0%

profile of v12, /device:TPU:0, one launch (start us, length us, event | category | flops | bytes accessed | tf_op | source)
XLA Modules:
  0.0 50.9 jit_solution(16083209174497099591)
XLA Ops:
  0.6 0.9 %copy.40 = bf16[8,8,4,128]{3,1,2,0:T(8,128)(2,1)S(1)} copy(bf16[8,8,4,128]{3,2,1,0:T(4,128)(2,1)} %bitcast.68) | data formatting | bytes 131072
  1.5 0.0 copy-start.3
  1.5 0.0 copy-start.2
  1.5 1.0 %pad_maximum_fusion.1 = bf16[320,512]{1,0:T(8,128)(2,1)S(1)} fusion(bf16[64,512]{1,0:T(8,128)(2,1)S(1)} %bitcast.53, bf16[256,512]{1,0:T(8,128)(2,1)} %bitcast.51), kind=kLoop, calls=%fused_computation.2 | loop fusion | flops 655360 | bytes 655360 | tf_op jit(solution)/shard_map/concatenate | solution.py:214
  2.5 0.0 copy-done.3
  2.6 0.0 copy-start.8
  2.6 0.0 copy-start.6
  2.6 1.4 %collective-permute-start.1 = (bf16[320,512]{1,0:T(8,128)(2,1)S(1)}, bf16[320,512]{1,0:T(8,128)(2,1)S(1)}, u32[]{:S(2)}, u32[]{:S(2)}) collective-permute-start(bf16[320,512]{1,0:T(8,128)(2,1)S(1)} %pad_maximum_fusion.1), channel_id=1, source_target_pairs={{4,0},{8,4},{12,8},{16,12},{20,16},{24,20},{28,24},{5,1},{9,5},{13... | collective-permute-start | bytes 983048 | tf_op jit(solution)/shard_map/ppermute | solution.py:17
  4.0 0.0 copy-done.2
  4.0 3.0 %collective-permute-start = (bf16[1,4,3,16,512]{4,3,2,1,0:T(8,128)(2,1)S(1)}, bf16[1,4,3,16,512]{4,3,2,1,0:T(8,128)(2,1)S(1)}, u32[]{:S(2)}, u32[]{:S(2)}) collective-permute-start(bf16[1,4,3,16,512]{4,3,2,1,0:T(8,128)(2,1)S(1)} %slice.52), channel_id=1, source_target_pairs={{0,4},{4,8},{8,12},{12,16},{16,20},{20,24},{24,28},{1,5},{5,9},{9,... | collective-permute-start | bytes 589832 | tf_op jit(solution)/shard_map/ppermute | solution.py:17
  7.1 0.0 copy-done.8
  7.2 0.0 copy-done.6
  7.3 0.1 pad_maximum_fusion.5
  7.4 0.1 maximum_bitcast_fusion.1
  7.5 0.1 maximum_bitcast_fusion
  7.5 0.1 pad_maximum_fusion.3
  7.7 0.1 copy.20
  7.8 0.1 reshape.89
  7.9 0.7 %copy.22.k1_ref = bf16[64,288]{1,0:T(8,128)(2,1)} copy(bf16[64,288]{0,1:T(8,128)(2,1)S(1)} %reshape.89) | data formatting | bytes 73728 | tf_op jit(solution)/shard_map/reshape | solution.py:195
  8.6 0.1 pad_maximum_fusion.2
  8.7 0.0 copy-start
  8.7 0.8 %copy.23.k2_ref = bf16[64,1152]{1,0:T(8,128)(2,1)} copy(bf16[64,1152]{0,1:T(8,128)(2,1)S(1)} %bitcast.49) | data formatting | bytes 294912 | tf_op jit(solution)/shard_map/reshape | solution.py:203
  9.5 0.0 collective-permute-done.vb_ref
  9.5 0.0 copy-start.7
  9.5 0.0 collective-permute-done.1.va_ref
  9.6 0.0 copy-start.4
  9.6 0.0 copy-done
  9.6 0.6 %copy-done.7 = bf16[1,4,3,16,512]{4,3,2,1,0:T(8,128)(2,1)} copy-done((bf16[1,4,3,16,512]{4,3,2,1,0:T(8,128)(2,1)}, bf16[1,4,3,16,512]{4,3,2,1,0:T(8,128)(2,1)S(1)}, u32[]{:S(2)}) %copy-start.7) | copy-done | bytes 196632
  10.2 0.1 copy-done.4
  10.3 6.4 %shard_map.75 = (bf16[64,512]{1,0:T(8,128)(2,1)}, bf16[512,256]{1,0:T(8,128)(2,1)}, f32[288,64]{1,0:T(8,128)}, f32[432,128]{1,0:T(8,128)}) custom-call(bf16[1,4,3,16,512]{4,3,2,1,0:T(8,128)(2,1)} %copy-done.7, bf16[1,4,4,16,512]{4,3,2,1,0:T(8,128)(2,1)} %vo_ref.1, bf16[320,512]{1,0:T(8,128)(2,1)} %copy-done.4, bf16[64,288]{1,0:T(8,128)(2,1)} %copy.22.k1_ref, ...), custom_call_target="tpu_custom_call" | custom-call | flops 60000000 | bytes 3000000 | tf_op jit(solution)/shard_map/pallas_call | solution.py:225
  16.7 1.1 %reshape.93 = f32[3,3,2,4,4,2,32]{6,5,4,3,2,1,0:T(2,128)S(1)} reshape(f32[288,64]{1,0:T(8,128)} %get-tuple-element.10) | data formatting | bytes 147456 | tf_op jit(solution)/shard_map/reshape | solution.py:252
  17.8 0.1 fusion.2
  17.9 0.0 copy-start.1
  18.0 0.1 reshape.94
  18.1 0.8 %copy-done.1 = f32[432,128]{1,0:T(8,128)S(1)} copy-done((f32[432,128]{1,0:T(8,128)S(1)}, f32[432,128]{1,0:T(8,128)}, u32[]{:S(2)}) %copy-start.1) | copy-done | bytes 221208
  18.9 2.9 %collective-permute-start.2 = (f32[232,128]{1,0:T(8,128)S(1)}, f32[232,128]{1,0:T(8,128)S(1)}, u32[]{:S(2)}, u32[]{:S(2)}) collective-permute-start(f32[232,128]{1,0:T(8,128)S(1)} %fusion.1), channel_id=1, source_target_pairs={{0,4},{4,0},{8,12},{12,8},{16,20},{20,16},{24,28},{28,24},{1,5},{5... | collective-permute-start | bytes 356360 | tf_op jit(solution)/shard_map/ppermute | solution.py:36
  21.8 1.0 %collective-permute-done.2 = f32[232,128]{1,0:T(8,128)S(1)} collective-permute-done((f32[232,128]{1,0:T(8,128)S(1)}, f32[232,128]{1,0:T(8,128)S(1)}, u32[]{:S(2)}, u32[]{:S(2)}) %collective-permute-start.2) | collective-permute-done | bytes 118816 | tf_op jit(solution)/shard_map/ppermute | solution.py:36
  22.8 3.9 %collective-permute-start.3 = (f32[232,128]{1,0:T(8,128)S(1)}, f32[232,128]{1,0:T(8,128)S(1)}, u32[]{:S(2)}, u32[]{:S(2)}) collective-permute-start(f32[232,128]{1,0:T(8,128)S(1)} %select_add_fusion), channel_id=1, source_target_pairs={{0,8},{4,12},{8,0},{12,4},{16,24},{20,28},{24,16},{28,20},{1,9},{5... | collective-permute-start | bytes 356360 | tf_op jit(solution)/shard_map/ppermute | solution.py:38
  26.6 3.7 %collective-permute-done.3 = f32[232,128]{1,0:T(8,128)S(1)} collective-permute-done((f32[232,128]{1,0:T(8,128)S(1)}, f32[232,128]{1,0:T(8,128)S(1)}, u32[]{:S(2)}, u32[]{:S(2)}) %collective-permute-start.3) | collective-permute-done | bytes 118816 | tf_op jit(solution)/shard_map/ppermute | solution.py:38
  30.4 2.2 %collective-permute-start.4 = (f32[232,128]{1,0:T(8,128)S(1)}, f32[232,128]{1,0:T(8,128)S(1)}, u32[]{:S(2)}, u32[]{:S(2)}) collective-permute-start(f32[232,128]{1,0:T(8,128)S(1)} %add.71), channel_id=1, source_target_pairs={{0,16},{4,20},{8,24},{12,28},{16,0},{20,4},{24,8},{28,12},{1,17},{... | collective-permute-start | bytes 356360 | tf_op jit(solution)/shard_map/ppermute | solution.py:38
  32.6 2.8 %collective-permute-done.4 = f32[232,128]{1,0:T(8,128)S(1)} collective-permute-done((f32[232,128]{1,0:T(8,128)S(1)}, f32[232,128]{1,0:T(8,128)S(1)}, u32[]{:S(2)}, u32[]{:S(2)}) %collective-permute-start.4) | collective-permute-done | bytes 118816 | tf_op jit(solution)/shard_map/ppermute | solution.py:38
  35.4 1.6 %collective-permute-start.5 = (f32[232,128]{1,0:T(8,128)S(1)}, f32[232,128]{1,0:T(8,128)S(1)}, u32[]{:S(2)}, u32[]{:S(2)}) collective-permute-start(f32[232,128]{1,0:T(8,128)S(1)} %add.72), channel_id=1, source_target_pairs={{0,1},{1,0},{2,3},{3,2},{4,5},{5,4},{6,7},{7,6},{8,9},{9,8},{10,11... | collective-permute-start | bytes 356360 | tf_op jit(solution)/shard_map/ppermute | solution.py:38
  37.1 3.3 %collective-permute-done.5 = f32[232,128]{1,0:T(8,128)S(1)} collective-permute-done((f32[232,128]{1,0:T(8,128)S(1)}, f32[232,128]{1,0:T(8,128)S(1)}, u32[]{:S(2)}, u32[]{:S(2)}) %collective-permute-start.5) | collective-permute-done | bytes 118816 | tf_op jit(solution)/shard_map/ppermute | solution.py:38
  40.4 0.0 copy-start.5
  40.4 2.7 %collective-permute-start.6 = (f32[232,128]{1,0:T(8,128)S(1)}, f32[232,128]{1,0:T(8,128)S(1)}, u32[]{:S(2)}, u32[]{:S(2)}) collective-permute-start(f32[232,128]{1,0:T(8,128)S(1)} %add.73), channel_id=1, source_target_pairs={{0,2},{1,3},{2,0},{3,1},{4,6},{5,7},{6,4},{7,5},{8,10},{9,11},{10,... | collective-permute-start | bytes 356360 | tf_op jit(solution)/shard_map/ppermute | solution.py:38
  43.0 4.4 %collective-permute-done.6 = f32[232,128]{1,0:T(8,128)S(1)} collective-permute-done((f32[232,128]{1,0:T(8,128)S(1)}, f32[232,128]{1,0:T(8,128)S(1)}, u32[]{:S(2)}, u32[]{:S(2)}) %collective-permute-start.6) | collective-permute-done | bytes 118816 | tf_op jit(solution)/shard_map/ppermute | solution.py:38
  47.5 0.1 collective-permute-start.7
  47.5 0.0 copy-done.5
  47.6 0.0 copy-start.9
  47.6 0.9 %copy.39 = bf16[2,8,32,256]{3,1,0,2:T(8,128)(2,1)} copy(bf16[2,8,32,256]{3,2,1,0:T(8,128)(2,1)S(1)} %bitcast.56) | data formatting | bytes 524288 | tf_op jit(solution)/shard_map/reshape | solution.py:250
  48.4 0.0 copy-done.9
  48.4 0.6 %reshape.91 = bf16[1,64,1,4,128]{4,3,1,2,0:T(4,128)(2,1)} reshape(bf16[64,512]{1,0:T(8,128)(2,1)S(1)} %copy-done.9) | data formatting | bytes 131072 | tf_op jit(solution)/shard_map/reshape | solution.py:249
  49.1 0.0 collective-permute-done.7
  49.1 0.3 reshape.96
  49.4 0.8 %copy.30 = f32[27,2,16,64]{3,2,1,0:T(8,128)} copy(f32[27,2,16,64]{3,1,2,0:T(2,128)S(1)} %bitcast.52) | data formatting | bytes 442368 | tf_op jit(solution)/shard_map/transpose | solution.py:266
  50.2 0.7 %reshape.95 = f32[3,3,3,4,32]{4,3,2,1,0:T(4,128)} reshape(f32[27,128]{1,0:T(8,128)S(1)} %slice_multiply_fusion.1) | data formatting | bytes 27648 | tf_op jit(solution)/shard_map/reshape | solution.py:265
  (23 shorter events, 0.4 us)
Async XLA Ops:
  1.5 1.1 %copy-start.3 = (bf16[8,8,4,128]{3,1,2,0:T(8,128)(2,1)}, bf16[8,8,4,128]{3,1,2,0:T(8,128)(2,1)S(1)}, u32[]{:S(2)}) copy-start(bf16[8,8,4,128]{3,1,2,0:T(8,128)(2,1)S(1)} %copy.40) | copy-start | bytes 196612
  1.5 2.5 %copy-start.2 = (bf16[1,4,4,16,512]{4,3,2,1,0:T(8,128)(2,1)S(1)}, bf16[1,4,4,16,512]{4,3,2,1,0:T(8,128)(2,1)}, u32[]{:S(2)}) copy-start(bf16[1,4,4,16,512]{4,3,2,1,0:T(8,128)(2,1)} %vo_ref.1) | copy-start | bytes 786436
  2.6 4.5 %copy-start.8 = (bf16[32,4,3,3,3]{0,1,4,3,2:T(4,128)(2,1)S(1)}, bf16[32,4,3,3,3]{0,1,4,3,2:T(4,128)(2,1)}, u32[]{:S(2)}) copy-start(bf16[32,4,3,3,3]{0,1,4,3,2:T(4,128)(2,1)} %param.5) | copy-start | bytes 20740
  2.6 4.6 %copy-start.6 = (bf16[64,32,3,3,3]{0,1,4,3,2:T(8,128)(2,1)S(1)}, bf16[64,32,3,3,3]{0,1,4,3,2:T(8,128)(2,1)}, u32[]{:S(2)}) copy-start(bf16[64,32,3,3,3]{0,1,4,3,2:T(8,128)(2,1)} %param.6) | copy-start | bytes 331780
  2.6 7.0 %collective-permute-start.1 = (bf16[320,512]{1,0:T(8,128)(2,1)S(1)}, bf16[320,512]{1,0:T(8,128)(2,1)S(1)}, u32[]{:S(2)}, u32[]{:S(2)}) collective-permute-start(bf16[320,512]{1,0:T(8,128)(2,1)S(1)} %pad_maximum_fusion.1), channel_id=1, source_target_pairs={{4,0},{8,4},{12,8},{16,12},{20,16},{24,20},{28,24},{5,1},{9,5},{13... | collective-permute-start | bytes 983048 | tf_op jit(solution)/shard_map/ppermute | solution.py:17
  4.0 5.5 %collective-permute-start = (bf16[1,4,3,16,512]{4,3,2,1,0:T(8,128)(2,1)S(1)}, bf16[1,4,3,16,512]{4,3,2,1,0:T(8,128)(2,1)S(1)}, u32[]{:S(2)}, u32[]{:S(2)}) collective-permute-start(bf16[1,4,3,16,512]{4,3,2,1,0:T(8,128)(2,1)S(1)} %slice.52), channel_id=1, source_target_pairs={{0,4},{4,8},{8,12},{12,16},{16,20},{20,24},{24,28},{1,5},{5,9},{9,... | collective-permute-start | bytes 589832 | tf_op jit(solution)/shard_map/ppermute | solution.py:17
  8.7 0.9 %copy-start = (bf16[64,3,3,2,2,32]{0,5,4,3,2,1:T(8,128)(2,1)}, bf16[64,3,3,2,2,32]{0,5,4,3,2,1:T(8,128)(2,1)S(1)}, u32[]{:S(2)}) copy-start(bf16[64,3,3,2,2,32]{0,5,4,3,2,1:T(8,128)(2,1)S(1)} %copy.21) | copy-start | bytes 442372
  9.5 0.7 %copy-start.7 = (bf16[1,4,3,16,512]{4,3,2,1,0:T(8,128)(2,1)}, bf16[1,4,3,16,512]{4,3,2,1,0:T(8,128)(2,1)S(1)}, u32[]{:S(2)}) copy-start(bf16[1,4,3,16,512]{4,3,2,1,0:T(8,128)(2,1)S(1)} %collective-permute-done.vb_ref) | copy-start | bytes 589828
  9.6 0.8 %copy-start.4 = (bf16[320,512]{1,0:T(8,128)(2,1)}, bf16[320,512]{1,0:T(8,128)(2,1)S(1)}, u32[]{:S(2)}) copy-start(bf16[320,512]{1,0:T(8,128)(2,1)S(1)} %collective-permute-done.1.va_ref) | copy-start | bytes 983044
  17.9 0.9 %copy-start.1 = (f32[432,128]{1,0:T(8,128)S(1)}, f32[432,128]{1,0:T(8,128)}, u32[]{:S(2)}) copy-start(f32[432,128]{1,0:T(8,128)} %get-tuple-element.11) | copy-start | bytes 663556
  18.9 3.8 %collective-permute-start.2 = (f32[232,128]{1,0:T(8,128)S(1)}, f32[232,128]{1,0:T(8,128)S(1)}, u32[]{:S(2)}, u32[]{:S(2)}) collective-permute-start(f32[232,128]{1,0:T(8,128)S(1)} %fusion.1), channel_id=1, source_target_pairs={{0,4},{4,0},{8,12},{12,8},{16,20},{20,16},{24,28},{28,24},{1,5},{5... | collective-permute-start | bytes 356360 | tf_op jit(solution)/shard_map/ppermute | solution.py:36
  22.8 7.6 %collective-permute-start.3 = (f32[232,128]{1,0:T(8,128)S(1)}, f32[232,128]{1,0:T(8,128)S(1)}, u32[]{:S(2)}, u32[]{:S(2)}) collective-permute-start(f32[232,128]{1,0:T(8,128)S(1)} %select_add_fusion), channel_id=1, source_target_pairs={{0,8},{4,12},{8,0},{12,4},{16,24},{20,28},{24,16},{28,20},{1,9},{5... | collective-permute-start | bytes 356360 | tf_op jit(solution)/shard_map/ppermute | solution.py:38
  30.4 5.0 %collective-permute-start.4 = (f32[232,128]{1,0:T(8,128)S(1)}, f32[232,128]{1,0:T(8,128)S(1)}, u32[]{:S(2)}, u32[]{:S(2)}) collective-permute-start(f32[232,128]{1,0:T(8,128)S(1)} %add.71), channel_id=1, source_target_pairs={{0,16},{4,20},{8,24},{12,28},{16,0},{20,4},{24,8},{28,12},{1,17},{... | collective-permute-start | bytes 356360 | tf_op jit(solution)/shard_map/ppermute | solution.py:38
  35.4 4.9 %collective-permute-start.5 = (f32[232,128]{1,0:T(8,128)S(1)}, f32[232,128]{1,0:T(8,128)S(1)}, u32[]{:S(2)}, u32[]{:S(2)}) collective-permute-start(f32[232,128]{1,0:T(8,128)S(1)} %add.72), channel_id=1, source_target_pairs={{0,1},{1,0},{2,3},{3,2},{4,5},{5,4},{6,7},{7,6},{8,9},{9,8},{10,11... | collective-permute-start | bytes 356360 | tf_op jit(solution)/shard_map/ppermute | solution.py:38
  40.4 7.2 %copy-start.5 = (bf16[512,256]{1,0:T(8,128)(2,1)S(1)}, bf16[512,256]{1,0:T(8,128)(2,1)}, u32[]{:S(2)}) copy-start(bf16[512,256]{1,0:T(8,128)(2,1)} %get-tuple-element.9) | copy-start | bytes 786436
  40.4 7.1 %collective-permute-start.6 = (f32[232,128]{1,0:T(8,128)S(1)}, f32[232,128]{1,0:T(8,128)S(1)}, u32[]{:S(2)}, u32[]{:S(2)}) collective-permute-start(f32[232,128]{1,0:T(8,128)S(1)} %add.73), channel_id=1, source_target_pairs={{0,2},{1,3},{2,0},{3,1},{4,6},{5,7},{6,4},{7,5},{8,10},{9,11},{10,... | collective-permute-start | bytes 356360 | tf_op jit(solution)/shard_map/ppermute | solution.py:38
  47.5 1.6 %collective-permute-start.7 = (f32[232,128]{1,0:T(8,128)S(1)}, f32[232,128]{1,0:T(8,128)S(1)}, u32[]{:S(2)}, u32[]{:S(2)}) collective-permute-start(f32[232,128]{1,0:T(8,128)S(1)} %add.74), channel_id=1, source_target_pairs={{0,4},{4,0},{8,12},{12,8},{16,20},{20,16},{24,28},{28,24},{1,5},{5... | collective-permute-start | bytes 356360 | tf_op jit(solution)/shard_map/ppermute | solution.py:39
  47.6 0.9 %copy-start.9 = (bf16[64,512]{1,0:T(8,128)(2,1)S(1)}, bf16[64,512]{1,0:T(8,128)(2,1)}, u32[]{:S(2)}) copy-start(bf16[64,512]{1,0:T(8,128)(2,1)} %get-tuple-element.8) | copy-start | bytes 196612

commit v13 on v12

--- a/solution.py
+++ b/solution.py
@@ -65,7 +65,7 @@
     c0, ny, nx = vo_ref.shape[1], vo_ref.shape[3], vo_ref.shape[4]
     lanes = nx // 4
     nzi = tp.shape[0]
-    n_act = p1.shape[0]
+    n_act = p1.shape[1] // (vo_ref.shape[3] // 2 * vo_ref.shape[4] // 4)
     ny1 = ny // 2
     ny2 = ny1 // 2
     c2 = t2.shape[2]
@@ -104,13 +104,14 @@
     for a in range(n_act):
         for d in range(3):
             for y1 in range(ny1):
-                p1[a, d * 3 * 2 * rows0:(d + 1) * 3 * 2 * rows0, y1 * lanes:(y1 + 1) * lanes] = (
+                p1[d * 3 * 2 * rows0:(d + 1) * 3 * 2 * rows0, (a * ny1 + y1) * lanes:(a * ny1 + y1 + 1) * lanes] = (
                     tp[2 * a + d, 2 * y1:2 * y1 + 3].reshape(3 * 2 * rows0, lanes))
 
     k1 = k1_ref[...]
     t2[:, 0] = jnp.zeros((n_act, c2, lanes), BF16)
+    pre_all = jnp.dot(k1, p1[...], preferred_element_type=F32)
     for a in range(n_act):
-        pre = jnp.dot(k1, p1[a], preferred_element_type=F32)
+        pre = pre_all[:, a * ny1 * lanes:(a + 1) * ny1 * lanes]
         if a in (1, 2):
             pre1[a - 1] = pre
         act = pre * _sigmoid(pre)
@@ -121,20 +122,22 @@
     for tt in range(2):
         for d in range(3):
             for y2 in range(ny2):
-                p2[tt, d * 3 * c2:(d + 1) * 3 * c2, y2 * lanes:(y2 + 1) * lanes] = (
+                p2[d * 3 * c2:(d + 1) * 3 * c2, (tt * ny2 + y2) * lanes:(tt * ny2 + y2 + 1) * lanes] = (
                     t2[2 * tt + d, 2 * y2:2 * y2 + 3].reshape(3 * c2, lanes))
 
-    k2 = k2_ref[...]
+    pre2 = jnp.dot(k2_ref[...], p2[...], preferred_element_type=F32)
+    n2 = ny2 * lanes
     for tt in range(2):
-        pre = jnp.dot(k2, p2[tt], preferred_element_type=F32)
+        pre = pre2[:, tt * n2:(tt + 1) * n2]
         sig = _sigmoid(pre)
         if tt == 0:
             lvl_ref[...] = (pre * sig).astype(BF16)
         slope = sig * (1.0 + pre * (1.0 - sig))
         cot_t = cot_ref[...] if tt == 0 else va_ref[va_ref.shape[0] - c1:]
-        bt[tt] = (cot_t.astype(F32) * slope).astype(BF16)
-
-    dup = _nt(p2[0], jnp.concatenate([bt[0], bt[0]], axis=0))
+        bt[:, tt * n2:(tt + 1) * n2] = (cot_t.astype(F32) * slope).astype(BF16)
+
+    bt0 = bt[:, :n2]
+    dup = _nt(p2[:, :n2], jnp.concatenate([bt0, bt0], axis=0))
     c2n = dup.shape[1] // 2
     qi = c1 // 4
     lane2 = lax.broadcasted_iota(jnp.int32, (qi, 2 * c2n), 1)
@@ -145,14 +148,9 @@
                 lane2 < c2n, dup[r0:r0 + qi], dup[r0 + qi:r0 + 2 * qi])
 
     gacc[...] = jnp.zeros(gacc.shape, F32)
-    k2t = k2t_ref[...]
+    gs[...] = jnp.dot(k2t_ref[...], bt[...], preferred_element_type=F32)
     for tt in range(2):
-        if tt == 0:
-            gs[...] = jnp.dot(k2t, bt[0], preferred_element_type=F32)
-            taps_d = (1, 2)
-        else:
-            gs[0:3 * c2] = jnp.dot(k2t[0:3 * c2], bt[1], preferred_element_type=F32)
-            taps_d = (0,)
+        taps_d = (1, 2) if tt == 0 else (0,)
         for d in taps_d:
             a = 2 * tt + d
             for h in range(3):
@@ -161,7 +159,7 @@
                     if y1 < 0:
                         continue
                     r0 = (d * 3 + h) * c2
-                    blk = gs[r0:r0 + c2, y2 * lanes:(y2 + 1) * lanes]
+                    blk = gs[r0:r0 + c2, (tt * ny2 + y2) * lanes:(tt * ny2 + y2 + 1) * lanes]
                     gacc[a - 1, :, y1 * lanes:(y1 + 1) * lanes] += blk[:c1] + _shift_left(blk[c1:])
 
     half = c1 // 2
@@ -176,7 +174,7 @@
             blk = gb[:, y1 * lanes:(y1 + 1) * lanes]
             r0 = (a_ * ny1 + y1) * half
             g1s[r0:r0 + half] = jnp.concatenate([blk[:half], blk[half:]], axis=1)
-    s1_ref[...] = _nt(p1[1], b1[0]) + _nt(p1[2], b1[1])
+    s1_ref[...] = _nt(p1[:, ny1 * lanes:3 * ny1 * lanes], jnp.concatenate([b1[0], b1[1]], axis=1))
 
     n2 = 2 * lanes
     row = lax.broadcasted_iota(jnp.int32, (n2, n2), 0)
@@ -232,12 +230,12 @@
         ),
         scratch_shapes=[
             vm((nzi, ny + 1, 8 * c0, q), BF16),
-            vm((n_act, k1m.shape[1], ny1 * q), BF16),
+            vm((k1m.shape[1], n_act * ny1 * q), BF16),
             vm((n_act, ny1 + 1, 4 * c1, q), BF16),
             vm((2, 2 * c1, ny1 * q), F32),
-            vm((2, k2m.shape[1], n2), BF16),
-            vm((2, c2, n2), BF16),
-            vm((k2m.shape[1], n2), F32),
+            vm((k2m.shape[1], 2 * n2), BF16),
+            vm((c2, 2 * n2), BF16),
+            vm((k2m.shape[1], 2 * n2), F32),
             vm((2, 2 * c1, ny1 * q), F32),
             vm((2, 2 * c1, ny1 * q), BF16),
             vm((2 * ny1 * c1, 2 * q), BF16),

time: 51.3 us -> 51.3 us (level)
  no operation moved by 1% of the time
where the time goes in v13:
time: 51.3 us; the launch traced here: 50.9 us
  starting transfers between devices  17.8 us (35%)
  waiting for transfers between devices  15.2 us (30%)
  local copies, waits for them, and re-layouts  8.81 us (17%)
  Pallas kernels  6.37 us (12%)
  other arithmetic  1.78 us (3%)
  between operations  0.99 us (2%)
    ppermute x4, waiting for transfers between devices, _all_sum(): part = part + lax.ppermute(part, axis, [(i, i ^ k) for i in range(n)])  14.2 us
    ppermute x4, starting transfers between devices, _all_sum(): part = part + lax.ppermute(part, axis, [(i, i ^ k) for i in range(n)])  10.4 us
    pallas_call x1, Pallas kernels, per_device(): pl.pallas_call(_kernel, out_shape=(jax.ShapeDtypeStruct((c2, n2), BF16),...  6.37 us
    ppermute x2, starting transfers between devices, shifted(): return lax.ppermute(block, axis, route)  4.47 us
    ppermute x1, starting transfers between devices, _all_sum(): lax.ppermute(jnp.where(low, hi, lo), axis0, pair)  2.87 us
    unnamed x21, local copies, waits for them, and re-layouts  2.42 us
    reshape x1, local copies, waits for them, and re-layouts, per_device(): s1r = s1.reshape(3, 3, 2, c0, 4, 2, c1)  1.11 us
    concatenate x1, other arithmetic, per_device(): jnp.concatenate([volume[0].reshape(-1, nx), cot], 0)  1.04 us
  transfers between devices with their start and end apart: 8, of which 5 were waited for; matrix products, arithmetic and copies ran while one was open for 8% of the time, Pallas kernels for 0%

profile of v13, /device:TPU:0, one launch (start us, length us, event | category | flops | bytes accessed | tf_op | source)
XLA Modules:
  0.0 50.9 jit_solution(12406617519622873671)
XLA Ops:
  0.6 0.9 %copy.40 = bf16[8,8,4,128]{3,1,2,0:T(8,128)(2,1)S(1)} copy(bf16[8,8,4,128]{3,2,1,0:T(4,128)(2,1)} %bitcast.68) | data formatting | bytes 131072
  1.5 0.0 copy-start.3
  1.5 0.0 copy-start.2
  1.5 1.0 %pad_maximum_fusion.1 = bf16[320,512]{1,0:T(8,128)(2,1)S(1)} fusion(bf16[64,512]{1,0:T(8,128)(2,1)S(1)} %bitcast.53, bf16[256,512]{1,0:T(8,128)(2,1)} %bitcast.51), kind=kLoop, calls=%fused_computation.2 | loop fusion | flops 655360 | bytes 655360 | tf_op jit(solution)/shard_map/concatenate | solution.py:212
  2.5 0.0 copy-done.3
  2.6 0.0 copy-start.8
  2.6 0.0 copy-start.6
  2.6 1.4 %collective-permute-start.1 = (bf16[320,512]{1,0:T(8,128)(2,1)S(1)}, bf16[320,512]{1,0:T(8,128)(2,1)S(1)}, u32[]{:S(2)}, u32[]{:S(2)}) collective-permute-start(bf16[320,512]{1,0:T(8,128)(2,1)S(1)} %pad_maximum_fusion.1), channel_id=1, source_target_pairs={{4,0},{8,4},{12,8},{16,12},{20,16},{24,20},{28,24},{5,1},{9,5},{13... | collective-permute-start | bytes 983048 | tf_op jit(solution)/shard_map/ppermute | solution.py:17
  4.0 0.0 copy-done.2
  4.0 3.0 %collective-permute-start = (bf16[1,4,3,16,512]{4,3,2,1,0:T(8,128)(2,1)S(1)}, bf16[1,4,3,16,512]{4,3,2,1,0:T(8,128)(2,1)S(1)}, u32[]{:S(2)}, u32[]{:S(2)}) collective-permute-start(bf16[1,4,3,16,512]{4,3,2,1,0:T(8,128)(2,1)S(1)} %slice.52), channel_id=1, source_target_pairs={{0,4},{4,8},{8,12},{12,16},{16,20},{20,24},{24,28},{1,5},{5,9},{9,... | collective-permute-start | bytes 589832 | tf_op jit(solution)/shard_map/ppermute | solution.py:17
  7.1 0.0 copy-done.8
  7.2 0.0 copy-done.6
  7.3 0.1 pad_maximum_fusion.5
  7.4 0.1 maximum_bitcast_fusion.1
  7.5 0.1 maximum_bitcast_fusion
  7.5 0.1 pad_maximum_fusion.3
  7.7 0.1 copy.20
  7.8 0.1 reshape.89
  7.9 0.7 %copy.22.k1_ref = bf16[64,288]{1,0:T(8,128)(2,1)} copy(bf16[64,288]{0,1:T(8,128)(2,1)S(1)} %reshape.89) | data formatting | bytes 73728 | tf_op jit(solution)/shard_map/reshape | solution.py:193
  8.6 0.1 pad_maximum_fusion.2
  8.7 0.0 copy-start
  8.7 0.8 %copy.23.k2_ref = bf16[64,1152]{1,0:T(8,128)(2,1)} copy(bf16[64,1152]{0,1:T(8,128)(2,1)S(1)} %bitcast.49) | data formatting | bytes 294912 | tf_op jit(solution)/shard_map/reshape | solution.py:201
  9.5 0.0 collective-permute-done.vb_ref
  9.5 0.0 copy-start.7
  9.5 0.0 collective-permute-done.1.va_ref
  9.6 0.0 copy-start.4
  9.6 0.0 copy-done
  9.6 0.6 %copy-done.7 = bf16[1,4,3,16,512]{4,3,2,1,0:T(8,128)(2,1)} copy-done((bf16[1,4,3,16,512]{4,3,2,1,0:T(8,128)(2,1)}, bf16[1,4,3,16,512]{4,3,2,1,0:T(8,128)(2,1)S(1)}, u32[]{:S(2)}) %copy-start.7) | copy-done | bytes 196632
  10.2 0.1 copy-done.4
  10.3 6.4 %shard_map.75 = (bf16[64,512]{1,0:T(8,128)(2,1)}, bf16[512,256]{1,0:T(8,128)(2,1)}, f32[288,64]{1,0:T(8,128)}, f32[432,128]{1,0:T(8,128)}) custom-call(bf16[1,4,3,16,512]{4,3,2,1,0:T(8,128)(2,1)} %copy-done.7, bf16[1,4,4,16,512]{4,3,2,1,0:T(8,128)(2,1)} %vo_ref.1, bf16[320,512]{1,0:T(8,128)(2,1)} %copy-done.4, bf16[64,288]{1,0:T(8,128)(2,1)} %copy.22.k1_ref, ...), custom_call_target="tpu_custom_call" | custom-call | flops 60000000 | bytes 3000000 | tf_op jit(solution)/shard_map/pallas_call | solution.py:223
  16.7 1.1 %reshape.93 = f32[3,3,2,4,4,2,32]{6,5,4,3,2,1,0:T(2,128)S(1)} reshape(f32[288,64]{1,0:T(8,128)} %get-tuple-element.10) | data formatting | bytes 147456 | tf_op jit(solution)/shard_map/reshape | solution.py:250
  17.8 0.1 fusion.2
  17.9 0.0 copy-start.1
  18.0 0.1 reshape.94
  18.1 0.8 %copy-done.1 = f32[432,128]{1,0:T(8,128)S(1)} copy-done((f32[432,128]{1,0:T(8,128)S(1)}, f32[432,128]{1,0:T(8,128)}, u32[]{:S(2)}) %copy-start.1) | copy-done | bytes 221208
  18.9 2.9 %collective-permute-start.2 = (f32[232,128]{1,0:T(8,128)S(1)}, f32[232,128]{1,0:T(8,128)S(1)}, u32[]{:S(2)}, u32[]{:S(2)}) collective-permute-start(f32[232,128]{1,0:T(8,128)S(1)} %fusion.1), channel_id=1, source_target_pairs={{0,4},{4,0},{8,12},{12,8},{16,20},{20,16},{24,28},{28,24},{1,5},{5... | collective-permute-start | bytes 356360 | tf_op jit(solution)/shard_map/ppermute | solution.py:36
  21.8 1.0 %collective-permute-done.2 = f32[232,128]{1,0:T(8,128)S(1)} collective-permute-done((f32[232,128]{1,0:T(8,128)S(1)}, f32[232,128]{1,0:T(8,128)S(1)}, u32[]{:S(2)}, u32[]{:S(2)}) %collective-permute-start.2) | collective-permute-done | bytes 118816 | tf_op jit(solution)/shard_map/ppermute | solution.py:36
  22.8 3.9 %collective-permute-start.3 = (f32[232,128]{1,0:T(8,128)S(1)}, f32[232,128]{1,0:T(8,128)S(1)}, u32[]{:S(2)}, u32[]{:S(2)}) collective-permute-start(f32[232,128]{1,0:T(8,128)S(1)} %select_add_fusion), channel_id=1, source_target_pairs={{0,8},{4,12},{8,0},{12,4},{16,24},{20,28},{24,16},{28,20},{1,9},{5... | collective-permute-start | bytes 356360 | tf_op jit(solution)/shard_map/ppermute | solution.py:38
  26.7 3.7 %collective-permute-done.3 = f32[232,128]{1,0:T(8,128)S(1)} collective-permute-done((f32[232,128]{1,0:T(8,128)S(1)}, f32[232,128]{1,0:T(8,128)S(1)}, u32[]{:S(2)}, u32[]{:S(2)}) %collective-permute-start.3) | collective-permute-done | bytes 118816 | tf_op jit(solution)/shard_map/ppermute | solution.py:38
  30.4 2.2 %collective-permute-start.4 = (f32[232,128]{1,0:T(8,128)S(1)}, f32[232,128]{1,0:T(8,128)S(1)}, u32[]{:S(2)}, u32[]{:S(2)}) collective-permute-start(f32[232,128]{1,0:T(8,128)S(1)} %add.71), channel_id=1, source_target_pairs={{0,16},{4,20},{8,24},{12,28},{16,0},{20,4},{24,8},{28,12},{1,17},{... | collective-permute-start | bytes 356360 | tf_op jit(solution)/shard_map/ppermute | solution.py:38
  32.6 2.8 %collective-permute-done.4 = f32[232,128]{1,0:T(8,128)S(1)} collective-permute-done((f32[232,128]{1,0:T(8,128)S(1)}, f32[232,128]{1,0:T(8,128)S(1)}, u32[]{:S(2)}, u32[]{:S(2)}) %collective-permute-start.4) | collective-permute-done | bytes 118816 | tf_op jit(solution)/shard_map/ppermute | solution.py:38
  35.4 1.6 %collective-permute-start.5 = (f32[232,128]{1,0:T(8,128)S(1)}, f32[232,128]{1,0:T(8,128)S(1)}, u32[]{:S(2)}, u32[]{:S(2)}) collective-permute-start(f32[232,128]{1,0:T(8,128)S(1)} %add.72), channel_id=1, source_target_pairs={{0,1},{1,0},{2,3},{3,2},{4,5},{5,4},{6,7},{7,6},{8,9},{9,8},{10,11... | collective-permute-start | bytes 356360 | tf_op jit(solution)/shard_map/ppermute | solution.py:38
  37.1 3.3 %collective-permute-done.5 = f32[232,128]{1,0:T(8,128)S(1)} collective-permute-done((f32[232,128]{1,0:T(8,128)S(1)}, f32[232,128]{1,0:T(8,128)S(1)}, u32[]{:S(2)}, u32[]{:S(2)}) %collective-permute-start.5) | collective-permute-done | bytes 118816 | tf_op jit(solution)/shard_map/ppermute | solution.py:38
  40.4 0.0 copy-start.5
  40.4 2.7 %collective-permute-start.6 = (f32[232,128]{1,0:T(8,128)S(1)}, f32[232,128]{1,0:T(8,128)S(1)}, u32[]{:S(2)}, u32[]{:S(2)}) collective-permute-start(f32[232,128]{1,0:T(8,128)S(1)} %add.73), channel_id=1, source_target_pairs={{0,2},{1,3},{2,0},{3,1},{4,6},{5,7},{6,4},{7,5},{8,10},{9,11},{10,... | collective-permute-start | bytes 356360 | tf_op jit(solution)/shard_map/ppermute | solution.py:38
  43.1 4.4 %collective-permute-done.6 = f32[232,128]{1,0:T(8,128)S(1)} collective-permute-done((f32[232,128]{1,0:T(8,128)S(1)}, f32[232,128]{1,0:T(8,128)S(1)}, u32[]{:S(2)}, u32[]{:S(2)}) %collective-permute-start.6) | collective-permute-done | bytes 118816 | tf_op jit(solution)/shard_map/ppermute | solution.py:38
  47.5 0.1 collective-permute-start.7
  47.6 0.0 copy-done.5
  47.6 0.0 copy-start.9
  47.6 0.9 %copy.39 = bf16[2,8,32,256]{3,1,0,2:T(8,128)(2,1)} copy(bf16[2,8,32,256]{3,2,1,0:T(8,128)(2,1)S(1)} %bitcast.56) | data formatting | bytes 524288 | tf_op jit(solution)/shard_map/reshape | solution.py:248
  48.4 0.0 copy-done.9
  48.4 0.6 %reshape.91 = bf16[1,64,1,4,128]{4,3,1,2,0:T(4,128)(2,1)} reshape(bf16[64,512]{1,0:T(8,128)(2,1)S(1)} %copy-done.9) | data formatting | bytes 131072 | tf_op jit(solution)/shard_map/reshape | solution.py:247
  49.1 0.0 collective-permute-done.7
  49.2 0.3 reshape.96
  49.4 0.8 %copy.30 = f32[27,2,16,64]{3,2,1,0:T(8,128)} copy(f32[27,2,16,64]{3,1,2,0:T(2,128)S(1)} %bitcast.52) | data formatting | bytes 442368 | tf_op jit(solution)/shard_map/transpose | solution.py:264
  50.2 0.7 %reshape.95 = f32[3,3,3,4,32]{4,3,2,1,0:T(4,128)} reshape(f32[27,128]{1,0:T(8,128)S(1)} %slice_multiply_fusion.1) | data formatting | bytes 27648 | tf_op jit(solution)/shard_map/reshape | solution.py:263
  (23 shorter events, 0.4 us)
Async XLA Ops:
  1.5 1.1 %copy-start.3 = (bf16[8,8,4,128]{3,1,2,0:T(8,128)(2,1)}, bf16[8,8,4,128]{3,1,2,0:T(8,128)(2,1)S(1)}, u32[]{:S(2)}) copy-start(bf16[8,8,4,128]{3,1,2,0:T(8,128)(2,1)S(1)} %copy.40) | copy-start | bytes 196612
  1.5 2.5 %copy-start.2 = (bf16[1,4,4,16,512]{4,3,2,1,0:T(8,128)(2,1)S(1)}, bf16[1,4,4,16,512]{4,3,2,1,0:T(8,128)(2,1)}, u32[]{:S(2)}) copy-start(bf16[1,4,4,16,512]{4,3,2,1,0:T(8,128)(2,1)} %vo_ref.1) | copy-start | bytes 786436
  2.6 4.5 %copy-start.8 = (bf16[32,4,3,3,3]{0,1,4,3,2:T(4,128)(2,1)S(1)}, bf16[32,4,3,3,3]{0,1,4,3,2:T(4,128)(2,1)}, u32[]{:S(2)}) copy-start(bf16[32,4,3,3,3]{0,1,4,3,2:T(4,128)(2,1)} %param.5) | copy-start | bytes 20740
  2.6 4.6 %copy-start.6 = (bf16[64,32,3,3,3]{0,1,4,3,2:T(8,128)(2,1)S(1)}, bf16[64,32,3,3,3]{0,1,4,3,2:T(8,128)(2,1)}, u32[]{:S(2)}) copy-start(bf16[64,32,3,3,3]{0,1,4,3,2:T(8,128)(2,1)} %param.6) | copy-start | bytes 331780
  2.6 7.0 %collective-permute-start.1 = (bf16[320,512]{1,0:T(8,128)(2,1)S(1)}, bf16[320,512]{1,0:T(8,128)(2,1)S(1)}, u32[]{:S(2)}, u32[]{:S(2)}) collective-permute-start(bf16[320,512]{1,0:T(8,128)(2,1)S(1)} %pad_maximum_fusion.1), channel_id=1, source_target_pairs={{4,0},{8,4},{12,8},{16,12},{20,16},{24,20},{28,24},{5,1},{9,5},{13... | collective-permute-start | bytes 983048 | tf_op jit(solution)/shard_map/ppermute | solution.py:17
  4.0 5.5 %collective-permute-start = (bf16[1,4,3,16,512]{4,3,2,1,0:T(8,128)(2,1)S(1)}, bf16[1,4,3,16,512]{4,3,2,1,0:T(8,128)(2,1)S(1)}, u32[]{:S(2)}, u32[]{:S(2)}) collective-permute-start(bf16[1,4,3,16,512]{4,3,2,1,0:T(8,128)(2,1)S(1)} %slice.52), channel_id=1, source_target_pairs={{0,4},{4,8},{8,12},{12,16},{16,20},{20,24},{24,28},{1,5},{5,9},{9,... | collective-permute-start | bytes 589832 | tf_op jit(solution)/shard_map/ppermute | solution.py:17
  8.7 0.9 %copy-start = (bf16[64,3,3,2,2,32]{0,5,4,3,2,1:T(8,128)(2,1)}, bf16[64,3,3,2,2,32]{0,5,4,3,2,1:T(8,128)(2,1)S(1)}, u32[]{:S(2)}) copy-start(bf16[64,3,3,2,2,32]{0,5,4,3,2,1:T(8,128)(2,1)S(1)} %copy.21) | copy-start | bytes 442372
  9.5 0.7 %copy-start.7 = (bf16[1,4,3,16,512]{4,3,2,1,0:T(8,128)(2,1)}, bf16[1,4,3,16,512]{4,3,2,1,0:T(8,128)(2,1)S(1)}, u32[]{:S(2)}) copy-start(bf16[1,4,3,16,512]{4,3,2,1,0:T(8,128)(2,1)S(1)} %collective-permute-done.vb_ref) | copy-start | bytes 589828
  9.6 0.8 %copy-start.4 = (bf16[320,512]{1,0:T(8,128)(2,1)}, bf16[320,512]{1,0:T(8,128)(2,1)S(1)}, u32[]{:S(2)}) copy-start(bf16[320,512]{1,0:T(8,128)(2,1)S(1)} %collective-permute-done.1.va_ref) | copy-start | bytes 983044
  17.9 0.9 %copy-start.1 = (f32[432,128]{1,0:T(8,128)S(1)}, f32[432,128]{1,0:T(8,128)}, u32[]{:S(2)}) copy-start(f32[432,128]{1,0:T(8,128)} %get-tuple-element.11) | copy-start | bytes 663556
  18.9 3.8 %collective-permute-start.2 = (f32[232,128]{1,0:T(8,128)S(1)}, f32[232,128]{1,0:T(8,128)S(1)}, u32[]{:S(2)}, u32[]{:S(2)}) collective-permute-start(f32[232,128]{1,0:T(8,128)S(1)} %fusion.1), channel_id=1, source_target_pairs={{0,4},{4,0},{8,12},{12,8},{16,20},{20,16},{24,28},{28,24},{1,5},{5... | collective-permute-start | bytes 356360 | tf_op jit(solution)/shard_map/ppermute | solution.py:36
  22.8 7.6 %collective-permute-start.3 = (f32[232,128]{1,0:T(8,128)S(1)}, f32[232,128]{1,0:T(8,128)S(1)}, u32[]{:S(2)}, u32[]{:S(2)}) collective-permute-start(f32[232,128]{1,0:T(8,128)S(1)} %select_add_fusion), channel_id=1, source_target_pairs={{0,8},{4,12},{8,0},{12,4},{16,24},{20,28},{24,16},{28,20},{1,9},{5... | collective-permute-start | bytes 356360 | tf_op jit(solution)/shard_map/ppermute | solution.py:38
  30.4 5.0 %collective-permute-start.4 = (f32[232,128]{1,0:T(8,128)S(1)}, f32[232,128]{1,0:T(8,128)S(1)}, u32[]{:S(2)}, u32[]{:S(2)}) collective-permute-start(f32[232,128]{1,0:T(8,128)S(1)} %add.71), channel_id=1, source_target_pairs={{0,16},{4,20},{8,24},{12,28},{16,0},{20,4},{24,8},{28,12},{1,17},{... | collective-permute-start | bytes 356360 | tf_op jit(solution)/shard_map/ppermute | solution.py:38
  35.4 4.9 %collective-permute-start.5 = (f32[232,128]{1,0:T(8,128)S(1)}, f32[232,128]{1,0:T(8,128)S(1)}, u32[]{:S(2)}, u32[]{:S(2)}) collective-permute-start(f32[232,128]{1,0:T(8,128)S(1)} %add.72), channel_id=1, source_target_pairs={{0,1},{1,0},{2,3},{3,2},{4,5},{5,4},{6,7},{7,6},{8,9},{9,8},{10,11... | collective-permute-start | bytes 356360 | tf_op jit(solution)/shard_map/ppermute | solution.py:38
  40.4 7.2 %copy-start.5 = (bf16[512,256]{1,0:T(8,128)(2,1)S(1)}, bf16[512,256]{1,0:T(8,128)(2,1)}, u32[]{:S(2)}) copy-start(bf16[512,256]{1,0:T(8,128)(2,1)} %get-tuple-element.9) | copy-start | bytes 786436
  40.4 7.1 %collective-permute-start.6 = (f32[232,128]{1,0:T(8,128)S(1)}, f32[232,128]{1,0:T(8,128)S(1)}, u32[]{:S(2)}, u32[]{:S(2)}) collective-permute-start(f32[232,128]{1,0:T(8,128)S(1)} %add.73), channel_id=1, source_target_pairs={{0,2},{1,3},{2,0},{3,1},{4,6},{5,7},{6,4},{7,5},{8,10},{9,11},{10,... | collective-permute-start | bytes 356360 | tf_op jit(solution)/shard_map/ppermute | solution.py:38
  47.5 1.6 %collective-permute-start.7 = (f32[232,128]{1,0:T(8,128)S(1)}, f32[232,128]{1,0:T(8,128)S(1)}, u32[]{:S(2)}, u32[]{:S(2)}) collective-permute-start(f32[232,128]{1,0:T(8,128)S(1)} %add.74), channel_id=1, source_target_pairs={{0,4},{4,0},{8,12},{12,8},{16,20},{20,16},{24,28},{28,24},{1,5},{5... | collective-permute-start | bytes 356360 | tf_op jit(solution)/shard_map/ppermute | solution.py:39
  47.6 0.9 %copy-start.9 = (bf16[64,512]{1,0:T(8,128)(2,1)S(1)}, bf16[64,512]{1,0:T(8,128)(2,1)}, u32[]{:S(2)}) copy-start(bf16[64,512]{1,0:T(8,128)(2,1)} %get-tuple-element.8) | copy-start | bytes 196612

commit v14 on v13

--- a/solution.py
+++ b/solution.py
@@ -61,7 +61,7 @@
 
 def _kernel(vb_ref, vo_ref, va_ref, k1_ref, k2_ref, k2t_ref, cot_ref,
             lvl_ref, g1_ref, s1_ref, s2_ref,
-            tp, p1, t2, pre1, p2, bt, gs, gacc, b1, g1s, qs):
+            tp, p1, t2, pre1, p2, bt, gs, gacc, b1, g1s, qs, vbuf, vsem):
     c0, ny, nx = vo_ref.shape[1], vo_ref.shape[3], vo_ref.shape[4]
     lanes = nx // 4
     nzi = tp.shape[0]
@@ -83,20 +83,24 @@
     perm = jnp.where(icol == ((s_ * 4 + r_) * c0 + i_) * ny + y_, 1.0, 0.0).astype(BF16)
 
     tp[:, 0] = jnp.zeros((nzi, 2 * rows0, lanes), BF16)
-    zi = 0
+    vb_copy = pltpu.make_async_copy(vb_ref, vbuf, vsem)
+    vb_copy.start()
     nz_own = vo_ref.shape[2]
-    for ref, nzp in ((vb_ref, vb_ref.shape[2]), (vo_ref, nz_own), (va_ref, nz_own)):
+    nzb = vbuf.shape[2]
+    for ref, nzp, zi0 in ((vo_ref, nz_own, nzb), (va_ref, nz_own, nzb + nz_own), (vbuf, nzb, 0)):
         if ref is va_ref:
             zmat = ref[0:c0 * nzp * ny]
         else:
+            if ref is vbuf:
+                vb_copy.wait()
             zmat = ref[0].reshape(c0 * nzp * ny, nx)
         whole = jnp.dot(zmat, sel_x, preferred_element_type=F32)
         for z in range(nzp):
+            zi = zi0 + z
             ymat = jnp.concatenate([whole[(i * nzp + z) * ny:(i * nzp + z + 1) * ny] for i in range(c0)], axis=0)
             blocks = [ymat[:, r * lanes:(r + 1) * lanes] for r in range(4)]
             qs[:, zi * lanes:(zi + 1) * lanes] = jnp.concatenate(
                 blocks + [_shift_right(b) for b in blocks], axis=0).astype(BF16)
-            zi += 1
     tall = jnp.dot(perm, qs[...], preferred_element_type=F32).astype(BF16)
     for zi in range(nzi):
         tp[zi, 1:] = tall[:, zi * lanes:(zi + 1) * lanes].reshape(ny, 2 * rows0, lanes)
@@ -222,6 +226,7 @@
     vm = pltpu.VMEM
     lvl, g1, s1, s2 = pl.pallas_call(
         _kernel,
+        in_specs=[pl.BlockSpec(memory_space=pl.ANY)] + [pl.BlockSpec(memory_space=vm)] * 6,
         out_shape=(
             jax.ShapeDtypeStruct((c2, n2), BF16),
             jax.ShapeDtypeStruct((2 * ny1 * c1, 2 * q), BF16),
@@ -240,6 +245,8 @@
             vm((2, 2 * c1, ny1 * q), BF16),
             vm((2 * ny1 * c1, 2 * q), BF16),
             vm((8 * c0 * ny, nzi * q), BF16),
+            vm(below.shape, BF16),
+            pltpu.SemaphoreType.DMA(()),
         ],
         cost_estimate=pl.CostEstimate(flops=60_000_000, transcendentals=200_000, bytes_accessed=3_000_000),
     )(below, volume, above, k1m, k2m, k2t, cot)

time: 51.3 us -> 52.1 us (1.016)
  Pallas kernels: 6.37 us -> 7.11 us
    pallas_call x1, Pallas kernels: 6.37 us -> 7.11 us  [per_device(): pl.pallas_call(_kernel, in_specs=[pl.BlockSpec(memory_space=pl.ANY)] + [p...]
  transfers between devices with their start and end apart: 8 -> 8, of which waited for: 5 -> 5; matrix products, arithmetic and copies ran while one was open for 8% -> 7% of each run, Pallas kernels for 0% -> 0%
where the time goes in v14:
time: 52.1 us; the launch traced here: 51.7 us
  starting transfers between devices  17.8 us (34%)
  waiting for transfers between devices  15.2 us (29%)
  local copies, waits for them, and re-layouts  8.81 us (17%)
  Pallas kernels  7.11 us (14%)
  other arithmetic  1.78 us (3%)
  between operations  1 us (2%)
    ppermute x4, waiting for transfers between devices, _all_sum(): part = part + lax.ppermute(part, axis, [(i, i ^ k) for i in range(n)])  14.2 us
    ppermute x4, starting transfers between devices, _all_sum(): part = part + lax.ppermute(part, axis, [(i, i ^ k) for i in range(n)])  10.4 us
    pallas_call x1, Pallas kernels, per_device(): pl.pallas_call(_kernel, in_specs=[pl.BlockSpec(memory_space=pl.ANY)] + [p...  7.11 us
    ppermute x2, starting transfers between devices, shifted(): return lax.ppermute(block, axis, route)  4.47 us
    ppermute x1, starting transfers between devices, _all_sum(): lax.ppermute(jnp.where(low, hi, lo), axis0, pair)  2.88 us
    unnamed x21, local copies, waits for them, and re-layouts  2.42 us
    reshape x1, local copies, waits for them, and re-layouts, per_device(): s1r = s1.reshape(3, 3, 2, c0, 4, 2, c1)  1.11 us
  transfers between devices with their start and end apart: 8, of which 5 were waited for; matrix products, arithmetic and copies ran while one was open for 7% of the time, Pallas kernels for 0%

profile of v14, /device:TPU:0, one launch (start us, length us, event | category | flops | bytes accessed | tf_op | source)
XLA Modules:
  0.0 51.7 jit_solution(3570554753090457653)
XLA Ops:
  0.6 0.9 %copy.40 = bf16[8,8,4,128]{3,1,2,0:T(8,128)(2,1)S(1)} copy(bf16[8,8,4,128]{3,2,1,0:T(4,128)(2,1)} %bitcast.68) | data formatting | bytes 131072
  1.5 0.0 copy-start.3
  1.5 0.0 copy-start.2
  1.5 1.0 %pad_maximum_fusion.1 = bf16[320,512]{1,0:T(8,128)(2,1)S(1)} fusion(bf16[64,512]{1,0:T(8,128)(2,1)S(1)} %bitcast.53, bf16[256,512]{1,0:T(8,128)(2,1)} %bitcast.51), kind=kLoop, calls=%fused_computation.2 | loop fusion | flops 655360 | bytes 655360 | tf_op jit(solution)/shard_map/concatenate | solution.py:216
  2.5 0.0 copy-done.3
  2.6 0.0 copy-start.8
  2.6 0.0 copy-start.6
  2.6 1.4 %collective-permute-start.1 = (bf16[320,512]{1,0:T(8,128)(2,1)S(1)}, bf16[320,512]{1,0:T(8,128)(2,1)S(1)}, u32[]{:S(2)}, u32[]{:S(2)}) collective-permute-start(bf16[320,512]{1,0:T(8,128)(2,1)S(1)} %pad_maximum_fusion.1), channel_id=1, source_target_pairs={{4,0},{8,4},{12,8},{16,12},{20,16},{24,20},{28,24},{5,1},{9,5},{13... | collective-permute-start | bytes 983048 | tf_op jit(solution)/shard_map/ppermute | solution.py:17
  4.0 0.0 copy-done.2
  4.0 3.0 %collective-permute-start = (bf16[1,4,3,16,512]{4,3,2,1,0:T(8,128)(2,1)S(1)}, bf16[1,4,3,16,512]{4,3,2,1,0:T(8,128)(2,1)S(1)}, u32[]{:S(2)}, u32[]{:S(2)}) collective-permute-start(bf16[1,4,3,16,512]{4,3,2,1,0:T(8,128)(2,1)S(1)} %slice.52), channel_id=1, source_target_pairs={{0,4},{4,8},{8,12},{12,16},{16,20},{20,24},{24,28},{1,5},{5,9},{9,... | collective-permute-start | bytes 589832 | tf_op jit(solution)/shard_map/ppermute | solution.py:17
  7.1 0.0 copy-done.8
  7.2 0.0 copy-done.6
  7.3 0.1 pad_maximum_fusion.5
  7.4 0.1 maximum_bitcast_fusion.1
  7.5 0.1 maximum_bitcast_fusion
  7.5 0.1 pad_maximum_fusion.3
  7.7 0.1 copy.20
  7.8 0.1 reshape.89
  7.9 0.7 %copy.22.k1_ref = bf16[64,288]{1,0:T(8,128)(2,1)} copy(bf16[64,288]{0,1:T(8,128)(2,1)S(1)} %reshape.89) | data formatting | bytes 73728 | tf_op jit(solution)/shard_map/reshape | solution.py:197
  8.6 0.1 pad_maximum_fusion.2
  8.7 0.0 copy-start
  8.7 0.8 %copy.23.k2_ref = bf16[64,1152]{1,0:T(8,128)(2,1)} copy(bf16[64,1152]{0,1:T(8,128)(2,1)S(1)} %bitcast.49) | data formatting | bytes 294912 | tf_op jit(solution)/shard_map/reshape | solution.py:205
  9.5 0.0 collective-permute-done.vb_ref
  9.5 0.0 copy-start.7
  9.5 0.0 collective-permute-done.1.va_ref
  9.6 0.0 copy-start.4
  9.6 0.0 copy-done
  9.6 0.6 %copy-done.7 = bf16[1,4,3,16,512]{4,3,2,1,0:T(8,128)(2,1)} copy-done((bf16[1,4,3,16,512]{4,3,2,1,0:T(8,128)(2,1)}, bf16[1,4,3,16,512]{4,3,2,1,0:T(8,128)(2,1)S(1)}, u32[]{:S(2)}) %copy-start.7) | copy-done | bytes 196632
  10.2 0.1 copy-done.4
  10.3 7.1 %shard_map.75 = (bf16[64,512]{1,0:T(8,128)(2,1)}, bf16[512,256]{1,0:T(8,128)(2,1)}, f32[288,64]{1,0:T(8,128)}, f32[432,128]{1,0:T(8,128)}) custom-call(bf16[1,4,3,16,512]{4,3,2,1,0:T(8,128)(2,1)} %copy-done.7, bf16[1,4,4,16,512]{4,3,2,1,0:T(8,128)(2,1)} %vo_ref.1, bf16[320,512]{1,0:T(8,128)(2,1)} %copy-done.4, bf16[64,288]{1,0:T(8,128)(2,1)} %copy.22.k1_ref, ...), custom_call_target="tpu_custom_call" | custom-call | flops 60000000 | bytes 3000000 | tf_op jit(solution)/shard_map/pallas_call | solution.py:227
  17.4 1.1 %reshape.93 = f32[3,3,2,4,4,2,32]{6,5,4,3,2,1,0:T(2,128)S(1)} reshape(f32[288,64]{1,0:T(8,128)} %get-tuple-element.10) | data formatting | bytes 147456 | tf_op jit(solution)/shard_map/reshape | solution.py:257
  18.6 0.1 fusion.2
  18.7 0.0 copy-start.1
  18.8 0.1 reshape.94
  18.8 0.8 %copy-done.1 = f32[432,128]{1,0:T(8,128)S(1)} copy-done((f32[432,128]{1,0:T(8,128)S(1)}, f32[432,128]{1,0:T(8,128)}, u32[]{:S(2)}) %copy-start.1) | copy-done | bytes 221208
  19.6 2.9 %collective-permute-start.2 = (f32[232,128]{1,0:T(8,128)S(1)}, f32[232,128]{1,0:T(8,128)S(1)}, u32[]{:S(2)}, u32[]{:S(2)}) collective-permute-start(f32[232,128]{1,0:T(8,128)S(1)} %fusion.1), channel_id=1, source_target_pairs={{0,4},{4,0},{8,12},{12,8},{16,20},{20,16},{24,28},{28,24},{1,5},{5... | collective-permute-start | bytes 356360 | tf_op jit(solution)/shard_map/ppermute | solution.py:36
  22.5 1.0 %collective-permute-done.2 = f32[232,128]{1,0:T(8,128)S(1)} collective-permute-done((f32[232,128]{1,0:T(8,128)S(1)}, f32[232,128]{1,0:T(8,128)S(1)}, u32[]{:S(2)}, u32[]{:S(2)}) %collective-permute-start.2) | collective-permute-done | bytes 118816 | tf_op jit(solution)/shard_map/ppermute | solution.py:36
  23.5 3.9 %collective-permute-start.3 = (f32[232,128]{1,0:T(8,128)S(1)}, f32[232,128]{1,0:T(8,128)S(1)}, u32[]{:S(2)}, u32[]{:S(2)}) collective-permute-start(f32[232,128]{1,0:T(8,128)S(1)} %select_add_fusion), channel_id=1, source_target_pairs={{0,8},{4,12},{8,0},{12,4},{16,24},{20,28},{24,16},{28,20},{1,9},{5... | collective-permute-start | bytes 356360 | tf_op jit(solution)/shard_map/ppermute | solution.py:38
  27.4 3.7 %collective-permute-done.3 = f32[232,128]{1,0:T(8,128)S(1)} collective-permute-done((f32[232,128]{1,0:T(8,128)S(1)}, f32[232,128]{1,0:T(8,128)S(1)}, u32[]{:S(2)}, u32[]{:S(2)}) %collective-permute-start.3) | collective-permute-done | bytes 118816 | tf_op jit(solution)/shard_map/ppermute | solution.py:38
  31.2 2.2 %collective-permute-start.4 = (f32[232,128]{1,0:T(8,128)S(1)}, f32[232,128]{1,0:T(8,128)S(1)}, u32[]{:S(2)}, u32[]{:S(2)}) collective-permute-start(f32[232,128]{1,0:T(8,128)S(1)} %add.71), channel_id=1, source_target_pairs={{0,16},{4,20},{8,24},{12,28},{16,0},{20,4},{24,8},{28,12},{1,17},{... | collective-permute-start | bytes 356360 | tf_op jit(solution)/shard_map/ppermute | solution.py:38
  33.4 2.8 %collective-permute-done.4 = f32[232,128]{1,0:T(8,128)S(1)} collective-permute-done((f32[232,128]{1,0:T(8,128)S(1)}, f32[232,128]{1,0:T(8,128)S(1)}, u32[]{:S(2)}, u32[]{:S(2)}) %collective-permute-start.4) | collective-permute-done | bytes 118816 | tf_op jit(solution)/shard_map/ppermute | solution.py:38
  36.2 1.6 %collective-permute-start.5 = (f32[232,128]{1,0:T(8,128)S(1)}, f32[232,128]{1,0:T(8,128)S(1)}, u32[]{:S(2)}, u32[]{:S(2)}) collective-permute-start(f32[232,128]{1,0:T(8,128)S(1)} %add.72), channel_id=1, source_target_pairs={{0,1},{1,0},{2,3},{3,2},{4,5},{5,4},{6,7},{7,6},{8,9},{9,8},{10,11... | collective-permute-start | bytes 356360 | tf_op jit(solution)/shard_map/ppermute | solution.py:38
  37.8 3.3 %collective-permute-done.5 = f32[232,128]{1,0:T(8,128)S(1)} collective-permute-done((f32[232,128]{1,0:T(8,128)S(1)}, f32[232,128]{1,0:T(8,128)S(1)}, u32[]{:S(2)}, u32[]{:S(2)}) %collective-permute-start.5) | collective-permute-done | bytes 118816 | tf_op jit(solution)/shard_map/ppermute | solution.py:38
  41.1 0.0 copy-start.5
  41.1 2.7 %collective-permute-start.6 = (f32[232,128]{1,0:T(8,128)S(1)}, f32[232,128]{1,0:T(8,128)S(1)}, u32[]{:S(2)}, u32[]{:S(2)}) collective-permute-start(f32[232,128]{1,0:T(8,128)S(1)} %add.73), channel_id=1, source_target_pairs={{0,2},{1,3},{2,0},{3,1},{4,6},{5,7},{6,4},{7,5},{8,10},{9,11},{10,... | collective-permute-start | bytes 356360 | tf_op jit(solution)/shard_map/ppermute | solution.py:38
  43.8 4.4 %collective-permute-done.6 = f32[232,128]{1,0:T(8,128)S(1)} collective-permute-done((f32[232,128]{1,0:T(8,128)S(1)}, f32[232,128]{1,0:T(8,128)S(1)}, u32[]{:S(2)}, u32[]{:S(2)}) %collective-permute-start.6) | collective-permute-done | bytes 118816 | tf_op jit(solution)/shard_map/ppermute | solution.py:38
  48.2 0.1 collective-permute-start.7
  48.3 0.0 copy-done.5
  48.3 0.0 copy-start.9
  48.3 0.9 %copy.39 = bf16[2,8,32,256]{3,1,0,2:T(8,128)(2,1)} copy(bf16[2,8,32,256]{3,2,1,0:T(8,128)(2,1)S(1)} %bitcast.56) | data formatting | bytes 524288 | tf_op jit(solution)/shard_map/reshape | solution.py:255
  49.2 0.0 copy-done.9
  49.2 0.6 %reshape.91 = bf16[1,64,1,4,128]{4,3,1,2,0:T(4,128)(2,1)} reshape(bf16[64,512]{1,0:T(8,128)(2,1)S(1)} %copy-done.9) | data formatting | bytes 131072 | tf_op jit(solution)/shard_map/reshape | solution.py:254
  49.8 0.0 collective-permute-done.7
  49.9 0.3 reshape.96
  50.2 0.8 %copy.30 = f32[27,2,16,64]{3,2,1,0:T(8,128)} copy(f32[27,2,16,64]{3,1,2,0:T(2,128)S(1)} %bitcast.52) | data formatting | bytes 442368 | tf_op jit(solution)/shard_map/transpose | solution.py:271
  51.0 0.7 %reshape.95 = f32[3,3,3,4,32]{4,3,2,1,0:T(4,128)} reshape(f32[27,128]{1,0:T(8,128)S(1)} %slice_multiply_fusion.1) | data formatting | bytes 27648 | tf_op jit(solution)/shard_map/reshape | solution.py:270
  (23 shorter events, 0.4 us)
Async XLA Ops:
  1.5 1.1 %copy-start.3 = (bf16[8,8,4,128]{3,1,2,0:T(8,128)(2,1)}, bf16[8,8,4,128]{3,1,2,0:T(8,128)(2,1)S(1)}, u32[]{:S(2)}) copy-start(bf16[8,8,4,128]{3,1,2,0:T(8,128)(2,1)S(1)} %copy.40) | copy-start | bytes 196612
  1.5 2.5 %copy-start.2 = (bf16[1,4,4,16,512]{4,3,2,1,0:T(8,128)(2,1)S(1)}, bf16[1,4,4,16,512]{4,3,2,1,0:T(8,128)(2,1)}, u32[]{:S(2)}) copy-start(bf16[1,4,4,16,512]{4,3,2,1,0:T(8,128)(2,1)} %vo_ref.1) | copy-start | bytes 786436
  2.6 4.5 %copy-start.8 = (bf16[32,4,3,3,3]{0,1,4,3,2:T(4,128)(2,1)S(1)}, bf16[32,4,3,3,3]{0,1,4,3,2:T(4,128)(2,1)}, u32[]{:S(2)}) copy-start(bf16[32,4,3,3,3]{0,1,4,3,2:T(4,128)(2,1)} %param.5) | copy-start | bytes 20740
  2.6 4.6 %copy-start.6 = (bf16[64,32,3,3,3]{0,1,4,3,2:T(8,128)(2,1)S(1)}, bf16[64,32,3,3,3]{0,1,4,3,2:T(8,128)(2,1)}, u32[]{:S(2)}) copy-start(bf16[64,32,3,3,3]{0,1,4,3,2:T(8,128)(2,1)} %param.6) | copy-start | bytes 331780
  2.6 7.0 %collective-permute-start.1 = (bf16[320,512]{1,0:T(8,128)(2,1)S(1)}, bf16[320,512]{1,0:T(8,128)(2,1)S(1)}, u32[]{:S(2)}, u32[]{:S(2)}) collective-permute-start(bf16[320,512]{1,0:T(8,128)(2,1)S(1)} %pad_maximum_fusion.1), channel_id=1, source_target_pairs={{4,0},{8,4},{12,8},{16,12},{20,16},{24,20},{28,24},{5,1},{9,5},{13... | collective-permute-start | bytes 983048 | tf_op jit(solution)/shard_map/ppermute | solution.py:17
  4.0 5.5 %collective-permute-start = (bf16[1,4,3,16,512]{4,3,2,1,0:T(8,128)(2,1)S(1)}, bf16[1,4,3,16,512]{4,3,2,1,0:T(8,128)(2,1)S(1)}, u32[]{:S(2)}, u32[]{:S(2)}) collective-permute-start(bf16[1,4,3,16,512]{4,3,2,1,0:T(8,128)(2,1)S(1)} %slice.52), channel_id=1, source_target_pairs={{0,4},{4,8},{8,12},{12,16},{16,20},{20,24},{24,28},{1,5},{5,9},{9,... | collective-permute-start | bytes 589832 | tf_op jit(solution)/shard_map/ppermute | solution.py:17
  8.7 0.9 %copy-start = (bf16[64,3,3,2,2,32]{0,5,4,3,2,1:T(8,128)(2,1)}, bf16[64,3,3,2,2,32]{0,5,4,3,2,1:T(8,128)(2,1)S(1)}, u32[]{:S(2)}) copy-start(bf16[64,3,3,2,2,32]{0,5,4,3,2,1:T(8,128)(2,1)S(1)} %copy.21) | copy-start | bytes 442372
  9.5 0.7 %copy-start.7 = (bf16[1,4,3,16,512]{4,3,2,1,0:T(8,128)(2,1)}, bf16[1,4,3,16,512]{4,3,2,1,0:T(8,128)(2,1)S(1)}, u32[]{:S(2)}) copy-start(bf16[1,4,3,16,512]{4,3,2,1,0:T(8,128)(2,1)S(1)} %collective-permute-done.vb_ref) | copy-start | bytes 589828
  9.6 0.8 %copy-start.4 = (bf16[320,512]{1,0:T(8,128)(2,1)}, bf16[320,512]{1,0:T(8,128)(2,1)S(1)}, u32[]{:S(2)}) copy-start(bf16[320,512]{1,0:T(8,128)(2,1)S(1)} %collective-permute-done.1.va_ref) | copy-start | bytes 983044
  18.7 0.9 %copy-start.1 = (f32[432,128]{1,0:T(8,128)S(1)}, f32[432,128]{1,0:T(8,128)}, u32[]{:S(2)}) copy-start(f32[432,128]{1,0:T(8,128)} %get-tuple-element.11) | copy-start | bytes 663556
  19.6 3.9 %collective-permute-start.2 = (f32[232,128]{1,0:T(8,128)S(1)}, f32[232,128]{1,0:T(8,128)S(1)}, u32[]{:S(2)}, u32[]{:S(2)}) collective-permute-start(f32[232,128]{1,0:T(8,128)S(1)} %fusion.1), channel_id=1, source_target_pairs={{0,4},{4,0},{8,12},{12,8},{16,20},{20,16},{24,28},{28,24},{1,5},{5... | collective-permute-start | bytes 356360 | tf_op jit(solution)/shard_map/ppermute | solution.py:36
  23.5 7.6 %collective-permute-start.3 = (f32[232,128]{1,0:T(8,128)S(1)}, f32[232,128]{1,0:T(8,128)S(1)}, u32[]{:S(2)}, u32[]{:S(2)}) collective-permute-start(f32[232,128]{1,0:T(8,128)S(1)} %select_add_fusion), channel_id=1, source_target_pairs={{0,8},{4,12},{8,0},{12,4},{16,24},{20,28},{24,16},{28,20},{1,9},{5... | collective-permute-start | bytes 356360 | tf_op jit(solution)/shard_map/ppermute | solution.py:38
  31.2 5.0 %collective-permute-start.4 = (f32[232,128]{1,0:T(8,128)S(1)}, f32[232,128]{1,0:T(8,128)S(1)}, u32[]{:S(2)}, u32[]{:S(2)}) collective-permute-start(f32[232,128]{1,0:T(8,128)S(1)} %add.71), channel_id=1, source_target_pairs={{0,16},{4,20},{8,24},{12,28},{16,0},{20,4},{24,8},{28,12},{1,17},{... | collective-permute-start | bytes 356360 | tf_op jit(solution)/shard_map/ppermute | solution.py:38
  36.2 4.9 %collective-permute-start.5 = (f32[232,128]{1,0:T(8,128)S(1)}, f32[232,128]{1,0:T(8,128)S(1)}, u32[]{:S(2)}, u32[]{:S(2)}) collective-permute-start(f32[232,128]{1,0:T(8,128)S(1)} %add.72), channel_id=1, source_target_pairs={{0,1},{1,0},{2,3},{3,2},{4,5},{5,4},{6,7},{7,6},{8,9},{9,8},{10,11... | collective-permute-start | bytes 356360 | tf_op jit(solution)/shard_map/ppermute | solution.py:38
  41.1 7.2 %copy-start.5 = (bf16[512,256]{1,0:T(8,128)(2,1)S(1)}, bf16[512,256]{1,0:T(8,128)(2,1)}, u32[]{:S(2)}) copy-start(bf16[512,256]{1,0:T(8,128)(2,1)} %get-tuple-element.9) | copy-start | bytes 786436
  41.1 7.1 %collective-permute-start.6 = (f32[232,128]{1,0:T(8,128)S(1)}, f32[232,128]{1,0:T(8,128)S(1)}, u32[]{:S(2)}, u32[]{:S(2)}) collective-permute-start(f32[232,128]{1,0:T(8,128)S(1)} %add.73), channel_id=1, source_target_pairs={{0,2},{1,3},{2,0},{3,1},{4,6},{5,7},{6,4},{7,5},{8,10},{9,11},{10,... | collective-permute-start | bytes 356360 | tf_op jit(solution)/shard_map/ppermute | solution.py:38
  48.2 1.6 %collective-permute-start.7 = (f32[232,128]{1,0:T(8,128)S(1)}, f32[232,128]{1,0:T(8,128)S(1)}, u32[]{:S(2)}, u32[]{:S(2)}) collective-permute-start(f32[232,128]{1,0:T(8,128)S(1)} %add.74), channel_id=1, source_target_pairs={{0,4},{4,0},{8,12},{12,8},{16,20},{20,16},{24,28},{28,24},{1,5},{5... | collective-permute-start | bytes 356360 | tf_op jit(solution)/shard_map/ppermute | solution.py:39
  48.3 0.9 %copy-start.9 = (bf16[64,512]{1,0:T(8,128)(2,1)S(1)}, bf16[64,512]{1,0:T(8,128)(2,1)}, u32[]{:S(2)}) copy-start(bf16[64,512]{1,0:T(8,128)(2,1)} %get-tuple-element.8) | copy-start | bytes 196612

commit v15 on v13

--- a/solution.py
+++ b/solution.py
@@ -60,8 +60,8 @@
 
 
 def _kernel(vb_ref, vo_ref, va_ref, k1_ref, k2_ref, k2t_ref, cot_ref,
-            lvl_ref, g1_ref, s1_ref, s2_ref,
-            tp, p1, t2, pre1, p2, bt, gs, gacc, b1, g1s, qs):
+            lvl_ref, g1_ref, s2_ref,
+            tp, p1, t2, pre1, p2, bt, gs, gacc, b1, g1s, qs, s1s):
     c0, ny, nx = vo_ref.shape[1], vo_ref.shape[3], vo_ref.shape[4]
     lanes = nx // 4
     nzi = tp.shape[0]
@@ -141,6 +141,8 @@
     c2n = dup.shape[1] // 2
     qi = c1 // 4
     lane2 = lax.broadcasted_iota(jnp.int32, (qi, 2 * c2n), 1)
+    n_s2 = 27 * qi
+    s2_ref[n_s2:] = jnp.zeros((s2_ref.shape[0] - n_s2, s2_ref.shape[1]), F32)
     for dh in range(9):
         for w, off in enumerate((3 * c1 // 2, 0, c1 // 2)):
             r0 = dh * c2 + off
@@ -174,7 +176,27 @@
             blk = gb[:, y1 * lanes:(y1 + 1) * lanes]
             r0 = (a_ * ny1 + y1) * half
             g1s[r0:r0 + half] = jnp.concatenate([blk[:half], blk[half:]], axis=1)
-    s1_ref[...] = _nt(p1[:, ny1 * lanes:3 * ny1 * lanes], jnp.concatenate([b1[0], b1[1]], axis=1))
+    bcat = jnp.concatenate([b1[0], b1[1]], axis=1)
+    s1s[...] = _nt(p1[:, ny1 * lanes:3 * ny1 * lanes],
+                   jnp.concatenate([bcat, jnp.zeros(bcat.shape, BF16)], axis=0))
+    qo = c1 // 2
+    lane1 = lax.broadcasted_iota(jnp.int32, (1, 4 * qo), 1)
+    taps = (((1, 3), (0, 1)), ((0, 0), (0, 2)), ((0, 1), (0, 3)))
+    out_rows = []
+    for dh in range(9):
+        for (sa, ra), (sb, rb) in taps:
+            acc = jnp.zeros((1, 4 * qo), F32)
+            for i in range(c0):
+                xa = s1s[pl.ds(dh * 2 * rows0 + sa * rows0 + i * 4 + ra, 1), :]
+                xb = s1s[pl.ds(dh * 2 * rows0 + sb * rows0 + i * 4 + rb, 1), :]
+                if i:
+                    xa = pltpu.roll(xa, i * qo, 1)
+                xb = pltpu.roll(xb, (i * qo - qo) % (4 * qo), 1)
+                m = (lane1 >= i * qo) & (lane1 < (i + 1) * qo)
+                acc = acc + jnp.where(m, xa + xb, 0.0)
+            out_rows.append(acc)
+    n_s2 = 27 * qi
+    s2_ref[n_s2:n_s2 + 27] = jnp.concatenate(out_rows, axis=0)
 
     n2 = 2 * lanes
     row = lax.broadcasted_iota(jnp.int32, (n2, n2), 0)
@@ -219,14 +241,16 @@
 
     ny1, ny2 = ny // 2, ny // 4
     n_act = 5
+    n_s2 = 27 * c1 // 2
+    n_g1 = 27 * c0 * c1 // (2 * c2)
+    n_pay = -(-(n_s2 + n_g1) // 16) * 16
     vm = pltpu.VMEM
-    lvl, g1, s1, s2 = pl.pallas_call(
+    lvl, g1, pay = pl.pallas_call(
         _kernel,
         out_shape=(
             jax.ShapeDtypeStruct((c2, n2), BF16),
             jax.ShapeDtypeStruct((2 * ny1 * c1, 2 * q), BF16),
-            jax.ShapeDtypeStruct((k1m.shape[1], k1m.shape[0]), F32),
-            jax.ShapeDtypeStruct((27 * c1 // 2, 2 * c2), F32),
+            jax.ShapeDtypeStruct((n_pay, 2 * c2), F32),
         ),
         scratch_shapes=[
             vm((nzi, ny + 1, 8 * c0, q), BF16),
@@ -240,6 +264,7 @@
             vm((2, 2 * c1, ny1 * q), BF16),
             vm((2 * ny1 * c1, 2 * q), BF16),
             vm((8 * c0 * ny, nzi * q), BF16),
+            vm((k1m.shape[1], 2 * k1m.shape[0]), F32),
         ],
         cost_estimate=pl.CostEstimate(flops=60_000_000, transcendentals=200_000, bytes_accessed=3_000_000),
     )(below, volume, above, k1m, k2m, k2t, cot)
@@ -247,19 +272,12 @@
     level_two = lvl.reshape(1, c2, 1, ny2, n2 // ny2)
     grad_one = g1.reshape(2, ny1, c1, 2 * q).transpose(2, 0, 1, 3)[None]
 
-    s1r = s1.reshape(3, 3, 2, c0, 4, 2, c1)
-    gk1 = jnp.stack([
-        s1r[:, :, 1, :, 3, 0] + s1r[:, :, 0, :, 1, 1],
-        s1r[:, :, 0, :, 0, 0] + s1r[:, :, 0, :, 2, 1],
-        s1r[:, :, 0, :, 1, 0] + s1r[:, :, 0, :, 3, 1],
-    ], 2)
-    rows1 = gk1.size // s2.shape[1]
-    total = _all_sum(jnp.concatenate([gk1.reshape(rows1, s2.shape[1]), s2], 0), ("gz", "sa"))
+    total = _all_sum(pay, ("gz", "sa"))
     samples = volume.shape[0] * lax.axis_size("sa")
     cells_one = samples * (nz // 2) * lax.axis_size("gz") * ny1 * (nx // 2)
     cells_two = samples * cotangent.shape[2] * lax.axis_size("gz") * cotangent.shape[3] * cotangent.shape[4]
-    t1 = total[:rows1] / math.sqrt(float(cells_one))
-    t2 = total[rows1:] / math.sqrt(float(cells_two))
+    t1 = total[n_s2:n_s2 + n_g1] / math.sqrt(float(cells_one))
+    t2 = total[:n_s2] / math.sqrt(float(cells_two))
     grad_kernel_one = t1.reshape(3, 3, 3, c0, c1).transpose(4, 3, 0, 1, 2)
     t2 = t2.reshape(27, c1 // 2, 2, c2).transpose(0, 2, 1, 3).reshape(3, 3, 3, c1, c2)
     grad_kernel_two = t2.transpose(4, 3, 0, 1, 2)

time: 51.3 us -> 50.2 us (0.979)
  local copies, waits for them, and re-layouts: 8.81 us -> 6.84 us
  other arithmetic: 1.78 us -> 2.6 us
    reshape x2 -> x0, local copies, waits for them, and re-layouts: 1.2 us -> none  [the longest x1 1.11 us: per_device(): s1r = s1.reshape(3, 3, 2, c0, 4, 2, c1)]
    select_n x1, other arithmetic: 0.02 us -> 1.01 us  [_all_sum(): jnp.where(low, hi, lo)]
    unnamed x21, local copies, waits for them, and re-layouts: 2.42 us -> 1.66 us
where the time goes in v15:
time: 50.2 us; the launch traced here: 49.9 us
  starting transfers between devices  17.8 us (35%)
  waiting for transfers between devices  15.2 us (30%)
  local copies, waits for them, and re-layouts  6.84 us (14%)
  Pallas kernels  6.53 us (13%)
  other arithmetic  2.6 us (5%)
  between operations  0.94 us (2%)
    ppermute x4, waiting for transfers between devices, _all_sum(): part = part + lax.ppermute(part, axis, [(i, i ^ k) for i in range(n)])  14.2 us
    ppermute x4, starting transfers between devices, _all_sum(): part = part + lax.ppermute(part, axis, [(i, i ^ k) for i in range(n)])  10.4 us
    pallas_call x1, Pallas kernels, per_device(): pl.pallas_call(_kernel, out_shape=(jax.ShapeDtypeStruct((c2, n2), BF16),...  6.53 us
    ppermute x2, starting transfers between devices, shifted(): return lax.ppermute(block, axis, route)  4.47 us
    ppermute x1, starting transfers between devices, _all_sum(): lax.ppermute(jnp.where(low, hi, lo), axis0, pair)  2.88 us
    unnamed x21, local copies, waits for them, and re-layouts  1.66 us
    concatenate x1, other arithmetic, per_device(): jnp.concatenate([volume[0].reshape(-1, nx), cot], 0)  1.04 us
    select_n x1, other arithmetic, _all_sum(): jnp.where(low, hi, lo)  1.01 us
  transfers between devices with their start and end apart: 8, of which 5 were waited for; matrix products, arithmetic and copies ran while one was open for 8% of the time, Pallas kernels for 0%

profile of v15, /device:TPU:0, one launch (start us, length us, event | category | flops | bytes accessed | tf_op | source)
XLA Modules:
  0.0 49.9 jit_solution(490686683168942290)
XLA Ops:
  0.6 0.9 %copy.25 = bf16[8,8,4,128]{3,1,2,0:T(8,128)(2,1)S(1)} copy(bf16[8,8,4,128]{3,2,1,0:T(4,128)(2,1)} %bitcast.54) | data formatting | bytes 131072
  1.5 0.0 copy-start.3
  1.5 0.0 copy-start.1
  1.5 1.0 %pad_maximum_fusion = bf16[320,512]{1,0:T(8,128)(2,1)S(1)} fusion(bf16[64,512]{1,0:T(8,128)(2,1)S(1)} %bitcast.44, bf16[256,512]{1,0:T(8,128)(2,1)} %bitcast.42), kind=kLoop, calls=%fused_computation | loop fusion | flops 655360 | bytes 655360 | tf_op jit(solution)/shard_map/concatenate | solution.py:234
  2.5 0.0 copy-done.3
  2.6 0.0 copy-start.8
  2.6 0.0 copy-start.6
  2.6 1.4 %collective-permute-start.1 = (bf16[320,512]{1,0:T(8,128)(2,1)S(1)}, bf16[320,512]{1,0:T(8,128)(2,1)S(1)}, u32[]{:S(2)}, u32[]{:S(2)}) collective-permute-start(bf16[320,512]{1,0:T(8,128)(2,1)S(1)} %pad_maximum_fusion), channel_id=1, source_target_pairs={{4,0},{8,4},{12,8},{16,12},{20,16},{24,20},{28,24},{5,1},{9,5},{13... | collective-permute-start | bytes 983048 | tf_op jit(solution)/shard_map/ppermute | solution.py:17
  4.0 0.0 copy-done.1
  4.0 3.0 %collective-permute-start = (bf16[1,4,3,16,512]{4,3,2,1,0:T(8,128)(2,1)S(1)}, bf16[1,4,3,16,512]{4,3,2,1,0:T(8,128)(2,1)S(1)}, u32[]{:S(2)}, u32[]{:S(2)}) collective-permute-start(bf16[1,4,3,16,512]{4,3,2,1,0:T(8,128)(2,1)S(1)} %slice.30), channel_id=1, source_target_pairs={{0,4},{4,8},{8,12},{12,16},{16,20},{20,24},{24,28},{1,5},{5,9},{9,... | collective-permute-start | bytes 589832 | tf_op jit(solution)/shard_map/ppermute | solution.py:17
  7.1 0.0 copy-done.8
  7.2 0.0 copy-done.6
  7.3 0.1 pad_maximum_fusion.3
  7.4 0.1 maximum_bitcast_fusion.1
  7.5 0.1 maximum_bitcast_fusion
  7.5 0.1 pad_maximum_fusion.2
  7.7 0.1 copy.14
  7.8 0.1 reshape.29
  7.9 0.7 %copy.16.k1_ref = bf16[64,288]{1,0:T(8,128)(2,1)} copy(bf16[64,288]{0,1:T(8,128)(2,1)S(1)} %reshape.29) | data formatting | bytes 73728 | tf_op jit(solution)/shard_map/reshape | solution.py:215
  8.6 0.1 pad_maximum_fusion.1
  8.7 0.0 copy-start
  8.7 0.8 %copy.17.k2_ref = bf16[64,1152]{1,0:T(8,128)(2,1)} copy(bf16[64,1152]{0,1:T(8,128)(2,1)S(1)} %bitcast.40) | data formatting | bytes 294912 | tf_op jit(solution)/shard_map/reshape | solution.py:223
  9.5 0.0 collective-permute-done.vb_ref
  9.5 0.0 copy-start.7
  9.5 0.0 collective-permute-done.1.va_ref
  9.6 0.0 copy-start.4
  9.6 0.0 copy-done
  9.6 0.6 %copy-done.7 = bf16[1,4,3,16,512]{4,3,2,1,0:T(8,128)(2,1)} copy-done((bf16[1,4,3,16,512]{4,3,2,1,0:T(8,128)(2,1)}, bf16[1,4,3,16,512]{4,3,2,1,0:T(8,128)(2,1)S(1)}, u32[]{:S(2)}) %copy-start.7) | copy-done | bytes 196632
  10.2 0.1 copy-done.4
  10.3 6.5 %shard_map.75 = (bf16[64,512]{1,0:T(8,128)(2,1)}, bf16[512,256]{1,0:T(8,128)(2,1)}, f32[464,128]{1,0:T(8,128)}) custom-call(bf16[1,4,3,16,512]{4,3,2,1,0:T(8,128)(2,1)} %copy-done.7, bf16[1,4,4,16,512]{4,3,2,1,0:T(8,128)(2,1)} %vo_ref.1, bf16[320,512]{1,0:T(8,128)(2,1)} %copy-done.4, bf16[64,288]{1,0:T(8,128)(2,1)} %copy.16.k1_ref, ...), custom_call_target="tpu_custom_call" | custom-call | flops 60000000 | bytes 3000000 | tf_op jit(solution)/shard_map/pallas_call | solution.py:248
  16.9 0.0 copy-start.2
  16.9 1.0 %slice_select_fusion = f32[232,128]{1,0:T(8,128)S(1)} fusion(f32[464,128]{1,0:T(8,128)} %get-tuple-element.9, pred[]{:T(512)S(6)} %eq.3), kind=kLoop, calls=%fused_computation.9 | loop fusion | flops 29696 | bytes 356353 | tf_op jit(solution)/shard_map/jit(_where)/select_n | solution.py:36
  17.9 2.9 %collective-permute-start.2 = (f32[232,128]{1,0:T(8,128)S(1)}, f32[232,128]{1,0:T(8,128)S(1)}, u32[]{:S(2)}, u32[]{:S(2)}) collective-permute-start(f32[232,128]{1,0:T(8,128)S(1)} %slice_select_fusion), channel_id=1, source_target_pairs={{0,4},{4,0},{8,12},{12,8},{16,20},{20,16},{24,28},{28,24},{1,5},{5... | collective-permute-start | bytes 356360 | tf_op jit(solution)/shard_map/ppermute | solution.py:36
  20.8 1.0 %collective-permute-done.2 = f32[232,128]{1,0:T(8,128)S(1)} collective-permute-done((f32[232,128]{1,0:T(8,128)S(1)}, f32[232,128]{1,0:T(8,128)S(1)}, u32[]{:S(2)}, u32[]{:S(2)}) %collective-permute-start.2) | collective-permute-done | bytes 118816 | tf_op jit(solution)/shard_map/ppermute | solution.py:36
  21.7 0.0 copy-done.2
  21.8 3.9 %collective-permute-start.3 = (f32[232,128]{1,0:T(8,128)S(1)}, f32[232,128]{1,0:T(8,128)S(1)}, u32[]{:S(2)}, u32[]{:S(2)}) collective-permute-start(f32[232,128]{1,0:T(8,128)S(1)} %select_add_fusion), channel_id=1, source_target_pairs={{0,8},{4,12},{8,0},{12,4},{16,24},{20,28},{24,16},{28,20},{1,9},{5... | collective-permute-start | bytes 356360 | tf_op jit(solution)/shard_map/ppermute | solution.py:38
  25.6 3.7 %collective-permute-done.3 = f32[232,128]{1,0:T(8,128)S(1)} collective-permute-done((f32[232,128]{1,0:T(8,128)S(1)}, f32[232,128]{1,0:T(8,128)S(1)}, u32[]{:S(2)}, u32[]{:S(2)}) %collective-permute-start.3) | collective-permute-done | bytes 118816 | tf_op jit(solution)/shard_map/ppermute | solution.py:38
  29.4 2.2 %collective-permute-start.4 = (f32[232,128]{1,0:T(8,128)S(1)}, f32[232,128]{1,0:T(8,128)S(1)}, u32[]{:S(2)}, u32[]{:S(2)}) collective-permute-start(f32[232,128]{1,0:T(8,128)S(1)} %add.24), channel_id=1, source_target_pairs={{0,16},{4,20},{8,24},{12,28},{16,0},{20,4},{24,8},{28,12},{1,17},{... | collective-permute-start | bytes 356360 | tf_op jit(solution)/shard_map/ppermute | solution.py:38
  31.6 2.8 %collective-permute-done.4 = f32[232,128]{1,0:T(8,128)S(1)} collective-permute-done((f32[232,128]{1,0:T(8,128)S(1)}, f32[232,128]{1,0:T(8,128)S(1)}, u32[]{:S(2)}, u32[]{:S(2)}) %collective-permute-start.4) | collective-permute-done | bytes 118816 | tf_op jit(solution)/shard_map/ppermute | solution.py:38
  34.4 1.6 %collective-permute-start.5 = (f32[232,128]{1,0:T(8,128)S(1)}, f32[232,128]{1,0:T(8,128)S(1)}, u32[]{:S(2)}, u32[]{:S(2)}) collective-permute-start(f32[232,128]{1,0:T(8,128)S(1)} %add.25), channel_id=1, source_target_pairs={{0,1},{1,0},{2,3},{3,2},{4,5},{5,4},{6,7},{7,6},{8,9},{9,8},{10,11... | collective-permute-start | bytes 356360 | tf_op jit(solution)/shard_map/ppermute | solution.py:38
  36.1 3.3 %collective-permute-done.5 = f32[232,128]{1,0:T(8,128)S(1)} collective-permute-done((f32[232,128]{1,0:T(8,128)S(1)}, f32[232,128]{1,0:T(8,128)S(1)}, u32[]{:S(2)}, u32[]{:S(2)}) %collective-permute-start.5) | collective-permute-done | bytes 118816 | tf_op jit(solution)/shard_map/ppermute | solution.py:38
  39.4 0.0 copy-start.5
  39.4 2.7 %collective-permute-start.6 = (f32[232,128]{1,0:T(8,128)S(1)}, f32[232,128]{1,0:T(8,128)S(1)}, u32[]{:S(2)}, u32[]{:S(2)}) collective-permute-start(f32[232,128]{1,0:T(8,128)S(1)} %add.26), channel_id=1, source_target_pairs={{0,2},{1,3},{2,0},{3,1},{4,6},{5,7},{6,4},{7,5},{8,10},{9,11},{10,... | collective-permute-start | bytes 356360 | tf_op jit(solution)/shard_map/ppermute | solution.py:38
  42.0 4.4 %collective-permute-done.6 = f32[232,128]{1,0:T(8,128)S(1)} collective-permute-done((f32[232,128]{1,0:T(8,128)S(1)}, f32[232,128]{1,0:T(8,128)S(1)}, u32[]{:S(2)}, u32[]{:S(2)}) %collective-permute-start.6) | collective-permute-done | bytes 118816 | tf_op jit(solution)/shard_map/ppermute | solution.py:38
  46.5 0.1 collective-permute-start.7
  46.5 0.0 copy-done.5
  46.5 0.0 copy-start.9
  46.6 0.9 %copy.24 = bf16[2,8,32,256]{3,1,0,2:T(8,128)(2,1)} copy(bf16[2,8,32,256]{3,2,1,0:T(8,128)(2,1)S(1)} %bitcast.47) | data formatting | bytes 524288 | tf_op jit(solution)/shard_map/reshape | solution.py:273
  47.4 0.0 copy-done.9
  47.4 0.6 %reshape.31 = bf16[1,64,1,4,128]{4,3,1,2,0:T(4,128)(2,1)} reshape(bf16[64,512]{1,0:T(8,128)(2,1)S(1)} %copy-done.9) | data formatting | bytes 131072 | tf_op jit(solution)/shard_map/reshape | solution.py:272
  48.1 0.0 collective-permute-done.7
  48.1 0.3 reshape.34
  48.4 0.8 %copy.19 = f32[27,2,16,64]{3,2,1,0:T(8,128)} copy(f32[27,2,16,64]{3,1,2,0:T(2,128)S(1)} %bitcast.43) | data formatting | bytes 442368 | tf_op jit(solution)/shard_map/transpose | solution.py:282
  49.2 0.7 %reshape.33 = f32[3,3,3,4,32]{4,3,2,1,0:T(4,128)} reshape(f32[27,128]{1,0:T(8,128)S(1)} %slice_multiply_fusion.1) | data formatting | bytes 27648 | tf_op jit(solution)/shard_map/reshape | solution.py:281
  (17 shorter events, 0.3 us)
Async XLA Ops:
  1.5 1.1 %copy-start.3 = (bf16[8,8,4,128]{3,1,2,0:T(8,128)(2,1)}, bf16[8,8,4,128]{3,1,2,0:T(8,128)(2,1)S(1)}, u32[]{:S(2)}) copy-start(bf16[8,8,4,128]{3,1,2,0:T(8,128)(2,1)S(1)} %copy.25) | copy-start | bytes 196612
  1.5 2.5 %copy-start.1 = (bf16[1,4,4,16,512]{4,3,2,1,0:T(8,128)(2,1)S(1)}, bf16[1,4,4,16,512]{4,3,2,1,0:T(8,128)(2,1)}, u32[]{:S(2)}) copy-start(bf16[1,4,4,16,512]{4,3,2,1,0:T(8,128)(2,1)} %vo_ref.1) | copy-start | bytes 786436
  2.6 4.5 %copy-start.8 = (bf16[32,4,3,3,3]{0,1,4,3,2:T(4,128)(2,1)S(1)}, bf16[32,4,3,3,3]{0,1,4,3,2:T(4,128)(2,1)}, u32[]{:S(2)}) copy-start(bf16[32,4,3,3,3]{0,1,4,3,2:T(4,128)(2,1)} %param.5) | copy-start | bytes 20740
  2.6 4.6 %copy-start.6 = (bf16[64,32,3,3,3]{0,1,4,3,2:T(8,128)(2,1)S(1)}, bf16[64,32,3,3,3]{0,1,4,3,2:T(8,128)(2,1)}, u32[]{:S(2)}) copy-start(bf16[64,32,3,3,3]{0,1,4,3,2:T(8,128)(2,1)} %param.6) | copy-start | bytes 331780
  2.6 7.0 %collective-permute-start.1 = (bf16[320,512]{1,0:T(8,128)(2,1)S(1)}, bf16[320,512]{1,0:T(8,128)(2,1)S(1)}, u32[]{:S(2)}, u32[]{:S(2)}) collective-permute-start(bf16[320,512]{1,0:T(8,128)(2,1)S(1)} %pad_maximum_fusion), channel_id=1, source_target_pairs={{4,0},{8,4},{12,8},{16,12},{20,16},{24,20},{28,24},{5,1},{9,5},{13... | collective-permute-start | bytes 983048 | tf_op jit(solution)/shard_map/ppermute | solution.py:17
  4.0 5.5 %collective-permute-start = (bf16[1,4,3,16,512]{4,3,2,1,0:T(8,128)(2,1)S(1)}, bf16[1,4,3,16,512]{4,3,2,1,0:T(8,128)(2,1)S(1)}, u32[]{:S(2)}, u32[]{:S(2)}) collective-permute-start(bf16[1,4,3,16,512]{4,3,2,1,0:T(8,128)(2,1)S(1)} %slice.30), channel_id=1, source_target_pairs={{0,4},{4,8},{8,12},{12,16},{16,20},{20,24},{24,28},{1,5},{5,9},{9,... | collective-permute-start | bytes 589832 | tf_op jit(solution)/shard_map/ppermute | solution.py:17
  8.7 0.9 %copy-start = (bf16[64,3,3,2,2,32]{0,5,4,3,2,1:T(8,128)(2,1)}, bf16[64,3,3,2,2,32]{0,5,4,3,2,1:T(8,128)(2,1)S(1)}, u32[]{:S(2)}) copy-start(bf16[64,3,3,2,2,32]{0,5,4,3,2,1:T(8,128)(2,1)S(1)} %copy.15) | copy-start | bytes 442372
  9.5 0.7 %copy-start.7 = (bf16[1,4,3,16,512]{4,3,2,1,0:T(8,128)(2,1)}, bf16[1,4,3,16,512]{4,3,2,1,0:T(8,128)(2,1)S(1)}, u32[]{:S(2)}) copy-start(bf16[1,4,3,16,512]{4,3,2,1,0:T(8,128)(2,1)S(1)} %collective-permute-done.vb_ref) | copy-start | bytes 589828
  9.6 0.8 %copy-start.4 = (bf16[320,512]{1,0:T(8,128)(2,1)}, bf16[320,512]{1,0:T(8,128)(2,1)S(1)}, u32[]{:S(2)}) copy-start(bf16[320,512]{1,0:T(8,128)(2,1)S(1)} %collective-permute-done.1.va_ref) | copy-start | bytes 983044
  16.9 4.9 %copy-start.2 = (f32[464,128]{1,0:T(8,128)S(1)}, f32[464,128]{1,0:T(8,128)}, u32[]{:S(2)}) copy-start(f32[464,128]{1,0:T(8,128)} %get-tuple-element.9) | copy-start | bytes 712708
  17.9 3.9 %collective-permute-start.2 = (f32[232,128]{1,0:T(8,128)S(1)}, f32[232,128]{1,0:T(8,128)S(1)}, u32[]{:S(2)}, u32[]{:S(2)}) collective-permute-start(f32[232,128]{1,0:T(8,128)S(1)} %slice_select_fusion), channel_id=1, source_target_pairs={{0,4},{4,0},{8,12},{12,8},{16,20},{20,16},{24,28},{28,24},{1,5},{5... | collective-permute-start | bytes 356360 | tf_op jit(solution)/shard_map/ppermute | solution.py:36
  21.8 7.6 %collective-permute-start.3 = (f32[232,128]{1,0:T(8,128)S(1)}, f32[232,128]{1,0:T(8,128)S(1)}, u32[]{:S(2)}, u32[]{:S(2)}) collective-permute-start(f32[232,128]{1,0:T(8,128)S(1)} %select_add_fusion), channel_id=1, source_target_pairs={{0,8},{4,12},{8,0},{12,4},{16,24},{20,28},{24,16},{28,20},{1,9},{5... | collective-permute-start | bytes 356360 | tf_op jit(solution)/shard_map/ppermute | solution.py:38
  29.4 5.0 %collective-permute-start.4 = (f32[232,128]{1,0:T(8,128)S(1)}, f32[232,128]{1,0:T(8,128)S(1)}, u32[]{:S(2)}, u32[]{:S(2)}) collective-permute-start(f32[232,128]{1,0:T(8,128)S(1)} %add.24), channel_id=1, source_target_pairs={{0,16},{4,20},{8,24},{12,28},{16,0},{20,4},{24,8},{28,12},{1,17},{... | collective-permute-start | bytes 356360 | tf_op jit(solution)/shard_map/ppermute | solution.py:38
  34.4 4.9 %collective-permute-start.5 = (f32[232,128]{1,0:T(8,128)S(1)}, f32[232,128]{1,0:T(8,128)S(1)}, u32[]{:S(2)}, u32[]{:S(2)}) collective-permute-start(f32[232,128]{1,0:T(8,128)S(1)} %add.25), channel_id=1, source_target_pairs={{0,1},{1,0},{2,3},{3,2},{4,5},{5,4},{6,7},{7,6},{8,9},{9,8},{10,11... | collective-permute-start | bytes 356360 | tf_op jit(solution)/shard_map/ppermute | solution.py:38
  39.4 7.2 %copy-start.5 = (bf16[512,256]{1,0:T(8,128)(2,1)S(1)}, bf16[512,256]{1,0:T(8,128)(2,1)}, u32[]{:S(2)}) copy-start(bf16[512,256]{1,0:T(8,128)(2,1)} %get-tuple-element.8) | copy-start | bytes 786436
  39.4 7.1 %collective-permute-start.6 = (f32[232,128]{1,0:T(8,128)S(1)}, f32[232,128]{1,0:T(8,128)S(1)}, u32[]{:S(2)}, u32[]{:S(2)}) collective-permute-start(f32[232,128]{1,0:T(8,128)S(1)} %add.26), channel_id=1, source_target_pairs={{0,2},{1,3},{2,0},{3,1},{4,6},{5,7},{6,4},{7,5},{8,10},{9,11},{10,... | collective-permute-start | bytes 356360 | tf_op jit(solution)/shard_map/ppermute | solution.py:38
  46.5 1.6 %collective-permute-start.7 = (f32[232,128]{1,0:T(8,128)S(1)}, f32[232,128]{1,0:T(8,128)S(1)}, u32[]{:S(2)}, u32[]{:S(2)}) collective-permute-start(f32[232,128]{1,0:T(8,128)S(1)} %add.27), channel_id=1, source_target_pairs={{0,4},{4,0},{8,12},{12,8},{16,20},{20,16},{24,28},{28,24},{1,5},{5... | collective-permute-start | bytes 356360 | tf_op jit(solution)/shard_map/ppermute | solution.py:39
  46.5 0.9 %copy-start.9 = (bf16[64,512]{1,0:T(8,128)(2,1)S(1)}, bf16[64,512]{1,0:T(8,128)(2,1)}, u32[]{:S(2)}) copy-start(bf16[64,512]{1,0:T(8,128)(2,1)} %get-tuple-element.7) | copy-start | bytes 196612

commit v16 on v15

--- a/solution.py
+++ b/solution.py
@@ -17,7 +17,7 @@
     return lax.ppermute(block, axis, route)
 
 
-def _all_sum(x, axes):
+def _all_sum(keep, send, axes):
     steps = []
     for axis in axes:
         n = lax.axis_size(axis)
@@ -27,17 +27,14 @@
             steps.append((axis, n, k))
             k *= 2
     axis0, n0, k0 = steps[0]
-    rows = x.shape[0]
-    half = -(-rows // 16) * 8
-    x = jnp.pad(x, ((0, 2 * half - rows), (0, 0)))
+    assert axis0 == "gz" and k0 == 1
     low = (lax.axis_index(axis0) & k0) == 0
-    lo, hi = x[:half], x[half:]
     pair = [(i, i ^ k0) for i in range(n0)]
-    part = jnp.where(low, lo, hi) + lax.ppermute(jnp.where(low, hi, lo), axis0, pair)
+    part = keep + lax.ppermute(send, axis0, pair)
     for axis, n, k in steps[1:]:
         part = part + lax.ppermute(part, axis, [(i, i ^ k) for i in range(n)])
     other = lax.ppermute(part, axis0, pair)
-    return jnp.where(low, jnp.concatenate([part, other], 0), jnp.concatenate([other, part], 0))[:rows]
+    return jnp.where(low, jnp.concatenate([part, other], 0), jnp.concatenate([other, part], 0))
 
 
 def _sigmoid(v):
@@ -60,8 +57,8 @@
 
 
 def _kernel(vb_ref, vo_ref, va_ref, k1_ref, k2_ref, k2t_ref, cot_ref,
-            lvl_ref, g1_ref, s2_ref,
-            tp, p1, t2, pre1, p2, bt, gs, gacc, b1, g1s, qs, s1s):
+            lvl_ref, g1_ref, keep_ref, send_ref,
+            tp, p1, t2, pre1, p2, bt, gs, gacc, b1, g1s, qs, s1s, s2_ref):
     c0, ny, nx = vo_ref.shape[1], vo_ref.shape[3], vo_ref.shape[4]
     lanes = nx // 4
     nzi = tp.shape[0]
@@ -197,6 +194,11 @@
             out_rows.append(acc)
     n_s2 = 27 * qi
     s2_ref[n_s2:n_s2 + 27] = jnp.concatenate(out_rows, axis=0)
+    half_rows = keep_ref.shape[0]
+    low = jnp.full((half_rows, s2_ref.shape[1]), lax.axis_index("gz") % 2) == 0
+    lo_h, hi_h = s2_ref[:half_rows], s2_ref[half_rows:]
+    keep_ref[...] = jnp.where(low, lo_h, hi_h)
+    send_ref[...] = jnp.where(low, hi_h, lo_h)
 
     n2 = 2 * lanes
     row = lax.broadcasted_iota(jnp.int32, (n2, n2), 0)
@@ -245,12 +247,13 @@
     n_g1 = 27 * c0 * c1 // (2 * c2)
     n_pay = -(-(n_s2 + n_g1) // 16) * 16
     vm = pltpu.VMEM
-    lvl, g1, pay = pl.pallas_call(
+    lvl, g1, keep, send = pl.pallas_call(
         _kernel,
         out_shape=(
             jax.ShapeDtypeStruct((c2, n2), BF16),
             jax.ShapeDtypeStruct((2 * ny1 * c1, 2 * q), BF16),
-            jax.ShapeDtypeStruct((n_pay, 2 * c2), F32),
+            jax.ShapeDtypeStruct((n_pay // 2, 2 * c2), F32),
+            jax.ShapeDtypeStruct((n_pay // 2, 2 * c2), F32),
         ),
         scratch_shapes=[
             vm((nzi, ny + 1, 8 * c0, q), BF16),
@@ -265,6 +268,7 @@
             vm((2 * ny1 * c1, 2 * q), BF16),
             vm((8 * c0 * ny, nzi * q), BF16),
             vm((k1m.shape[1], 2 * k1m.shape[0]), F32),
+            vm((n_pay, 2 * c2), F32),
         ],
         cost_estimate=pl.CostEstimate(flops=60_000_000, transcendentals=200_000, bytes_accessed=3_000_000),
     )(below, volume, above, k1m, k2m, k2t, cot)
@@ -272,7 +276,7 @@
     level_two = lvl.reshape(1, c2, 1, ny2, n2 // ny2)
     grad_one = g1.reshape(2, ny1, c1, 2 * q).transpose(2, 0, 1, 3)[None]
 
-    total = _all_sum(pay, ("gz", "sa"))
+    total = _all_sum(keep, send, ("gz", "sa"))
     samples = volume.shape[0] * lax.axis_size("sa")
     cells_one = samples * (nz // 2) * lax.axis_size("gz") * ny1 * (nx // 2)
     cells_two = samples * cotangent.shape[2] * lax.axis_size("gz") * cotangent.shape[3] * cotangent.shape[4]

time: 50.2 us -> 50.2 us (level)
    select_n x1 -> x0, other arithmetic: 1.01 us -> none  [_all_sum(): jnp.where(low, hi, lo)]
    add x1, other arithmetic: 0.02 us -> 0.92 us  [_all_sum(): part = keep + lax.ppermute(send, axis0, pair)]
    unnamed x21 -> x19, local copies, waits for them, and re-layouts: 1.66 us -> 1.66 us
where the time goes in v16:
time: 50.2 us; the launch traced here: 49.9 us
  starting transfers between devices  17.7 us (35%)
  waiting for transfers between devices  15.4 us (31%)
  local copies, waits for them, and re-layouts  6.84 us (14%)
  Pallas kernels  6.52 us (13%)
  other arithmetic  2.49 us (5%)
  between operations  0.93 us (2%)
    ppermute x4, waiting for transfers between devices, _all_sum(): part = part + lax.ppermute(part, axis, [(i, i ^ k) for i in range(n)])  14.2 us
    ppermute x4, starting transfers between devices, _all_sum(): part = part + lax.ppermute(part, axis, [(i, i ^ k) for i in range(n)])  10.4 us
    pallas_call x1, Pallas kernels, per_device(): pl.pallas_call(_kernel, out_shape=(jax.ShapeDtypeStruct((c2, n2), BF16),...  6.52 us
    ppermute x2, starting transfers between devices, shifted(): return lax.ppermute(block, axis, route)  4.47 us
    ppermute x1, starting transfers between devices, _all_sum(): part = keep + lax.ppermute(send, axis0, pair)  2.82 us
    unnamed x19, local copies, waits for them, and re-layouts  1.66 us
    ppermute x1, waiting for transfers between devices, _all_sum(): part = keep + lax.ppermute(send, axis0, pair)  1.18 us
    concatenate x1, other arithmetic, per_device(): jnp.concatenate([volume[0].reshape(-1, nx), cot], 0)  1.04 us
  transfers between devices with their start and end apart: 8, of which 5 were waited for; matrix products, arithmetic and copies ran while one was open for 8% of the time, Pallas kernels for 0%

profile of v16, /device:TPU:0, one launch (start us, length us, event | category | flops | bytes accessed | tf_op | source)
XLA Modules:
  0.0 49.9 jit_solution(8510184864151269823)
XLA Ops:
  0.6 0.9 %copy.25 = bf16[8,8,4,128]{3,1,2,0:T(8,128)(2,1)S(1)} copy(bf16[8,8,4,128]{3,2,1,0:T(4,128)(2,1)} %bitcast.54) | data formatting | bytes 131072
  1.5 0.0 copy-start.2
  1.5 0.0 copy-start.1
  1.5 1.0 %pad_maximum_fusion = bf16[320,512]{1,0:T(8,128)(2,1)S(1)} fusion(bf16[64,512]{1,0:T(8,128)(2,1)S(1)} %bitcast.44, bf16[256,512]{1,0:T(8,128)(2,1)} %bitcast.42), kind=kLoop, calls=%fused_computation | loop fusion | flops 655360 | bytes 655360 | tf_op jit(solution)/shard_map/concatenate | solution.py:236
  2.5 0.0 copy-done.2
  2.6 0.0 copy-start.7
  2.6 0.0 copy-start.5
  2.6 1.4 %collective-permute-start.1 = (bf16[320,512]{1,0:T(8,128)(2,1)S(1)}, bf16[320,512]{1,0:T(8,128)(2,1)S(1)}, u32[]{:S(2)}, u32[]{:S(2)}) collective-permute-start(bf16[320,512]{1,0:T(8,128)(2,1)S(1)} %pad_maximum_fusion), channel_id=1, source_target_pairs={{4,0},{8,4},{12,8},{16,12},{20,16},{24,20},{28,24},{5,1},{9,5},{13... | collective-permute-start | bytes 983048 | tf_op jit(solution)/shard_map/ppermute | solution.py:17
  4.0 0.0 copy-done.1
  4.0 3.0 %collective-permute-start = (bf16[1,4,3,16,512]{4,3,2,1,0:T(8,128)(2,1)S(1)}, bf16[1,4,3,16,512]{4,3,2,1,0:T(8,128)(2,1)S(1)}, u32[]{:S(2)}, u32[]{:S(2)}) collective-permute-start(bf16[1,4,3,16,512]{4,3,2,1,0:T(8,128)(2,1)S(1)} %slice.24), channel_id=1, source_target_pairs={{0,4},{4,8},{8,12},{12,16},{16,20},{20,24},{24,28},{1,5},{5,9},{9,... | collective-permute-start | bytes 589832 | tf_op jit(solution)/shard_map/ppermute | solution.py:17
  7.1 0.0 copy-done.7
  7.2 0.0 copy-done.5
  7.3 0.1 pad_maximum_fusion.3
  7.4 0.1 maximum_bitcast_fusion.1
  7.4 0.1 maximum_bitcast_fusion
  7.5 0.1 pad_maximum_fusion.2
  7.7 0.1 copy.14
  7.8 0.1 reshape.29
  7.9 0.7 %copy.16.k1_ref = bf16[64,288]{1,0:T(8,128)(2,1)} copy(bf16[64,288]{0,1:T(8,128)(2,1)S(1)} %reshape.29) | data formatting | bytes 73728 | tf_op jit(solution)/shard_map/reshape | solution.py:217
  8.6 0.1 pad_maximum_fusion.1
  8.7 0.0 copy-start
  8.7 0.8 %copy.17.k2_ref = bf16[64,1152]{1,0:T(8,128)(2,1)} copy(bf16[64,1152]{0,1:T(8,128)(2,1)S(1)} %bitcast.40) | data formatting | bytes 294912 | tf_op jit(solution)/shard_map/reshape | solution.py:225
  9.5 0.0 collective-permute-done.vb_ref
  9.5 0.0 copy-start.6
  9.5 0.0 collective-permute-done.1.va_ref
  9.5 0.0 copy-start.3
  9.6 0.0 copy-done
  9.6 0.6 %copy-done.6 = bf16[1,4,3,16,512]{4,3,2,1,0:T(8,128)(2,1)} copy-done((bf16[1,4,3,16,512]{4,3,2,1,0:T(8,128)(2,1)}, bf16[1,4,3,16,512]{4,3,2,1,0:T(8,128)(2,1)S(1)}, u32[]{:S(2)}) %copy-start.6) | copy-done | bytes 196632
  10.2 0.1 copy-done.3
  10.3 6.5 %shard_map.75 = (bf16[64,512]{1,0:T(8,128)(2,1)}, bf16[512,256]{1,0:T(8,128)(2,1)}, f32[232,128]{1,0:T(8,128)}, f32[232,128]{1,0:T(8,128)}) custom-call(bf16[1,4,3,16,512]{4,3,2,1,0:T(8,128)(2,1)} %copy-done.6, bf16[1,4,4,16,512]{4,3,2,1,0:T(8,128)(2,1)} %vo_ref.1, bf16[320,512]{1,0:T(8,128)(2,1)} %copy-done.3, bf16[64,288]{1,0:T(8,128)(2,1)} %copy.16.k1_ref, ...), custom_call_target="tpu_custom_call" | custom-call | flops 60000000 | bytes 3000000 | tf_op jit(solution)/shard_map/pallas_call | solution.py:250
  16.8 2.8 %collective-permute-start.2 = (f32[232,128]{1,0:T(8,128)}, f32[232,128]{1,0:T(8,128)S(1)}, u32[]{:S(2)}, u32[]{:S(2)}) collective-permute-start(f32[232,128]{1,0:T(8,128)} %get-tuple-element.11), channel_id=1, source_target_pairs={{0,4},{4,0},{8,12},{12,8},{16,20},{20,16},{24,28},{28,24},{1,5},{5... | collective-permute-start | bytes 356360 | tf_op jit(solution)/shard_map/ppermute | solution.py:33
  19.7 1.2 %collective-permute-done.2 = f32[232,128]{1,0:T(8,128)S(1)} collective-permute-done((f32[232,128]{1,0:T(8,128)}, f32[232,128]{1,0:T(8,128)S(1)}, u32[]{:S(2)}, u32[]{:S(2)}) %collective-permute-start.2) | collective-permute-done | bytes 118816 | tf_op jit(solution)/shard_map/ppermute | solution.py:33
  20.8 0.9 %add.23 = f32[232,128]{1,0:T(8,128)S(1)} add(f32[232,128]{1,0:T(8,128)} %get-tuple-element.10, f32[232,128]{1,0:T(8,128)S(1)} %collective-permute-done.2) | non-fusion elementwise | flops 29696 | bytes 356352 | tf_op jit(solution)/shard_map/add | solution.py:33
  21.8 3.9 %collective-permute-start.3 = (f32[232,128]{1,0:T(8,128)S(1)}, f32[232,128]{1,0:T(8,128)S(1)}, u32[]{:S(2)}, u32[]{:S(2)}) collective-permute-start(f32[232,128]{1,0:T(8,128)S(1)} %add.23), channel_id=1, source_target_pairs={{0,8},{4,12},{8,0},{12,4},{16,24},{20,28},{24,16},{28,20},{1,9},{5... | collective-permute-start | bytes 356360 | tf_op jit(solution)/shard_map/ppermute | solution.py:35
  25.6 3.7 %collective-permute-done.3 = f32[232,128]{1,0:T(8,128)S(1)} collective-permute-done((f32[232,128]{1,0:T(8,128)S(1)}, f32[232,128]{1,0:T(8,128)S(1)}, u32[]{:S(2)}, u32[]{:S(2)}) %collective-permute-start.3) | collective-permute-done | bytes 118816 | tf_op jit(solution)/shard_map/ppermute | solution.py:35
  29.4 2.2 %collective-permute-start.4 = (f32[232,128]{1,0:T(8,128)S(1)}, f32[232,128]{1,0:T(8,128)S(1)}, u32[]{:S(2)}, u32[]{:S(2)}) collective-permute-start(f32[232,128]{1,0:T(8,128)S(1)} %add.24), channel_id=1, source_target_pairs={{0,16},{4,20},{8,24},{12,28},{16,0},{20,4},{24,8},{28,12},{1,17},{... | collective-permute-start | bytes 356360 | tf_op jit(solution)/shard_map/ppermute | solution.py:35
  31.6 2.8 %collective-permute-done.4 = f32[232,128]{1,0:T(8,128)S(1)} collective-permute-done((f32[232,128]{1,0:T(8,128)S(1)}, f32[232,128]{1,0:T(8,128)S(1)}, u32[]{:S(2)}, u32[]{:S(2)}) %collective-permute-start.4) | collective-permute-done | bytes 118816 | tf_op jit(solution)/shard_map/ppermute | solution.py:35
  34.4 1.6 %collective-permute-start.5 = (f32[232,128]{1,0:T(8,128)S(1)}, f32[232,128]{1,0:T(8,128)S(1)}, u32[]{:S(2)}, u32[]{:S(2)}) collective-permute-start(f32[232,128]{1,0:T(8,128)S(1)} %add.25), channel_id=1, source_target_pairs={{0,1},{1,0},{2,3},{3,2},{4,5},{5,4},{6,7},{7,6},{8,9},{9,8},{10,11... | collective-permute-start | bytes 356360 | tf_op jit(solution)/shard_map/ppermute | solution.py:35
  36.1 3.3 %collective-permute-done.5 = f32[232,128]{1,0:T(8,128)S(1)} collective-permute-done((f32[232,128]{1,0:T(8,128)S(1)}, f32[232,128]{1,0:T(8,128)S(1)}, u32[]{:S(2)}, u32[]{:S(2)}) %collective-permute-start.5) | collective-permute-done | bytes 118816 | tf_op jit(solution)/shard_map/ppermute | solution.py:35
  39.4 0.0 copy-start.4
  39.4 2.7 %collective-permute-start.6 = (f32[232,128]{1,0:T(8,128)S(1)}, f32[232,128]{1,0:T(8,128)S(1)}, u32[]{:S(2)}, u32[]{:S(2)}) collective-permute-start(f32[232,128]{1,0:T(8,128)S(1)} %add.26), channel_id=1, source_target_pairs={{0,2},{1,3},{2,0},{3,1},{4,6},{5,7},{6,4},{7,5},{8,10},{9,11},{10,... | collective-permute-start | bytes 356360 | tf_op jit(solution)/shard_map/ppermute | solution.py:35
  42.0 4.4 %collective-permute-done.6 = f32[232,128]{1,0:T(8,128)S(1)} collective-permute-done((f32[232,128]{1,0:T(8,128)S(1)}, f32[232,128]{1,0:T(8,128)S(1)}, u32[]{:S(2)}, u32[]{:S(2)}) %collective-permute-start.6) | collective-permute-done | bytes 118816 | tf_op jit(solution)/shard_map/ppermute | solution.py:35
  46.5 0.1 collective-permute-start.7
  46.5 0.0 copy-done.4
  46.6 0.0 copy-start.8
  46.6 0.9 %copy.24 = bf16[2,8,32,256]{3,1,0,2:T(8,128)(2,1)} copy(bf16[2,8,32,256]{3,2,1,0:T(8,128)(2,1)S(1)} %bitcast.47) | data formatting | bytes 524288 | tf_op jit(solution)/shard_map/reshape | solution.py:277
  47.4 0.0 copy-done.8
  47.4 0.6 %reshape.31 = bf16[1,64,1,4,128]{4,3,1,2,0:T(4,128)(2,1)} reshape(bf16[64,512]{1,0:T(8,128)(2,1)S(1)} %copy-done.8) | data formatting | bytes 131072 | tf_op jit(solution)/shard_map/reshape | solution.py:276
  48.1 0.0 collective-permute-done.7
  48.1 0.3 reshape.34
  48.4 0.8 %copy.19 = f32[27,2,16,64]{3,2,1,0:T(8,128)} copy(f32[27,2,16,64]{3,1,2,0:T(2,128)S(1)} %bitcast.43) | data formatting | bytes 442368 | tf_op jit(solution)/shard_map/transpose | solution.py:286
  49.2 0.7 %reshape.33 = f32[3,3,3,4,32]{4,3,2,1,0:T(4,128)} reshape(f32[27,128]{1,0:T(8,128)S(1)} %slice_multiply_fusion.1) | data formatting | bytes 27648 | tf_op jit(solution)/shard_map/reshape | solution.py:285
  (16 shorter events, 0.3 us)
Async XLA Ops:
  1.5 1.1 %copy-start.2 = (bf16[8,8,4,128]{3,1,2,0:T(8,128)(2,1)}, bf16[8,8,4,128]{3,1,2,0:T(8,128)(2,1)S(1)}, u32[]{:S(2)}) copy-start(bf16[8,8,4,128]{3,1,2,0:T(8,128)(2,1)S(1)} %copy.25) | copy-start | bytes 196612
  1.5 2.5 %copy-start.1 = (bf16[1,4,4,16,512]{4,3,2,1,0:T(8,128)(2,1)S(1)}, bf16[1,4,4,16,512]{4,3,2,1,0:T(8,128)(2,1)}, u32[]{:S(2)}) copy-start(bf16[1,4,4,16,512]{4,3,2,1,0:T(8,128)(2,1)} %vo_ref.1) | copy-start | bytes 786436
  2.6 4.5 %copy-start.7 = (bf16[32,4,3,3,3]{0,1,4,3,2:T(4,128)(2,1)S(1)}, bf16[32,4,3,3,3]{0,1,4,3,2:T(4,128)(2,1)}, u32[]{:S(2)}) copy-start(bf16[32,4,3,3,3]{0,1,4,3,2:T(4,128)(2,1)} %param.5) | copy-start | bytes 20740
  2.6 4.6 %copy-start.5 = (bf16[64,32,3,3,3]{0,1,4,3,2:T(8,128)(2,1)S(1)}, bf16[64,32,3,3,3]{0,1,4,3,2:T(8,128)(2,1)}, u32[]{:S(2)}) copy-start(bf16[64,32,3,3,3]{0,1,4,3,2:T(8,128)(2,1)} %param.6) | copy-start | bytes 331780
  2.6 7.0 %collective-permute-start.1 = (bf16[320,512]{1,0:T(8,128)(2,1)S(1)}, bf16[320,512]{1,0:T(8,128)(2,1)S(1)}, u32[]{:S(2)}, u32[]{:S(2)}) collective-permute-start(bf16[320,512]{1,0:T(8,128)(2,1)S(1)} %pad_maximum_fusion), channel_id=1, source_target_pairs={{4,0},{8,4},{12,8},{16,12},{20,16},{24,20},{28,24},{5,1},{9,5},{13... | collective-permute-start | bytes 983048 | tf_op jit(solution)/shard_map/ppermute | solution.py:17
  4.0 5.5 %collective-permute-start = (bf16[1,4,3,16,512]{4,3,2,1,0:T(8,128)(2,1)S(1)}, bf16[1,4,3,16,512]{4,3,2,1,0:T(8,128)(2,1)S(1)}, u32[]{:S(2)}, u32[]{:S(2)}) collective-permute-start(bf16[1,4,3,16,512]{4,3,2,1,0:T(8,128)(2,1)S(1)} %slice.24), channel_id=1, source_target_pairs={{0,4},{4,8},{8,12},{12,16},{16,20},{20,24},{24,28},{1,5},{5,9},{9,... | collective-permute-start | bytes 589832 | tf_op jit(solution)/shard_map/ppermute | solution.py:17
  8.7 0.8 %copy-start = (bf16[64,3,3,2,2,32]{0,5,4,3,2,1:T(8,128)(2,1)}, bf16[64,3,3,2,2,32]{0,5,4,3,2,1:T(8,128)(2,1)S(1)}, u32[]{:S(2)}) copy-start(bf16[64,3,3,2,2,32]{0,5,4,3,2,1:T(8,128)(2,1)S(1)} %copy.15) | copy-start | bytes 442372
  9.5 0.7 %copy-start.6 = (bf16[1,4,3,16,512]{4,3,2,1,0:T(8,128)(2,1)}, bf16[1,4,3,16,512]{4,3,2,1,0:T(8,128)(2,1)S(1)}, u32[]{:S(2)}) copy-start(bf16[1,4,3,16,512]{4,3,2,1,0:T(8,128)(2,1)S(1)} %collective-permute-done.vb_ref) | copy-start | bytes 589828
  9.5 0.8 %copy-start.3 = (bf16[320,512]{1,0:T(8,128)(2,1)}, bf16[320,512]{1,0:T(8,128)(2,1)S(1)}, u32[]{:S(2)}) copy-start(bf16[320,512]{1,0:T(8,128)(2,1)S(1)} %collective-permute-done.1.va_ref) | copy-start | bytes 983044
  16.8 4.0 %collective-permute-start.2 = (f32[232,128]{1,0:T(8,128)}, f32[232,128]{1,0:T(8,128)S(1)}, u32[]{:S(2)}, u32[]{:S(2)}) collective-permute-start(f32[232,128]{1,0:T(8,128)} %get-tuple-element.11), channel_id=1, source_target_pairs={{0,4},{4,0},{8,12},{12,8},{16,20},{20,16},{24,28},{28,24},{1,5},{5... | collective-permute-start | bytes 356360 | tf_op jit(solution)/shard_map/ppermute | solution.py:33
  21.8 7.6 %collective-permute-start.3 = (f32[232,128]{1,0:T(8,128)S(1)}, f32[232,128]{1,0:T(8,128)S(1)}, u32[]{:S(2)}, u32[]{:S(2)}) collective-permute-start(f32[232,128]{1,0:T(8,128)S(1)} %add.23), channel_id=1, source_target_pairs={{0,8},{4,12},{8,0},{12,4},{16,24},{20,28},{24,16},{28,20},{1,9},{5... | collective-permute-start | bytes 356360 | tf_op jit(solution)/shard_map/ppermute | solution.py:35
  29.4 5.0 %collective-permute-start.4 = (f32[232,128]{1,0:T(8,128)S(1)}, f32[232,128]{1,0:T(8,128)S(1)}, u32[]{:S(2)}, u32[]{:S(2)}) collective-permute-start(f32[232,128]{1,0:T(8,128)S(1)} %add.24), channel_id=1, source_target_pairs={{0,16},{4,20},{8,24},{12,28},{16,0},{20,4},{24,8},{28,12},{1,17},{... | collective-permute-start | bytes 356360 | tf_op jit(solution)/shard_map/ppermute | solution.py:35
  34.4 4.9 %collective-permute-start.5 = (f32[232,128]{1,0:T(8,128)S(1)}, f32[232,128]{1,0:T(8,128)S(1)}, u32[]{:S(2)}, u32[]{:S(2)}) collective-permute-start(f32[232,128]{1,0:T(8,128)S(1)} %add.25), channel_id=1, source_target_pairs={{0,1},{1,0},{2,3},{3,2},{4,5},{5,4},{6,7},{7,6},{8,9},{9,8},{10,11... | collective-permute-start | bytes 356360 | tf_op jit(solution)/shard_map/ppermute | solution.py:35
  39.4 7.2 %copy-start.4 = (bf16[512,256]{1,0:T(8,128)(2,1)S(1)}, bf16[512,256]{1,0:T(8,128)(2,1)}, u32[]{:S(2)}) copy-start(bf16[512,256]{1,0:T(8,128)(2,1)} %get-tuple-element.9) | copy-start | bytes 786436
  39.4 7.1 %collective-permute-start.6 = (f32[232,128]{1,0:T(8,128)S(1)}, f32[232,128]{1,0:T(8,128)S(1)}, u32[]{:S(2)}, u32[]{:S(2)}) collective-permute-start(f32[232,128]{1,0:T(8,128)S(1)} %add.26), channel_id=1, source_target_pairs={{0,2},{1,3},{2,0},{3,1},{4,6},{5,7},{6,4},{7,5},{8,10},{9,11},{10,... | collective-permute-start | bytes 356360 | tf_op jit(solution)/shard_map/ppermute | solution.py:35
  46.5 1.6 %collective-permute-start.7 = (f32[232,128]{1,0:T(8,128)S(1)}, f32[232,128]{1,0:T(8,128)S(1)}, u32[]{:S(2)}, u32[]{:S(2)}) collective-permute-start(f32[232,128]{1,0:T(8,128)S(1)} %add.27), channel_id=1, source_target_pairs={{0,4},{4,0},{8,12},{12,8},{16,20},{20,16},{24,28},{28,24},{1,5},{5... | collective-permute-start | bytes 356360 | tf_op jit(solution)/shard_map/ppermute | solution.py:36
  46.6 0.9 %copy-start.8 = (bf16[64,512]{1,0:T(8,128)(2,1)S(1)}, bf16[64,512]{1,0:T(8,128)(2,1)}, u32[]{:S(2)}) copy-start(bf16[64,512]{1,0:T(8,128)(2,1)} %get-tuple-element.8) | copy-start | bytes 196612

commit v17 on v15

--- a/solution.py
+++ b/solution.py
@@ -17,7 +17,7 @@
     return lax.ppermute(block, axis, route)
 
 
-def _all_sum(x, axes):
+def _all_sum(x, axes, early=()):
     steps = []
     for axis in axes:
         n = lax.axis_size(axis)
@@ -34,10 +34,11 @@
     lo, hi = x[:half], x[half:]
     pair = [(i, i ^ k0) for i in range(n0)]
     part = jnp.where(low, lo, hi) + lax.ppermute(jnp.where(low, hi, lo), axis0, pair)
+    part, early = lax.optimization_barrier((part, early))
     for axis, n, k in steps[1:]:
         part = part + lax.ppermute(part, axis, [(i, i ^ k) for i in range(n)])
     other = lax.ppermute(part, axis0, pair)
-    return jnp.where(low, jnp.concatenate([part, other], 0), jnp.concatenate([other, part], 0))[:rows]
+    return jnp.where(low, jnp.concatenate([part, other], 0), jnp.concatenate([other, part], 0))[:rows], early
 
 
 def _sigmoid(v):
@@ -272,7 +273,8 @@
     level_two = lvl.reshape(1, c2, 1, ny2, n2 // ny2)
     grad_one = g1.reshape(2, ny1, c1, 2 * q).transpose(2, 0, 1, 3)[None]
 
-    total = _all_sum(pay, ("gz", "sa"))
+
+    total, (level_two, grad_one) = _all_sum(pay, ("gz", "sa"), (level_two, grad_one))
     samples = volume.shape[0] * lax.axis_size("sa")
     cells_one = samples * (nz // 2) * lax.axis_size("gz") * ny1 * (nx // 2)
     cells_two = samples * cotangent.shape[2] * lax.axis_size("gz") * cotangent.shape[3] * cotangent.shape[4]

time: 50.2 us -> 50.8 us (1.012)
    ppermute x1, waiting for transfers between devices: 0.01 us -> 1.32 us  [_all_sum(): other = lax.ppermute(part, axis0, pair)]
    ppermute x1, waiting for transfers between devices: 0.97 us -> 0.01 us  [_all_sum(): lax.ppermute(jnp.where(low, hi, lo), axis0, pair)]
where the time goes in v17:
time: 50.8 us; the launch traced here: 50.5 us
  starting transfers between devices  18.1 us (36%)
  waiting for transfers between devices  15.5 us (31%)
  local copies, waits for them, and re-layouts  6.84 us (13%)
  Pallas kernels  6.53 us (13%)
  other arithmetic  2.61 us (5%)
  between operations  0.91 us (2%)
    ppermute x4, waiting for transfers between devices, _all_sum(): part = part + lax.ppermute(part, axis, [(i, i ^ k) for i in range(n)])  14.2 us
    ppermute x4, starting transfers between devices, _all_sum(): part = part + lax.ppermute(part, axis, [(i, i ^ k) for i in range(n)])  10.7 us
    pallas_call x1, Pallas kernels, per_device(): pl.pallas_call(_kernel, out_shape=(jax.ShapeDtypeStruct((c2, n2), BF16),...  6.53 us
    ppermute x2, starting transfers between devices, shifted(): return lax.ppermute(block, axis, route)  4.47 us
    ppermute x1, starting transfers between devices, _all_sum(): lax.ppermute(jnp.where(low, hi, lo), axis0, pair)  2.88 us
    unnamed x21, local copies, waits for them, and re-layouts  1.66 us
    ppermute x1, waiting for transfers between devices, _all_sum(): other = lax.ppermute(part, axis0, pair)  1.32 us
    concatenate x1, other arithmetic, per_device(): jnp.concatenate([volume[0].reshape(-1, nx), cot], 0)  1.04 us
  transfers between devices with their start and end apart: 8, of which 5 were waited for; matrix products, arithmetic and copies ran while one was open for 8% of the time, Pallas kernels for 0%

profile of v17, /device:TPU:0, one launch (start us, length us, event | category | flops | bytes accessed | tf_op | source)
XLA Modules:
  0.0 50.5 jit_solution(2072042007045209527)
XLA Ops:
  0.6 0.9 %copy.25 = bf16[8,8,4,128]{3,1,2,0:T(8,128)(2,1)S(1)} copy(bf16[8,8,4,128]{3,2,1,0:T(4,128)(2,1)} %bitcast.54) | data formatting | bytes 131072
  1.5 0.0 copy-start.3
  1.5 0.0 copy-start.1
  1.5 1.0 %pad_maximum_fusion = bf16[320,512]{1,0:T(8,128)(2,1)S(1)} fusion(bf16[64,512]{1,0:T(8,128)(2,1)S(1)} %bitcast.44, bf16[256,512]{1,0:T(8,128)(2,1)} %bitcast.42), kind=kLoop, calls=%fused_computation | loop fusion | flops 655360 | bytes 655360 | tf_op jit(solution)/shard_map/concatenate | solution.py:235
  2.5 0.0 copy-done.3
  2.6 0.0 copy-start.8
  2.6 0.0 copy-start.6
  2.6 1.4 %collective-permute-start.1 = (bf16[320,512]{1,0:T(8,128)(2,1)S(1)}, bf16[320,512]{1,0:T(8,128)(2,1)S(1)}, u32[]{:S(2)}, u32[]{:S(2)}) collective-permute-start(bf16[320,512]{1,0:T(8,128)(2,1)S(1)} %pad_maximum_fusion), channel_id=1, source_target_pairs={{4,0},{8,4},{12,8},{16,12},{20,16},{24,20},{28,24},{5,1},{9,5},{13... | collective-permute-start | bytes 983048 | tf_op jit(solution)/shard_map/ppermute | solution.py:17
  4.0 0.0 copy-done.1
  4.0 3.0 %collective-permute-start = (bf16[1,4,3,16,512]{4,3,2,1,0:T(8,128)(2,1)S(1)}, bf16[1,4,3,16,512]{4,3,2,1,0:T(8,128)(2,1)S(1)}, u32[]{:S(2)}, u32[]{:S(2)}) collective-permute-start(bf16[1,4,3,16,512]{4,3,2,1,0:T(8,128)(2,1)S(1)} %slice.30), channel_id=1, source_target_pairs={{0,4},{4,8},{8,12},{12,16},{16,20},{20,24},{24,28},{1,5},{5,9},{9,... | collective-permute-start | bytes 589832 | tf_op jit(solution)/shard_map/ppermute | solution.py:17
  7.1 0.0 copy-done.8
  7.2 0.0 copy-done.6
  7.3 0.1 pad_maximum_fusion.3
  7.4 0.1 maximum_bitcast_fusion.1
  7.5 0.1 maximum_bitcast_fusion
  7.5 0.1 pad_maximum_fusion.2
  7.7 0.1 copy.14
  7.8 0.1 reshape.29
  7.9 0.7 %copy.16.k1_ref = bf16[64,288]{1,0:T(8,128)(2,1)} copy(bf16[64,288]{0,1:T(8,128)(2,1)S(1)} %reshape.29) | data formatting | bytes 73728 | tf_op jit(solution)/shard_map/reshape | solution.py:216
  8.6 0.1 pad_maximum_fusion.1
  8.7 0.0 copy-start
  8.7 0.8 %copy.17.k2_ref = bf16[64,1152]{1,0:T(8,128)(2,1)} copy(bf16[64,1152]{0,1:T(8,128)(2,1)S(1)} %bitcast.40) | data formatting | bytes 294912 | tf_op jit(solution)/shard_map/reshape | solution.py:224
  9.5 0.0 collective-permute-done.vb_ref
  9.5 0.0 copy-start.7
  9.5 0.0 collective-permute-done.1.va_ref
  9.6 0.0 copy-start.4
  9.6 0.0 copy-done
  9.6 0.6 %copy-done.7 = bf16[1,4,3,16,512]{4,3,2,1,0:T(8,128)(2,1)} copy-done((bf16[1,4,3,16,512]{4,3,2,1,0:T(8,128)(2,1)}, bf16[1,4,3,16,512]{4,3,2,1,0:T(8,128)(2,1)S(1)}, u32[]{:S(2)}) %copy-start.7) | copy-done | bytes 196632
  10.2 0.1 copy-done.4
  10.3 6.5 %shard_map.75 = (bf16[64,512]{1,0:T(8,128)(2,1)}, bf16[512,256]{1,0:T(8,128)(2,1)}, f32[464,128]{1,0:T(8,128)}) custom-call(bf16[1,4,3,16,512]{4,3,2,1,0:T(8,128)(2,1)} %copy-done.7, bf16[1,4,4,16,512]{4,3,2,1,0:T(8,128)(2,1)} %vo_ref.1, bf16[320,512]{1,0:T(8,128)(2,1)} %copy-done.4, bf16[64,288]{1,0:T(8,128)(2,1)} %copy.16.k1_ref, ...), custom_call_target="tpu_custom_call" | custom-call | flops 60000000 | bytes 3000000 | tf_op jit(solution)/shard_map/pallas_call | solution.py:249
  16.9 0.0 copy-start.5
  16.9 1.0 %slice_select_fusion = f32[232,128]{1,0:T(8,128)S(1)} fusion(f32[464,128]{1,0:T(8,128)} %get-tuple-element.10, pred[]{:T(512)S(6)} %eq.3), kind=kLoop, calls=%fused_computation.9 | loop fusion | flops 29696 | bytes 356353 | tf_op jit(solution)/shard_map/jit(_where)/select_n | solution.py:36
  17.9 2.9 %collective-permute-start.2 = (f32[232,128]{1,0:T(8,128)S(1)}, f32[232,128]{1,0:T(8,128)S(1)}, u32[]{:S(2)}, u32[]{:S(2)}) collective-permute-start(f32[232,128]{1,0:T(8,128)S(1)} %slice_select_fusion), channel_id=1, source_target_pairs={{0,4},{4,0},{8,12},{12,8},{16,20},{20,16},{24,28},{28,24},{1,5},{5... | collective-permute-start | bytes 356360 | tf_op jit(solution)/shard_map/ppermute | solution.py:36
  20.8 0.0 copy-done.5
  20.8 0.0 copy-start.9
  20.8 0.0 copy-start.2
  20.8 0.9 %copy.24 = bf16[2,8,32,256]{3,1,0,2:T(8,128)(2,1)} copy(bf16[2,8,32,256]{3,2,1,0:T(8,128)(2,1)S(1)} %bitcast.48) | data formatting | bytes 524288 | tf_op jit(solution)/shard_map/reshape | solution.py:274
  21.6 0.0 copy-done.9
  21.6 0.6 %reshape.31 = bf16[1,64,1,4,128]{4,3,1,2,0:T(4,128)(2,1)} reshape(bf16[64,512]{1,0:T(8,128)(2,1)S(1)} %copy-done.9) | data formatting | bytes 131072 | tf_op jit(solution)/shard_map/reshape | solution.py:273
  22.3 0.0 collective-permute-done.2
  22.3 0.0 copy-done.2
  22.3 3.9 %collective-permute-start.3 = (f32[232,128]{1,0:T(8,128)S(1)}, f32[232,128]{1,0:T(8,128)S(1)}, u32[]{:S(2)}, u32[]{:S(2)}) collective-permute-start(f32[232,128]{1,0:T(8,128)S(1)} %select_add_fusion), channel_id=1, source_target_pairs={{0,8},{4,12},{8,0},{12,4},{16,24},{20,28},{24,16},{28,20},{1,9},{5... | collective-permute-start | bytes 356360 | tf_op jit(solution)/shard_map/ppermute | solution.py:39
  26.2 3.4 %collective-permute-done.3 = f32[232,128]{1,0:T(8,128)S(1)} collective-permute-done((f32[232,128]{1,0:T(8,128)S(1)}, f32[232,128]{1,0:T(8,128)S(1)}, u32[]{:S(2)}, u32[]{:S(2)}) %collective-permute-start.3) | collective-permute-done | bytes 118816 | tf_op jit(solution)/shard_map/ppermute | solution.py:39
  29.6 2.5 %collective-permute-start.4 = (f32[232,128]{1,0:T(8,128)S(1)}, f32[232,128]{1,0:T(8,128)S(1)}, u32[]{:S(2)}, u32[]{:S(2)}) collective-permute-start(f32[232,128]{1,0:T(8,128)S(1)} %add.24), channel_id=1, source_target_pairs={{0,16},{4,20},{8,24},{12,28},{16,0},{20,4},{24,8},{28,12},{1,17},{... | collective-permute-start | bytes 356360 | tf_op jit(solution)/shard_map/ppermute | solution.py:39
  32.1 3.1 %collective-permute-done.4 = f32[232,128]{1,0:T(8,128)S(1)} collective-permute-done((f32[232,128]{1,0:T(8,128)S(1)}, f32[232,128]{1,0:T(8,128)S(1)}, u32[]{:S(2)}, u32[]{:S(2)}) %collective-permute-start.4) | collective-permute-done | bytes 118816 | tf_op jit(solution)/shard_map/ppermute | solution.py:39
  35.3 1.6 %collective-permute-start.5 = (f32[232,128]{1,0:T(8,128)S(1)}, f32[232,128]{1,0:T(8,128)S(1)}, u32[]{:S(2)}, u32[]{:S(2)}) collective-permute-start(f32[232,128]{1,0:T(8,128)S(1)} %add.25), channel_id=1, source_target_pairs={{0,1},{1,0},{2,3},{3,2},{4,5},{5,4},{6,7},{7,6},{8,9},{9,8},{10,11... | collective-permute-start | bytes 356360 | tf_op jit(solution)/shard_map/ppermute | solution.py:39
  36.9 3.3 %collective-permute-done.5 = f32[232,128]{1,0:T(8,128)S(1)} collective-permute-done((f32[232,128]{1,0:T(8,128)S(1)}, f32[232,128]{1,0:T(8,128)S(1)}, u32[]{:S(2)}, u32[]{:S(2)}) %collective-permute-start.5) | collective-permute-done | bytes 118816 | tf_op jit(solution)/shard_map/ppermute | solution.py:39
  40.2 2.6 %collective-permute-start.6 = (f32[232,128]{1,0:T(8,128)S(1)}, f32[232,128]{1,0:T(8,128)S(1)}, u32[]{:S(2)}, u32[]{:S(2)}) collective-permute-start(f32[232,128]{1,0:T(8,128)S(1)} %add.26), channel_id=1, source_target_pairs={{0,2},{1,3},{2,0},{3,1},{4,6},{5,7},{6,4},{7,5},{8,10},{9,11},{10,... | collective-permute-start | bytes 356360 | tf_op jit(solution)/shard_map/ppermute | solution.py:39
  42.8 4.4 %collective-permute-done.6 = f32[232,128]{1,0:T(8,128)S(1)} collective-permute-done((f32[232,128]{1,0:T(8,128)S(1)}, f32[232,128]{1,0:T(8,128)S(1)}, u32[]{:S(2)}, u32[]{:S(2)}) %collective-permute-start.6) | collective-permute-done | bytes 118816 | tf_op jit(solution)/shard_map/ppermute | solution.py:39
  47.3 0.1 collective-permute-start.7
  47.3 1.3 %collective-permute-done.7 = f32[232,128]{1,0:T(8,128)S(1)} collective-permute-done((f32[232,128]{1,0:T(8,128)S(1)}, f32[232,128]{1,0:T(8,128)S(1)}, u32[]{:S(2)}, u32[]{:S(2)}) %collective-permute-start.7) | collective-permute-done | bytes 118816 | tf_op jit(solution)/shard_map/ppermute | solution.py:40
  48.7 0.3 reshape.34
  49.0 0.8 %copy.19 = f32[27,2,16,64]{3,2,1,0:T(8,128)} copy(f32[27,2,16,64]{3,1,2,0:T(2,128)S(1)} %bitcast.43) | data formatting | bytes 442368 | tf_op jit(solution)/shard_map/transpose | solution.py:284
  49.8 0.7 %reshape.33 = f32[3,3,3,4,32]{4,3,2,1,0:T(4,128)} reshape(f32[27,128]{1,0:T(8,128)S(1)} %slice_multiply_fusion.1) | data formatting | bytes 27648 | tf_op jit(solution)/shard_map/reshape | solution.py:283
  (17 shorter events, 0.3 us)
Async XLA Ops:
  1.5 1.1 %copy-start.3 = (bf16[8,8,4,128]{3,1,2,0:T(8,128)(2,1)}, bf16[8,8,4,128]{3,1,2,0:T(8,128)(2,1)S(1)}, u32[]{:S(2)}) copy-start(bf16[8,8,4,128]{3,1,2,0:T(8,128)(2,1)S(1)} %copy.25) | copy-start | bytes 196612
  1.5 2.5 %copy-start.1 = (bf16[1,4,4,16,512]{4,3,2,1,0:T(8,128)(2,1)S(1)}, bf16[1,4,4,16,512]{4,3,2,1,0:T(8,128)(2,1)}, u32[]{:S(2)}) copy-start(bf16[1,4,4,16,512]{4,3,2,1,0:T(8,128)(2,1)} %vo_ref.1) | copy-start | bytes 786436
  2.6 4.5 %copy-start.8 = (bf16[32,4,3,3,3]{0,1,4,3,2:T(4,128)(2,1)S(1)}, bf16[32,4,3,3,3]{0,1,4,3,2:T(4,128)(2,1)}, u32[]{:S(2)}) copy-start(bf16[32,4,3,3,3]{0,1,4,3,2:T(4,128)(2,1)} %param.5) | copy-start | bytes 20740
  2.6 4.6 %copy-start.6 = (bf16[64,32,3,3,3]{0,1,4,3,2:T(8,128)(2,1)S(1)}, bf16[64,32,3,3,3]{0,1,4,3,2:T(8,128)(2,1)}, u32[]{:S(2)}) copy-start(bf16[64,32,3,3,3]{0,1,4,3,2:T(8,128)(2,1)} %param.6) | copy-start | bytes 331780
  2.6 7.0 %collective-permute-start.1 = (bf16[320,512]{1,0:T(8,128)(2,1)S(1)}, bf16[320,512]{1,0:T(8,128)(2,1)S(1)}, u32[]{:S(2)}, u32[]{:S(2)}) collective-permute-start(bf16[320,512]{1,0:T(8,128)(2,1)S(1)} %pad_maximum_fusion), channel_id=1, source_target_pairs={{4,0},{8,4},{12,8},{16,12},{20,16},{24,20},{28,24},{5,1},{9,5},{13... | collective-permute-start | bytes 983048 | tf_op jit(solution)/shard_map/ppermute | solution.py:17
  4.0 5.5 %collective-permute-start = (bf16[1,4,3,16,512]{4,3,2,1,0:T(8,128)(2,1)S(1)}, bf16[1,4,3,16,512]{4,3,2,1,0:T(8,128)(2,1)S(1)}, u32[]{:S(2)}, u32[]{:S(2)}) collective-permute-start(bf16[1,4,3,16,512]{4,3,2,1,0:T(8,128)(2,1)S(1)} %slice.30), channel_id=1, source_target_pairs={{0,4},{4,8},{8,12},{12,16},{16,20},{20,24},{24,28},{1,5},{5,9},{9,... | collective-permute-start | bytes 589832 | tf_op jit(solution)/shard_map/ppermute | solution.py:17
  8.7 0.9 %copy-start = (bf16[64,3,3,2,2,32]{0,5,4,3,2,1:T(8,128)(2,1)}, bf16[64,3,3,2,2,32]{0,5,4,3,2,1:T(8,128)(2,1)S(1)}, u32[]{:S(2)}) copy-start(bf16[64,3,3,2,2,32]{0,5,4,3,2,1:T(8,128)(2,1)S(1)} %copy.15) | copy-start | bytes 442372
  9.5 0.7 %copy-start.7 = (bf16[1,4,3,16,512]{4,3,2,1,0:T(8,128)(2,1)}, bf16[1,4,3,16,512]{4,3,2,1,0:T(8,128)(2,1)S(1)}, u32[]{:S(2)}) copy-start(bf16[1,4,3,16,512]{4,3,2,1,0:T(8,128)(2,1)S(1)} %collective-permute-done.vb_ref) | copy-start | bytes 589828
  9.6 0.8 %copy-start.4 = (bf16[320,512]{1,0:T(8,128)(2,1)}, bf16[320,512]{1,0:T(8,128)(2,1)S(1)}, u32[]{:S(2)}) copy-start(bf16[320,512]{1,0:T(8,128)(2,1)S(1)} %collective-permute-done.1.va_ref) | copy-start | bytes 983044
  16.9 3.9 %copy-start.5 = (bf16[512,256]{1,0:T(8,128)(2,1)S(1)}, bf16[512,256]{1,0:T(8,128)(2,1)}, u32[]{:S(2)}) copy-start(bf16[512,256]{1,0:T(8,128)(2,1)} %get-tuple-element.12) | copy-start | bytes 786436
  17.9 4.4 %collective-permute-start.2 = (f32[232,128]{1,0:T(8,128)S(1)}, f32[232,128]{1,0:T(8,128)S(1)}, u32[]{:S(2)}, u32[]{:S(2)}) collective-permute-start(f32[232,128]{1,0:T(8,128)S(1)} %slice_select_fusion), channel_id=1, source_target_pairs={{0,4},{4,0},{8,12},{12,8},{16,20},{20,16},{24,28},{28,24},{1,5},{5... | collective-permute-start | bytes 356360 | tf_op jit(solution)/shard_map/ppermute | solution.py:36
  20.8 0.9 %copy-start.9 = (bf16[64,512]{1,0:T(8,128)(2,1)S(1)}, bf16[64,512]{1,0:T(8,128)(2,1)}, u32[]{:S(2)}) copy-start(bf16[64,512]{1,0:T(8,128)(2,1)} %get-tuple-element.11) | copy-start | bytes 196612
  20.8 1.5 %copy-start.2 = (f32[464,128]{1,0:T(8,128)S(1)}, f32[464,128]{1,0:T(8,128)}, u32[]{:S(2)}) copy-start(f32[464,128]{1,0:T(8,128)} %get-tuple-element.10) | copy-start | bytes 712708
  22.3 7.3 %collective-permute-start.3 = (f32[232,128]{1,0:T(8,128)S(1)}, f32[232,128]{1,0:T(8,128)S(1)}, u32[]{:S(2)}, u32[]{:S(2)}) collective-permute-start(f32[232,128]{1,0:T(8,128)S(1)} %select_add_fusion), channel_id=1, source_target_pairs={{0,8},{4,12},{8,0},{12,4},{16,24},{20,28},{24,16},{28,20},{1,9},{5... | collective-permute-start | bytes 356360 | tf_op jit(solution)/shard_map/ppermute | solution.py:39
  29.6 5.6 %collective-permute-start.4 = (f32[232,128]{1,0:T(8,128)S(1)}, f32[232,128]{1,0:T(8,128)S(1)}, u32[]{:S(2)}, u32[]{:S(2)}) collective-permute-start(f32[232,128]{1,0:T(8,128)S(1)} %add.24), channel_id=1, source_target_pairs={{0,16},{4,20},{8,24},{12,28},{16,0},{20,4},{24,8},{28,12},{1,17},{... | collective-permute-start | bytes 356360 | tf_op jit(solution)/shard_map/ppermute | solution.py:39
  35.3 4.9 %collective-permute-start.5 = (f32[232,128]{1,0:T(8,128)S(1)}, f32[232,128]{1,0:T(8,128)S(1)}, u32[]{:S(2)}, u32[]{:S(2)}) collective-permute-start(f32[232,128]{1,0:T(8,128)S(1)} %add.25), channel_id=1, source_target_pairs={{0,1},{1,0},{2,3},{3,2},{4,5},{5,4},{6,7},{7,6},{8,9},{9,8},{10,11... | collective-permute-start | bytes 356360 | tf_op jit(solution)/shard_map/ppermute | solution.py:39
  40.2 7.1 %collective-permute-start.6 = (f32[232,128]{1,0:T(8,128)S(1)}, f32[232,128]{1,0:T(8,128)S(1)}, u32[]{:S(2)}, u32[]{:S(2)}) collective-permute-start(f32[232,128]{1,0:T(8,128)S(1)} %add.26), channel_id=1, source_target_pairs={{0,2},{1,3},{2,0},{3,1},{4,6},{5,7},{6,4},{7,5},{8,10},{9,11},{10,... | collective-permute-start | bytes 356360 | tf_op jit(solution)/shard_map/ppermute | solution.py:39
  47.3 1.4 %collective-permute-start.7 = (f32[232,128]{1,0:T(8,128)S(1)}, f32[232,128]{1,0:T(8,128)S(1)}, u32[]{:S(2)}, u32[]{:S(2)}) collective-permute-start(f32[232,128]{1,0:T(8,128)S(1)} %add.27), channel_id=1, source_target_pairs={{0,4},{4,0},{8,12},{12,8},{16,20},{20,16},{24,28},{28,24},{1,5},{5... | collective-permute-start | bytes 356360 | tf_op jit(solution)/shard_map/ppermute | solution.py:40

commit v18 on v15

--- a/solution.py
+++ b/solution.py
@@ -41,7 +41,7 @@
 
 
 def _sigmoid(v):
-    return 1.0 / (1.0 + jnp.exp(-v))
+    return 0.5 * (jnp.tanh(0.5 * v) + 1.0)
 
 
 def _shift_right(x):

time: 50.2 us -> 50.2 us (level)
  no operation moved by 1% of the time
where the time goes in v18:
time: 50.2 us; the launch traced here: 49.8 us
  starting transfers between devices  17.8 us (35%)
  waiting for transfers between devices  15.2 us (30%)
  local copies, waits for them, and re-layouts  6.84 us (14%)
  Pallas kernels  6.44 us (13%)
  other arithmetic  2.6 us (5%)
  between operations  0.94 us (2%)
    ppermute x4, waiting for transfers between devices, _all_sum(): part = part + lax.ppermute(part, axis, [(i, i ^ k) for i in range(n)])  14.2 us
    ppermute x4, starting transfers between devices, _all_sum(): part = part + lax.ppermute(part, axis, [(i, i ^ k) for i in range(n)])  10.4 us
    pallas_call x1, Pallas kernels, per_device(): pl.pallas_call(_kernel, out_shape=(jax.ShapeDtypeStruct((c2, n2), BF16),...  6.44 us
    ppermute x2, starting transfers between devices, shifted(): return lax.ppermute(block, axis, route)  4.47 us
    ppermute x1, starting transfers between devices, _all_sum(): lax.ppermute(jnp.where(low, hi, lo), axis0, pair)  2.89 us
    unnamed x21, local copies, waits for them, and re-layouts  1.66 us
    concatenate x1, other arithmetic, per_device(): jnp.concatenate([volume[0].reshape(-1, nx), cot], 0)  1.04 us
    select_n x1, other arithmetic, _all_sum(): jnp.where(low, hi, lo)  1.01 us
  transfers between devices with their start and end apart: 8, of which 5 were waited for; matrix products, arithmetic and copies ran while one was open for 8% of the time, Pallas kernels for 0%

profile of v18, /device:TPU:0, one launch (start us, length us, event | category | flops | bytes accessed | tf_op | source)
XLA Modules:
  0.0 49.8 jit_solution(3927153631379566565)
XLA Ops:
  0.6 0.9 %copy.25 = bf16[8,8,4,128]{3,1,2,0:T(8,128)(2,1)S(1)} copy(bf16[8,8,4,128]{3,2,1,0:T(4,128)(2,1)} %bitcast.54) | data formatting | bytes 131072
  1.5 0.0 copy-start.3
  1.5 0.0 copy-start.1
  1.5 1.0 %pad_maximum_fusion = bf16[320,512]{1,0:T(8,128)(2,1)S(1)} fusion(bf16[64,512]{1,0:T(8,128)(2,1)S(1)} %bitcast.44, bf16[256,512]{1,0:T(8,128)(2,1)} %bitcast.42), kind=kLoop, calls=%fused_computation | loop fusion | flops 655360 | bytes 655360 | tf_op jit(solution)/shard_map/concatenate | solution.py:234
  2.5 0.0 copy-done.3
  2.6 0.0 copy-start.8
  2.6 0.0 copy-start.6
  2.6 1.4 %collective-permute-start.1 = (bf16[320,512]{1,0:T(8,128)(2,1)S(1)}, bf16[320,512]{1,0:T(8,128)(2,1)S(1)}, u32[]{:S(2)}, u32[]{:S(2)}) collective-permute-start(bf16[320,512]{1,0:T(8,128)(2,1)S(1)} %pad_maximum_fusion), channel_id=1, source_target_pairs={{4,0},{8,4},{12,8},{16,12},{20,16},{24,20},{28,24},{5,1},{9,5},{13... | collective-permute-start | bytes 983048 | tf_op jit(solution)/shard_map/ppermute | solution.py:17
  4.0 0.0 copy-done.1
  4.0 3.0 %collective-permute-start = (bf16[1,4,3,16,512]{4,3,2,1,0:T(8,128)(2,1)S(1)}, bf16[1,4,3,16,512]{4,3,2,1,0:T(8,128)(2,1)S(1)}, u32[]{:S(2)}, u32[]{:S(2)}) collective-permute-start(bf16[1,4,3,16,512]{4,3,2,1,0:T(8,128)(2,1)S(1)} %slice.30), channel_id=1, source_target_pairs={{0,4},{4,8},{8,12},{12,16},{16,20},{20,24},{24,28},{1,5},{5,9},{9,... | collective-permute-start | bytes 589832 | tf_op jit(solution)/shard_map/ppermute | solution.py:17
  7.1 0.0 copy-done.8
  7.2 0.0 copy-done.6
  7.3 0.1 pad_maximum_fusion.3
  7.4 0.1 maximum_bitcast_fusion.1
  7.5 0.1 maximum_bitcast_fusion
  7.5 0.1 pad_maximum_fusion.2
  7.7 0.1 copy.14
  7.8 0.1 reshape.29
  7.9 0.7 %copy.16.k1_ref = bf16[64,288]{1,0:T(8,128)(2,1)} copy(bf16[64,288]{0,1:T(8,128)(2,1)S(1)} %reshape.29) | data formatting | bytes 73728 | tf_op jit(solution)/shard_map/reshape | solution.py:215
  8.6 0.1 pad_maximum_fusion.1
  8.7 0.0 copy-start
  8.7 0.8 %copy.17.k2_ref = bf16[64,1152]{1,0:T(8,128)(2,1)} copy(bf16[64,1152]{0,1:T(8,128)(2,1)S(1)} %bitcast.40) | data formatting | bytes 294912 | tf_op jit(solution)/shard_map/reshape | solution.py:223
  9.5 0.0 collective-permute-done.vb_ref
  9.5 0.0 copy-start.7
  9.5 0.0 collective-permute-done.1.va_ref
  9.6 0.0 copy-start.4
  9.6 0.0 copy-done
  9.6 0.6 %copy-done.7 = bf16[1,4,3,16,512]{4,3,2,1,0:T(8,128)(2,1)} copy-done((bf16[1,4,3,16,512]{4,3,2,1,0:T(8,128)(2,1)}, bf16[1,4,3,16,512]{4,3,2,1,0:T(8,128)(2,1)S(1)}, u32[]{:S(2)}) %copy-start.7) | copy-done | bytes 196632
  10.2 0.1 copy-done.4
  10.3 6.4 %shard_map.75 = (bf16[64,512]{1,0:T(8,128)(2,1)}, bf16[512,256]{1,0:T(8,128)(2,1)}, f32[464,128]{1,0:T(8,128)}) custom-call(bf16[1,4,3,16,512]{4,3,2,1,0:T(8,128)(2,1)} %copy-done.7, bf16[1,4,4,16,512]{4,3,2,1,0:T(8,128)(2,1)} %vo_ref.1, bf16[320,512]{1,0:T(8,128)(2,1)} %copy-done.4, bf16[64,288]{1,0:T(8,128)(2,1)} %copy.16.k1_ref, ...), custom_call_target="tpu_custom_call" | custom-call | flops 60000000 | bytes 3000000 | tf_op jit(solution)/shard_map/pallas_call | solution.py:248
  16.8 0.0 copy-start.2
  16.8 1.0 %slice_select_fusion = f32[232,128]{1,0:T(8,128)S(1)} fusion(f32[464,128]{1,0:T(8,128)} %get-tuple-element.9, pred[]{:T(512)S(6)} %eq.3), kind=kLoop, calls=%fused_computation.9 | loop fusion | flops 29696 | bytes 356353 | tf_op jit(solution)/shard_map/jit(_where)/select_n | solution.py:36
  17.8 2.9 %collective-permute-start.2 = (f32[232,128]{1,0:T(8,128)S(1)}, f32[232,128]{1,0:T(8,128)S(1)}, u32[]{:S(2)}, u32[]{:S(2)}) collective-permute-start(f32[232,128]{1,0:T(8,128)S(1)} %slice_select_fusion), channel_id=1, source_target_pairs={{0,4},{4,0},{8,12},{12,8},{16,20},{20,16},{24,28},{28,24},{1,5},{5... | collective-permute-start | bytes 356360 | tf_op jit(solution)/shard_map/ppermute | solution.py:36
  20.7 1.0 %collective-permute-done.2 = f32[232,128]{1,0:T(8,128)S(1)} collective-permute-done((f32[232,128]{1,0:T(8,128)S(1)}, f32[232,128]{1,0:T(8,128)S(1)}, u32[]{:S(2)}, u32[]{:S(2)}) %collective-permute-start.2) | collective-permute-done | bytes 118816 | tf_op jit(solution)/shard_map/ppermute | solution.py:36
  21.7 0.0 copy-done.2
  21.7 3.9 %collective-permute-start.3 = (f32[232,128]{1,0:T(8,128)S(1)}, f32[232,128]{1,0:T(8,128)S(1)}, u32[]{:S(2)}, u32[]{:S(2)}) collective-permute-start(f32[232,128]{1,0:T(8,128)S(1)} %select_add_fusion), channel_id=1, source_target_pairs={{0,8},{4,12},{8,0},{12,4},{16,24},{20,28},{24,16},{28,20},{1,9},{5... | collective-permute-start | bytes 356360 | tf_op jit(solution)/shard_map/ppermute | solution.py:38
  25.5 3.7 %collective-permute-done.3 = f32[232,128]{1,0:T(8,128)S(1)} collective-permute-done((f32[232,128]{1,0:T(8,128)S(1)}, f32[232,128]{1,0:T(8,128)S(1)}, u32[]{:S(2)}, u32[]{:S(2)}) %collective-permute-start.3) | collective-permute-done | bytes 118816 | tf_op jit(solution)/shard_map/ppermute | solution.py:38
  29.3 2.2 %collective-permute-start.4 = (f32[232,128]{1,0:T(8,128)S(1)}, f32[232,128]{1,0:T(8,128)S(1)}, u32[]{:S(2)}, u32[]{:S(2)}) collective-permute-start(f32[232,128]{1,0:T(8,128)S(1)} %add.24), channel_id=1, source_target_pairs={{0,16},{4,20},{8,24},{12,28},{16,0},{20,4},{24,8},{28,12},{1,17},{... | collective-permute-start | bytes 356360 | tf_op jit(solution)/shard_map/ppermute | solution.py:38
  31.5 2.8 %collective-permute-done.4 = f32[232,128]{1,0:T(8,128)S(1)} collective-permute-done((f32[232,128]{1,0:T(8,128)S(1)}, f32[232,128]{1,0:T(8,128)S(1)}, u32[]{:S(2)}, u32[]{:S(2)}) %collective-permute-start.4) | collective-permute-done | bytes 118816 | tf_op jit(solution)/shard_map/ppermute | solution.py:38
  34.3 1.6 %collective-permute-start.5 = (f32[232,128]{1,0:T(8,128)S(1)}, f32[232,128]{1,0:T(8,128)S(1)}, u32[]{:S(2)}, u32[]{:S(2)}) collective-permute-start(f32[232,128]{1,0:T(8,128)S(1)} %add.25), channel_id=1, source_target_pairs={{0,1},{1,0},{2,3},{3,2},{4,5},{5,4},{6,7},{7,6},{8,9},{9,8},{10,11... | collective-permute-start | bytes 356360 | tf_op jit(solution)/shard_map/ppermute | solution.py:38
  36.0 3.3 %collective-permute-done.5 = f32[232,128]{1,0:T(8,128)S(1)} collective-permute-done((f32[232,128]{1,0:T(8,128)S(1)}, f32[232,128]{1,0:T(8,128)S(1)}, u32[]{:S(2)}, u32[]{:S(2)}) %collective-permute-start.5) | collective-permute-done | bytes 118816 | tf_op jit(solution)/shard_map/ppermute | solution.py:38
  39.3 0.0 copy-start.5
  39.3 2.7 %collective-permute-start.6 = (f32[232,128]{1,0:T(8,128)S(1)}, f32[232,128]{1,0:T(8,128)S(1)}, u32[]{:S(2)}, u32[]{:S(2)}) collective-permute-start(f32[232,128]{1,0:T(8,128)S(1)} %add.26), channel_id=1, source_target_pairs={{0,2},{1,3},{2,0},{3,1},{4,6},{5,7},{6,4},{7,5},{8,10},{9,11},{10,... | collective-permute-start | bytes 356360 | tf_op jit(solution)/shard_map/ppermute | solution.py:38
  42.0 4.4 %collective-permute-done.6 = f32[232,128]{1,0:T(8,128)S(1)} collective-permute-done((f32[232,128]{1,0:T(8,128)S(1)}, f32[232,128]{1,0:T(8,128)S(1)}, u32[]{:S(2)}, u32[]{:S(2)}) %collective-permute-start.6) | collective-permute-done | bytes 118816 | tf_op jit(solution)/shard_map/ppermute | solution.py:38
  46.4 0.1 collective-permute-start.7
  46.5 0.0 copy-done.5
  46.5 0.0 copy-start.9
  46.5 0.9 %copy.24 = bf16[2,8,32,256]{3,1,0,2:T(8,128)(2,1)} copy(bf16[2,8,32,256]{3,2,1,0:T(8,128)(2,1)S(1)} %bitcast.47) | data formatting | bytes 524288 | tf_op jit(solution)/shard_map/reshape | solution.py:273
  47.3 0.0 copy-done.9
  47.3 0.6 %reshape.31 = bf16[1,64,1,4,128]{4,3,1,2,0:T(4,128)(2,1)} reshape(bf16[64,512]{1,0:T(8,128)(2,1)S(1)} %copy-done.9) | data formatting | bytes 131072 | tf_op jit(solution)/shard_map/reshape | solution.py:272
  48.0 0.0 collective-permute-done.7
  48.0 0.3 reshape.34
  48.3 0.8 %copy.19 = f32[27,2,16,64]{3,2,1,0:T(8,128)} copy(f32[27,2,16,64]{3,1,2,0:T(2,128)S(1)} %bitcast.43) | data formatting | bytes 442368 | tf_op jit(solution)/shard_map/transpose | solution.py:282
  49.1 0.7 %reshape.33 = f32[3,3,3,4,32]{4,3,2,1,0:T(4,128)} reshape(f32[27,128]{1,0:T(8,128)S(1)} %slice_multiply_fusion.1) | data formatting | bytes 27648 | tf_op jit(solution)/shard_map/reshape | solution.py:281
  (17 shorter events, 0.3 us)
Async XLA Ops:
  1.5 1.1 %copy-start.3 = (bf16[8,8,4,128]{3,1,2,0:T(8,128)(2,1)}, bf16[8,8,4,128]{3,1,2,0:T(8,128)(2,1)S(1)}, u32[]{:S(2)}) copy-start(bf16[8,8,4,128]{3,1,2,0:T(8,128)(2,1)S(1)} %copy.25) | copy-start | bytes 196612
  1.5 2.5 %copy-start.1 = (bf16[1,4,4,16,512]{4,3,2,1,0:T(8,128)(2,1)S(1)}, bf16[1,4,4,16,512]{4,3,2,1,0:T(8,128)(2,1)}, u32[]{:S(2)}) copy-start(bf16[1,4,4,16,512]{4,3,2,1,0:T(8,128)(2,1)} %vo_ref.1) | copy-start | bytes 786436
  2.6 4.5 %copy-start.8 = (bf16[32,4,3,3,3]{0,1,4,3,2:T(4,128)(2,1)S(1)}, bf16[32,4,3,3,3]{0,1,4,3,2:T(4,128)(2,1)}, u32[]{:S(2)}) copy-start(bf16[32,4,3,3,3]{0,1,4,3,2:T(4,128)(2,1)} %param.5) | copy-start | bytes 20740
  2.6 4.6 %copy-start.6 = (bf16[64,32,3,3,3]{0,1,4,3,2:T(8,128)(2,1)S(1)}, bf16[64,32,3,3,3]{0,1,4,3,2:T(8,128)(2,1)}, u32[]{:S(2)}) copy-start(bf16[64,32,3,3,3]{0,1,4,3,2:T(8,128)(2,1)} %param.6) | copy-start | bytes 331780
  2.6 7.0 %collective-permute-start.1 = (bf16[320,512]{1,0:T(8,128)(2,1)S(1)}, bf16[320,512]{1,0:T(8,128)(2,1)S(1)}, u32[]{:S(2)}, u32[]{:S(2)}) collective-permute-start(bf16[320,512]{1,0:T(8,128)(2,1)S(1)} %pad_maximum_fusion), channel_id=1, source_target_pairs={{4,0},{8,4},{12,8},{16,12},{20,16},{24,20},{28,24},{5,1},{9,5},{13... | collective-permute-start | bytes 983048 | tf_op jit(solution)/shard_map/ppermute | solution.py:17
  4.0 5.5 %collective-permute-start = (bf16[1,4,3,16,512]{4,3,2,1,0:T(8,128)(2,1)S(1)}, bf16[1,4,3,16,512]{4,3,2,1,0:T(8,128)(2,1)S(1)}, u32[]{:S(2)}, u32[]{:S(2)}) collective-permute-start(bf16[1,4,3,16,512]{4,3,2,1,0:T(8,128)(2,1)S(1)} %slice.30), channel_id=1, source_target_pairs={{0,4},{4,8},{8,12},{12,16},{16,20},{20,24},{24,28},{1,5},{5,9},{9,... | collective-permute-start | bytes 589832 | tf_op jit(solution)/shard_map/ppermute | solution.py:17
  8.7 0.9 %copy-start = (bf16[64,3,3,2,2,32]{0,5,4,3,2,1:T(8,128)(2,1)}, bf16[64,3,3,2,2,32]{0,5,4,3,2,1:T(8,128)(2,1)S(1)}, u32[]{:S(2)}) copy-start(bf16[64,3,3,2,2,32]{0,5,4,3,2,1:T(8,128)(2,1)S(1)} %copy.15) | copy-start | bytes 442372
  9.5 0.7 %copy-start.7 = (bf16[1,4,3,16,512]{4,3,2,1,0:T(8,128)(2,1)}, bf16[1,4,3,16,512]{4,3,2,1,0:T(8,128)(2,1)S(1)}, u32[]{:S(2)}) copy-start(bf16[1,4,3,16,512]{4,3,2,1,0:T(8,128)(2,1)S(1)} %collective-permute-done.vb_ref) | copy-start | bytes 589828
  9.6 0.8 %copy-start.4 = (bf16[320,512]{1,0:T(8,128)(2,1)}, bf16[320,512]{1,0:T(8,128)(2,1)S(1)}, u32[]{:S(2)}) copy-start(bf16[320,512]{1,0:T(8,128)(2,1)S(1)} %collective-permute-done.1.va_ref) | copy-start | bytes 983044
  16.8 4.9 %copy-start.2 = (f32[464,128]{1,0:T(8,128)S(1)}, f32[464,128]{1,0:T(8,128)}, u32[]{:S(2)}) copy-start(f32[464,128]{1,0:T(8,128)} %get-tuple-element.9) | copy-start | bytes 712708
  17.8 3.9 %collective-permute-start.2 = (f32[232,128]{1,0:T(8,128)S(1)}, f32[232,128]{1,0:T(8,128)S(1)}, u32[]{:S(2)}, u32[]{:S(2)}) collective-permute-start(f32[232,128]{1,0:T(8,128)S(1)} %slice_select_fusion), channel_id=1, source_target_pairs={{0,4},{4,0},{8,12},{12,8},{16,20},{20,16},{24,28},{28,24},{1,5},{5... | collective-permute-start | bytes 356360 | tf_op jit(solution)/shard_map/ppermute | solution.py:36
  21.7 7.6 %collective-permute-start.3 = (f32[232,128]{1,0:T(8,128)S(1)}, f32[232,128]{1,0:T(8,128)S(1)}, u32[]{:S(2)}, u32[]{:S(2)}) collective-permute-start(f32[232,128]{1,0:T(8,128)S(1)} %select_add_fusion), channel_id=1, source_target_pairs={{0,8},{4,12},{8,0},{12,4},{16,24},{20,28},{24,16},{28,20},{1,9},{5... | collective-permute-start | bytes 356360 | tf_op jit(solution)/shard_map/ppermute | solution.py:38
  29.3 5.0 %collective-permute-start.4 = (f32[232,128]{1,0:T(8,128)S(1)}, f32[232,128]{1,0:T(8,128)S(1)}, u32[]{:S(2)}, u32[]{:S(2)}) collective-permute-start(f32[232,128]{1,0:T(8,128)S(1)} %add.24), channel_id=1, source_target_pairs={{0,16},{4,20},{8,24},{12,28},{16,0},{20,4},{24,8},{28,12},{1,17},{... | collective-permute-start | bytes 356360 | tf_op jit(solution)/shard_map/ppermute | solution.py:38
  34.3 4.9 %collective-permute-start.5 = (f32[232,128]{1,0:T(8,128)S(1)}, f32[232,128]{1,0:T(8,128)S(1)}, u32[]{:S(2)}, u32[]{:S(2)}) collective-permute-start(f32[232,128]{1,0:T(8,128)S(1)} %add.25), channel_id=1, source_target_pairs={{0,1},{1,0},{2,3},{3,2},{4,5},{5,4},{6,7},{7,6},{8,9},{9,8},{10,11... | collective-permute-start | bytes 356360 | tf_op jit(solution)/shard_map/ppermute | solution.py:38
  39.3 7.2 %copy-start.5 = (bf16[512,256]{1,0:T(8,128)(2,1)S(1)}, bf16[512,256]{1,0:T(8,128)(2,1)}, u32[]{:S(2)}) copy-start(bf16[512,256]{1,0:T(8,128)(2,1)} %get-tuple-element.8) | copy-start | bytes 786436
  39.3 7.1 %collective-permute-start.6 = (f32[232,128]{1,0:T(8,128)S(1)}, f32[232,128]{1,0:T(8,128)S(1)}, u32[]{:S(2)}, u32[]{:S(2)}) collective-permute-start(f32[232,128]{1,0:T(8,128)S(1)} %add.26), channel_id=1, source_target_pairs={{0,2},{1,3},{2,0},{3,1},{4,6},{5,7},{6,4},{7,5},{8,10},{9,11},{10,... | collective-permute-start | bytes 356360 | tf_op jit(solution)/shard_map/ppermute | solution.py:38
  46.4 1.6 %collective-permute-start.7 = (f32[232,128]{1,0:T(8,128)S(1)}, f32[232,128]{1,0:T(8,128)S(1)}, u32[]{:S(2)}, u32[]{:S(2)}) collective-permute-start(f32[232,128]{1,0:T(8,128)S(1)} %add.27), channel_id=1, source_target_pairs={{0,4},{4,0},{8,12},{12,8},{16,20},{20,16},{24,28},{28,24},{1,5},{5... | collective-permute-start | bytes 356360 | tf_op jit(solution)/shard_map/ppermute | solution.py:39
  46.5 0.9 %copy-start.9 = (bf16[64,512]{1,0:T(8,128)(2,1)S(1)}, bf16[64,512]{1,0:T(8,128)(2,1)}, u32[]{:S(2)}) copy-start(bf16[64,512]{1,0:T(8,128)(2,1)} %get-tuple-element.7) | copy-start | bytes 196612

commit v19 on v15

--- a/solution.py
+++ b/solution.py
@@ -27,6 +27,7 @@
             steps.append((axis, n, k))
             k *= 2
     axis0, n0, k0 = steps[0]
+    steps = steps[:1] + [st for st in steps[1:] if st[0] != axis0] + [st for st in steps[1:] if st[0] == axis0]
     rows = x.shape[0]
     half = -(-rows // 16) * 8
     x = jnp.pad(x, ((0, 2 * half - rows), (0, 0)))

time: 50.2 us -> 51.1 us (1.018)
  waiting for transfers between devices: 15.2 us -> 16.1 us
    ppermute x4, waiting for transfers between devices: 14.2 us -> 15.1 us  [_all_sum(): part = part + lax.ppermute(part, axis, [(i, i ^ k) for i in range(n)])]
where the time goes in v19:
time: 51.1 us; the launch traced here: 50.8 us
  starting transfers between devices  17.8 us (35%)
  waiting for transfers between devices  16.1 us (32%)
  local copies, waits for them, and re-layouts  6.84 us (13%)
  Pallas kernels  6.53 us (13%)
  other arithmetic  2.6 us (5%)
  between operations  0.94 us (2%)
    ppermute x4, waiting for transfers between devices, _all_sum(): part = part + lax.ppermute(part, axis, [(i, i ^ k) for i in range(n)])  15.1 us
    ppermute x4, starting transfers between devices, _all_sum(): part = part + lax.ppermute(part, axis, [(i, i ^ k) for i in range(n)])  10.4 us
    pallas_call x1, Pallas kernels, per_device(): pl.pallas_call(_kernel, out_shape=(jax.ShapeDtypeStruct((c2, n2), BF16),...  6.53 us
    ppermute x2, starting transfers between devices, shifted(): return lax.ppermute(block, axis, route)  4.47 us
    ppermute x1, starting transfers between devices, _all_sum(): lax.ppermute(jnp.where(low, hi, lo), axis0, pair)  2.88 us
    unnamed x21, local copies, waits for them, and re-layouts  1.66 us
    concatenate x1, other arithmetic, per_device(): jnp.concatenate([volume[0].reshape(-1, nx), cot], 0)  1.04 us
  transfers between devices with their start and end apart: 8, of which 5 were waited for; matrix products, arithmetic and copies ran while one was open for 8% of the time, Pallas kernels for 0%

profile of v19, /device:TPU:0, one launch (start us, length us, event | category | flops | bytes accessed | tf_op | source)
XLA Modules:
  0.0 50.8 jit_solution(3368296577431878468)
XLA Ops:
  0.6 0.9 %copy.25 = bf16[8,8,4,128]{3,1,2,0:T(8,128)(2,1)S(1)} copy(bf16[8,8,4,128]{3,2,1,0:T(4,128)(2,1)} %bitcast.54) | data formatting | bytes 131072
  1.5 0.0 copy-start.3
  1.5 0.0 copy-start.1
  1.5 1.0 %pad_maximum_fusion = bf16[320,512]{1,0:T(8,128)(2,1)S(1)} fusion(bf16[64,512]{1,0:T(8,128)(2,1)S(1)} %bitcast.44, bf16[256,512]{1,0:T(8,128)(2,1)} %bitcast.42), kind=kLoop, calls=%fused_computation | loop fusion | flops 655360 | bytes 655360 | tf_op jit(solution)/shard_map/concatenate | solution.py:235
  2.5 0.0 copy-done.3
  2.6 0.0 copy-start.8
  2.6 0.0 copy-start.6
  2.6 1.4 %collective-permute-start.1 = (bf16[320,512]{1,0:T(8,128)(2,1)S(1)}, bf16[320,512]{1,0:T(8,128)(2,1)S(1)}, u32[]{:S(2)}, u32[]{:S(2)}) collective-permute-start(bf16[320,512]{1,0:T(8,128)(2,1)S(1)} %pad_maximum_fusion), channel_id=1, source_target_pairs={{4,0},{8,4},{12,8},{16,12},{20,16},{24,20},{28,24},{5,1},{9,5},{13... | collective-permute-start | bytes 983048 | tf_op jit(solution)/shard_map/ppermute | solution.py:17
  4.0 0.0 copy-done.1
  4.0 3.0 %collective-permute-start = (bf16[1,4,3,16,512]{4,3,2,1,0:T(8,128)(2,1)S(1)}, bf16[1,4,3,16,512]{4,3,2,1,0:T(8,128)(2,1)S(1)}, u32[]{:S(2)}, u32[]{:S(2)}) collective-permute-start(bf16[1,4,3,16,512]{4,3,2,1,0:T(8,128)(2,1)S(1)} %slice.30), channel_id=1, source_target_pairs={{0,4},{4,8},{8,12},{12,16},{16,20},{20,24},{24,28},{1,5},{5,9},{9,... | collective-permute-start | bytes 589832 | tf_op jit(solution)/shard_map/ppermute | solution.py:17
  7.1 0.0 copy-done.8
  7.2 0.0 copy-done.6
  7.3 0.1 pad_maximum_fusion.3
  7.4 0.1 maximum_bitcast_fusion.1
  7.5 0.1 maximum_bitcast_fusion
  7.5 0.1 pad_maximum_fusion.2
  7.7 0.1 copy.14
  7.8 0.1 reshape.29
  7.9 0.7 %copy.16.k1_ref = bf16[64,288]{1,0:T(8,128)(2,1)} copy(bf16[64,288]{0,1:T(8,128)(2,1)S(1)} %reshape.29) | data formatting | bytes 73728 | tf_op jit(solution)/shard_map/reshape | solution.py:216
  8.6 0.1 pad_maximum_fusion.1
  8.7 0.0 copy-start
  8.7 0.8 %copy.17.k2_ref = bf16[64,1152]{1,0:T(8,128)(2,1)} copy(bf16[64,1152]{0,1:T(8,128)(2,1)S(1)} %bitcast.40) | data formatting | bytes 294912 | tf_op jit(solution)/shard_map/reshape | solution.py:224
  9.5 0.0 collective-permute-done.vb_ref
  9.5 0.0 copy-start.7
  9.5 0.0 collective-permute-done.1.va_ref
  9.6 0.0 copy-start.4
  9.6 0.0 copy-done
  9.6 0.6 %copy-done.7 = bf16[1,4,3,16,512]{4,3,2,1,0:T(8,128)(2,1)} copy-done((bf16[1,4,3,16,512]{4,3,2,1,0:T(8,128)(2,1)}, bf16[1,4,3,16,512]{4,3,2,1,0:T(8,128)(2,1)S(1)}, u32[]{:S(2)}) %copy-start.7) | copy-done | bytes 196632
  10.2 0.1 copy-done.4
  10.3 6.5 %shard_map.75 = (bf16[64,512]{1,0:T(8,128)(2,1)}, bf16[512,256]{1,0:T(8,128)(2,1)}, f32[464,128]{1,0:T(8,128)}) custom-call(bf16[1,4,3,16,512]{4,3,2,1,0:T(8,128)(2,1)} %copy-done.7, bf16[1,4,4,16,512]{4,3,2,1,0:T(8,128)(2,1)} %vo_ref.1, bf16[320,512]{1,0:T(8,128)(2,1)} %copy-done.4, bf16[64,288]{1,0:T(8,128)(2,1)} %copy.16.k1_ref, ...), custom_call_target="tpu_custom_call" | custom-call | flops 60000000 | bytes 3000000 | tf_op jit(solution)/shard_map/pallas_call | solution.py:249
  16.9 0.0 copy-start.2
  16.9 1.0 %slice_select_fusion = f32[232,128]{1,0:T(8,128)S(1)} fusion(f32[464,128]{1,0:T(8,128)} %get-tuple-element.9, pred[]{:T(512)S(6)} %eq.3), kind=kLoop, calls=%fused_computation.9 | loop fusion | flops 29696 | bytes 356353 | tf_op jit(solution)/shard_map/jit(_where)/select_n | solution.py:37
  17.9 2.9 %collective-permute-start.2 = (f32[232,128]{1,0:T(8,128)S(1)}, f32[232,128]{1,0:T(8,128)S(1)}, u32[]{:S(2)}, u32[]{:S(2)}) collective-permute-start(f32[232,128]{1,0:T(8,128)S(1)} %slice_select_fusion), channel_id=1, source_target_pairs={{0,4},{4,0},{8,12},{12,8},{16,20},{20,16},{24,28},{28,24},{1,5},{5... | collective-permute-start | bytes 356360 | tf_op jit(solution)/shard_map/ppermute | solution.py:37
  20.8 1.0 %collective-permute-done.2 = f32[232,128]{1,0:T(8,128)S(1)} collective-permute-done((f32[232,128]{1,0:T(8,128)S(1)}, f32[232,128]{1,0:T(8,128)S(1)}, u32[]{:S(2)}, u32[]{:S(2)}) %collective-permute-start.2) | collective-permute-done | bytes 118816 | tf_op jit(solution)/shard_map/ppermute | solution.py:37
  21.7 0.0 copy-done.2
  21.8 1.7 %collective-permute-start.3 = (f32[232,128]{1,0:T(8,128)S(1)}, f32[232,128]{1,0:T(8,128)S(1)}, u32[]{:S(2)}, u32[]{:S(2)}) collective-permute-start(f32[232,128]{1,0:T(8,128)S(1)} %select_add_fusion), channel_id=1, source_target_pairs={{0,1},{1,0},{2,3},{3,2},{4,5},{5,4},{6,7},{7,6},{8,9},{9,8},{10,11... | collective-permute-start | bytes 356360 | tf_op jit(solution)/shard_map/ppermute | solution.py:39
  23.4 3.9 %collective-permute-done.3 = f32[232,128]{1,0:T(8,128)S(1)} collective-permute-done((f32[232,128]{1,0:T(8,128)S(1)}, f32[232,128]{1,0:T(8,128)S(1)}, u32[]{:S(2)}, u32[]{:S(2)}) %collective-permute-start.3) | collective-permute-done | bytes 118816 | tf_op jit(solution)/shard_map/ppermute | solution.py:39
  27.4 2.7 %collective-permute-start.4 = (f32[232,128]{1,0:T(8,128)S(1)}, f32[232,128]{1,0:T(8,128)S(1)}, u32[]{:S(2)}, u32[]{:S(2)}) collective-permute-start(f32[232,128]{1,0:T(8,128)S(1)} %add.24), channel_id=1, source_target_pairs={{0,2},{1,3},{2,0},{3,1},{4,6},{5,7},{6,4},{7,5},{8,10},{9,11},{10,... | collective-permute-start | bytes 356360 | tf_op jit(solution)/shard_map/ppermute | solution.py:39
  30.0 5.5 %collective-permute-done.4 = f32[232,128]{1,0:T(8,128)S(1)} collective-permute-done((f32[232,128]{1,0:T(8,128)S(1)}, f32[232,128]{1,0:T(8,128)S(1)}, u32[]{:S(2)}, u32[]{:S(2)}) %collective-permute-start.4) | collective-permute-done | bytes 118816 | tf_op jit(solution)/shard_map/ppermute | solution.py:39
  35.6 3.9 %collective-permute-start.5 = (f32[232,128]{1,0:T(8,128)S(1)}, f32[232,128]{1,0:T(8,128)S(1)}, u32[]{:S(2)}, u32[]{:S(2)}) collective-permute-start(f32[232,128]{1,0:T(8,128)S(1)} %add.25), channel_id=1, source_target_pairs={{0,8},{4,12},{8,0},{12,4},{16,24},{20,28},{24,16},{28,20},{1,9},{5... | collective-permute-start | bytes 356360 | tf_op jit(solution)/shard_map/ppermute | solution.py:39
  39.4 2.8 %collective-permute-done.5 = f32[232,128]{1,0:T(8,128)S(1)} collective-permute-done((f32[232,128]{1,0:T(8,128)S(1)}, f32[232,128]{1,0:T(8,128)S(1)}, u32[]{:S(2)}, u32[]{:S(2)}) %collective-permute-start.5) | collective-permute-done | bytes 118816 | tf_op jit(solution)/shard_map/ppermute | solution.py:39
  42.3 0.0 copy-start.5
  42.3 2.3 %collective-permute-start.6 = (f32[232,128]{1,0:T(8,128)S(1)}, f32[232,128]{1,0:T(8,128)S(1)}, u32[]{:S(2)}, u32[]{:S(2)}) collective-permute-start(f32[232,128]{1,0:T(8,128)S(1)} %add.26), channel_id=1, source_target_pairs={{0,16},{4,20},{8,24},{12,28},{16,0},{20,4},{24,8},{28,12},{1,17},{... | collective-permute-start | bytes 356360 | tf_op jit(solution)/shard_map/ppermute | solution.py:39
  44.5 2.8 %collective-permute-done.6 = f32[232,128]{1,0:T(8,128)S(1)} collective-permute-done((f32[232,128]{1,0:T(8,128)S(1)}, f32[232,128]{1,0:T(8,128)S(1)}, u32[]{:S(2)}, u32[]{:S(2)}) %collective-permute-start.6) | collective-permute-done | bytes 118816 | tf_op jit(solution)/shard_map/ppermute | solution.py:39
  47.4 0.1 collective-permute-start.7
  47.4 0.0 copy-done.5
  47.4 0.0 copy-start.9
  47.5 0.9 %copy.24 = bf16[2,8,32,256]{3,1,0,2:T(8,128)(2,1)} copy(bf16[2,8,32,256]{3,2,1,0:T(8,128)(2,1)S(1)} %bitcast.47) | data formatting | bytes 524288 | tf_op jit(solution)/shard_map/reshape | solution.py:274
  48.3 0.0 copy-done.9
  48.3 0.6 %reshape.31 = bf16[1,64,1,4,128]{4,3,1,2,0:T(4,128)(2,1)} reshape(bf16[64,512]{1,0:T(8,128)(2,1)S(1)} %copy-done.9) | data formatting | bytes 131072 | tf_op jit(solution)/shard_map/reshape | solution.py:273
  49.0 0.0 collective-permute-done.7
  49.0 0.3 reshape.34
  49.3 0.8 %copy.19 = f32[27,2,16,64]{3,2,1,0:T(8,128)} copy(f32[27,2,16,64]{3,1,2,0:T(2,128)S(1)} %bitcast.43) | data formatting | bytes 442368 | tf_op jit(solution)/shard_map/transpose | solution.py:283
  50.1 0.7 %reshape.33 = f32[3,3,3,4,32]{4,3,2,1,0:T(4,128)} reshape(f32[27,128]{1,0:T(8,128)S(1)} %slice_multiply_fusion.1) | data formatting | bytes 27648 | tf_op jit(solution)/shard_map/reshape | solution.py:282
  (17 shorter events, 0.3 us)
Async XLA Ops:
  1.5 1.1 %copy-start.3 = (bf16[8,8,4,128]{3,1,2,0:T(8,128)(2,1)}, bf16[8,8,4,128]{3,1,2,0:T(8,128)(2,1)S(1)}, u32[]{:S(2)}) copy-start(bf16[8,8,4,128]{3,1,2,0:T(8,128)(2,1)S(1)} %copy.25) | copy-start | bytes 196612
  1.5 2.5 %copy-start.1 = (bf16[1,4,4,16,512]{4,3,2,1,0:T(8,128)(2,1)S(1)}, bf16[1,4,4,16,512]{4,3,2,1,0:T(8,128)(2,1)}, u32[]{:S(2)}) copy-start(bf16[1,4,4,16,512]{4,3,2,1,0:T(8,128)(2,1)} %vo_ref.1) | copy-start | bytes 786436
  2.6 4.5 %copy-start.8 = (bf16[32,4,3,3,3]{0,1,4,3,2:T(4,128)(2,1)S(1)}, bf16[32,4,3,3,3]{0,1,4,3,2:T(4,128)(2,1)}, u32[]{:S(2)}) copy-start(bf16[32,4,3,3,3]{0,1,4,3,2:T(4,128)(2,1)} %param.5) | copy-start | bytes 20740
  2.6 4.6 %copy-start.6 = (bf16[64,32,3,3,3]{0,1,4,3,2:T(8,128)(2,1)S(1)}, bf16[64,32,3,3,3]{0,1,4,3,2:T(8,128)(2,1)}, u32[]{:S(2)}) copy-start(bf16[64,32,3,3,3]{0,1,4,3,2:T(8,128)(2,1)} %param.6) | copy-start | bytes 331780
  2.6 7.0 %collective-permute-start.1 = (bf16[320,512]{1,0:T(8,128)(2,1)S(1)}, bf16[320,512]{1,0:T(8,128)(2,1)S(1)}, u32[]{:S(2)}, u32[]{:S(2)}) collective-permute-start(bf16[320,512]{1,0:T(8,128)(2,1)S(1)} %pad_maximum_fusion), channel_id=1, source_target_pairs={{4,0},{8,4},{12,8},{16,12},{20,16},{24,20},{28,24},{5,1},{9,5},{13... | collective-permute-start | bytes 983048 | tf_op jit(solution)/shard_map/ppermute | solution.py:17
  4.0 5.5 %collective-permute-start = (bf16[1,4,3,16,512]{4,3,2,1,0:T(8,128)(2,1)S(1)}, bf16[1,4,3,16,512]{4,3,2,1,0:T(8,128)(2,1)S(1)}, u32[]{:S(2)}, u32[]{:S(2)}) collective-permute-start(bf16[1,4,3,16,512]{4,3,2,1,0:T(8,128)(2,1)S(1)} %slice.30), channel_id=1, source_target_pairs={{0,4},{4,8},{8,12},{12,16},{16,20},{20,24},{24,28},{1,5},{5,9},{9,... | collective-permute-start | bytes 589832 | tf_op jit(solution)/shard_map/ppermute | solution.py:17
  8.7 0.9 %copy-start = (bf16[64,3,3,2,2,32]{0,5,4,3,2,1:T(8,128)(2,1)}, bf16[64,3,3,2,2,32]{0,5,4,3,2,1:T(8,128)(2,1)S(1)}, u32[]{:S(2)}) copy-start(bf16[64,3,3,2,2,32]{0,5,4,3,2,1:T(8,128)(2,1)S(1)} %copy.15) | copy-start | bytes 442372
  9.5 0.7 %copy-start.7 = (bf16[1,4,3,16,512]{4,3,2,1,0:T(8,128)(2,1)}, bf16[1,4,3,16,512]{4,3,2,1,0:T(8,128)(2,1)S(1)}, u32[]{:S(2)}) copy-start(bf16[1,4,3,16,512]{4,3,2,1,0:T(8,128)(2,1)S(1)} %collective-permute-done.vb_ref) | copy-start | bytes 589828
  9.6 0.8 %copy-start.4 = (bf16[320,512]{1,0:T(8,128)(2,1)}, bf16[320,512]{1,0:T(8,128)(2,1)S(1)}, u32[]{:S(2)}) copy-start(bf16[320,512]{1,0:T(8,128)(2,1)S(1)} %collective-permute-done.1.va_ref) | copy-start | bytes 983044
  16.9 4.9 %copy-start.2 = (f32[464,128]{1,0:T(8,128)S(1)}, f32[464,128]{1,0:T(8,128)}, u32[]{:S(2)}) copy-start(f32[464,128]{1,0:T(8,128)} %get-tuple-element.9) | copy-start | bytes 712708
  17.9 3.9 %collective-permute-start.2 = (f32[232,128]{1,0:T(8,128)S(1)}, f32[232,128]{1,0:T(8,128)S(1)}, u32[]{:S(2)}, u32[]{:S(2)}) collective-permute-start(f32[232,128]{1,0:T(8,128)S(1)} %slice_select_fusion), channel_id=1, source_target_pairs={{0,4},{4,0},{8,12},{12,8},{16,20},{20,16},{24,28},{28,24},{1,5},{5... | collective-permute-start | bytes 356360 | tf_op jit(solution)/shard_map/ppermute | solution.py:37
  21.8 5.6 %collective-permute-start.3 = (f32[232,128]{1,0:T(8,128)S(1)}, f32[232,128]{1,0:T(8,128)S(1)}, u32[]{:S(2)}, u32[]{:S(2)}) collective-permute-start(f32[232,128]{1,0:T(8,128)S(1)} %select_add_fusion), channel_id=1, source_target_pairs={{0,1},{1,0},{2,3},{3,2},{4,5},{5,4},{6,7},{7,6},{8,9},{9,8},{10,11... | collective-permute-start | bytes 356360 | tf_op jit(solution)/shard_map/ppermute | solution.py:39
  27.4 8.2 %collective-permute-start.4 = (f32[232,128]{1,0:T(8,128)S(1)}, f32[232,128]{1,0:T(8,128)S(1)}, u32[]{:S(2)}, u32[]{:S(2)}) collective-permute-start(f32[232,128]{1,0:T(8,128)S(1)} %add.24), channel_id=1, source_target_pairs={{0,2},{1,3},{2,0},{3,1},{4,6},{5,7},{6,4},{7,5},{8,10},{9,11},{10,... | collective-permute-start | bytes 356360 | tf_op jit(solution)/shard_map/ppermute | solution.py:39
  35.6 6.7 %collective-permute-start.5 = (f32[232,128]{1,0:T(8,128)S(1)}, f32[232,128]{1,0:T(8,128)S(1)}, u32[]{:S(2)}, u32[]{:S(2)}) collective-permute-start(f32[232,128]{1,0:T(8,128)S(1)} %add.25), channel_id=1, source_target_pairs={{0,8},{4,12},{8,0},{12,4},{16,24},{20,28},{24,16},{28,20},{1,9},{5... | collective-permute-start | bytes 356360 | tf_op jit(solution)/shard_map/ppermute | solution.py:39
  42.3 5.2 %copy-start.5 = (bf16[512,256]{1,0:T(8,128)(2,1)S(1)}, bf16[512,256]{1,0:T(8,128)(2,1)}, u32[]{:S(2)}) copy-start(bf16[512,256]{1,0:T(8,128)(2,1)} %get-tuple-element.8) | copy-start | bytes 786436
  42.3 5.1 %collective-permute-start.6 = (f32[232,128]{1,0:T(8,128)S(1)}, f32[232,128]{1,0:T(8,128)S(1)}, u32[]{:S(2)}, u32[]{:S(2)}) collective-permute-start(f32[232,128]{1,0:T(8,128)S(1)} %add.26), channel_id=1, source_target_pairs={{0,16},{4,20},{8,24},{12,28},{16,0},{20,4},{24,8},{28,12},{1,17},{... | collective-permute-start | bytes 356360 | tf_op jit(solution)/shard_map/ppermute | solution.py:39
  47.4 1.6 %collective-permute-start.7 = (f32[232,128]{1,0:T(8,128)S(1)}, f32[232,128]{1,0:T(8,128)S(1)}, u32[]{:S(2)}, u32[]{:S(2)}) collective-permute-start(f32[232,128]{1,0:T(8,128)S(1)} %add.27), channel_id=1, source_target_pairs={{0,4},{4,0},{8,12},{12,8},{16,20},{20,16},{24,28},{28,24},{1,5},{5... | collective-permute-start | bytes 356360 | tf_op jit(solution)/shard_map/ppermute | solution.py:40
  47.4 0.9 %copy-start.9 = (bf16[64,512]{1,0:T(8,128)(2,1)S(1)}, bf16[64,512]{1,0:T(8,128)(2,1)}, u32[]{:S(2)}) copy-start(bf16[64,512]{1,0:T(8,128)(2,1)} %get-tuple-element.7) | copy-start | bytes 196612
